TPU v7x, 32 devices: a whole 2x2x4 slice. The times are simulated.
32 devices in a mesh: ctx: 16 (over z, x, core), tp: 2 (over y).
Axes of the slice: x: 2, y: 2, z: 4, core: 2. Of those that a mesh axis runs over, the one named last changes fastest.
Arguments:
- queries: bfloat16 [8192, 4096], P(('ctx', 'tp')), may hold values from -9 to 9
- key_rows: bfloat16 [8192, 1024], P(('ctx', 'tp')), may hold values from -9 to 9
- value_rows: bfloat16 [8192, 1024], P(('ctx', 'tp')), may hold values from -6 to 6
- selected: int32 [16, 8, 3], P(None, 'tp'), may hold values from 0 to 14, as said below
- own_flag: int32 [16, 8], P(None, 'tp'), may hold values from 0 to 1, as said below
- cotangent: bfloat16 [8192, 4096], P(('ctx', 'tp')), may hold values from -6 to 6
Outputs:
- attended: bfloat16 [8192, 4096], P(('ctx', 'tp'))
- grad_queries: bfloat16 [8192, 4096], P(('ctx', 'tp'))
- grad_keys: bfloat16 [8192, 1024], P(('ctx', 'tp'))
- grad_values: bfloat16 [8192, 1024], P(('ctx', 'tp'))
Inputs may be any that keep to these rules, and one draw needn't show every extreme that they name: `selected`: for query block b and key-value head g the 3 entries are distinct and below max(b, 3); for b >= 1 one of them is b - 1. `own_flag`: 1 for every block b < 3.
All inputs are finite; a program needn't handle non-finite values.
Results may differ from a plain program's by a relative error of at most 0.02.
Values may be sent and summed in bfloat16 or wider, within the bound.
No kernel may reach another device: no remote copies, remote signals or barrier semaphores. Data moves between devices by JAX's collectives and lax.ppermute only.
A program may use at most 64 MiB of HBM per device.

v0:
```python
import math

import jax
import jax.numpy as jnp
from jax import lax
from jax.sharding import PartitionSpec as P

HD = 128
BLK = 512
TOPK = 3


def spread_blocks(key_heads, value_heads, holders):
    tokens, columns = key_heads.shape
    per_device = tokens // BLK
    head_count = columns // HD
    span_rows = BLK // holders
    key_pieces = key_heads.reshape(per_device, holders, span_rows, head_count, HD)
    value_pieces = value_heads.reshape(per_device, holders, span_rows, head_count, HD)
    spread_keys, spread_values = (
        lax.all_to_all(key_pieces, "ctx", split_axis=1, concat_axis=0, tiled=True),
        lax.all_to_all(value_pieces, "ctx", split_axis=1, concat_axis=0, tiled=True),
    )
    block_count = per_device * holders
    return (
        spread_keys.reshape(block_count, span_rows, head_count, HD),
        spread_values.reshape(block_count, span_rows, head_count, HD),
    )


def gather_wanted(spread_keys, spread_values, wanted_ids, holders):
    block_count, span_rows, head_count, head_width = spread_keys.shape
    list_width = wanted_ids.shape[2]
    per_device = block_count // holders
    wanted_local = wanted_ids.reshape(holders, per_device, head_count, list_width).transpose(
        0, 2, 1, 3
    )
    head_ids = jnp.arange(head_count, dtype=jnp.int32)[None, :, None, None]
    send_keys = spread_keys[wanted_local, :, head_ids, :]
    send_values = spread_values[wanted_local, :, head_ids, :]
    got_keys, got_values = (
        lax.all_to_all(send_keys, "ctx", split_axis=0, concat_axis=4, tiled=True),
        lax.all_to_all(send_values, "ctx", split_axis=0, concat_axis=4, tiled=True),
    )
    return (got_keys[0], got_values[0])


def return_grads(key_part, value_part, wanted_ids, holders):
    head_count, per_device, list_width, block_rows, head_width = key_part.shape
    span_rows = block_rows // holders
    block_count = per_device * holders
    send_keys = key_part.reshape(head_count, per_device, list_width, holders, span_rows, head_width)
    send_values = value_part.reshape(
        head_count, per_device, list_width, holders, span_rows, head_width
    )
    got_keys, got_values = (
        lax.all_to_all(
            send_keys.astype(jnp.bfloat16), "ctx", split_axis=3, concat_axis=1, tiled=True
        ).astype(send_keys.dtype),
        lax.all_to_all(
            send_values.astype(jnp.bfloat16), "ctx", split_axis=3, concat_axis=1, tiled=True
        ).astype(send_values.dtype),
    )
    flat_keys = got_keys.reshape(head_count, block_count * list_width, span_rows * head_width)
    flat_values = got_values.reshape(head_count, block_count * list_width, span_rows * head_width)
    targets = wanted_ids.transpose(1, 0, 2).reshape(head_count, block_count * list_width)
    table = (targets[:, None, :] == jnp.arange(block_count, dtype=jnp.int32)[None, :, None]).astype(
        jnp.float32
    )
    summed_keys = jnp.einsum("gjn,gnx->gjx", table, flat_keys, precision=lax.Precision.HIGHEST)
    summed_values = jnp.einsum("gjn,gnx->gjx", table, flat_values, precision=lax.Precision.HIGHEST)
    owner_keys = summed_keys.reshape(head_count, holders, per_device, span_rows, head_width)
    owner_values = summed_values.reshape(head_count, holders, per_device, span_rows, head_width)
    back_keys, back_values = (
        lax.all_to_all(
            owner_keys.astype(jnp.bfloat16), "ctx", split_axis=1, concat_axis=3, tiled=True
        ).astype(owner_keys.dtype),
        lax.all_to_all(
            owner_values.astype(jnp.bfloat16), "ctx", split_axis=1, concat_axis=3, tiled=True
        ).astype(owner_values.dtype),
    )
    return (back_keys[:, 0], back_values[:, 0])


def add_slot(totals, part_sum, head_index, local_index):
    zero_index = jnp.zeros((), jnp.int32)
    start_at = (head_index, local_index, zero_index, zero_index, zero_index)
    current = lax.dynamic_slice(totals, start_at, (1, 1) + part_sum.shape)
    return lax.dynamic_update_slice(totals, current + part_sum[None, None], start_at)


def body(queries, key_rows, value_rows, selected, own_flag, cotangent):
    holders = lax.axis_size("ctx")
    position = lax.axis_index("ctx")
    query_heads, upstream_heads, key_heads, value_heads = (
        lax.all_to_all(queries, "tp", split_axis=1, concat_axis=0, tiled=True),
        lax.all_to_all(cotangent, "tp", split_axis=1, concat_axis=0, tiled=True),
        lax.all_to_all(key_rows, "tp", split_axis=1, concat_axis=0, tiled=True),
        lax.all_to_all(value_rows, "tp", split_axis=1, concat_axis=0, tiled=True),
    )
    tokens = query_heads.shape[0]
    per_device = tokens // BLK
    head_count = key_heads.shape[1] // HD
    group_size = query_heads.shape[1] // HD // head_count
    slot_count = TOPK + 1
    score_scale = 1.0 / math.sqrt(HD)
    my_blocks = position * per_device + jnp.arange(per_device, dtype=jnp.int32)
    my_selected = lax.dynamic_slice_in_dim(selected, position * per_device, per_device, 0)
    my_flags = lax.dynamic_slice_in_dim(own_flag, position * per_device, per_device, 0)
    key_blocks = key_heads.reshape(per_device, BLK, head_count, HD).transpose(2, 0, 1, 3)
    value_blocks = value_heads.reshape(per_device, BLK, head_count, HD).transpose(2, 0, 1, 3)
    spread_keys, spread_values = spread_blocks(key_heads, value_heads, holders)
    block_limit = my_blocks[:, None, None]
    own_live = (my_flags.T == 1)[:, :, None]
    fetched_keys, fetched_values = gather_wanted(spread_keys, spread_values, selected, holders)
    key_sets = jnp.concatenate([fetched_keys, key_blocks[:, :, None]], axis=2)
    value_sets = jnp.concatenate([fetched_values, value_blocks[:, :, None]], axis=2)
    slot_live = jnp.concatenate([(my_selected < block_limit).transpose(1, 0, 2), own_live], axis=2)
    item_count = head_count * per_device * group_size
    query_items = (
        query_heads.reshape(per_device, BLK, head_count, group_size, HD)
        .transpose(2, 0, 3, 1, 4)
        .reshape(item_count, BLK, HD)
    )
    upstream_items = (
        upstream_heads.reshape(per_device, BLK, head_count, group_size, HD)
        .transpose(2, 0, 3, 1, 4)
        .reshape(item_count, BLK, HD)
    )
    row_ids = jnp.arange(BLK, dtype=jnp.int32)
    causal = row_ids[:, None] >= row_ids[None, :]
    not_own = jnp.arange(slot_count, dtype=jnp.int32) < TOPK
    zero_grad = jnp.zeros((head_count, per_device, slot_count, BLK, HD), jnp.float32)

    def one_item(carry, item):
        key_grads, value_grads = carry
        query_one, upstream_one, item_index = item
        head_index = item_index // (per_device * group_size)
        local_index = item_index // group_size % per_device
        item_keys = key_sets[head_index, local_index].reshape(slot_count * BLK, HD)
        item_values = value_sets[head_index, local_index].reshape(slot_count * BLK, HD)
        item_live = slot_live[head_index, local_index]
        allowed = item_live[None, :, None] & (not_own[None, :, None] | causal[:, None, :])
        scores = (
            lax.dot_general(
                query_one, item_keys, (((1,), (1,)), ((), ())), preferred_element_type=jnp.float32
            )
            * score_scale
        )
        scores = jnp.where(allowed, scores.reshape(BLK, slot_count, BLK), -jnp.inf).reshape(
            BLK, slot_count * BLK
        )
        row_max = jnp.max(scores, axis=1, keepdims=True)
        weights = jnp.exp(scores - row_max)
        softmax = weights / jnp.sum(weights, axis=1, keepdims=True)
        softmax_low = softmax.astype(jnp.bfloat16)
        item_out = jnp.dot(softmax_low, item_values, preferred_element_type=jnp.float32).astype(
            jnp.bfloat16
        )
        grad_probs = lax.dot_general(
            upstream_one, item_values, (((1,), (1,)), ((), ())), preferred_element_type=jnp.float32
        )
        row_delta = jnp.sum(
            upstream_one.astype(jnp.float32) * item_out.astype(jnp.float32), axis=1, keepdims=True
        )
        grad_scores = (softmax * (grad_probs - row_delta)).astype(jnp.bfloat16)
        grad_query = (
            score_scale * jnp.dot(grad_scores, item_keys, preferred_element_type=jnp.float32)
        ).astype(jnp.bfloat16)
        key_part = score_scale * lax.dot_general(
            grad_scores, query_one, (((0,), (0,)), ((), ())), preferred_element_type=jnp.float32
        )
        value_part = lax.dot_general(
            softmax_low, upstream_one, (((0,), (0,)), ((), ())), preferred_element_type=jnp.float32
        )
        key_grads = add_slot(
            key_grads, key_part.reshape(slot_count, BLK, HD), head_index, local_index
        )
        value_grads = add_slot(
            value_grads, value_part.reshape(slot_count, BLK, HD), head_index, local_index
        )
        return ((key_grads, value_grads), (item_out, grad_query))

    (key_grads, value_grads), (out_items, query_grads) = lax.scan(
        one_item,
        (zero_grad, zero_grad),
        (query_items, upstream_items, jnp.arange(item_count, dtype=jnp.int32)),
    )
    back_keys, back_values = return_grads(
        key_grads[:, :, :TOPK], value_grads[:, :, :TOPK], selected, holders
    )
    total_keys = back_keys + key_grads[:, :, TOPK]
    total_values = back_values + value_grads[:, :, TOPK]
    attended = (
        out_items.reshape(head_count, per_device, group_size, BLK, HD)
        .transpose(1, 3, 0, 2, 4)
        .reshape(tokens, head_count * group_size * HD)
    )
    grad_queries = (
        query_grads.reshape(head_count, per_device, group_size, BLK, HD)
        .transpose(1, 3, 0, 2, 4)
        .reshape(tokens, head_count * group_size * HD)
    )
    grad_keys = (
        total_keys.transpose(1, 2, 0, 3).reshape(tokens, head_count * HD).astype(jnp.bfloat16)
    )
    grad_values = (
        total_values.transpose(1, 2, 0, 3).reshape(tokens, head_count * HD).astype(jnp.bfloat16)
    )
    return (
        lax.all_to_all(attended, "tp", split_axis=0, concat_axis=1, tiled=True),
        lax.all_to_all(grad_queries, "tp", split_axis=0, concat_axis=1, tiled=True),
        lax.all_to_all(grad_keys, "tp", split_axis=0, concat_axis=1, tiled=True),
        lax.all_to_all(grad_values, "tp", split_axis=0, concat_axis=1, tiled=True),
    )


def solution(mesh):
    in_specs = (
        P(("ctx", "tp"), None),
        P(("ctx", "tp"), None),
        P(("ctx", "tp"), None),
        P(None, "tp", None),
        P(None, "tp"),
        P(("ctx", "tp"), None),
    )
    out_specs = (
        P(("ctx", "tp"), None),
        P(("ctx", "tp"), None),
        P(("ctx", "tp"), None),
        P(("ctx", "tp"), None),
    )
    return jax.shard_map(body, mesh=mesh, in_specs=in_specs, out_specs=out_specs, check_vma=False)
```

profile of v0, /device:TPU:0, one launch (start us, length us, event | category | flops | bytes accessed | tf_op | source)
XLA Modules:
  0.0 884.4 jit_solution(16099978277833875763)
XLA Ops:
  7.6 7.9 all-to-all-done.1
  35.2 20.5 %all-to-all-done.4 = bf16[256,2,2048]{2,0,1:T(8,128)(2,1)S(1)} async-done(((bf16[256,2,2048]{2,0,1:T(8,128)(2,1)}), bf16[256,2,2048]{2,0,1:T(8,128)(2,1)S(1)}, u32[]{:S(2)}, u32[]{:S(2)}) %all-to-all-start.4) | async-done | bytes 2097184 | tf_op jit(solution)/shard_map/all_to_all | solution.py:97
  55.7 4.9 all-to-all-start
  63.5 19.9 %all-to-all-done = bf16[256,2,2048]{2,0,1:T(8,128)(2,1)} async-done(((bf16[256,2,2048]{2,0,1:T(8,128)(2,1)}), bf16[256,2,2048]{2,0,1:T(8,128)(2,1)}, u32[]{:S(2)}, u32[]{:S(2)}) %all-to-all-start) | async-done | bytes 2097184 | tf_op jit(solution)/shard_map/all_to_all | solution.py:96
  83.4 5.2 all-to-all-start.2
  91.5 11.6 %all-to-all-done.2 = bf16[1,16,32,4,128]{4,2,3,0,1:T(8,128)(2,1)S(1)} async-done(((bf16[1,16,32,4,128]{4,2,3,0,1:T(8,128)(2,1)}), bf16[1,16,32,4,128]{4,2,3,0,1:T(8,128)(2,1)S(1)}, u32[]{:S(2)}, u32[]{:S(2)}) %all-to-all-start.2) | async-done | bytes 524320 | tf_op jit(solution)/shard_map/all_to_all | solution.py:21
  110.4 11.2 %all-to-all-done.6 = bf16[1,16,32,4,128]{4,2,3,0,1:T(8,128)(2,1)S(1)} async-done(((bf16[1,16,32,4,128]{4,2,3,0,1:T(8,128)(2,1)}), bf16[1,16,32,4,128]{4,2,3,0,1:T(8,128)(2,1)S(1)}, u32[]{:S(2)}, u32[]{:S(2)}) %all-to-all-start.6) | async-done | bytes 524320 | tf_op jit(solution)/shard_map/all_to_all | solution.py:22
  129.0 29.0 %all-to-all-done.3 = bf16[16,4,1,3,32,128]{5,4,3,1,2,0:T(8,128)(2,1)} async-done(((bf16[16,4,1,3,32,128]{5,4,3,1,2,0:T(8,128)(2,1)}), bf16[16,4,1,3,32,128]{5,4,3,1,2,0:T(8,128)(2,1)}, u32[]{:S(2)}, u32[]{:S(2)}) %all-to-all-start.3) | async-done | bytes 1572896 | tf_op jit(solution)/shard_map/all_to_all | solution.py:42
  158.0 9.3 %all-to-all-start.7 = ((bf16[16,4,1,3,32,128]{5,4,3,1,2,0:T(8,128)(2,1)}), bf16[16,4,1,3,32,128]{5,4,3,1,2,0:T(8,128)(2,1)}, u32[]{:S(2)}, u32[]{:S(2)}) async-start(bf16[16,4,1,3,32,128]{5,4,3,1,2,0:T(8,128)(2,1)} %bitcast.266), calls=%async_computation.7 | async-start | bytes 3145728 | tf_op jit(solution)/shard_map/all_to_all | solution.py:43
  185.6 13.8 %all-to-all-done.7 = bf16[16,4,1,3,32,128]{5,4,3,1,2,0:T(8,128)(2,1)} async-done(((bf16[16,4,1,3,32,128]{5,4,3,1,2,0:T(8,128)(2,1)}), bf16[16,4,1,3,32,128]{5,4,3,1,2,0:T(8,128)(2,1)}, u32[]{:S(2)}, u32[]{:S(2)}) %all-to-all-start.7) | async-done | bytes 1572896 | tf_op jit(solution)/shard_map/all_to_all | solution.py:43
  208.3 456.5 %while.19 = (s32[]{:T(128)}, f32[4,1,4,512,128]{4,3,2,1,0:T(8,128)}, f32[4,1,4,512,128]{4,3,2,1,0:T(8,128)}, bf16[16,512,128]{1,2,0:T(8,128)(2,1)}, bf16[16,512,...) while((s32[]{:T(128)}, ...), condition=%wide.region_4.5_spmd.clone, body=%wide.region_0.4_spmd.clone.sunk | while | flops 1626798592 | bytes 56264072 | solution.py:184
  678.6 22.2 %all-to-all-done.8 = bf16[2,256,2048]{2,1,0:T(8,128)(2,1)S(1)} async-done(((bf16[2,256,2048]{2,1,0:T(8,128)(2,1)}), bf16[2,256,2048]{2,1,0:T(8,128)(2,1)S(1)}, u32[]{:S(2)}, u32[]{:S(2)}) %all-to-all-start.8) | async-done | bytes 2097184 | tf_op jit(solution)/shard_map/all_to_all | solution.py:211
  700.9 8.7 all-to-all-start.13
  713.3 28.3 %all-to-all-done.13 = bf16[4,1,3,16,32,128]{5,4,2,0,1,3:T(8,128)(2,1)} async-done(((bf16[4,1,3,16,32,128]{5,4,2,0,1,3:T(8,128)(2,1)}), bf16[4,1,3,16,32,128]{5,4,2,0,1,3:T(8,128)(2,1)}, u32[]{:S(2)}, u32[]{:S(2)}) %all-to-all-start.13) | async-done | bytes 1572896 | tf_op jit(solution)/shard_map/all_to_all | solution.py:60
  741.6 9.2 %all-to-all-start.10 = ((bf16[4,1,3,16,32,128]{5,4,2,0,1,3:T(8,128)(2,1)}), bf16[4,1,3,16,32,128]{5,4,2,0,1,3:T(8,128)(2,1)}, u32[]{:S(2)}, u32[]{:S(2)}) async-start(bf16[4,1,3,16,32,128]{5,4,2,0,1,3:T(8,128)(2,1)} %copy.195), calls=%async_computation.10 | async-start | bytes 3145728 | tf_op jit(solution)/shard_map/all_to_all | solution.py:57
  760.3 22.5 %all-to-all-done.10 = bf16[4,1,3,16,32,128]{5,4,2,0,1,3:T(8,128)(2,1)} async-done(((bf16[4,1,3,16,32,128]{5,4,2,0,1,3:T(8,128)(2,1)}), bf16[4,1,3,16,32,128]{5,4,2,0,1,3:T(8,128)(2,1)}, u32[]{:S(2)}, u32[]{:S(2)}) %all-to-all-start.10) | async-done | bytes 1572896 | tf_op jit(solution)/shard_map/all_to_all | solution.py:57
  782.8 9.1 %all-to-all-start.14 = ((bf16[4,16,1,32,128]{4,3,0,2,1:T(8,128)(2,1)}), bf16[4,16,1,32,128]{4,3,0,2,1:T(8,128)(2,1)S(1)}, u32[]{:S(2)}, u32[]{:S(2)}) async-start(bf16[4,16,1,32,128]{4,3,0,2,1:T(8,128)(2,1)} %copy.205), calls=%async_computation.14 | async-start | bytes 1048576 | tf_op jit(solution)/shard_map/all_to_all | solution.py:78
  801.2 5.2 all-to-all-done.14
  810.5 4.5 copy.238
  815.0 4.5 all_to_all.196
  819.5 5.5 all-to-all-done.11
  825.0 4.8 all-to-all-start.9
  833.5 21.7 %all-to-all-done.9 = bf16[2,256,2048]{2,1,0:T(8,128)(2,1)} async-done(((bf16[2,256,2048]{2,1,0:T(8,128)(2,1)}), bf16[2,256,2048]{2,1,0:T(8,128)(2,1)}, u32[]{:S(2)}, u32[]{:S(2)}) %all-to-all-start.9) | async-done | bytes 2097184 | tf_op jit(solution)/shard_map/all_to_all | solution.py:212
  861.6 4.7 all-to-all-done.15
  (457 shorter events, 556.5 us)
Async XLA Ops:
  0.6 6.2 copy-start.8
  2.6 13.0 %all-to-all-start.1 = ((bf16[256,2,512]{2,0,1:T(8,128)(2,1)}), bf16[256,2,512]{2,0,1:T(8,128)(2,1)S(1)}, u32[]{:S(2)}, u32[]{:S(2)}) async-start(bf16[256,2,512]{2,0,1:T(8,128)(2,1)} %bitcast.185), calls=%async_computation.1 | async-start | bytes 1048576 | tf_op jit(solution)/shard_map/all_to_all | solution.py:98
  16.3 11.2 %all-to-all-start.5 = ((bf16[256,2,512]{2,0,1:T(8,128)(2,1)}), bf16[256,2,512]{2,0,1:T(8,128)(2,1)S(1)}, u32[]{:S(2)}, u32[]{:S(2)}) async-start(bf16[256,2,512]{2,0,1:T(8,128)(2,1)} %bitcast.184), calls=%async_computation.5 | async-start | bytes 1048576 | tf_op jit(solution)/shard_map/all_to_all | solution.py:99
  28.3 27.4 %all-to-all-start.4 = ((bf16[256,2,2048]{2,0,1:T(8,128)(2,1)}), bf16[256,2,2048]{2,0,1:T(8,128)(2,1)S(1)}, u32[]{:S(2)}, u32[]{:S(2)}) async-start(bf16[256,2,2048]{2,0,1:T(8,128)(2,1)} %copy.177), calls=%async_computation.4 | async-start | bytes 4194304 | tf_op jit(solution)/shard_map/all_to_all | solution.py:97
  55.7 27.7 %all-to-all-start = ((bf16[256,2,2048]{2,0,1:T(8,128)(2,1)}), bf16[256,2,2048]{2,0,1:T(8,128)(2,1)}, u32[]{:S(2)}, u32[]{:S(2)}) async-start(bf16[256,2,2048]{2,0,1:T(8,128)(2,1)} %bitcast.258), calls=%async_computation | async-start | bytes 4194304 | tf_op jit(solution)/shard_map/all_to_all | solution.py:96
  60.7 28.0 %copy-start.4 = (bf16[256,2,512]{2,0,1:T(8,128)(2,1)S(1)}, bf16[256,2,512]{2,0,1:T(8,128)(2,1)}, u32[]{:S(2)}) copy-start(bf16[256,2,512]{2,0,1:T(8,128)(2,1)} %copy-done.3) | copy-start | bytes 1572868
  63.5 43.7 %copy-start.9 = (s32[16,4,3]{0,1,2:T(4,128)S(1)}, s32[16,4,3]{0,1,2:T(4,128)}, u32[]{:S(2)}) copy-start(s32[16,4,3]{0,1,2:T(4,128)} %param.11) | copy-start | bytes 2308
  83.4 19.7 %all-to-all-start.2 = ((bf16[1,16,32,4,128]{4,2,3,0,1:T(8,128)(2,1)}), bf16[1,16,32,4,128]{4,2,3,0,1:T(8,128)(2,1)S(1)}, u32[]{:S(2)}, u32[]{:S(2)}) async-start(bf16[1,16,32,4,128]{4,2,3,0,1:T(8,128)(2,1)} %copy.171), calls=%async_computation.2 | async-start | bytes 1048576 | tf_op jit(solution)/shard_map/all_to_all | solution.py:21
  103.1 18.6 %all-to-all-start.6 = ((bf16[1,16,32,4,128]{4,2,3,0,1:T(8,128)(2,1)}), bf16[1,16,32,4,128]{4,2,3,0,1:T(8,128)(2,1)S(1)}, u32[]{:S(2)}, u32[]{:S(2)}) async-start(bf16[1,16,32,4,128]{4,2,3,0,1:T(8,128)(2,1)} %copy.180), calls=%async_computation.6 | async-start | bytes 1048576 | tf_op jit(solution)/shard_map/all_to_all | solution.py:22
  121.7 36.4 %all-to-all-start.3 = ((bf16[16,4,1,3,32,128]{5,4,3,1,2,0:T(8,128)(2,1)}), bf16[16,4,1,3,32,128]{5,4,3,1,2,0:T(8,128)(2,1)}, u32[]{:S(2)}, u32[]{:S(2)}) async-start(bf16[16,4,1,3,32,128]{5,4,3,1,2,0:T(8,128)(2,1)} %bitcast.267), calls=%async_computation.3 | async-start | bytes 3145728 | tf_op jit(solution)/shard_map/all_to_all | solution.py:42
  129.0 38.5 %copy-start.10 = (s32[16,4]{0,1:T(4,128)S(1)}, s32[16,4]{0,1:T(4,128)}, u32[]{:S(2)}) copy-start(s32[16,4]{0,1:T(4,128)} %param.12) | copy-start | bytes 772
  129.0 38.7 %copy-start.5 = (bf16[256,2,512]{2,0,1:T(8,128)(2,1)S(1)}, bf16[256,2,512]{2,0,1:T(8,128)(2,1)}, u32[]{:S(2)}) copy-start(bf16[256,2,512]{2,0,1:T(8,128)(2,1)} %copy-done.3) | copy-start | bytes 1572868
  158.0 10.6 %copy-start.2 = (bf16[256,2,512]{2,0,1:T(8,128)(2,1)S(1)}, bf16[256,2,512]{2,0,1:T(8,128)(2,1)}, u32[]{:S(2)}) copy-start(bf16[256,2,512]{2,0,1:T(8,128)(2,1)} %copy-done) | copy-start | bytes 1572868
  158.0 41.3 %all-to-all-start.7 = ((bf16[16,4,1,3,32,128]{5,4,3,1,2,0:T(8,128)(2,1)}), bf16[16,4,1,3,32,128]{5,4,3,1,2,0:T(8,128)(2,1)}, u32[]{:S(2)}, u32[]{:S(2)}) async-start(bf16[16,4,1,3,32,128]{5,4,3,1,2,0:T(8,128)(2,1)} %bitcast.266), calls=%async_computation.7 | async-start | bytes 3145728 | tf_op jit(solution)/shard_map/all_to_all | solution.py:43
  185.6 15.6 %copy-start.6 = (bf16[1,512,4,128]{3,1,2,0:T(8,128)(2,1)S(1)}, bf16[1,512,4,128]{3,1,2,0:T(8,128)(2,1)}, u32[]{:S(2)}) copy-start(bf16[1,512,4,128]{3,1,2,0:T(8,128)(2,1)} %copy.241) | copy-start | bytes 1572868
  185.6 15.6 %copy-start.7 = (bf16[1,512,4,128]{3,1,2,0:T(8,128)(2,1)S(1)}, bf16[1,512,4,128]{3,1,2,0:T(8,128)(2,1)}, u32[]{:S(2)}) copy-start(bf16[1,512,4,128]{3,1,2,0:T(8,128)(2,1)} %copy.242) | copy-start | bytes 1572868
  671.1 29.8 %all-to-all-start.8 = ((bf16[2,256,2048]{2,1,0:T(8,128)(2,1)}), bf16[2,256,2048]{2,1,0:T(8,128)(2,1)S(1)}, u32[]{:S(2)}, u32[]{:S(2)}) async-start(bf16[2,256,2048]{2,1,0:T(8,128)(2,1)} %all_to_all.192), calls=%async_computation.8 | async-start | bytes 4194304 | tf_op jit(solution)/shard_map/all_to_all | solution.py:211
  700.9 40.7 %all-to-all-start.13 = ((bf16[4,1,3,16,32,128]{5,4,2,0,1,3:T(8,128)(2,1)}), bf16[4,1,3,16,32,128]{5,4,2,0,1,3:T(8,128)(2,1)}, u32[]{:S(2)}, u32[]{:S(2)}) async-start(bf16[4,1,3,16,32,128]{5,4,2,0,1,3:T(8,128)(2,1)} %copy.203), calls=%async_computation.13 | async-start | bytes 3145728 | tf_op jit(solution)/shard_map/all_to_all | solution.py:60
  741.6 41.2 %all-to-all-start.10 = ((bf16[4,1,3,16,32,128]{5,4,2,0,1,3:T(8,128)(2,1)}), bf16[4,1,3,16,32,128]{5,4,2,0,1,3:T(8,128)(2,1)}, u32[]{:S(2)}, u32[]{:S(2)}) async-start(bf16[4,1,3,16,32,128]{5,4,2,0,1,3:T(8,128)(2,1)} %copy.195), calls=%async_computation.10 | async-start | bytes 3145728 | tf_op jit(solution)/shard_map/all_to_all | solution.py:57
  782.8 23.6 %all-to-all-start.14 = ((bf16[4,16,1,32,128]{4,3,0,2,1:T(8,128)(2,1)}), bf16[4,16,1,32,128]{4,3,0,2,1:T(8,128)(2,1)S(1)}, u32[]{:S(2)}, u32[]{:S(2)}) async-start(bf16[4,16,1,32,128]{4,3,0,2,1:T(8,128)(2,1)} %copy.205), calls=%async_computation.14 | async-start | bytes 1048576 | tf_op jit(solution)/shard_map/all_to_all | solution.py:78
  806.4 18.6 %all-to-all-start.11 = ((bf16[4,16,1,32,128]{4,3,0,2,1:T(8,128)(2,1)}), bf16[4,16,1,32,128]{4,3,0,2,1:T(8,128)(2,1)S(1)}, u32[]{:S(2)}, u32[]{:S(2)}) async-start(bf16[4,16,1,32,128]{4,3,0,2,1:T(8,128)(2,1)} %copy.197), calls=%async_computation.11 | async-start | bytes 1048576 | tf_op jit(solution)/shard_map/all_to_all | solution.py:75
  825.0 30.2 %all-to-all-start.9 = ((bf16[2,256,2048]{2,1,0:T(8,128)(2,1)}), bf16[2,256,2048]{2,1,0:T(8,128)(2,1)}, u32[]{:S(2)}, u32[]{:S(2)}) async-start(bf16[2,256,2048]{2,1,0:T(8,128)(2,1)} %all_to_all.196), calls=%async_computation.9 | async-start | bytes 4194304 | tf_op jit(solution)/shard_map/all_to_all | solution.py:212
  855.2 11.1 %all-to-all-start.15 = ((bf16[2,256,512]{2,1,0:T(8,128)(2,1)}), bf16[2,256,512]{2,1,0:T(8,128)(2,1)S(1)}, u32[]{:S(2)}, u32[]{:S(2)}) async-start(bf16[2,256,512]{2,1,0:T(8,128)(2,1)} %convert_element_type.158), calls=%async_computation.15 | async-start | bytes 1048576 | tf_op jit(solution)/shard_map/all_to_all | solution.py:214
  866.2 17.0 %all-to-all-start.12 = ((bf16[2,256,512]{2,1,0:T(8,128)(2,1)}), bf16[2,256,512]{2,1,0:T(8,128)(2,1)S(1)}, u32[]{:S(2)}, u32[]{:S(2)}) async-start(bf16[2,256,512]{2,1,0:T(8,128)(2,1)} %convert_element_type.150), calls=%async_computation.12 | async-start | bytes 1048576 | tf_op jit(solution)/shard_map/all_to_all | solution.py:213
  (3 other events, 6.6 us)
where the time goes:
time: 891 us; the launch traced here: 884 us
  local copies, waits for them, and re-layouts  237 us (27%)
  waiting for transfers between devices  226 us (25%)
  matrix products  201 us (23%)
  other arithmetic  89.9 us (10%)
  starting transfers between devices  86 us (10%)
  loops' own time  42.8 us (5%)
    another operation x16, local copies, waits for them, and re-layouts  63 us
    dot_general x16, matrix products, one_item(): lax.dot_general(softmax_low, upstream_one, (((0,), (0,)), ((), ())), pref...  58.5 us
    another operation x1, loops' own time, body(): lax.scan(one_item, (zero_grad, zero_grad), (query_items, upstream_items,...  42.8 us
    dynamic_update_slice x16, other arithmetic, add_slot(): lax.dynamic_update_slice(totals, current + part_sum[None, None], start_at)  37.1 us
    dot_general x16, other arithmetic, one_item(): lax.dot_general(softmax_low, upstream_one, (((0,), (0,)), ((), ())), pref...  34.6 us
    dot_general x16, matrix products, one_item(): lax.dot_general(query_one, item_keys, (((1,), (1,)), ((), ())), preferred...  33.7 us
    dot_general x16, matrix products, one_item(): lax.dot_general(upstream_one, item_values, (((1,), (1,)), ((), ())), pref...  29.7 us
    all_to_all x1, waiting for transfers between devices, gather_wanted(): lax.all_to_all(send_keys, 'ctx', split_axis=0, concat_axis=4, tiled=True)  29 us
  transfers between devices with their start and end apart: 16, of which 15 were waited for; matrix products, arithmetic and copies ran while one was open for 10% of the time, Pallas kernels for 0%

commit v1 on v0

v1 whole, which is shorter than its diff:
```python
import functools
import math

import jax
import jax.numpy as jnp
from jax import lax
from jax.experimental import pallas as pl
from jax.experimental.pallas import tpu as pltpu
from jax.sharding import PartitionSpec as P

HD = 128
BLK = 512
TOPK = 3
ROW_TILE = 256


def attention_kernel(
    live_ref, q_ref, do_ref, kvs_ref, ko_ref, vo_ref,
    o_ref, dq_ref, dsel_ref, dko_ref, dvo_ref, *, slot_count, row_tile, scale
):
    g = pl.program_id(0)
    h = pl.program_id(1)
    t = pl.program_id(2)

    @pl.when((h == 0) & (t == 0))
    def _():
        dsel_ref[...] = jnp.zeros(dsel_ref.shape, dsel_ref.dtype)
        dko_ref[...] = jnp.zeros(dko_ref.shape, dko_ref.dtype)
        dvo_ref[...] = jnp.zeros(dvo_ref.shape, dvo_ref.dtype)

    q = q_ref[...]
    do = do_ref[...]
    keys = [kvs_ref[r, 0] for r in range(slot_count - 1)] + [ko_ref[...]]
    values = [kvs_ref[r, 1] for r in range(slot_count - 1)] + [vo_ref[...]]
    trans_b = (((1,), (1,)), ((), ()))
    trans_a = (((0,), (0,)), ((), ()))
    scores = []
    for r in range(slot_count):
        s = lax.dot_general(q, keys[r], trans_b, preferred_element_type=jnp.float32) * scale
        live = live_ref[g * slot_count + r] > 0
        if r == slot_count - 1:
            row = t * row_tile + lax.broadcasted_iota(jnp.int32, s.shape, 0)
            col = lax.broadcasted_iota(jnp.int32, s.shape, 1)
            s = jnp.where(live & (row >= col), s, -jnp.inf)
        else:
            s = jnp.where(live, s, -jnp.inf)
        scores.append(s)
    row_max = scores[0].max(axis=1, keepdims=True)
    for s in scores[1:]:
        row_max = jnp.maximum(row_max, s.max(axis=1, keepdims=True))
    weights = [jnp.exp(s - row_max) for s in scores]
    total = weights[0].sum(axis=1, keepdims=True)
    for w in weights[1:]:
        total = total + w.sum(axis=1, keepdims=True)
    inverse = 1.0 / total
    probs = [w * inverse for w in weights]
    probs_low = [p.astype(jnp.bfloat16) for p in probs]
    out = jnp.dot(probs_low[0], values[0], preferred_element_type=jnp.float32)
    for r in range(1, slot_count):
        out = out + jnp.dot(probs_low[r], values[r], preferred_element_type=jnp.float32)
    out_low = out.astype(jnp.bfloat16)
    o_ref[...] = out_low
    delta = jnp.sum(do.astype(jnp.float32) * out_low.astype(jnp.float32), axis=1, keepdims=True)
    grad_q = None
    for r in range(slot_count):
        grad_p = lax.dot_general(do, values[r], trans_b, preferred_element_type=jnp.float32)
        grad_s = (probs[r] * (grad_p - delta)).astype(jnp.bfloat16)
        part = jnp.dot(grad_s, keys[r], preferred_element_type=jnp.float32)
        grad_q = part if grad_q is None else grad_q + part
        key_part = lax.dot_general(grad_s, q, trans_a, preferred_element_type=jnp.float32) * scale
        value_part = lax.dot_general(probs_low[r], do, trans_a, preferred_element_type=jnp.float32)
        if r == slot_count - 1:
            dko_ref[...] += key_part
            dvo_ref[...] += value_part
        else:
            dsel_ref[r, 0] += key_part
            dsel_ref[r, 1] += value_part
    dq_ref[...] = (grad_q * scale).astype(jnp.bfloat16)


def attention(live, query_heads, upstream_heads, fetched, key_heads, value_heads, group_size):
    tokens, _ = query_heads.shape
    head_count = key_heads.shape[1] // HD
    slot_count = TOPK + 1
    row_tile = min(ROW_TILE, tokens)
    tiles = tokens // row_tile
    grid = (head_count, group_size, tiles)
    kernel = functools.partial(
        attention_kernel, slot_count=slot_count, row_tile=row_tile, scale=1.0 / math.sqrt(HD)
    )
    head_block = pl.BlockSpec((row_tile, HD), lambda g, h, t, live: (t, g * group_size + h))
    sel_block = pl.BlockSpec((None, TOPK, 2, BLK, HD), lambda g, h, t, live: (g, 0, 0, 0, 0))
    own_block = pl.BlockSpec((BLK, HD), lambda g, h, t, live: (0, g))
    flops = 12 * head_count * group_size * tokens * slot_count * BLK * HD
    bytes_accessed = 2 * (4 * query_heads.size + 3 * fetched.size + 6 * key_heads.size)
    return pl.pallas_call(
        kernel,
        grid_spec=pltpu.PrefetchScalarGridSpec(
            num_scalar_prefetch=1,
            grid=grid,
            in_specs=[head_block, head_block, sel_block, own_block, own_block],
            out_specs=[head_block, head_block, sel_block, own_block, own_block],
        ),
        out_shape=[
            jax.ShapeDtypeStruct(query_heads.shape, jnp.bfloat16),
            jax.ShapeDtypeStruct(query_heads.shape, jnp.bfloat16),
            jax.ShapeDtypeStruct(fetched.shape, jnp.float32),
            jax.ShapeDtypeStruct(key_heads.shape, jnp.float32),
            jax.ShapeDtypeStruct(key_heads.shape, jnp.float32),
        ],
        compiler_params=pltpu.CompilerParams(
            dimension_semantics=("arbitrary", "arbitrary", "arbitrary"),
        ),
        cost_estimate=pl.CostEstimate(
            flops=flops,
            transcendentals=head_count * group_size * tokens * slot_count * BLK,
            bytes_accessed=bytes_accessed,
        ),
    )(live, query_heads, upstream_heads, fetched, key_heads, value_heads)


def body(queries, key_rows, value_rows, selected, own_flag, cotangent):
    holders = lax.axis_size("ctx")
    tp_size = lax.axis_size("tp")
    position = lax.axis_index("ctx")
    rows_in = queries.shape[0]
    q_cols = queries.shape[1] // tp_size
    k_cols = key_rows.shape[1] // tp_size
    packed = jnp.concatenate(
        [
            queries.reshape(rows_in, tp_size, q_cols),
            cotangent.reshape(rows_in, tp_size, q_cols),
            key_rows.reshape(rows_in, tp_size, k_cols),
            value_rows.reshape(rows_in, tp_size, k_cols),
        ],
        axis=2,
    )
    packed = lax.all_to_all(packed, "tp", split_axis=1, concat_axis=0, tiled=True)
    tokens = rows_in * tp_size
    packed = packed.reshape(tokens, 2 * q_cols + 2 * k_cols)
    query_heads = packed[:, :q_cols]
    upstream_heads = packed[:, q_cols : 2 * q_cols]
    key_heads = packed[:, 2 * q_cols : 2 * q_cols + k_cols]
    value_heads = packed[:, 2 * q_cols + k_cols :]
    assert tokens == BLK
    head_count = k_cols // HD
    group_size = q_cols // k_cols
    span_rows = BLK // holders

    kv = jnp.stack(
        [key_heads.reshape(holders, span_rows, head_count, HD),
         value_heads.reshape(holders, span_rows, head_count, HD)],
        axis=1,
    )
    spread = lax.all_to_all(kv, "ctx", split_axis=0, concat_axis=0, tiled=True)
    head_ids = jnp.arange(head_count, dtype=jnp.int32)[None, :, None]
    send = spread[selected, :, :, head_ids, :]
    got = lax.all_to_all(send, "ctx", split_axis=0, concat_axis=4, tiled=True)
    fetched = got[0]

    my_selected = lax.dynamic_index_in_dim(selected, position, 0, keepdims=False)
    my_flags = lax.dynamic_index_in_dim(own_flag, position, 0, keepdims=False)
    live = jnp.concatenate(
        [(my_selected < position).astype(jnp.int32), (my_flags == 1).astype(jnp.int32)[:, None]],
        axis=1,
    ).reshape(-1)

    attended, grad_queries, grad_sel, grad_key_own, grad_value_own = attention(
        live, query_heads, upstream_heads, fetched, key_heads, value_heads, group_size
    )

    send_back = grad_sel.astype(jnp.bfloat16).reshape(head_count, TOPK, 2, holders, span_rows, HD)
    got_back = lax.all_to_all(send_back, "ctx", split_axis=3, concat_axis=1, tiled=True)
    flat = got_back.reshape(head_count, holders * TOPK, 2 * span_rows * HD).astype(jnp.float32)
    targets = selected.transpose(1, 0, 2).reshape(head_count, holders * TOPK)
    table = (targets[:, None, :] == jnp.arange(holders, dtype=jnp.int32)[None, :, None]).astype(
        jnp.float32
    )
    summed = jnp.einsum("gjn,gnx->gjx", table, flat, precision=lax.Precision.HIGHEST)
    owner = summed.reshape(head_count, holders, 2, span_rows, HD).astype(jnp.bfloat16)
    back = lax.all_to_all(owner, "ctx", split_axis=1, concat_axis=3, tiled=True)
    back = back[:, 0].astype(jnp.float32)
    total_keys = back[:, 0].transpose(1, 0, 2).reshape(tokens, k_cols) + grad_key_own
    total_values = back[:, 1].transpose(1, 0, 2).reshape(tokens, k_cols) + grad_value_own

    out = jnp.concatenate(
        [attended, grad_queries, total_keys.astype(jnp.bfloat16), total_values.astype(jnp.bfloat16)],
        axis=1,
    )
    out = out.reshape(tp_size, rows_in, 2 * q_cols + 2 * k_cols)
    out = lax.all_to_all(out, "tp", split_axis=0, concat_axis=0, tiled=True)
    out = out.reshape(tp_size, rows_in, 2 * q_cols + 2 * k_cols).transpose(1, 0, 2)

    def columns(lo, width):
        return out[:, :, lo : lo + width].reshape(rows_in, tp_size * width)

    return (
        columns(0, q_cols),
        columns(q_cols, q_cols),
        columns(2 * q_cols, k_cols),
        columns(2 * q_cols + k_cols, k_cols),
    )


def solution(mesh):
    in_specs = (
        P(("ctx", "tp"), None),
        P(("ctx", "tp"), None),
        P(("ctx", "tp"), None),
        P(None, "tp", None),
        P(None, "tp"),
        P(("ctx", "tp"), None),
    )
    out_specs = (
        P(("ctx", "tp"), None),
        P(("ctx", "tp"), None),
        P(("ctx", "tp"), None),
        P(("ctx", "tp"), None),
    )
    return jax.shard_map(body, mesh=mesh, in_specs=in_specs, out_specs=out_specs, check_vma=False)
```

time: 891 us -> 472 us (0.53)
  local copies, waits for them, and re-layouts: 237 us -> 35.4 us
  matrix products: 201 us -> 0.53 us
  blocking collectives: 0 us -> 166 us
  Pallas kernels: 0 us -> 96.1 us
  waiting for transfers between devices: 226 us -> 135 us
  other arithmetic: 89.9 us -> 8.99 us
  starting transfers between devices: 86 us -> 28.5 us
  loops' own time: 42.8 us -> 0 us
    dot_general x98 -> x1, matrix products: 201 us -> 0.53 us  [body(): jnp.einsum('gjn,gnx->gjx', table, flat, precision=lax.Precision.HIGHEST)]
    all_to_all x0 -> x3, blocking collectives: none -> 166 us  [the longest x1 62.9 us: body(): lax.all_to_all(packed, 'tp', split_axis=1, concat_axis=0, tiled=True)]
    pallas_call x0 -> x1, Pallas kernels: none -> 96.1 us  [attention(): pl.pallas_call(kernel, grid_spec=pltpu.PrefetchScalarGridSpec(num_scalar_...]
    all_to_all x16 -> x3, waiting for transfers between devices: 226 us -> 135 us  [the longest x1 59.2 us: body(): lax.all_to_all(send_back, 'ctx', split_axis=3, concat_axis=1, tiled=True)]
    another operation x16 -> x4, local copies, waits for them, and re-layouts: 63 us -> 0.47 us  [body(): jnp.stack([key_heads.reshape(holders, span_rows, head_count, HD), value_h...]
    all_to_all x16 -> x3, starting transfers between devices: 86 us -> 28.5 us  [the longest x1 15.4 us: body(): lax.all_to_all(send_back, 'ctx', split_axis=3, concat_axis=1, tiled=True)]
    another operation x1 -> x0, loops' own time: 42.8 us -> none  [body(): lax.scan(one_item, (zero_grad, zero_grad), (query_items, upstream_items,...]
    dynamic_update_slice x16 -> x0, other arithmetic: 37.1 us -> none  [add_slot(): lax.dynamic_update_slice(totals, current + part_sum[None, None], start_at)]
  transfers between devices with their start and end apart: 16 -> 3, of which waited for: 15 -> 3; matrix products, arithmetic and copies ran while one was open for 10% -> 1% of each run, Pallas kernels for 0% -> 0%
where the time goes in v1:
time: 472 us; the launch traced here: 471 us
  blocking collectives  166 us (35%)
  waiting for transfers between devices  135 us (29%)
  Pallas kernels  96.1 us (20%)
  local copies, waits for them, and re-layouts  35.4 us (8%)
  starting transfers between devices  28.5 us (6%)
  other arithmetic  8.99 us (2%)
    pallas_call x1, Pallas kernels, attention(): pl.pallas_call(kernel, grid_spec=pltpu.PrefetchScalarGridSpec(num_scalar_...  96.1 us
    all_to_all x1, blocking collectives, body(): lax.all_to_all(packed, 'tp', split_axis=1, concat_axis=0, tiled=True)  62.9 us
    all_to_all x1, blocking collectives, body(): out = lax.all_to_all(out, 'tp', split_axis=0, concat_axis=0, tiled=True)  62.6 us
    all_to_all x1, waiting for transfers between devices, body(): lax.all_to_all(send_back, 'ctx', split_axis=3, concat_axis=1, tiled=True)  59.2 us
    all_to_all x1, waiting for transfers between devices, body(): got = lax.all_to_all(send, 'ctx', split_axis=0, concat_axis=4, tiled=True)  53.6 us
    all_to_all x1, blocking collectives, body(): back = lax.all_to_all(owner, 'ctx', split_axis=1, concat_axis=3, tiled=True)  40.1 us
    all_to_all x1, waiting for transfers between devices, body(): spread = lax.all_to_all(kv, 'ctx', split_axis=0, concat_axis=0, tiled=True)  22.7 us
    all_to_all x1, starting transfers between devices, body(): lax.all_to_all(send_back, 'ctx', split_axis=3, concat_axis=1, tiled=True)  15.4 us
  transfers between devices with their start and end apart: 3, of which 3 were waited for; matrix products, arithmetic and copies ran while one was open for 1% of the time, Pallas kernels for 0%

profile of v1, /device:TPU:0, one launch (start us, length us, event | category | flops | bytes accessed | tf_op | source)
XLA Modules:
  0.0 471.5 jit_solution(8314485367954361856)
XLA Ops:
  0.7 2.9 copy_bitcast_fusion
  3.6 1.3 pad_maximum_fusion
  4.9 62.9 %all_to_all.64 = bf16[256,2,5120]{2,0,1:T(8,128)(2,1)S(1)} all-to-all(bf16[256,2,5120]{2,0,1:T(8,128)(2,1)S(1)} %pad_maximum_fusion), channel_id=1, replica_groups=mesh['ctx'=16,'tp'=2] {'tp'}, dimensions={1} | all-to-all | bytes 10485760 | tf_op jit(solution)/shard_map/all_to_all | solution.py:138
  67.8 2.4 copy-done
  70.8 1.1 pad_maximum_fusion.2
  71.9 6.1 %all-to-all-start.1 = ((bf16[16,2,32,4,128]{4,2,3,1,0:T(8,128)(2,1)}), bf16[16,2,32,4,128]{4,2,3,1,0:T(8,128)(2,1)S(1)}, u32[]{:S(2)}, u32[]{:S(2)}) async-start(bf16[16,2,32,4,128]{4,2,3,1,0:T(8,128)(2,1)} %pad_maximum_fusion.2), calls=%async_computation.1 | async-start | bytes 2097152 | tf_op jit(solution)/shard_map/all_to_all | solution.py:155
  78.3 22.7 %all-to-all-done.1 = bf16[16,2,32,4,128]{4,2,3,1,0:T(8,128)(2,1)S(1)} async-done(((bf16[16,2,32,4,128]{4,2,3,1,0:T(8,128)(2,1)}), bf16[16,2,32,4,128]{4,2,3,1,0:T(8,128)(2,1)S(1)}, u32[]{:S(2)}, u32[]{:S(2)}) %all-to-all-start.1) | async-done | bytes 1048608 | tf_op jit(solution)/shard_map/all_to_all | solution.py:155
  100.9 3.7 gather_fusion
  104.6 7.0 %all-to-all-start.2 = ((bf16[16,4,3,2,32,128]{5,4,3,2,1,0:T(8,128)(2,1)}), bf16[16,4,3,2,32,128]{5,4,3,2,1,0:T(8,128)(2,1)S(1)}, u32[]{:S(2)}, u32[]{:S(2)}) async-start(bf16[16,4,3,2,32,128]{5,4,3,2,1,0:T(8,128)(2,1)} %bitcast.90), calls=%async_computation.2 | async-start | bytes 6291456 | tf_op jit(solution)/shard_map/all_to_all | solution.py:158
  112.5 4.8 %fusion.9 = (bf16[512,2048]{1,0:T(8,128)(2,1)}, bf16[512,2048]{1,0:T(8,128)(2,1)}) fusion(bf16[512,5120]{1,0:T(8,128)(2,1)} %bitcast.85), kind=kLoop, calls=%fused_computation.33 | loop fusion | bytes 8388608 | tf_op jit(solution)/shard_map/slice | solution.py:142
  117.4 53.6 %all-to-all-done.2 = bf16[16,4,3,2,32,128]{5,4,3,2,1,0:T(8,128)(2,1)S(1)} async-done(((bf16[16,4,3,2,32,128]{5,4,3,2,1,0:T(8,128)(2,1)}), bf16[16,4,3,2,32,128]{5,4,3,2,1,0:T(8,128)(2,1)S(1)}, u32[]{:S(2)}, u32[]{:S(2)}) %all-to-all-start.2) | async-done | bytes 3145760 | tf_op jit(solution)/shard_map/all_to_all | solution.py:158
  171.0 2.4 copy.88
  173.4 96.1 %shard_map.93 = (bf16[512,2048]{1,0:T(8,128)(2,1)}, bf16[512,2048]{1,0:T(8,128)(2,1)}, f32[4,3,2,512,128]{4,3,2,1,0:T(8,128)}, f32[512,512]{1,0:T(8,128)}, f32[512,512]{1,0:T(8,128)}) custom-call(s32[16]{0:T(128)} %reshape.107.live_ref, bf16[512,2048]{1,0:T(8,128)(2,1)} %get-tuple-element.21.q_ref, bf16[512,2048]{1,0:T(8,128)(2,1)} %get-tuple-element.20.do_ref, ...), custom_call_target="tpu_custom_call" | custom-call | flops 25769803776 | bytes 20971520 | tf_op jit(solution)/shard_map/pallas_call | solution.py:96
  269.5 3.4 convert_element_type.46
  272.9 2.6 copy.90
  275.5 15.4 %all-to-all-start.3 = ((bf16[4,3,2,16,32,128]{5,4,2,1,0,3:T(8,128)(2,1)}), bf16[4,3,2,16,32,128]{5,4,2,1,0,3:T(8,128)(2,1)S(1)}, u32[]{:S(2)}, u32[]{:S(2)}) async-start(bf16[4,3,2,16,32,128]{5,4,2,1,0,3:T(8,128)(2,1)} %copy.90), calls=%async_computation.3 | async-start | bytes 6291456 | tf_op jit(solution)/shard_map/all_to_all | solution.py:173
  291.2 59.2 %all-to-all-done.3 = bf16[4,3,2,16,32,128]{5,4,2,1,0,3:T(8,128)(2,1)S(1)} async-done(((bf16[4,3,2,16,32,128]{5,4,2,1,0,3:T(8,128)(2,1)}), bf16[4,3,2,16,32,128]{5,4,2,1,0,3:T(8,128)(2,1)S(1)}, u32[]{:S(2)}, u32[]{:S(2)}) %all-to-all-start.3) | async-done | bytes 3145760 | tf_op jit(solution)/shard_map/all_to_all | solution.py:173
  350.3 2.6 copy.91
  352.9 4.1 reshape.98
  357.9 40.1 %all_to_all.65 = bf16[4,16,2,32,128]{4,3,2,0,1:T(8,128)(2,1)S(1)} all-to-all(bf16[4,16,2,32,128]{4,3,2,0,1:T(8,128)(2,1)S(1)} %copy.92), channel_id=1, replica_groups=mesh['ctx'=16,'tp'=2] {'ctx'}, dimensions={1} | all-to-all | bytes 2097152 | tf_op jit(solution)/shard_map/all_to_all | solution.py:181
  401.0 2.5 pad_maximum_fusion.1
  403.5 62.6 %all_to_all.66 = bf16[2,256,5120]{2,1,0:T(8,128)(2,1)S(1)} all-to-all(bf16[2,256,5120]{2,1,0:T(8,128)(2,1)S(1)} %bitcast.88), channel_id=1, replica_groups=mesh['ctx'=16,'tp'=2] {'tp'}, dimensions={0} | all-to-all | bytes 10485760 | tf_op jit(solution)/shard_map/all_to_all | solution.py:191
  466.6 1.6 copy.107
  468.2 1.6 copy.108
  (49 shorter events, 8.1 us)
Async XLA Ops:
  0.6 2.9 copy-start.7
  0.6 2.9 copy-start.8
  67.8 2.4 copy-start
  70.2 1.6 copy-start.3
  70.3 1.6 copy-start.4
  70.5 7.5 %copy-start.9 = (s32[16,4,3]{0,1,2:T(4,128)S(1)}, s32[16,4,3]{0,1,2:T(4,128)}, u32[]{:S(2)}) copy-start(s32[16,4,3]{0,1,2:T(4,128)} %param.9) | copy-start | bytes 2308
  71.9 29.1 %all-to-all-start.1 = ((bf16[16,2,32,4,128]{4,2,3,1,0:T(8,128)(2,1)}), bf16[16,2,32,4,128]{4,2,3,1,0:T(8,128)(2,1)S(1)}, u32[]{:S(2)}, u32[]{:S(2)}) async-start(bf16[16,2,32,4,128]{4,2,3,1,0:T(8,128)(2,1)} %pad_maximum_fusion.2), calls=%async_computation.1 | async-start | bytes 2097152 | tf_op jit(solution)/shard_map/all_to_all | solution.py:155
  104.6 7.2 %copy-start.10 = (s32[16,4]{0,1:T(4,128)S(1)}, s32[16,4]{0,1:T(4,128)}, u32[]{:S(2)}) copy-start(s32[16,4]{0,1:T(4,128)} %param.10) | copy-start | bytes 772
  104.6 66.4 %all-to-all-start.2 = ((bf16[16,4,3,2,32,128]{5,4,3,2,1,0:T(8,128)(2,1)}), bf16[16,4,3,2,32,128]{5,4,3,2,1,0:T(8,128)(2,1)S(1)}, u32[]{:S(2)}, u32[]{:S(2)}) async-start(bf16[16,4,3,2,32,128]{5,4,3,2,1,0:T(8,128)(2,1)} %bitcast.90), calls=%async_computation.2 | async-start | bytes 6291456 | tf_op jit(solution)/shard_map/all_to_all | solution.py:158
  275.5 74.8 %all-to-all-start.3 = ((bf16[4,3,2,16,32,128]{5,4,2,1,0,3:T(8,128)(2,1)}), bf16[4,3,2,16,32,128]{5,4,2,1,0,3:T(8,128)(2,1)S(1)}, u32[]{:S(2)}, u32[]{:S(2)}) async-start(bf16[4,3,2,16,32,128]{5,4,2,1,0,3:T(8,128)(2,1)} %copy.90), calls=%async_computation.3 | async-start | bytes 6291456 | tf_op jit(solution)/shard_map/all_to_all | solution.py:173
  398.0 1.2 copy-start.6
  398.3 1.3 copy-start.5
  398.5 1.9 copy-start.1
  398.5 2.5 copy-start.2

commit v2 on v1

--- a/solution.py
+++ b/solution.py
@@ -11,11 +11,10 @@
 HD = 128
 BLK = 512
 TOPK = 3
-ROW_TILE = 256
 
 
 def attention_kernel(
-    live_ref, q_ref, do_ref, kvs_ref, ko_ref, vo_ref,
+    live_ref, tp_ref, q_ref, do_ref, kvs_ref, ko_ref, vo_ref,
     o_ref, dq_ref, dsel_ref, dko_ref, dvo_ref, *, slot_count, row_tile, scale
 ):
     g = pl.program_id(0)
@@ -78,32 +77,39 @@
     dq_ref[...] = (grad_q * scale).astype(jnp.bfloat16)
 
 
-def attention(live, query_heads, upstream_heads, fetched, key_heads, value_heads, group_size):
-    tokens, _ = query_heads.shape
+def attention(live, tp_info, query_stack, upstream_stack, fetched, key_heads, value_heads, group_size):
+    tp_size, row_tile, q_cols = query_stack.shape
+    tokens = tp_size * row_tile
     head_count = key_heads.shape[1] // HD
     slot_count = TOPK + 1
-    row_tile = min(ROW_TILE, tokens)
-    tiles = tokens // row_tile
-    grid = (head_count, group_size, tiles)
+    grid = (head_count, group_size, tp_size)
     kernel = functools.partial(
         attention_kernel, slot_count=slot_count, row_tile=row_tile, scale=1.0 / math.sqrt(HD)
     )
-    head_block = pl.BlockSpec((row_tile, HD), lambda g, h, t, live: (t, g * group_size + h))
-    sel_block = pl.BlockSpec((None, TOPK, 2, BLK, HD), lambda g, h, t, live: (g, 0, 0, 0, 0))
-    own_block = pl.BlockSpec((BLK, HD), lambda g, h, t, live: (0, g))
+
+    def piece_in(g, h, t, live, tp):
+        return ((tp[0] - t + tp_size) % tp_size, 0, g * group_size + h)
+
+    def piece_out(g, h, t, live, tp):
+        return ((t - tp[0] + tp_size) % tp_size, 0, g * group_size + h)
+
+    in_block = pl.BlockSpec((None, row_tile, HD), piece_in)
+    out_block = pl.BlockSpec((None, row_tile, HD), piece_out)
+    sel_block = pl.BlockSpec((None, TOPK, 2, BLK, HD), lambda g, h, t, live, tp: (g, 0, 0, 0, 0))
+    own_block = pl.BlockSpec((BLK, HD), lambda g, h, t, live, tp: (0, g))
     flops = 12 * head_count * group_size * tokens * slot_count * BLK * HD
-    bytes_accessed = 2 * (4 * query_heads.size + 3 * fetched.size + 6 * key_heads.size)
+    bytes_accessed = 2 * (4 * query_stack.size + 3 * fetched.size + 6 * key_heads.size)
     return pl.pallas_call(
         kernel,
         grid_spec=pltpu.PrefetchScalarGridSpec(
-            num_scalar_prefetch=1,
+            num_scalar_prefetch=2,
             grid=grid,
-            in_specs=[head_block, head_block, sel_block, own_block, own_block],
-            out_specs=[head_block, head_block, sel_block, own_block, own_block],
+            in_specs=[in_block, in_block, sel_block, own_block, own_block],
+            out_specs=[out_block, out_block, sel_block, own_block, own_block],
         ),
         out_shape=[
-            jax.ShapeDtypeStruct(query_heads.shape, jnp.bfloat16),
-            jax.ShapeDtypeStruct(query_heads.shape, jnp.bfloat16),
+            jax.ShapeDtypeStruct(query_stack.shape, jnp.bfloat16),
+            jax.ShapeDtypeStruct(query_stack.shape, jnp.bfloat16),
             jax.ShapeDtypeStruct(fetched.shape, jnp.float32),
             jax.ShapeDtypeStruct(key_heads.shape, jnp.float32),
             jax.ShapeDtypeStruct(key_heads.shape, jnp.float32),
@@ -116,33 +122,48 @@
             transcendentals=head_count * group_size * tokens * slot_count * BLK,
             bytes_accessed=bytes_accessed,
         ),
-    )(live, query_heads, upstream_heads, fetched, key_heads, value_heads)
+    )(live, tp_info, query_stack, upstream_stack, fetched, key_heads, value_heads)
+
+
+def shift(x, axis, step, size):
+    return lax.ppermute(x, axis, perm=[(s, (s + step) % size) for s in range(size)])
+
+
+def tp_receive(x, me, size):
+    width = x.shape[1] // size
+    pieces = [lax.dynamic_slice_in_dim(x, me * width, width, 1)]
+    for step in range(1, size):
+        dest = (me + step) % size
+        pieces.append(shift(lax.dynamic_slice_in_dim(x, dest * width, width, 1), "tp", step, size))
+    return jnp.stack(pieces)
+
+
+def tp_send(stack, me, size):
+    pieces = [stack[0]] + [shift(stack[step], "tp", step, size) for step in range(1, size)]
+    order = (me - jnp.arange(size, dtype=jnp.int32)) % size
+    arranged = jnp.take(jnp.stack(pieces), order, axis=0)
+    return arranged.transpose(1, 0, 2).reshape(stack.shape[1], size * stack.shape[2])
+
+
+def source_order(stack, me, size):
+    order = (me - jnp.arange(size, dtype=jnp.int32)) % size
+    return jnp.take(stack, order, axis=0)
 
 
 def body(queries, key_rows, value_rows, selected, own_flag, cotangent):
     holders = lax.axis_size("ctx")
     tp_size = lax.axis_size("tp")
     position = lax.axis_index("ctx")
+    me = lax.axis_index("tp")
     rows_in = queries.shape[0]
     q_cols = queries.shape[1] // tp_size
     k_cols = key_rows.shape[1] // tp_size
-    packed = jnp.concatenate(
-        [
-            queries.reshape(rows_in, tp_size, q_cols),
-            cotangent.reshape(rows_in, tp_size, q_cols),
-            key_rows.reshape(rows_in, tp_size, k_cols),
-            value_rows.reshape(rows_in, tp_size, k_cols),
-        ],
-        axis=2,
-    )
-    packed = lax.all_to_all(packed, "tp", split_axis=1, concat_axis=0, tiled=True)
     tokens = rows_in * tp_size
-    packed = packed.reshape(tokens, 2 * q_cols + 2 * k_cols)
-    query_heads = packed[:, :q_cols]
-    upstream_heads = packed[:, q_cols : 2 * q_cols]
-    key_heads = packed[:, 2 * q_cols : 2 * q_cols + k_cols]
-    value_heads = packed[:, 2 * q_cols + k_cols :]
     assert tokens == BLK
+    key_heads = source_order(tp_receive(key_rows, me, tp_size), me, tp_size).reshape(tokens, k_cols)
+    value_heads = source_order(tp_receive(value_rows, me, tp_size), me, tp_size).reshape(tokens, k_cols)
+    query_stack = tp_receive(queries, me, tp_size)
+    upstream_stack = tp_receive(cotangent, me, tp_size)
     head_count = k_cols // HD
     group_size = q_cols // k_cols
     span_rows = BLK // holders
@@ -165,9 +186,12 @@
         axis=1,
     ).reshape(-1)
 
+    tp_info = me.astype(jnp.int32).reshape(1)
     attended, grad_queries, grad_sel, grad_key_own, grad_value_own = attention(
-        live, query_heads, upstream_heads, fetched, key_heads, value_heads, group_size
-    )
+        live, tp_info, query_stack, upstream_stack, fetched, key_heads, value_heads, group_size
+    )
+    attended = tp_send(attended, me, tp_size)
+    grad_queries = tp_send(grad_queries, me, tp_size)
 
     send_back = grad_sel.astype(jnp.bfloat16).reshape(head_count, TOPK, 2, holders, span_rows, HD)
     got_back = lax.all_to_all(send_back, "ctx", split_axis=3, concat_axis=1, tiled=True)
@@ -183,23 +207,12 @@
     total_keys = back[:, 0].transpose(1, 0, 2).reshape(tokens, k_cols) + grad_key_own
     total_values = back[:, 1].transpose(1, 0, 2).reshape(tokens, k_cols) + grad_value_own
 
-    out = jnp.concatenate(
-        [attended, grad_queries, total_keys.astype(jnp.bfloat16), total_values.astype(jnp.bfloat16)],
-        axis=1,
-    )
-    out = out.reshape(tp_size, rows_in, 2 * q_cols + 2 * k_cols)
-    out = lax.all_to_all(out, "tp", split_axis=0, concat_axis=0, tiled=True)
-    out = out.reshape(tp_size, rows_in, 2 * q_cols + 2 * k_cols).transpose(1, 0, 2)
-
-    def columns(lo, width):
-        return out[:, :, lo : lo + width].reshape(rows_in, tp_size * width)
-
-    return (
-        columns(0, q_cols),
-        columns(q_cols, q_cols),
-        columns(2 * q_cols, k_cols),
-        columns(2 * q_cols + k_cols, k_cols),
-    )
+    def rows_by_destination(total):
+        stack = total.astype(jnp.bfloat16).reshape(tp_size, rows_in, k_cols)
+        order = (me + jnp.arange(tp_size, dtype=jnp.int32)) % tp_size
+        return tp_send(jnp.take(stack, order, axis=0), me, tp_size)
+
+    return (attended, grad_queries, rows_by_destination(total_keys), rows_by_destination(total_values))
 
 
 def solution(mesh):

time: 472 us -> 399 us (0.85)
  blocking collectives: 166 us -> 0 us
  waiting for transfers between devices: 135 us -> 179 us
  starting transfers between devices: 28.5 us -> 54.1 us
  local copies, waits for them, and re-layouts: 35.4 us -> 49.3 us
  other arithmetic: 8.99 us -> 17.1 us
    all_to_all x3 -> x0, blocking collectives: 166 us -> none  [the longest x1 62.9 us: body(): lax.all_to_all(packed, 'tp', split_axis=1, concat_axis=0, tiled=True)]
    ppermute x0 -> x8, waiting for transfers between devices: none -> 92.2 us  [shift(): lax.ppermute(x, axis, perm=[(s, (s + step) % size) for s in range(size)])]
    all_to_all x1, waiting for transfers between devices: 53.6 us -> 5.06 us  [body(): got = lax.all_to_all(send, 'ctx', split_axis=0, concat_axis=4, tiled=True)]
    all_to_all x0 -> x1, starting transfers between devices: none -> 15.4 us  [body(): back = lax.all_to_all(owner, 'ctx', split_axis=1, concat_axis=3, tiled=True)]
    ppermute x0 -> x8, starting transfers between devices: none -> 10.3 us  [shift(): lax.ppermute(x, axis, perm=[(s, (s + step) % size) for s in range(size)])]
    another operation x0 -> x8, other arithmetic: none -> 8.95 us  [the longest x4 5.98 us: tp_receive(): return jnp.stack(pieces)]
    gather x0 -> x8, local copies, waits for them, and re-layouts: none -> 7.48 us  [the longest x4 5.16 us: tp_send(): arranged = jnp.take(jnp.stack(pieces), order, axis=0)]
    another operation x0 -> x4, local copies, waits for them, and re-layouts: none -> 6.87 us  [tp_receive(): return jnp.stack(pieces)]
  transfers between devices with their start and end apart: 3 -> 12, of which waited for: 3 -> 9; matrix products, arithmetic and copies ran while one was open for 1% -> 9% of each run, Pallas kernels for 0% -> 0%
where the time goes in v2:
time: 399 us; the launch traced here: 398 us
  waiting for transfers between devices  179 us (45%)
  Pallas kernels  97 us (24%)
  starting transfers between devices  54.1 us (14%)
  local copies, waits for them, and re-layouts  49.3 us (12%)
  other arithmetic  17.1 us (4%)
    pallas_call x1, Pallas kernels, attention(): pl.pallas_call(kernel, grid_spec=pltpu.PrefetchScalarGridSpec(num_scalar_...  97 us
    ppermute x8, waiting for transfers between devices, shift(): lax.ppermute(x, axis, perm=[(s, (s + step) % size) for s in range(size)])  92.2 us
    all_to_all x1, waiting for transfers between devices, body(): lax.all_to_all(send_back, 'ctx', split_axis=3, concat_axis=1, tiled=True)  59.2 us
    all_to_all x1, waiting for transfers between devices, body(): spread = lax.all_to_all(kv, 'ctx', split_axis=0, concat_axis=0, tiled=True)  22.7 us
    all_to_all x1, starting transfers between devices, body(): back = lax.all_to_all(owner, 'ctx', split_axis=1, concat_axis=3, tiled=True)  15.4 us
    all_to_all x1, starting transfers between devices, body(): lax.all_to_all(send_back, 'ctx', split_axis=3, concat_axis=1, tiled=True)  15.4 us
    ppermute x8, starting transfers between devices, shift(): lax.ppermute(x, axis, perm=[(s, (s + step) % size) for s in range(size)])  10.3 us
  transfers between devices with their start and end apart: 12, of which 9 were waited for; matrix products, arithmetic and copies ran while one was open for 9% of the time, Pallas kernels for 0%

profile of v2, /device:TPU:0, one launch (start us, length us, event | category | flops | bytes accessed | tf_op | source)
XLA Modules:
  0.0 398.3 jit_solution(10770240661029704680)
XLA Ops:
  1.7 3.0 collective-permute-start.3
  6.0 5.9 %collective-permute-done.3 = bf16[256,512]{1,0:T(8,128)(2,1)S(1)} collective-permute-done((bf16[256,512]{1,0:T(8,128)(2,1)S(1)}, bf16[256,512]{1,0:T(8,128)(2,1)S(1)}, u32[]{:S(2)}, u32[]{:S(2)}) %collective-permute-start.3) | collective-permute-done | bytes 262176 | tf_op jit(solution)/shard_map/ppermute | solution.py:129
  12.5 4.1 %collective-permute-done.2 = bf16[256,512]{1,0:T(8,128)(2,1)S(1)} collective-permute-done((bf16[256,512]{1,0:T(8,128)(2,1)S(1)}, bf16[256,512]{1,0:T(8,128)(2,1)S(1)}, u32[]{:S(2)}, u32[]{:S(2)}) %collective-permute-start.2) | collective-permute-done | bytes 262176 | tf_op jit(solution)/shard_map/ppermute | solution.py:129
  19.5 6.1 %all-to-all-start = ((bf16[16,2,32,4,128]{4,2,3,1,0:T(8,128)(2,1)}), bf16[16,2,32,4,128]{4,2,3,1,0:T(8,128)(2,1)S(1)}, u32[]{:S(2)}, u32[]{:S(2)}) async-start(bf16[16,2,32,4,128]{4,2,3,1,0:T(8,128)(2,1)} %pad_maximum_fusion.4), calls=%async_computation | async-start | bytes 2097152 | tf_op jit(solution)/shard_map/all_to_all | solution.py:176
  25.9 22.7 %all-to-all-done = bf16[16,2,32,4,128]{4,2,3,1,0:T(8,128)(2,1)S(1)} async-done(((bf16[16,2,32,4,128]{4,2,3,1,0:T(8,128)(2,1)}), bf16[16,2,32,4,128]{4,2,3,1,0:T(8,128)(2,1)S(1)}, u32[]{:S(2)}, u32[]{:S(2)}) %all-to-all-start) | async-done | bytes 1048608 | tf_op jit(solution)/shard_map/all_to_all | solution.py:176
  48.6 3.6 gather_fusion
  52.2 6.9 %all-to-all-start.1 = ((bf16[16,4,3,2,32,128]{5,4,3,2,1,0:T(8,128)(2,1)}), bf16[16,4,3,2,32,128]{5,4,3,2,1,0:T(8,128)(2,1)S(1)}, u32[]{:S(2)}, u32[]{:S(2)}) async-start(bf16[16,4,3,2,32,128]{5,4,3,2,1,0:T(8,128)(2,1)} %bitcast.97), calls=%async_computation.1 | async-start | bytes 6291456 | tf_op jit(solution)/shard_map/all_to_all | solution.py:179
  59.1 3.3 dynamic-slice_bitcast_fusion
  66.9 21.8 %collective-permute-done.1 = bf16[256,2048]{1,0:T(8,128)(2,1)} collective-permute-done((bf16[256,2048]{1,0:T(8,128)(2,1)}, bf16[256,2048]{1,0:T(8,128)(2,1)}, u32[]{:S(2)}, u32[]{:S(2)}) %collective-permute-start.1) | collective-permute-done | bytes 1048608 | tf_op jit(solution)/shard_map/ppermute | solution.py:129
  88.7 3.1 pad_maximum_fusion.1.do_ref
  91.8 18.9 %collective-permute-done = bf16[256,2048]{1,0:T(8,128)(2,1)} collective-permute-done((bf16[256,2048]{1,0:T(8,128)(2,1)}, bf16[256,2048]{1,0:T(8,128)(2,1)}, u32[]{:S(2)}, u32[]{:S(2)}) %collective-permute-start) | collective-permute-done | bytes 1048608 | tf_op jit(solution)/shard_map/ppermute | solution.py:129
  113.4 5.1 %all-to-all-done.1 = bf16[16,4,3,2,32,128]{5,4,3,2,1,0:T(8,128)(2,1)S(1)} async-done(((bf16[16,4,3,2,32,128]{5,4,3,2,1,0:T(8,128)(2,1)}), bf16[16,4,3,2,32,128]{5,4,3,2,1,0:T(8,128)(2,1)S(1)}, u32[]{:S(2)}, u32[]{:S(2)}) %all-to-all-start.1) | async-done | bytes 3145760 | tf_op jit(solution)/shard_map/all_to_all | solution.py:179
  120.9 97.0 %shard_map.93 = (bf16[2,256,2048]{2,1,0:T(8,128)(2,1)}, bf16[2,256,2048]{2,1,0:T(8,128)(2,1)}, f32[4,3,2,512,128]{4,3,2,1,0:T(8,128)}, f32[512,512]{1,0:T(8,128)}, f32[512,512]{1,0:T(8,128)}) custom-call(s32[16]{0:T(128)} %reshape.112.live_ref, s32[1]{0:T(128)} %bitcast.2.tp_ref, bf16[2,256,2048]{2,1,0:T(8,128)(2,1)} %pad_maximum_fusion.q_ref, ...), custom_call_target="tpu_custom_call" | custom-call | flops 25769803776 | bytes 20971520 | tf_op jit(solution)/shard_map/pallas_call | solution.py:102
  217.9 3.4 convert_element_type.46
  223.9 15.4 %all-to-all-start.2 = ((bf16[4,3,2,16,32,128]{5,4,2,1,0,3:T(8,128)(2,1)}), bf16[4,3,2,16,32,128]{5,4,2,1,0,3:T(8,128)(2,1)S(1)}, u32[]{:S(2)}, u32[]{:S(2)}) async-start(bf16[4,3,2,16,32,128]{5,4,2,1,0,3:T(8,128)(2,1)} %copy.88), calls=%async_computation.2 | async-start | bytes 6291456 | tf_op jit(solution)/shard_map/all_to_all | solution.py:197
  239.6 59.2 %all-to-all-done.2 = bf16[4,3,2,16,32,128]{5,4,2,1,0,3:T(8,128)(2,1)S(1)} async-done(((bf16[4,3,2,16,32,128]{5,4,2,1,0,3:T(8,128)(2,1)}), bf16[4,3,2,16,32,128]{5,4,2,1,0,3:T(8,128)(2,1)S(1)}, u32[]{:S(2)}, u32[]{:S(2)}) %all-to-all-start.2) | async-done | bytes 3145760 | tf_op jit(solution)/shard_map/all_to_all | solution.py:197
  301.3 4.1 %reshape.104 = bf16[4,48,8192]{2,1,0:T(8,128)(2,1)S(1)} reshape(bf16[4,16,3,2,1,32,128]{6,5,3,2,1,0,4:T(8,128)(2,1)} %copy.89) | data formatting | bytes 6291456 | tf_op jit(solution)/shard_map/reshape | solution.py:198
  307.4 15.4 %all-to-all-start.3 = ((bf16[4,16,2,32,128]{4,3,2,0,1:T(8,128)(2,1)}), bf16[4,16,2,32,128]{4,3,2,0,1:T(8,128)(2,1)S(1)}, u32[]{:S(2)}, u32[]{:S(2)}) async-start(bf16[4,16,2,32,128]{4,3,2,0,1:T(8,128)(2,1)} %copy.90), calls=%async_computation.3 | async-start | bytes 2097152 | tf_op jit(solution)/shard_map/all_to_all | solution.py:205
  327.4 21.6 %collective-permute-done.4 = bf16[256,2048]{1,0:T(8,128)(2,1)S(1)} collective-permute-done((bf16[256,2048]{1,0:T(8,128)(2,1)S(1)}, bf16[256,2048]{1,0:T(8,128)(2,1)S(1)}, u32[]{:S(2)}, u32[]{:S(2)}) %collective-permute-start.4) | collective-permute-done | bytes 1048608 | tf_op jit(solution)/shard_map/ppermute | solution.py:129
  351.2 19.9 %collective-permute-done.5 = bf16[256,2048]{1,0:T(8,128)(2,1)} collective-permute-done((bf16[256,2048]{1,0:T(8,128)(2,1)}, bf16[256,2048]{1,0:T(8,128)(2,1)}, u32[]{:S(2)}, u32[]{:S(2)}) %collective-permute-start.5) | collective-permute-done | bytes 1048608 | tf_op jit(solution)/shard_map/ppermute | solution.py:129
  382.8 2.8 copy.85
  385.6 2.9 copy.96
  388.5 2.8 copy.86
  391.3 2.9 copy.97
  (93 shorter events, 45.3 us)
Async XLA Ops:
  1.7 10.2 %collective-permute-start.3 = (bf16[256,512]{1,0:T(8,128)(2,1)S(1)}, bf16[256,512]{1,0:T(8,128)(2,1)S(1)}, u32[]{:S(2)}, u32[]{:S(2)}) collective-permute-start(bf16[256,512]{1,0:T(8,128)(2,1)S(1)} %get-tuple-element.53), channel_id=1, source_target_pairs={{0,1},{1,0},{2,3},{3,2},{4,5},{5,4},{6,7},{7,6},{8,9},{9,8},{10,11... | collective-permute-start | bytes 786440 | tf_op jit(solution)/shard_map/ppermute | solution.py:129
  5.8 10.9 %collective-permute-start.2 = (bf16[256,512]{1,0:T(8,128)(2,1)S(1)}, bf16[256,512]{1,0:T(8,128)(2,1)S(1)}, u32[]{:S(2)}, u32[]{:S(2)}) collective-permute-start(bf16[256,512]{1,0:T(8,128)(2,1)S(1)} %get-tuple-element.51), channel_id=1, source_target_pairs={{0,1},{1,0},{2,3},{3,2},{4,5},{5,4},{6,7},{7,6},{8,9},{9,8},{10,11... | collective-permute-start | bytes 786440 | tf_op jit(solution)/shard_map/ppermute | solution.py:129
  17.5 0.8 copy-start.4
  17.5 1.0 copy-start.5
  18.5 7.2 %copy-start.10 = (s32[16,4,3]{0,1,2:T(4,128)S(1)}, s32[16,4,3]{0,1,2:T(4,128)}, u32[]{:S(2)}) copy-start(s32[16,4,3]{0,1,2:T(4,128)} %param.13) | copy-start | bytes 2308
  19.5 29.1 %all-to-all-start = ((bf16[16,2,32,4,128]{4,2,3,1,0:T(8,128)(2,1)}), bf16[16,2,32,4,128]{4,2,3,1,0:T(8,128)(2,1)S(1)}, u32[]{:S(2)}, u32[]{:S(2)}) async-start(bf16[16,2,32,4,128]{4,2,3,1,0:T(8,128)(2,1)} %pad_maximum_fusion.4), calls=%async_computation | async-start | bytes 2097152 | tf_op jit(solution)/shard_map/all_to_all | solution.py:176
  52.2 66.2 %all-to-all-start.1 = ((bf16[16,4,3,2,32,128]{5,4,3,2,1,0:T(8,128)(2,1)}), bf16[16,4,3,2,32,128]{5,4,3,2,1,0:T(8,128)(2,1)S(1)}, u32[]{:S(2)}, u32[]{:S(2)}) async-start(bf16[16,4,3,2,32,128]{5,4,3,2,1,0:T(8,128)(2,1)} %bitcast.97), calls=%async_computation.1 | async-start | bytes 6291456 | tf_op jit(solution)/shard_map/all_to_all | solution.py:179
  59.1 4.8 %copy-start.3 = (bf16[256,4096]{1,0:T(8,128)(2,1)S(1)}, bf16[256,4096]{1,0:T(8,128)(2,1)}, u32[]{:S(2)}) copy-start(bf16[256,4096]{1,0:T(8,128)(2,1)} %param.10) | copy-start | bytes 6291460
  62.4 3.7 copy-start.11
  62.4 26.3 %collective-permute-start.1 = (bf16[256,2048]{1,0:T(8,128)(2,1)}, bf16[256,2048]{1,0:T(8,128)(2,1)}, u32[]{:S(2)}, u32[]{:S(2)}) collective-permute-start(bf16[256,2048]{1,0:T(8,128)(2,1)} %get-tuple-element.43), channel_id=1, source_target_pairs={{0,1},{1,0},{2,3},{3,2},{4,5},{5,4},{6,7},{7,6},{8,9},{9,8},{10,11... | collective-permute-start | bytes 3145736 | tf_op jit(solution)/shard_map/ppermute | solution.py:129
  65.4 45.3 %collective-permute-start = (bf16[256,2048]{1,0:T(8,128)(2,1)}, bf16[256,2048]{1,0:T(8,128)(2,1)}, u32[]{:S(2)}, u32[]{:S(2)}) collective-permute-start(bf16[256,2048]{1,0:T(8,128)(2,1)} %get-tuple-element.45), channel_id=1, source_target_pairs={{0,1},{1,0},{2,3},{3,2},{4,5},{5,4},{6,7},{7,6},{8,9},{9,8},{10,11... | collective-permute-start | bytes 3145736 | tf_op jit(solution)/shard_map/ppermute | solution.py:129
  88.7 22.0 %copy-start.2 = (bf16[1,256,2048]{2,1,0:T(8,128)(2,1)S(1)}, bf16[1,256,2048]{2,1,0:T(8,128)(2,1)}, u32[]{:S(2)}) copy-start(bf16[1,256,2048]{2,1,0:T(8,128)(2,1)} %get-tuple-element.44) | copy-start | bytes 3145732
  223.9 74.8 %all-to-all-start.2 = ((bf16[4,3,2,16,32,128]{5,4,2,1,0,3:T(8,128)(2,1)}), bf16[4,3,2,16,32,128]{5,4,2,1,0,3:T(8,128)(2,1)S(1)}, u32[]{:S(2)}, u32[]{:S(2)}) async-start(bf16[4,3,2,16,32,128]{5,4,2,1,0,3:T(8,128)(2,1)} %copy.88), calls=%async_computation.2 | async-start | bytes 6291456 | tf_op jit(solution)/shard_map/all_to_all | solution.py:197
  306.3 16.5 %copy-start.7 = (bf16[2,256,2048]{2,1,0:T(8,128)(2,1)S(1)}, bf16[2,256,2048]{2,1,0:T(8,128)(2,1)}, u32[]{:S(2)}) copy-start(bf16[2,256,2048]{2,1,0:T(8,128)(2,1)} %get-tuple-element.11) | copy-start | bytes 6291460
  307.4 67.5 %all-to-all-start.3 = ((bf16[4,16,2,32,128]{4,3,2,0,1:T(8,128)(2,1)}), bf16[4,16,2,32,128]{4,3,2,0,1:T(8,128)(2,1)S(1)}, u32[]{:S(2)}, u32[]{:S(2)}) async-start(bf16[4,16,2,32,128]{4,3,2,0,1:T(8,128)(2,1)} %copy.90), calls=%async_computation.3 | async-start | bytes 2097152 | tf_op jit(solution)/shard_map/all_to_all | solution.py:205
  322.8 1.7 copy-start.6
  323.0 26.0 %collective-permute-start.4 = (bf16[256,2048]{1,0:T(8,128)(2,1)S(1)}, bf16[256,2048]{1,0:T(8,128)(2,1)S(1)}, u32[]{:S(2)}, u32[]{:S(2)}) collective-permute-start(bf16[256,2048]{1,0:T(8,128)(2,1)S(1)} %get-tuple-element.41), channel_id=1, source_target_pairs={{0,1},{1,0},{2,3},{3,2},{4,5},{5,4},{6,7},{7,6},{8,9},{9,8},{10,11... | collective-permute-start | bytes 3145736 | tf_op jit(solution)/shard_map/ppermute | solution.py:129
  326.0 45.1 %collective-permute-start.5 = (bf16[256,2048]{1,0:T(8,128)(2,1)}, bf16[256,2048]{1,0:T(8,128)(2,1)}, u32[]{:S(2)}, u32[]{:S(2)}) collective-permute-start(bf16[256,2048]{1,0:T(8,128)(2,1)} %get-tuple-element.39), channel_id=1, source_target_pairs={{0,1},{1,0},{2,3},{3,2},{4,5},{5,4},{6,7},{7,6},{8,9},{9,8},{10,11... | collective-permute-start | bytes 3145736 | tf_op jit(solution)/shard_map/ppermute | solution.py:129
  375.1 1.2 copy-start.9
  375.3 1.8 copy-start.8
  377.9 2.4 copy-start
  377.9 2.4 copy-start.1
  378.1 16.1 %collective-permute-start.6 = (bf16[256,512]{1,0:T(8,128)(2,1)S(1)}, bf16[256,512]{1,0:T(8,128)(2,1)}, u32[]{:S(2)}, u32[]{:S(2)}) collective-permute-start(bf16[256,512]{1,0:T(8,128)(2,1)S(1)} %get-tuple-element.49), channel_id=1, source_target_pairs={{0,1},{1,0},{2,3},{3,2},{4,5},{5,4},{6,7},{7,6},{8,9},{9,8},{10,11... | collective-permute-start | bytes 786440 | tf_op jit(solution)/shard_map/ppermute | solution.py:129
  379.7 16.1 %collective-permute-start.7 = (bf16[256,512]{1,0:T(8,128)(2,1)S(1)}, bf16[256,512]{1,0:T(8,128)(2,1)S(1)}, u32[]{:S(2)}, u32[]{:S(2)}) collective-permute-start(bf16[256,512]{1,0:T(8,128)(2,1)S(1)} %get-tuple-element.47), channel_id=1, source_target_pairs={{0,1},{1,0},{2,3},{3,2},{4,5},{5,4},{6,7},{7,6},{8,9},{9,8},{10,11... | collective-permute-start | bytes 786440 | tf_op jit(solution)/shard_map/ppermute | solution.py:129

commit v3 on v2

--- a/solution.py
+++ b/solution.py
@@ -77,10 +77,11 @@
     dq_ref[...] = (grad_q * scale).astype(jnp.bfloat16)
 
 
-def attention(live, tp_info, query_stack, upstream_stack, fetched, key_heads, value_heads, group_size):
-    tp_size, row_tile, q_cols = query_stack.shape
+def attention(live, tp_info, query_stack, upstream_stack, fetched, key_heads, value_heads, group_size, first):
+    tp_size, row_tile, _ = query_stack.shape
     tokens = tp_size * row_tile
-    head_count = key_heads.shape[1] // HD
+    head_count = fetched.shape[0]
+    q_cols = head_count * group_size * HD
     slot_count = TOPK + 1
     grid = (head_count, group_size, tp_size)
     kernel = functools.partial(
@@ -88,7 +89,7 @@
     )
 
     def piece_in(g, h, t, live, tp):
-        return ((tp[0] - t + tp_size) % tp_size, 0, g * group_size + h)
+        return ((tp[0] - t + tp_size) % tp_size, 0, (first + g) * group_size + h)
 
     def piece_out(g, h, t, live, tp):
         return ((t - tp[0] + tp_size) % tp_size, 0, g * group_size + h)
@@ -96,23 +97,24 @@
     in_block = pl.BlockSpec((None, row_tile, HD), piece_in)
     out_block = pl.BlockSpec((None, row_tile, HD), piece_out)
     sel_block = pl.BlockSpec((None, TOPK, 2, BLK, HD), lambda g, h, t, live, tp: (g, 0, 0, 0, 0))
-    own_block = pl.BlockSpec((BLK, HD), lambda g, h, t, live, tp: (0, g))
+    own_in = pl.BlockSpec((BLK, HD), lambda g, h, t, live, tp: (0, first + g))
+    own_out = pl.BlockSpec((BLK, HD), lambda g, h, t, live, tp: (0, g))
     flops = 12 * head_count * group_size * tokens * slot_count * BLK * HD
-    bytes_accessed = 2 * (4 * query_stack.size + 3 * fetched.size + 6 * key_heads.size)
+    bytes_accessed = 2 * (4 * tokens * q_cols + 3 * fetched.size + 6 * tokens * head_count * HD)
     return pl.pallas_call(
         kernel,
         grid_spec=pltpu.PrefetchScalarGridSpec(
             num_scalar_prefetch=2,
             grid=grid,
-            in_specs=[in_block, in_block, sel_block, own_block, own_block],
-            out_specs=[out_block, out_block, sel_block, own_block, own_block],
+            in_specs=[in_block, in_block, sel_block, own_in, own_in],
+            out_specs=[out_block, out_block, sel_block, own_out, own_out],
         ),
         out_shape=[
-            jax.ShapeDtypeStruct(query_stack.shape, jnp.bfloat16),
-            jax.ShapeDtypeStruct(query_stack.shape, jnp.bfloat16),
+            jax.ShapeDtypeStruct((tp_size, row_tile, q_cols), jnp.bfloat16),
+            jax.ShapeDtypeStruct((tp_size, row_tile, q_cols), jnp.bfloat16),
             jax.ShapeDtypeStruct(fetched.shape, jnp.float32),
-            jax.ShapeDtypeStruct(key_heads.shape, jnp.float32),
-            jax.ShapeDtypeStruct(key_heads.shape, jnp.float32),
+            jax.ShapeDtypeStruct((tokens, head_count * HD), jnp.float32),
+            jax.ShapeDtypeStruct((tokens, head_count * HD), jnp.float32),
         ],
         compiler_params=pltpu.CompilerParams(
             dimension_semantics=("arbitrary", "arbitrary", "arbitrary"),
@@ -174,44 +176,68 @@
         axis=1,
     )
     spread = lax.all_to_all(kv, "ctx", split_axis=0, concat_axis=0, tiled=True)
-    head_ids = jnp.arange(head_count, dtype=jnp.int32)[None, :, None]
-    send = spread[selected, :, :, head_ids, :]
-    got = lax.all_to_all(send, "ctx", split_axis=0, concat_axis=4, tiled=True)
-    fetched = got[0]
-
     my_selected = lax.dynamic_index_in_dim(selected, position, 0, keepdims=False)
     my_flags = lax.dynamic_index_in_dim(own_flag, position, 0, keepdims=False)
-    live = jnp.concatenate(
+    live_all = jnp.concatenate(
         [(my_selected < position).astype(jnp.int32), (my_flags == 1).astype(jnp.int32)[:, None]],
         axis=1,
-    ).reshape(-1)
-
+    )
     tp_info = me.astype(jnp.int32).reshape(1)
-    attended, grad_queries, grad_sel, grad_key_own, grad_value_own = attention(
-        live, tp_info, query_stack, upstream_stack, fetched, key_heads, value_heads, group_size
-    )
-    attended = tp_send(attended, me, tp_size)
-    grad_queries = tp_send(grad_queries, me, tp_size)
-
-    send_back = grad_sel.astype(jnp.bfloat16).reshape(head_count, TOPK, 2, holders, span_rows, HD)
-    got_back = lax.all_to_all(send_back, "ctx", split_axis=3, concat_axis=1, tiled=True)
-    flat = got_back.reshape(head_count, holders * TOPK, 2 * span_rows * HD).astype(jnp.float32)
-    targets = selected.transpose(1, 0, 2).reshape(head_count, holders * TOPK)
-    table = (targets[:, None, :] == jnp.arange(holders, dtype=jnp.int32)[None, :, None]).astype(
-        jnp.float32
-    )
-    summed = jnp.einsum("gjn,gnx->gjx", table, flat, precision=lax.Precision.HIGHEST)
-    owner = summed.reshape(head_count, holders, 2, span_rows, HD).astype(jnp.bfloat16)
-    back = lax.all_to_all(owner, "ctx", split_axis=1, concat_axis=3, tiled=True)
-    back = back[:, 0].astype(jnp.float32)
-    total_keys = back[:, 0].transpose(1, 0, 2).reshape(tokens, k_cols) + grad_key_own
-    total_values = back[:, 1].transpose(1, 0, 2).reshape(tokens, k_cols) + grad_value_own
+    chunk_count = 2 if head_count % 2 == 0 else 1
+    chunk_heads = head_count // chunk_count
+    chunk_k_cols = chunk_heads * HD
+
+    results = []
+    for chunk in range(chunk_count):
+        first = chunk * chunk_heads
+        chunk_selected = selected[:, first : first + chunk_heads]
+        head_ids = jnp.arange(first, first + chunk_heads, dtype=jnp.int32)[None, :, None]
+        send = spread[chunk_selected, :, :, head_ids, :]
+        got = lax.all_to_all(send, "ctx", split_axis=0, concat_axis=4, tiled=True)
+        fetched = got[0]
+        live = live_all[first : first + chunk_heads].reshape(-1)
+        attended, grad_queries, grad_sel, grad_key_own, grad_value_own = attention(
+            live, tp_info, query_stack, upstream_stack, fetched, key_heads, value_heads,
+            group_size, first,
+        )
+        attended = tp_send(attended, me, tp_size)
+        grad_queries = tp_send(grad_queries, me, tp_size)
+
+        send_back = grad_sel.astype(jnp.bfloat16).reshape(
+            chunk_heads, TOPK, 2, holders, span_rows, HD
+        )
+        got_back = lax.all_to_all(send_back, "ctx", split_axis=3, concat_axis=1, tiled=True)
+        flat = got_back.reshape(chunk_heads, holders * TOPK, 2 * span_rows * HD).astype(
+            jnp.float32
+        )
+        targets = chunk_selected.transpose(1, 0, 2).reshape(chunk_heads, holders * TOPK)
+        table = (
+            targets[:, None, :] == jnp.arange(holders, dtype=jnp.int32)[None, :, None]
+        ).astype(jnp.float32)
+        summed = jnp.einsum("gjn,gnx->gjx", table, flat, precision=lax.Precision.HIGHEST)
+        owner = summed.reshape(chunk_heads, holders, 2, span_rows, HD).astype(jnp.bfloat16)
+        back = lax.all_to_all(owner, "ctx", split_axis=1, concat_axis=3, tiled=True)
+        back = back[:, 0].astype(jnp.float32)
+        total_keys = back[:, 0].transpose(1, 0, 2).reshape(tokens, chunk_k_cols) + grad_key_own
+        total_values = (
+            back[:, 1].transpose(1, 0, 2).reshape(tokens, chunk_k_cols) + grad_value_own
+        )
+        results.append((attended, grad_queries, total_keys, total_values))
 
     def rows_by_destination(total):
         stack = total.astype(jnp.bfloat16).reshape(tp_size, rows_in, k_cols)
         order = (me + jnp.arange(tp_size, dtype=jnp.int32)) % tp_size
         return tp_send(jnp.take(stack, order, axis=0), me, tp_size)
 
+    def interleave(parts, width):
+        stacked = jnp.stack([p.reshape(rows_in, tp_size, width) for p in parts], axis=2)
+        return stacked.reshape(rows_in, tp_size * len(parts) * width)
+
+    q_width = chunk_heads * group_size * HD
+    attended = interleave([r[0] for r in results], q_width)
+    grad_queries = interleave([r[1] for r in results], q_width)
+    total_keys = jnp.concatenate([r[2] for r in results], axis=1)
+    total_values = jnp.concatenate([r[3] for r in results], axis=1)
     return (attended, grad_queries, rows_by_destination(total_keys), rows_by_destination(total_values))
 
 

time: 399 us -> 383 us (0.960)
  waiting for transfers between devices: 179 us -> 133 us
  local copies, waits for them, and re-layouts: 49.3 us -> 61.5 us
  starting transfers between devices: 54.1 us -> 61.5 us
  other arithmetic: 17.1 us -> 23.6 us
    all_to_all x1 -> x2, waiting for transfers between devices: 59.2 us -> 18.2 us  [body(): lax.all_to_all(send_back, 'ctx', split_axis=3, concat_axis=1, tiled=True)]
    ppermute x8 -> x10, waiting for transfers between devices: 92.2 us -> 59 us  [shift(): lax.ppermute(x, axis, perm=[(s, (s + step) % size) for s in range(size)])]
    all_to_all x1 -> x2, waiting for transfers between devices: 5.06 us -> 29.4 us  [body(): got = lax.all_to_all(send, 'ctx', split_axis=0, concat_axis=4, tiled=True)]
    all_to_all x1 -> x2, starting transfers between devices: 6.86 us -> 16 us  [body(): got = lax.all_to_all(send, 'ctx', split_axis=0, concat_axis=4, tiled=True)]
    transpose x3, local copies, waits for them, and re-layouts: 5.8 us -> 0.18 us  [body(): chunk_selected.transpose(1, 0, 2).reshape(chunk_heads, holders * TOPK)]
    another operation x0 -> x2, local copies, waits for them, and re-layouts: none -> 5.16 us  [interleave(): jnp.stack([p.reshape(rows_in, tp_size, width) for p in parts], axis=2)]
    all_to_all x1 -> x2, starting transfers between devices: 15.4 us -> 11.8 us  [body(): lax.all_to_all(send_back, 'ctx', split_axis=3, concat_axis=1, tiled=True)]
    pallas_call x1 -> x2, Pallas kernels: 97 us -> 100 us  [attention(): pl.pallas_call(kernel, grid_spec=pltpu.PrefetchScalarGridSpec(num_scalar_...]
  transfers between devices with their start and end apart: 12 -> 17, of which waited for: 9 -> 11; matrix products, arithmetic and copies ran while one was open for 9% -> 19% of each run, Pallas kernels for 0% -> 26%
where the time goes in v3:
time: 383 us; the launch traced here: 382 us
  waiting for transfers between devices  133 us (35%)
  Pallas kernels  100 us (26%)
  local copies, waits for them, and re-layouts  61.5 us (16%)
  starting transfers between devices  61.5 us (16%)
  other arithmetic  23.6 us (6%)
    pallas_call x2, Pallas kernels, attention(): pl.pallas_call(kernel, grid_spec=pltpu.PrefetchScalarGridSpec(num_scalar_...  100 us
    ppermute x10, waiting for transfers between devices, shift(): lax.ppermute(x, axis, perm=[(s, (s + step) % size) for s in range(size)])  59 us
    all_to_all x2, waiting for transfers between devices, body(): got = lax.all_to_all(send, 'ctx', split_axis=0, concat_axis=4, tiled=True)  29.4 us
    all_to_all x1, waiting for transfers between devices, body(): spread = lax.all_to_all(kv, 'ctx', split_axis=0, concat_axis=0, tiled=True)  22.6 us
    all_to_all x2, waiting for transfers between devices, body(): lax.all_to_all(send_back, 'ctx', split_axis=3, concat_axis=1, tiled=True)  18.2 us
    all_to_all x2, starting transfers between devices, body(): got = lax.all_to_all(send, 'ctx', split_axis=0, concat_axis=4, tiled=True)  16 us
    all_to_all x2, starting transfers between devices, body(): back = lax.all_to_all(owner, 'ctx', split_axis=1, concat_axis=3, tiled=True)  15.1 us
    ppermute x10, starting transfers between devices, shift(): lax.ppermute(x, axis, perm=[(s, (s + step) % size) for s in range(size)])  12.4 us
  transfers between devices with their start and end apart: 17, of which 11 were waited for; matrix products, arithmetic and copies ran while one was open for 19% of the time, Pallas kernels for 26%

profile of v3, /device:TPU:0, one launch (start us, length us, event | category | flops | bytes accessed | tf_op | source)
XLA Modules:
  0.0 381.7 jit_solution(14350570872074357072)
XLA Ops:
  1.7 3.0 collective-permute-start.2
  6.0 5.9 %collective-permute-done.2 = bf16[256,512]{1,0:T(8,128)(2,1)S(1)} collective-permute-done((bf16[256,512]{1,0:T(8,128)(2,1)S(1)}, bf16[256,512]{1,0:T(8,128)(2,1)S(1)}, u32[]{:S(2)}, u32[]{:S(2)}) %collective-permute-start.2) | collective-permute-done | bytes 262176 | tf_op jit(solution)/shard_map/ppermute | solution.py:131
  12.5 4.1 %collective-permute-done.3 = bf16[256,512]{1,0:T(8,128)(2,1)S(1)} collective-permute-done((bf16[256,512]{1,0:T(8,128)(2,1)S(1)}, bf16[256,512]{1,0:T(8,128)(2,1)S(1)}, u32[]{:S(2)}, u32[]{:S(2)}) %collective-permute-start.3) | collective-permute-done | bytes 262176 | tf_op jit(solution)/shard_map/ppermute | solution.py:131
  19.6 6.3 %all-to-all-start = ((bf16[16,2,32,4,128]{4,2,3,1,0:T(8,128)(2,1)}), bf16[16,2,32,4,128]{4,2,3,1,0:T(8,128)(2,1)S(1)}, u32[]{:S(2)}, u32[]{:S(2)}) async-start(bf16[16,2,32,4,128]{4,2,3,1,0:T(8,128)(2,1)} %pad_maximum_fusion.4), calls=%async_computation | async-start | bytes 2097152 | tf_op jit(solution)/shard_map/all_to_all | solution.py:178
  26.2 22.6 %all-to-all-done = bf16[16,2,32,4,128]{4,2,3,1,0:T(8,128)(2,1)S(1)} async-done(((bf16[16,2,32,4,128]{4,2,3,1,0:T(8,128)(2,1)}), bf16[16,2,32,4,128]{4,2,3,1,0:T(8,128)(2,1)S(1)}, u32[]{:S(2)}, u32[]{:S(2)}) %all-to-all-start) | async-done | bytes 1048608 | tf_op jit(solution)/shard_map/all_to_all | solution.py:178
  51.2 6.9 %all-to-all-start.2 = ((bf16[16,2,3,2,32,128]{5,4,3,2,1,0:T(8,128)(2,1)}), bf16[16,2,3,2,32,128]{5,4,3,2,1,0:T(8,128)(2,1)S(1)}, u32[]{:S(2)}, u32[]{:S(2)}) async-start(bf16[16,2,3,2,32,128]{5,4,3,2,1,0:T(8,128)(2,1)} %bitcast.173), calls=%async_computation.2 | async-start | bytes 3145728 | tf_op jit(solution)/shard_map/all_to_all | solution.py:196
  60.7 29.4 %all-to-all-done.2 = bf16[16,2,3,2,32,128]{5,4,3,2,1,0:T(8,128)(2,1)S(1)} async-done(((bf16[16,2,3,2,32,128]{5,4,3,2,1,0:T(8,128)(2,1)}), bf16[16,2,3,2,32,128]{5,4,3,2,1,0:T(8,128)(2,1)S(1)}, u32[]{:S(2)}, u32[]{:S(2)}) %all-to-all-start.2) | async-done | bytes 1572896 | tf_op jit(solution)/shard_map/all_to_all | solution.py:196
  90.1 9.2 %all-to-all-start.1 = ((bf16[16,2,3,2,32,128]{5,4,3,2,1,0:T(8,128)(2,1)}), bf16[16,2,3,2,32,128]{5,4,3,2,1,0:T(8,128)(2,1)}, u32[]{:S(2)}, u32[]{:S(2)}) async-start(bf16[16,2,3,2,32,128]{5,4,3,2,1,0:T(8,128)(2,1)} %bitcast.171), calls=%async_computation.1 | async-start | bytes 3145728 | tf_op jit(solution)/shard_map/all_to_all | solution.py:196
  99.2 3.3 dynamic-slice_bitcast_fusion
  106.7 22.1 %collective-permute-done.1 = bf16[256,2048]{1,0:T(8,128)(2,1)} collective-permute-done((bf16[256,2048]{1,0:T(8,128)(2,1)}, bf16[256,2048]{1,0:T(8,128)(2,1)}, u32[]{:S(2)}, u32[]{:S(2)}) %collective-permute-start.1) | collective-permute-done | bytes 1048608 | tf_op jit(solution)/shard_map/ppermute | solution.py:131
  128.8 3.1 pad_maximum_fusion.1.do_ref
  131.9 18.9 %collective-permute-done = bf16[256,2048]{1,0:T(8,128)(2,1)} collective-permute-done((bf16[256,2048]{1,0:T(8,128)(2,1)}, bf16[256,2048]{1,0:T(8,128)(2,1)}, u32[]{:S(2)}, u32[]{:S(2)}) %collective-permute-start) | collective-permute-done | bytes 1048608 | tf_op jit(solution)/shard_map/ppermute | solution.py:131
  155.0 50.3 %shard_map.94 = (bf16[2,256,1024]{2,1,0:T(8,128)(2,1)}, bf16[2,256,1024]{2,1,0:T(8,128)(2,1)}, f32[2,3,2,512,128]{4,3,2,1,0:T(8,128)}, f32[512,256]{1,0:T(8,128)}, f32[512,256]{1,0:T(8,128)}) custom-call(s32[8]{0:T(128)} %reshape.135.live_ref, s32[1]{0:T(128)} %bitcast.2.tp_ref, bf16[2,256,2048]{2,1,0:T(8,128)(2,1)} %pad_maximum_fusion.q_ref, ...), custom_call_target="tpu_custom_call" | custom-call | flops 12884901888 | bytes 10485760 | tf_op jit(solution)/shard_map/pallas_call | solution.py:104
  209.3 5.8 %all-to-all-start.5 = ((bf16[2,3,2,16,32,128]{5,4,2,1,0,3:T(8,128)(2,1)}), bf16[2,3,2,16,32,128]{5,4,2,1,0,3:T(8,128)(2,1)S(1)}, u32[]{:S(2)}, u32[]{:S(2)}) async-start(bf16[2,3,2,16,32,128]{5,4,2,1,0,3:T(8,128)(2,1)} %copy.127), calls=%async_computation.5 | async-start | bytes 3145728 | tf_op jit(solution)/shard_map/all_to_all | solution.py:209
  218.6 50.1 %shard_map.93 = (bf16[2,256,1024]{2,1,0:T(8,128)(2,1)}, bf16[2,256,1024]{2,1,0:T(8,128)(2,1)}, f32[2,3,2,512,128]{4,3,2,1,0:T(8,128)}, f32[512,256]{1,0:T(8,128)}, f32[512,256]{1,0:T(8,128)}) custom-call(s32[8]{0:T(128)} %reshape.131.live_ref, s32[1]{0:T(128)} %bitcast.2.tp_ref, bf16[2,256,2048]{2,1,0:T(8,128)(2,1)} %pad_maximum_fusion.q_ref, ...), custom_call_target="tpu_custom_call" | custom-call | flops 12884901888 | bytes 10485760 | tf_op jit(solution)/shard_map/pallas_call | solution.py:104
  272.6 6.0 %all-to-all-start.3 = ((bf16[2,3,2,16,32,128]{5,4,2,1,0,3:T(8,128)(2,1)}), bf16[2,3,2,16,32,128]{5,4,2,1,0,3:T(8,128)(2,1)S(1)}, u32[]{:S(2)}, u32[]{:S(2)}) async-start(bf16[2,3,2,16,32,128]{5,4,2,1,0,3:T(8,128)(2,1)} %copy.121), calls=%async_computation.3 | async-start | bytes 3145728 | tf_op jit(solution)/shard_map/all_to_all | solution.py:209
  292.3 18.2 %all-to-all-done.3 = bf16[2,3,2,16,32,128]{5,4,2,1,0,3:T(8,128)(2,1)S(1)} async-done(((bf16[2,3,2,16,32,128]{5,4,2,1,0,3:T(8,128)(2,1)}), bf16[2,3,2,16,32,128]{5,4,2,1,0,3:T(8,128)(2,1)S(1)}, u32[]{:S(2)}, u32[]{:S(2)}) %all-to-all-start.3) | async-done | bytes 1572896 | tf_op jit(solution)/shard_map/all_to_all | solution.py:209
  310.5 9.2 %all-to-all-start.6 = ((bf16[2,16,2,32,128]{4,3,2,0,1:T(8,128)(2,1)}), bf16[2,16,2,32,128]{4,3,2,0,1:T(8,128)(2,1)}, u32[]{:S(2)}, u32[]{:S(2)}) async-start(bf16[2,16,2,32,128]{4,3,2,0,1:T(8,128)(2,1)} %copy.129), calls=%async_computation.6 | async-start | bytes 1048576 | tf_op jit(solution)/shard_map/all_to_all | solution.py:219
  330.6 4.7 %collective-permute-done.6 = bf16[256,1024]{1,0:T(8,128)(2,1)} collective-permute-done((bf16[256,1024]{1,0:T(8,128)(2,1)}, bf16[256,1024]{1,0:T(8,128)(2,1)}, u32[]{:S(2)}, u32[]{:S(2)}) %collective-permute-start.6) | collective-permute-done | bytes 524320 | tf_op jit(solution)/shard_map/ppermute | solution.py:131
  340.4 5.9 %all-to-all-start.4 = ((bf16[2,16,2,32,128]{4,3,2,0,1:T(8,128)(2,1)}), bf16[2,16,2,32,128]{4,3,2,0,1:T(8,128)(2,1)}, u32[]{:S(2)}, u32[]{:S(2)}) async-start(bf16[2,16,2,32,128]{4,3,2,0,1:T(8,128)(2,1)} %copy.123), calls=%async_computation.4 | async-start | bytes 1048576 | tf_op jit(solution)/shard_map/all_to_all | solution.py:219
  346.4 3.0 select_bitcast_fusion.1
  352.1 4.1 %copy.137 = bf16[256,4096]{1,0:T(8,128)(2,1)} copy(bf16[256,4096]{0,1:T(8,128)(2,1)} %bitcast.167) | data formatting | bytes 4194304
  357.4 3.4 all-to-all-done.4
  370.2 4.1 %copy.136 = bf16[256,4096]{1,0:T(8,128)(2,1)} copy(bf16[256,4096]{0,1:T(8,128)(2,1)} %bitcast.168) | data formatting | bytes 4194304
  (152 shorter events, 81.0 us)
Async XLA Ops:
  1.7 10.2 %collective-permute-start.2 = (bf16[256,512]{1,0:T(8,128)(2,1)S(1)}, bf16[256,512]{1,0:T(8,128)(2,1)S(1)}, u32[]{:S(2)}, u32[]{:S(2)}) collective-permute-start(bf16[256,512]{1,0:T(8,128)(2,1)S(1)} %get-tuple-element.67), channel_id=1, source_target_pairs={{0,1},{1,0},{2,3},{3,2},{4,5},{5,4},{6,7},{7,6},{8,9},{9,8},{10,11... | collective-permute-start | bytes 786440 | tf_op jit(solution)/shard_map/ppermute | solution.py:131
  5.8 10.9 %collective-permute-start.3 = (bf16[256,512]{1,0:T(8,128)(2,1)S(1)}, bf16[256,512]{1,0:T(8,128)(2,1)S(1)}, u32[]{:S(2)}, u32[]{:S(2)}) collective-permute-start(bf16[256,512]{1,0:T(8,128)(2,1)S(1)} %get-tuple-element.69), channel_id=1, source_target_pairs={{0,1},{1,0},{2,3},{3,2},{4,5},{5,4},{6,7},{7,6},{8,9},{9,8},{10,11... | collective-permute-start | bytes 786440 | tf_op jit(solution)/shard_map/ppermute | solution.py:131
  19.6 6.3 %copy-start.19 = (s32[16,4,3]{0,1,2:T(4,128)S(1)}, s32[16,4,3]{0,1,2:T(4,128)}, u32[]{:S(2)}) copy-start(s32[16,4,3]{0,1,2:T(4,128)} %param.13) | copy-start | bytes 2308
  19.6 29.2 %all-to-all-start = ((bf16[16,2,32,4,128]{4,2,3,1,0:T(8,128)(2,1)}), bf16[16,2,32,4,128]{4,2,3,1,0:T(8,128)(2,1)S(1)}, u32[]{:S(2)}, u32[]{:S(2)}) async-start(bf16[16,2,32,4,128]{4,2,3,1,0:T(8,128)(2,1)} %pad_maximum_fusion.4), calls=%async_computation | async-start | bytes 2097152 | tf_op jit(solution)/shard_map/all_to_all | solution.py:178
  51.2 38.8 %all-to-all-start.2 = ((bf16[16,2,3,2,32,128]{5,4,3,2,1,0:T(8,128)(2,1)}), bf16[16,2,3,2,32,128]{5,4,3,2,1,0:T(8,128)(2,1)S(1)}, u32[]{:S(2)}, u32[]{:S(2)}) async-start(bf16[16,2,3,2,32,128]{5,4,3,2,1,0:T(8,128)(2,1)} %bitcast.173), calls=%async_computation.2 | async-start | bytes 3145728 | tf_op jit(solution)/shard_map/all_to_all | solution.py:196
  90.1 119.2 %all-to-all-start.1 = ((bf16[16,2,3,2,32,128]{5,4,3,2,1,0:T(8,128)(2,1)}), bf16[16,2,3,2,32,128]{5,4,3,2,1,0:T(8,128)(2,1)}, u32[]{:S(2)}, u32[]{:S(2)}) async-start(bf16[16,2,3,2,32,128]{5,4,3,2,1,0:T(8,128)(2,1)} %bitcast.171), calls=%async_computation.1 | async-start | bytes 3145728 | tf_op jit(solution)/shard_map/all_to_all | solution.py:196
  102.5 26.3 %collective-permute-start.1 = (bf16[256,2048]{1,0:T(8,128)(2,1)}, bf16[256,2048]{1,0:T(8,128)(2,1)}, u32[]{:S(2)}, u32[]{:S(2)}) collective-permute-start(bf16[256,2048]{1,0:T(8,128)(2,1)} %get-tuple-element.47), channel_id=1, source_target_pairs={{0,1},{1,0},{2,3},{3,2},{4,5},{5,4},{6,7},{7,6},{8,9},{9,8},{10,11... | collective-permute-start | bytes 3145736 | tf_op jit(solution)/shard_map/ppermute | solution.py:131
  105.1 45.6 %collective-permute-start = (bf16[256,2048]{1,0:T(8,128)(2,1)}, bf16[256,2048]{1,0:T(8,128)(2,1)}, u32[]{:S(2)}, u32[]{:S(2)}) collective-permute-start(bf16[256,2048]{1,0:T(8,128)(2,1)} %get-tuple-element.49), channel_id=1, source_target_pairs={{0,1},{1,0},{2,3},{3,2},{4,5},{5,4},{6,7},{7,6},{8,9},{9,8},{10,11... | collective-permute-start | bytes 3145736 | tf_op jit(solution)/shard_map/ppermute | solution.py:131
  209.3 63.3 %all-to-all-start.5 = ((bf16[2,3,2,16,32,128]{5,4,2,1,0,3:T(8,128)(2,1)}), bf16[2,3,2,16,32,128]{5,4,2,1,0,3:T(8,128)(2,1)S(1)}, u32[]{:S(2)}, u32[]{:S(2)}) async-start(bf16[2,3,2,16,32,128]{5,4,2,1,0,3:T(8,128)(2,1)} %copy.127), calls=%async_computation.5 | async-start | bytes 3145728 | tf_op jit(solution)/shard_map/all_to_all | solution.py:209
  272.6 38.0 %all-to-all-start.3 = ((bf16[2,3,2,16,32,128]{5,4,2,1,0,3:T(8,128)(2,1)}), bf16[2,3,2,16,32,128]{5,4,2,1,0,3:T(8,128)(2,1)S(1)}, u32[]{:S(2)}, u32[]{:S(2)}) async-start(bf16[2,3,2,16,32,128]{5,4,2,1,0,3:T(8,128)(2,1)} %copy.121), calls=%async_computation.3 | async-start | bytes 3145728 | tf_op jit(solution)/shard_map/all_to_all | solution.py:209
  281.3 41.0 %collective-permute-start.4 = (bf16[256,1024]{1,0:T(8,128)(2,1)}, bf16[256,1024]{1,0:T(8,128)(2,1)}, u32[]{:S(2)}, u32[]{:S(2)}) collective-permute-start(bf16[256,1024]{1,0:T(8,128)(2,1)} %get-tuple-element.59), channel_id=1, source_target_pairs={{0,1},{1,0},{2,3},{3,2},{4,5},{5,4},{6,7},{7,6},{8,9},{9,8},{10,11... | collective-permute-start | bytes 1572872 | tf_op jit(solution)/shard_map/ppermute | solution.py:131
  283.9 41.2 %collective-permute-start.7 = (bf16[256,1024]{1,0:T(8,128)(2,1)}, bf16[256,1024]{1,0:T(8,128)(2,1)}, u32[]{:S(2)}, u32[]{:S(2)}) collective-permute-start(bf16[256,1024]{1,0:T(8,128)(2,1)} %get-tuple-element.57), channel_id=1, source_target_pairs={{0,1},{1,0},{2,3},{3,2},{4,5},{5,4},{6,7},{7,6},{8,9},{9,8},{10,11... | collective-permute-start | bytes 1572872 | tf_op jit(solution)/shard_map/ppermute | solution.py:131
  285.5 42.4 %collective-permute-start.5 = (bf16[256,1024]{1,0:T(8,128)(2,1)}, bf16[256,1024]{1,0:T(8,128)(2,1)}, u32[]{:S(2)}, u32[]{:S(2)}) collective-permute-start(bf16[256,1024]{1,0:T(8,128)(2,1)} %get-tuple-element.61), channel_id=1, source_target_pairs={{0,1},{1,0},{2,3},{3,2},{4,5},{5,4},{6,7},{7,6},{8,9},{9,8},{10,11... | collective-permute-start | bytes 1572872 | tf_op jit(solution)/shard_map/ppermute | solution.py:131
  291.3 28.4 %copy-start.12 = (bf16[2,256,1024]{2,1,0:T(8,128)(2,1)S(1)}, bf16[2,256,1024]{2,1,0:T(8,128)(2,1)}, u32[]{:S(2)}) copy-start(bf16[2,256,1024]{2,1,0:T(8,128)(2,1)} %get-tuple-element.18) | copy-start | bytes 3145732
  292.3 30.0 %copy-start.10 = (bf16[1,256,1024]{2,1,0:T(8,128)(2,1)S(1)}, bf16[1,256,1024]{2,1,0:T(8,128)(2,1)}, u32[]{:S(2)}) copy-start(bf16[1,256,1024]{2,1,0:T(8,128)(2,1)} %get-tuple-element.58) | copy-start | bytes 1572868
  310.5 29.9 %all-to-all-start.6 = ((bf16[2,16,2,32,128]{4,3,2,0,1:T(8,128)(2,1)}), bf16[2,16,2,32,128]{4,3,2,0,1:T(8,128)(2,1)}, u32[]{:S(2)}, u32[]{:S(2)}) async-start(bf16[2,16,2,32,128]{4,3,2,0,1:T(8,128)(2,1)} %copy.129), calls=%async_computation.6 | async-start | bytes 1048576 | tf_op jit(solution)/shard_map/all_to_all | solution.py:219
  320.8 14.5 %collective-permute-start.6 = (bf16[256,1024]{1,0:T(8,128)(2,1)}, bf16[256,1024]{1,0:T(8,128)(2,1)}, u32[]{:S(2)}, u32[]{:S(2)}) collective-permute-start(bf16[256,1024]{1,0:T(8,128)(2,1)} %get-tuple-element.55), channel_id=1, source_target_pairs={{0,1},{1,0},{2,3},{3,2},{4,5},{5,4},{6,7},{7,6},{8,9},{9,8},{10,11... | collective-permute-start | bytes 1572872 | tf_op jit(solution)/shard_map/ppermute | solution.py:131
  329.0 6.3 %copy-start.11 = (bf16[1,256,1024]{2,1,0:T(8,128)(2,1)S(1)}, bf16[1,256,1024]{2,1,0:T(8,128)(2,1)}, u32[]{:S(2)}) copy-start(bf16[1,256,1024]{2,1,0:T(8,128)(2,1)} %get-tuple-element.54) | copy-start | bytes 1572868
  339.4 6.9 %copy-start = (bf16[2,256,1024]{2,1,0:T(8,128)(2,1)S(1)}, bf16[2,256,1024]{2,1,0:T(8,128)(2,1)}, u32[]{:S(2)}) copy-start(bf16[2,256,1024]{2,1,0:T(8,128)(2,1)} %gather_fusion.4) | copy-start | bytes 3145732
  339.4 6.9 %copy-start.1 = (bf16[2,256,1024]{2,1,0:T(8,128)(2,1)S(1)}, bf16[2,256,1024]{2,1,0:T(8,128)(2,1)}, u32[]{:S(2)}) copy-start(bf16[2,256,1024]{2,1,0:T(8,128)(2,1)} %gather_fusion.7) | copy-start | bytes 3145732
  339.4 6.9 %copy-start.2 = (bf16[2,256,1024]{2,1,0:T(8,128)(2,1)S(1)}, bf16[2,256,1024]{2,1,0:T(8,128)(2,1)}, u32[]{:S(2)}) copy-start(bf16[2,256,1024]{2,1,0:T(8,128)(2,1)} %gather_fusion.5) | copy-start | bytes 3145732
  340.4 20.5 %all-to-all-start.4 = ((bf16[2,16,2,32,128]{4,3,2,0,1:T(8,128)(2,1)}), bf16[2,16,2,32,128]{4,3,2,0,1:T(8,128)(2,1)}, u32[]{:S(2)}, u32[]{:S(2)}) async-start(bf16[2,16,2,32,128]{4,3,2,0,1:T(8,128)(2,1)} %copy.123), calls=%async_computation.4 | async-start | bytes 1048576 | tf_op jit(solution)/shard_map/all_to_all | solution.py:219
  365.2 9.3 %collective-permute-start.8 = (bf16[256,512]{1,0:T(8,128)(2,1)S(1)}, bf16[256,512]{1,0:T(8,128)(2,1)}, u32[]{:S(2)}, u32[]{:S(2)}) collective-permute-start(bf16[256,512]{1,0:T(8,128)(2,1)S(1)} %get-tuple-element.65), channel_id=1, source_target_pairs={{0,1},{1,0},{2,3},{3,2},{4,5},{5,4},{6,7},{7,6},{8,9},{9,8},{10,11... | collective-permute-start | bytes 786440 | tf_op jit(solution)/shard_map/ppermute | solution.py:131
  366.8 12.3 %collective-permute-start.9 = (bf16[256,512]{1,0:T(8,128)(2,1)S(1)}, bf16[256,512]{1,0:T(8,128)(2,1)S(1)}, u32[]{:S(2)}, u32[]{:S(2)}) collective-permute-start(bf16[256,512]{1,0:T(8,128)(2,1)S(1)} %get-tuple-element.63), channel_id=1, source_target_pairs={{0,1},{1,0},{2,3},{3,2},{4,5},{5,4},{6,7},{7,6},{8,9},{9,8},{10,11... | collective-permute-start | bytes 786440 | tf_op jit(solution)/shard_map/ppermute | solution.py:131
  (14 other events, 32.6 us)

commit v4 on v3

--- a/solution.py
+++ b/solution.py
@@ -89,7 +89,7 @@
     )
 
     def piece_in(g, h, t, live, tp):
-        return ((tp[0] - t + tp_size) % tp_size, 0, (first + g) * group_size + h)
+        return ((tp[0] - t + tp_size) % tp_size, 0, g * group_size + h)
 
     def piece_out(g, h, t, live, tp):
         return ((t - tp[0] + tp_size) % tp_size, 0, g * group_size + h)
@@ -164,8 +164,6 @@
     assert tokens == BLK
     key_heads = source_order(tp_receive(key_rows, me, tp_size), me, tp_size).reshape(tokens, k_cols)
     value_heads = source_order(tp_receive(value_rows, me, tp_size), me, tp_size).reshape(tokens, k_cols)
-    query_stack = tp_receive(queries, me, tp_size)
-    upstream_stack = tp_receive(cotangent, me, tp_size)
     head_count = k_cols // HD
     group_size = q_cols // k_cols
     span_rows = BLK // holders
@@ -187,9 +185,18 @@
     chunk_heads = head_count // chunk_count
     chunk_k_cols = chunk_heads * HD
 
+    q_width = chunk_heads * group_size * HD
+
+    def chunk_columns(x, chunk):
+        return x.reshape(rows_in, tp_size, chunk_count, q_width)[:, :, chunk].reshape(
+            rows_in, tp_size * q_width
+        )
+
     results = []
     for chunk in range(chunk_count):
         first = chunk * chunk_heads
+        query_stack = tp_receive(chunk_columns(queries, chunk), me, tp_size)
+        upstream_stack = tp_receive(chunk_columns(cotangent, chunk), me, tp_size)
         chunk_selected = selected[:, first : first + chunk_heads]
         head_ids = jnp.arange(first, first + chunk_heads, dtype=jnp.int32)[None, :, None]
         send = spread[chunk_selected, :, :, head_ids, :]
@@ -233,7 +240,6 @@
         stacked = jnp.stack([p.reshape(rows_in, tp_size, width) for p in parts], axis=2)
         return stacked.reshape(rows_in, tp_size * len(parts) * width)
 
-    q_width = chunk_heads * group_size * HD
     attended = interleave([r[0] for r in results], q_width)
     grad_queries = interleave([r[1] for r in results], q_width)
     total_keys = jnp.concatenate([r[2] for r in results], axis=1)

time: 383 us -> 384 us (level)
  waiting for transfers between devices: 133 us -> 99.7 us
  local copies, waits for them, and re-layouts: 61.5 us -> 89.7 us
    slice x0 -> x2, local copies, waits for them, and re-layouts: none -> 21.7 us  [chunk_columns(): x.reshape(rows_in, tp_size, chunk_count, q_width)[:, :, chunk]]
    all_to_all x2, waiting for transfers between devices: 29.4 us -> 8.96 us  [body(): got = lax.all_to_all(send, 'ctx', split_axis=0, concat_axis=4, tiled=True)]
    ppermute x10 -> x12, waiting for transfers between devices: 59 us -> 46.5 us  [shift(): lax.ppermute(x, axis, perm=[(s, (s + step) % size) for s in range(size)])]
    reshape x0 -> x2, local copies, waits for them, and re-layouts: none -> 6.6 us  [chunk_columns(): x.reshape(rows_in, tp_size, chunk_count, q_width)[:, :, chunk]]
    ppermute x10 -> x12, starting transfers between devices: 12.4 us -> 16.1 us  [shift(): lax.ppermute(x, axis, perm=[(s, (s + step) % size) for s in range(size)])]
    another operation x4 -> x6, other arithmetic: 5.89 us -> 7.73 us  [tp_receive(): return jnp.stack(pieces)]
    unnamed x49 -> x55, local copies, waits for them, and re-layouts: 10.6 us -> 11.7 us
  transfers between devices with their start and end apart: 17 -> 19, of which waited for: 11 -> 12; matrix products, arithmetic and copies ran while one was open for 19% -> 27% of each run, Pallas kernels for 26% -> 26%
where the time goes in v4:
time: 384 us; the launch traced here: 382 us
  Pallas kernels  100 us (26%)
  waiting for transfers between devices  99.7 us (26%)
  local copies, waits for them, and re-layouts  89.7 us (23%)
  starting transfers between devices  65 us (17%)
  other arithmetic  25.5 us (7%)
    pallas_call x2, Pallas kernels, attention(): pl.pallas_call(kernel, grid_spec=pltpu.PrefetchScalarGridSpec(num_scalar_...  100 us
    ppermute x12, waiting for transfers between devices, shift(): lax.ppermute(x, axis, perm=[(s, (s + step) % size) for s in range(size)])  46.5 us
    all_to_all x1, waiting for transfers between devices, body(): spread = lax.all_to_all(kv, 'ctx', split_axis=0, concat_axis=0, tiled=True)  22.6 us
    slice x2, local copies, waits for them, and re-layouts, chunk_columns(): x.reshape(rows_in, tp_size, chunk_count, q_width)[:, :, chunk]  21.7 us
    all_to_all x2, waiting for transfers between devices, body(): lax.all_to_all(send_back, 'ctx', split_axis=3, concat_axis=1, tiled=True)  18.2 us
    ppermute x12, starting transfers between devices, shift(): lax.ppermute(x, axis, perm=[(s, (s + step) % size) for s in range(size)])  16.1 us
    all_to_all x2, starting transfers between devices, body(): got = lax.all_to_all(send, 'ctx', split_axis=0, concat_axis=4, tiled=True)  16.1 us
    all_to_all x2, starting transfers between devices, body(): back = lax.all_to_all(owner, 'ctx', split_axis=1, concat_axis=3, tiled=True)  15.1 us
  transfers between devices with their start and end apart: 19, of which 12 were waited for; matrix products, arithmetic and copies ran while one was open for 27% of the time, Pallas kernels for 26%

profile of v4, /device:TPU:0, one launch (start us, length us, event | category | flops | bytes accessed | tf_op | source)
XLA Modules:
  0.0 382.3 jit_solution(9264596154489016150)
XLA Ops:
  6.0 5.9 %collective-permute-done.2 = bf16[256,512]{1,0:T(8,128)(2,1)S(1)} collective-permute-done((bf16[256,512]{1,0:T(8,128)(2,1)S(1)}, bf16[256,512]{1,0:T(8,128)(2,1)S(1)}, u32[]{:S(2)}, u32[]{:S(2)}) %collective-permute-start.2) | collective-permute-done | bytes 262176 | tf_op jit(solution)/shard_map/ppermute | solution.py:131
  12.5 4.1 %collective-permute-done.3 = bf16[256,512]{1,0:T(8,128)(2,1)S(1)} collective-permute-done((bf16[256,512]{1,0:T(8,128)(2,1)S(1)}, bf16[256,512]{1,0:T(8,128)(2,1)S(1)}, u32[]{:S(2)}, u32[]{:S(2)}) %collective-permute-start.3) | collective-permute-done | bytes 262176 | tf_op jit(solution)/shard_map/ppermute | solution.py:131
  19.7 6.3 %all-to-all-start = ((bf16[16,2,32,4,128]{4,2,3,1,0:T(8,128)(2,1)}), bf16[16,2,32,4,128]{4,2,3,1,0:T(8,128)(2,1)S(1)}, u32[]{:S(2)}, u32[]{:S(2)}) async-start(bf16[16,2,32,4,128]{4,2,3,1,0:T(8,128)(2,1)} %pad_maximum_fusion.4), calls=%async_computation | async-start | bytes 2097152 | tf_op jit(solution)/shard_map/all_to_all | solution.py:176
  26.2 22.6 %all-to-all-done = bf16[16,2,32,4,128]{4,2,3,1,0:T(8,128)(2,1)S(1)} async-done(((bf16[16,2,32,4,128]{4,2,3,1,0:T(8,128)(2,1)}), bf16[16,2,32,4,128]{4,2,3,1,0:T(8,128)(2,1)S(1)}, u32[]{:S(2)}, u32[]{:S(2)}) %all-to-all-start) | async-done | bytes 1048608 | tf_op jit(solution)/shard_map/all_to_all | solution.py:176
  51.2 6.9 %all-to-all-start.2 = ((bf16[16,2,3,2,32,128]{5,4,3,2,1,0:T(8,128)(2,1)}), bf16[16,2,3,2,32,128]{5,4,3,2,1,0:T(8,128)(2,1)}, u32[]{:S(2)}, u32[]{:S(2)}) async-start(bf16[16,2,3,2,32,128]{5,4,3,2,1,0:T(8,128)(2,1)} %bitcast.27), calls=%async_computation.2 | async-start | bytes 3145728 | tf_op jit(solution)/shard_map/all_to_all | solution.py:203
  58.2 3.3 reshape.141
  61.5 11.0 %slice_reduce_fusion.3 = (bf16[256,2,1024]{2,1,0:T(2,128)(2,1)}, bf16[256,2,1024]{2,1,0:T(2,128)(2,1)S(1)}) fusion(bf16[256,2,2,1024]{3,2,1,0:T(2,128)(2,1)S(1)} %reshape.141), kind=kLoop, calls=%fused_computation.17 | loop fusion | bytes 4194304 | tf_op jit(solution)/shard_map/slice | solution.py:191
  81.2 9.0 %all-to-all-done.2 = bf16[16,2,3,2,32,128]{5,4,3,2,1,0:T(8,128)(2,1)} async-done(((bf16[16,2,3,2,32,128]{5,4,3,2,1,0:T(8,128)(2,1)}), bf16[16,2,3,2,32,128]{5,4,3,2,1,0:T(8,128)(2,1)}, u32[]{:S(2)}, u32[]{:S(2)}) %all-to-all-start.2) | async-done | bytes 1572896 | tf_op jit(solution)/shard_map/all_to_all | solution.py:203
  90.2 9.2 %all-to-all-start.1 = ((bf16[16,2,3,2,32,128]{5,4,3,2,1,0:T(8,128)(2,1)}), bf16[16,2,3,2,32,128]{5,4,3,2,1,0:T(8,128)(2,1)}, u32[]{:S(2)}, u32[]{:S(2)}) async-start(bf16[16,2,3,2,32,128]{5,4,3,2,1,0:T(8,128)(2,1)} %bitcast.185), calls=%async_computation.1 | async-start | bytes 3145728 | tf_op jit(solution)/shard_map/all_to_all | solution.py:203
  99.4 10.7 %slice_reduce_fusion.2 = (bf16[256,2,1024]{2,1,0:T(2,128)(2,1)S(1)}, bf16[256,2,1024]{2,1,0:T(2,128)(2,1)S(1)}) fusion(bf16[256,2,2,1024]{3,2,1,0:T(2,128)(2,1)S(1)} %reshape.142), kind=kLoop, calls=%fused_computation.16 | loop fusion | bytes 4194304 | tf_op jit(solution)/shard_map/slice | solution.py:191
  115.2 9.5 %collective-permute-done.6 = bf16[256,1024]{1,0:T(8,128)(2,1)S(1)} collective-permute-done((bf16[256,1024]{1,0:T(8,128)(2,1)S(1)}, bf16[256,1024]{1,0:T(8,128)(2,1)S(1)}, u32[]{:S(2)}, u32[]{:S(2)}) %collective-permute-start.6) | collective-permute-done | bytes 524320 | tf_op jit(solution)/shard_map/ppermute | solution.py:131
  128.6 50.3 %shard_map.94 = (bf16[2,256,1024]{2,1,0:T(8,128)(2,1)}, bf16[2,256,1024]{2,1,0:T(8,128)(2,1)}, f32[2,3,2,512,128]{4,3,2,1,0:T(8,128)}, f32[512,256]{1,0:T(8,128)}, f32[512,256]{1,0:T(8,128)}) custom-call(s32[8]{0:T(128)} %reshape.145.live_ref, s32[1]{0:T(128)} %bitcast.2.tp_ref, bf16[2,256,1024]{2,1,0:T(8,128)(2,1)} %pad_maximum_fusion.6.q_ref, ...), custom_call_target="tpu_custom_call" | custom-call | flops 12884901888 | bytes 10485760 | tf_op jit(solution)/shard_map/pallas_call | solution.py:104
  182.8 5.8 %all-to-all-start.5 = ((bf16[2,3,2,16,32,128]{5,4,2,1,0,3:T(8,128)(2,1)}), bf16[2,3,2,16,32,128]{5,4,2,1,0,3:T(8,128)(2,1)S(1)}, u32[]{:S(2)}, u32[]{:S(2)}) async-start(bf16[2,3,2,16,32,128]{5,4,2,1,0,3:T(8,128)(2,1)} %copy.151), calls=%async_computation.5 | async-start | bytes 3145728 | tf_op jit(solution)/shard_map/all_to_all | solution.py:216
  193.4 10.4 %collective-permute-done.1 = bf16[256,1024]{1,0:T(8,128)(2,1)} collective-permute-done((bf16[256,1024]{1,0:T(8,128)(2,1)S(1)}, bf16[256,1024]{1,0:T(8,128)(2,1)}, u32[]{:S(2)}, u32[]{:S(2)}) %collective-permute-start.1) | collective-permute-done | bytes 524320 | tf_op jit(solution)/shard_map/ppermute | solution.py:131
  206.0 8.6 %collective-permute-done = bf16[256,1024]{1,0:T(8,128)(2,1)} collective-permute-done((bf16[256,1024]{1,0:T(8,128)(2,1)}, bf16[256,1024]{1,0:T(8,128)(2,1)}, u32[]{:S(2)}, u32[]{:S(2)}) %collective-permute-start) | collective-permute-done | bytes 524320 | tf_op jit(solution)/shard_map/ppermute | solution.py:131
  219.6 50.1 %shard_map.93 = (bf16[2,256,1024]{2,1,0:T(8,128)(2,1)}, bf16[2,256,1024]{2,1,0:T(8,128)(2,1)}, f32[2,3,2,512,128]{4,3,2,1,0:T(8,128)}, f32[512,256]{1,0:T(8,128)}, f32[512,256]{1,0:T(8,128)}) custom-call(s32[8]{0:T(128)} %reshape.139.live_ref, s32[1]{0:T(128)} %bitcast.2.tp_ref, bf16[2,256,1024]{2,1,0:T(8,128)(2,1)} %pad_maximum_fusion.2.q_ref, ...), custom_call_target="tpu_custom_call" | custom-call | flops 12884901888 | bytes 10485760 | tf_op jit(solution)/shard_map/pallas_call | solution.py:104
  273.5 5.7 %all-to-all-start.3 = ((bf16[2,3,2,16,32,128]{5,4,2,1,0,3:T(8,128)(2,1)}), bf16[2,3,2,16,32,128]{5,4,2,1,0,3:T(8,128)(2,1)S(1)}, u32[]{:S(2)}, u32[]{:S(2)}) async-start(bf16[2,3,2,16,32,128]{5,4,2,1,0,3:T(8,128)(2,1)} %copy.145), calls=%async_computation.3 | async-start | bytes 3145728 | tf_op jit(solution)/shard_map/all_to_all | solution.py:216
  293.0 18.2 %all-to-all-done.3 = bf16[2,3,2,16,32,128]{5,4,2,1,0,3:T(8,128)(2,1)S(1)} async-done(((bf16[2,3,2,16,32,128]{5,4,2,1,0,3:T(8,128)(2,1)}), bf16[2,3,2,16,32,128]{5,4,2,1,0,3:T(8,128)(2,1)S(1)}, u32[]{:S(2)}, u32[]{:S(2)}) %all-to-all-start.3) | async-done | bytes 1572896 | tf_op jit(solution)/shard_map/all_to_all | solution.py:216
  311.2 9.2 %all-to-all-start.6 = ((bf16[2,16,2,32,128]{4,3,2,0,1:T(8,128)(2,1)}), bf16[2,16,2,32,128]{4,3,2,0,1:T(8,128)(2,1)}, u32[]{:S(2)}, u32[]{:S(2)}) async-start(bf16[2,16,2,32,128]{4,3,2,0,1:T(8,128)(2,1)} %copy.153), calls=%async_computation.6 | async-start | bytes 1048576 | tf_op jit(solution)/shard_map/all_to_all | solution.py:226
  331.3 4.7 %collective-permute-done.8 = bf16[256,1024]{1,0:T(8,128)(2,1)} collective-permute-done((bf16[256,1024]{1,0:T(8,128)(2,1)}, bf16[256,1024]{1,0:T(8,128)(2,1)}, u32[]{:S(2)}, u32[]{:S(2)}) %collective-permute-start.8) | collective-permute-done | bytes 524320 | tf_op jit(solution)/shard_map/ppermute | solution.py:131
  341.1 5.9 %all-to-all-start.4 = ((bf16[2,16,2,32,128]{4,3,2,0,1:T(8,128)(2,1)}), bf16[2,16,2,32,128]{4,3,2,0,1:T(8,128)(2,1)}, u32[]{:S(2)}, u32[]{:S(2)}) async-start(bf16[2,16,2,32,128]{4,3,2,0,1:T(8,128)(2,1)} %copy.147), calls=%async_computation.4 | async-start | bytes 1048576 | tf_op jit(solution)/shard_map/all_to_all | solution.py:226
  352.8 4.1 %copy.161 = bf16[256,4096]{1,0:T(8,128)(2,1)} copy(bf16[256,4096]{0,1:T(8,128)(2,1)} %bitcast.181) | data formatting | bytes 4194304
  358.1 3.4 all-to-all-done.4
  370.8 4.1 %copy.160 = bf16[256,4096]{1,0:T(8,128)(2,1)} copy(bf16[256,4096]{0,1:T(8,128)(2,1)} %bitcast.182) | data formatting | bytes 4194304
  (170 shorter events, 102.2 us)
Async XLA Ops:
  1.7 10.2 %collective-permute-start.2 = (bf16[256,512]{1,0:T(8,128)(2,1)S(1)}, bf16[256,512]{1,0:T(8,128)(2,1)S(1)}, u32[]{:S(2)}, u32[]{:S(2)}) collective-permute-start(bf16[256,512]{1,0:T(8,128)(2,1)S(1)} %get-tuple-element.75), channel_id=1, source_target_pairs={{0,1},{1,0},{2,3},{3,2},{4,5},{5,4},{6,7},{7,6},{8,9},{9,8},{10,11... | collective-permute-start | bytes 786440 | tf_op jit(solution)/shard_map/ppermute | solution.py:131
  5.8 10.9 %collective-permute-start.3 = (bf16[256,512]{1,0:T(8,128)(2,1)S(1)}, bf16[256,512]{1,0:T(8,128)(2,1)S(1)}, u32[]{:S(2)}, u32[]{:S(2)}) collective-permute-start(bf16[256,512]{1,0:T(8,128)(2,1)S(1)} %get-tuple-element.77), channel_id=1, source_target_pairs={{0,1},{1,0},{2,3},{3,2},{4,5},{5,4},{6,7},{7,6},{8,9},{9,8},{10,11... | collective-permute-start | bytes 786440 | tf_op jit(solution)/shard_map/ppermute | solution.py:131
  19.7 29.2 %all-to-all-start = ((bf16[16,2,32,4,128]{4,2,3,1,0:T(8,128)(2,1)}), bf16[16,2,32,4,128]{4,2,3,1,0:T(8,128)(2,1)S(1)}, u32[]{:S(2)}, u32[]{:S(2)}) async-start(bf16[16,2,32,4,128]{4,2,3,1,0:T(8,128)(2,1)} %pad_maximum_fusion.4), calls=%async_computation | async-start | bytes 2097152 | tf_op jit(solution)/shard_map/all_to_all | solution.py:176
  51.2 39.0 %all-to-all-start.2 = ((bf16[16,2,3,2,32,128]{5,4,3,2,1,0:T(8,128)(2,1)}), bf16[16,2,3,2,32,128]{5,4,3,2,1,0:T(8,128)(2,1)}, u32[]{:S(2)}, u32[]{:S(2)}) async-start(bf16[16,2,3,2,32,128]{5,4,3,2,1,0:T(8,128)(2,1)} %bitcast.27), calls=%async_computation.2 | async-start | bytes 3145728 | tf_op jit(solution)/shard_map/all_to_all | solution.py:203
  73.8 39.2 %collective-permute-start.5 = (bf16[256,1024]{1,0:T(8,128)(2,1)}, bf16[256,1024]{1,0:T(8,128)(2,1)}, u32[]{:S(2)}, u32[]{:S(2)}) collective-permute-start(bf16[256,1024]{1,0:T(8,128)(2,1)} %get-tuple-element.69), channel_id=1, source_target_pairs={{0,1},{1,0},{2,3},{3,2},{4,5},{5,4},{6,7},{7,6},{8,9},{9,8},{10,11... | collective-permute-start | bytes 1572872 | tf_op jit(solution)/shard_map/ppermute | solution.py:131
  90.2 92.6 %all-to-all-start.1 = ((bf16[16,2,3,2,32,128]{5,4,3,2,1,0:T(8,128)(2,1)}), bf16[16,2,3,2,32,128]{5,4,3,2,1,0:T(8,128)(2,1)}, u32[]{:S(2)}, u32[]{:S(2)}) async-start(bf16[16,2,3,2,32,128]{5,4,3,2,1,0:T(8,128)(2,1)} %bitcast.185), calls=%async_computation.1 | async-start | bytes 3145728 | tf_op jit(solution)/shard_map/all_to_all | solution.py:203
  110.4 14.2 %collective-permute-start.6 = (bf16[256,1024]{1,0:T(8,128)(2,1)S(1)}, bf16[256,1024]{1,0:T(8,128)(2,1)S(1)}, u32[]{:S(2)}, u32[]{:S(2)}) collective-permute-start(bf16[256,1024]{1,0:T(8,128)(2,1)S(1)} %get-tuple-element.67), channel_id=1, source_target_pairs={{0,1},{1,0},{2,3},{3,2},{4,5},{5,4},{6,7},{7,6},{8,9},{9,8},{10,11... | collective-permute-start | bytes 1572872 | tf_op jit(solution)/shard_map/ppermute | solution.py:131
  182.8 90.7 %all-to-all-start.5 = ((bf16[2,3,2,16,32,128]{5,4,2,1,0,3:T(8,128)(2,1)}), bf16[2,3,2,16,32,128]{5,4,2,1,0,3:T(8,128)(2,1)S(1)}, u32[]{:S(2)}, u32[]{:S(2)}) async-start(bf16[2,3,2,16,32,128]{5,4,2,1,0,3:T(8,128)(2,1)} %copy.151), calls=%async_computation.5 | async-start | bytes 3145728 | tf_op jit(solution)/shard_map/all_to_all | solution.py:216
  188.9 14.9 %collective-permute-start.1 = (bf16[256,1024]{1,0:T(8,128)(2,1)S(1)}, bf16[256,1024]{1,0:T(8,128)(2,1)}, u32[]{:S(2)}, u32[]{:S(2)}) collective-permute-start(bf16[256,1024]{1,0:T(8,128)(2,1)S(1)} %get-tuple-element.61), channel_id=1, source_target_pairs={{0,1},{1,0},{2,3},{3,2},{4,5},{5,4},{6,7},{7,6},{8,9},{9,8},{10,11... | collective-permute-start | bytes 1572872 | tf_op jit(solution)/shard_map/ppermute | solution.py:131
  191.6 22.9 %collective-permute-start = (bf16[256,1024]{1,0:T(8,128)(2,1)}, bf16[256,1024]{1,0:T(8,128)(2,1)}, u32[]{:S(2)}, u32[]{:S(2)}) collective-permute-start(bf16[256,1024]{1,0:T(8,128)(2,1)} %get-tuple-element.63), channel_id=1, source_target_pairs={{0,1},{1,0},{2,3},{3,2},{4,5},{5,4},{6,7},{7,6},{8,9},{9,8},{10,11... | collective-permute-start | bytes 1572872 | tf_op jit(solution)/shard_map/ppermute | solution.py:131
  273.5 37.7 %all-to-all-start.3 = ((bf16[2,3,2,16,32,128]{5,4,2,1,0,3:T(8,128)(2,1)}), bf16[2,3,2,16,32,128]{5,4,2,1,0,3:T(8,128)(2,1)S(1)}, u32[]{:S(2)}, u32[]{:S(2)}) async-start(bf16[2,3,2,16,32,128]{5,4,2,1,0,3:T(8,128)(2,1)} %copy.145), calls=%async_computation.3 | async-start | bytes 3145728 | tf_op jit(solution)/shard_map/all_to_all | solution.py:216
  282.0 41.0 %collective-permute-start.4 = (bf16[256,1024]{1,0:T(8,128)(2,1)}, bf16[256,1024]{1,0:T(8,128)(2,1)}, u32[]{:S(2)}, u32[]{:S(2)}) collective-permute-start(bf16[256,1024]{1,0:T(8,128)(2,1)} %get-tuple-element.59), channel_id=1, source_target_pairs={{0,1},{1,0},{2,3},{3,2},{4,5},{5,4},{6,7},{7,6},{8,9},{9,8},{10,11... | collective-permute-start | bytes 1572872 | tf_op jit(solution)/shard_map/ppermute | solution.py:131
  284.5 41.2 %collective-permute-start.9 = (bf16[256,1024]{1,0:T(8,128)(2,1)}, bf16[256,1024]{1,0:T(8,128)(2,1)}, u32[]{:S(2)}, u32[]{:S(2)}) collective-permute-start(bf16[256,1024]{1,0:T(8,128)(2,1)} %get-tuple-element.57), channel_id=1, source_target_pairs={{0,1},{1,0},{2,3},{3,2},{4,5},{5,4},{6,7},{7,6},{8,9},{9,8},{10,11... | collective-permute-start | bytes 1572872 | tf_op jit(solution)/shard_map/ppermute | solution.py:131
  286.1 42.4 %collective-permute-start.7 = (bf16[256,1024]{1,0:T(8,128)(2,1)}, bf16[256,1024]{1,0:T(8,128)(2,1)}, u32[]{:S(2)}, u32[]{:S(2)}) collective-permute-start(bf16[256,1024]{1,0:T(8,128)(2,1)} %get-tuple-element.65), channel_id=1, source_target_pairs={{0,1},{1,0},{2,3},{3,2},{4,5},{5,4},{6,7},{7,6},{8,9},{9,8},{10,11... | collective-permute-start | bytes 1572872 | tf_op jit(solution)/shard_map/ppermute | solution.py:131
  292.0 28.4 %copy-start.15 = (bf16[2,256,1024]{2,1,0:T(8,128)(2,1)S(1)}, bf16[2,256,1024]{2,1,0:T(8,128)(2,1)}, u32[]{:S(2)}) copy-start(bf16[2,256,1024]{2,1,0:T(8,128)(2,1)} %get-tuple-element.18) | copy-start | bytes 3145732
  293.0 30.0 %copy-start.11 = (bf16[1,256,1024]{2,1,0:T(8,128)(2,1)S(1)}, bf16[1,256,1024]{2,1,0:T(8,128)(2,1)}, u32[]{:S(2)}) copy-start(bf16[1,256,1024]{2,1,0:T(8,128)(2,1)} %get-tuple-element.58) | copy-start | bytes 1572868
  311.2 29.9 %all-to-all-start.6 = ((bf16[2,16,2,32,128]{4,3,2,0,1:T(8,128)(2,1)}), bf16[2,16,2,32,128]{4,3,2,0,1:T(8,128)(2,1)}, u32[]{:S(2)}, u32[]{:S(2)}) async-start(bf16[2,16,2,32,128]{4,3,2,0,1:T(8,128)(2,1)} %copy.153), calls=%async_computation.6 | async-start | bytes 1048576 | tf_op jit(solution)/shard_map/all_to_all | solution.py:226
  321.4 14.5 %collective-permute-start.8 = (bf16[256,1024]{1,0:T(8,128)(2,1)}, bf16[256,1024]{1,0:T(8,128)(2,1)}, u32[]{:S(2)}, u32[]{:S(2)}) collective-permute-start(bf16[256,1024]{1,0:T(8,128)(2,1)} %get-tuple-element.55), channel_id=1, source_target_pairs={{0,1},{1,0},{2,3},{3,2},{4,5},{5,4},{6,7},{7,6},{8,9},{9,8},{10,11... | collective-permute-start | bytes 1572872 | tf_op jit(solution)/shard_map/ppermute | solution.py:131
  340.1 6.9 %copy-start = (bf16[2,256,1024]{2,1,0:T(8,128)(2,1)S(1)}, bf16[2,256,1024]{2,1,0:T(8,128)(2,1)}, u32[]{:S(2)}) copy-start(bf16[2,256,1024]{2,1,0:T(8,128)(2,1)} %gather_fusion.4) | copy-start | bytes 3145732
  340.1 6.9 %copy-start.1 = (bf16[2,256,1024]{2,1,0:T(8,128)(2,1)S(1)}, bf16[2,256,1024]{2,1,0:T(8,128)(2,1)}, u32[]{:S(2)}) copy-start(bf16[2,256,1024]{2,1,0:T(8,128)(2,1)} %gather_fusion.7) | copy-start | bytes 3145732
  340.1 6.9 %copy-start.2 = (bf16[2,256,1024]{2,1,0:T(8,128)(2,1)S(1)}, bf16[2,256,1024]{2,1,0:T(8,128)(2,1)}, u32[]{:S(2)}) copy-start(bf16[2,256,1024]{2,1,0:T(8,128)(2,1)} %gather_fusion.5) | copy-start | bytes 3145732
  341.1 20.5 %all-to-all-start.4 = ((bf16[2,16,2,32,128]{4,3,2,0,1:T(8,128)(2,1)}), bf16[2,16,2,32,128]{4,3,2,0,1:T(8,128)(2,1)}, u32[]{:S(2)}, u32[]{:S(2)}) async-start(bf16[2,16,2,32,128]{4,3,2,0,1:T(8,128)(2,1)} %copy.147), calls=%async_computation.4 | async-start | bytes 1048576 | tf_op jit(solution)/shard_map/all_to_all | solution.py:226
  365.9 9.3 %collective-permute-start.10 = (bf16[256,512]{1,0:T(8,128)(2,1)S(1)}, bf16[256,512]{1,0:T(8,128)(2,1)}, u32[]{:S(2)}, u32[]{:S(2)}) collective-permute-start(bf16[256,512]{1,0:T(8,128)(2,1)S(1)} %get-tuple-element.73), channel_id=1, source_target_pairs={{0,1},{1,0},{2,3},{3,2},{4,5},{5,4},{6,7},{7,6},{8,9},{9,8},{10,11... | collective-permute-start | bytes 786440 | tf_op jit(solution)/shard_map/ppermute | solution.py:131
  367.5 12.3 %collective-permute-start.11 = (bf16[256,512]{1,0:T(8,128)(2,1)S(1)}, bf16[256,512]{1,0:T(8,128)(2,1)S(1)}, u32[]{:S(2)}, u32[]{:S(2)}) collective-permute-start(bf16[256,512]{1,0:T(8,128)(2,1)S(1)} %get-tuple-element.71), channel_id=1, source_target_pairs={{0,1},{1,0},{2,3},{3,2},{4,5},{5,4},{6,7},{7,6},{8,9},{9,8},{10,11... | collective-permute-start | bytes 786440 | tf_op jit(solution)/shard_map/ppermute | solution.py:131
  (17 other events, 43.3 us)

commit v5 on v4

--- a/solution.py
+++ b/solution.py
@@ -131,12 +131,14 @@
     return lax.ppermute(x, axis, perm=[(s, (s + step) % size) for s in range(size)])
 
 
-def tp_receive(x, me, size):
-    width = x.shape[1] // size
-    pieces = [lax.dynamic_slice_in_dim(x, me * width, width, 1)]
+def tp_receive(x, me, size, width=None, offset=0):
+    stride = x.shape[1] // size
+    width = stride if width is None else width
+    pieces = [lax.dynamic_slice_in_dim(x, me * stride + offset, width, 1)]
     for step in range(1, size):
         dest = (me + step) % size
-        pieces.append(shift(lax.dynamic_slice_in_dim(x, dest * width, width, 1), "tp", step, size))
+        piece = lax.dynamic_slice_in_dim(x, dest * stride + offset, width, 1)
+        pieces.append(shift(piece, "tp", step, size))
     return jnp.stack(pieces)
 
 
@@ -183,20 +185,14 @@
     tp_info = me.astype(jnp.int32).reshape(1)
     chunk_count = 2 if head_count % 2 == 0 else 1
     chunk_heads = head_count // chunk_count
-    chunk_k_cols = chunk_heads * HD
 
     q_width = chunk_heads * group_size * HD
-
-    def chunk_columns(x, chunk):
-        return x.reshape(rows_in, tp_size, chunk_count, q_width)[:, :, chunk].reshape(
-            rows_in, tp_size * q_width
-        )
 
     results = []
     for chunk in range(chunk_count):
         first = chunk * chunk_heads
-        query_stack = tp_receive(chunk_columns(queries, chunk), me, tp_size)
-        upstream_stack = tp_receive(chunk_columns(cotangent, chunk), me, tp_size)
+        query_stack = tp_receive(queries, me, tp_size, q_width, chunk * q_width)
+        upstream_stack = tp_receive(cotangent, me, tp_size, q_width, chunk * q_width)
         chunk_selected = selected[:, first : first + chunk_heads]
         head_ids = jnp.arange(first, first + chunk_heads, dtype=jnp.int32)[None, :, None]
         send = spread[chunk_selected, :, :, head_ids, :]
@@ -222,14 +218,16 @@
             targets[:, None, :] == jnp.arange(holders, dtype=jnp.int32)[None, :, None]
         ).astype(jnp.float32)
         summed = jnp.einsum("gjn,gnx->gjx", table, flat, precision=lax.Precision.HIGHEST)
-        owner = summed.reshape(chunk_heads, holders, 2, span_rows, HD).astype(jnp.bfloat16)
-        back = lax.all_to_all(owner, "ctx", split_axis=1, concat_axis=3, tiled=True)
-        back = back[:, 0].astype(jnp.float32)
-        total_keys = back[:, 0].transpose(1, 0, 2).reshape(tokens, chunk_k_cols) + grad_key_own
-        total_values = (
-            back[:, 1].transpose(1, 0, 2).reshape(tokens, chunk_k_cols) + grad_value_own
-        )
-        results.append((attended, grad_queries, total_keys, total_values))
+        results.append((attended, grad_queries, summed, grad_key_own, grad_value_own))
+
+    summed = jnp.concatenate([r[2] for r in results], axis=0)
+    owner = summed.reshape(head_count, holders, 2, span_rows, HD).astype(jnp.bfloat16)
+    back = lax.all_to_all(owner, "ctx", split_axis=1, concat_axis=3, tiled=True)
+    back = back[:, 0].astype(jnp.float32)
+    own_keys = jnp.concatenate([r[3] for r in results], axis=1)
+    own_values = jnp.concatenate([r[4] for r in results], axis=1)
+    total_keys = back[:, 0].transpose(1, 0, 2).reshape(tokens, k_cols) + own_keys
+    total_values = back[:, 1].transpose(1, 0, 2).reshape(tokens, k_cols) + own_values
 
     def rows_by_destination(total):
         stack = total.astype(jnp.bfloat16).reshape(tp_size, rows_in, k_cols)
@@ -242,8 +240,6 @@
 
     attended = interleave([r[0] for r in results], q_width)
     grad_queries = interleave([r[1] for r in results], q_width)
-    total_keys = jnp.concatenate([r[2] for r in results], axis=1)
-    total_values = jnp.concatenate([r[3] for r in results], axis=1)
     return (attended, grad_queries, rows_by_destination(total_keys), rows_by_destination(total_values))
 
 

time: 384 us -> 409 us (1.065)
  waiting for transfers between devices: 99.7 us -> 150 us
  local copies, waits for them, and re-layouts: 89.7 us -> 66.6 us
  starting transfers between devices: 65 us -> 57.5 us
  other arithmetic: 25.5 us -> 30.6 us
    ppermute x12, waiting for transfers between devices: 46.5 us -> 75.3 us  [shift(): lax.ppermute(x, axis, perm=[(s, (s + step) % size) for s in range(size)])]
    slice x2 -> x0, local copies, waits for them, and re-layouts: 21.7 us -> none  [chunk_columns(): x.reshape(rows_in, tp_size, chunk_count, q_width)[:, :, chunk]]
    all_to_all x2, waiting for transfers between devices: 8.96 us -> 29.4 us  [body(): got = lax.all_to_all(send, 'ctx', split_axis=0, concat_axis=4, tiled=True)]
    reshape x4 -> x2, local copies, waits for them, and re-layouts: 8.33 us -> 0.84 us  [the longest x1 0.42 us: body(): back[:, 0].transpose(1, 0, 2).reshape(tokens, k_cols) + own_keys]
    all_to_all x2 -> x1, starting transfers between devices: 15.1 us -> 9.3 us  [body(): back = lax.all_to_all(owner, 'ctx', split_axis=1, concat_axis=3, tiled=True)]
    all_to_all x2, waiting for transfers between devices: 18.2 us -> 22.7 us  [body(): lax.all_to_all(send_back, 'ctx', split_axis=3, concat_axis=1, tiled=True)]
    transpose x0 -> x5, local copies, waits for them, and re-layouts: none -> 4.1 us  [the longest x2 3.01 us: body(): back[:, 1].transpose(1, 0, 2).reshape(tokens, k_cols) + own_values]
    unnamed x55 -> x40, local copies, waits for them, and re-layouts: 11.7 us -> 13 us
  transfers between devices with their start and end apart: 19 -> 18, of which waited for: 12 -> 14; matrix products, arithmetic and copies ran while one was open for 27% -> 19% of each run, Pallas kernels for 26% -> 25%
where the time goes in v5:
time: 409 us; the launch traced here: 407 us
  waiting for transfers between devices  150 us (37%)
  Pallas kernels  100 us (24%)
  local copies, waits for them, and re-layouts  66.6 us (16%)
  starting transfers between devices  57.5 us (14%)
  other arithmetic  30.6 us (7%)
    pallas_call x2, Pallas kernels, attention(): pl.pallas_call(kernel, grid_spec=pltpu.PrefetchScalarGridSpec(num_scalar_...  100 us
    ppermute x12, waiting for transfers between devices, shift(): lax.ppermute(x, axis, perm=[(s, (s + step) % size) for s in range(size)])  75.3 us
    all_to_all x2, waiting for transfers between devices, body(): got = lax.all_to_all(send, 'ctx', split_axis=0, concat_axis=4, tiled=True)  29.4 us
    all_to_all x2, waiting for transfers between devices, body(): lax.all_to_all(send_back, 'ctx', split_axis=3, concat_axis=1, tiled=True)  22.7 us
    all_to_all x1, waiting for transfers between devices, body(): spread = lax.all_to_all(kv, 'ctx', split_axis=0, concat_axis=0, tiled=True)  22.6 us
    all_to_all x2, starting transfers between devices, body(): got = lax.all_to_all(send, 'ctx', split_axis=0, concat_axis=4, tiled=True)  16 us
    ppermute x12, starting transfers between devices, shift(): lax.ppermute(x, axis, perm=[(s, (s + step) % size) for s in range(size)])  14.5 us
    unnamed x40, local copies, waits for them, and re-layouts  13 us
  transfers between devices with their start and end apart: 18, of which 14 were waited for; matrix products, arithmetic and copies ran while one was open for 19% of the time, Pallas kernels for 25%

profile of v5, /device:TPU:0, one launch (start us, length us, event | category | flops | bytes accessed | tf_op | source)
XLA Modules:
  0.0 407.0 jit_solution(4761522414537512043)
XLA Ops:
  6.0 5.9 %collective-permute-done.2 = bf16[256,512]{1,0:T(8,128)(2,1)S(1)} collective-permute-done((bf16[256,512]{1,0:T(8,128)(2,1)S(1)}, bf16[256,512]{1,0:T(8,128)(2,1)S(1)}, u32[]{:S(2)}, u32[]{:S(2)}) %collective-permute-start.2) | collective-permute-done | bytes 262176 | tf_op jit(solution)/shard_map/ppermute | solution.py:131
  12.5 4.1 %collective-permute-done.3 = bf16[256,512]{1,0:T(8,128)(2,1)S(1)} collective-permute-done((bf16[256,512]{1,0:T(8,128)(2,1)S(1)}, bf16[256,512]{1,0:T(8,128)(2,1)S(1)}, u32[]{:S(2)}, u32[]{:S(2)}) %collective-permute-start.3) | collective-permute-done | bytes 262176 | tf_op jit(solution)/shard_map/ppermute | solution.py:131
  19.7 6.3 %all-to-all-start = ((bf16[16,2,32,4,128]{4,2,3,1,0:T(8,128)(2,1)}), bf16[16,2,32,4,128]{4,2,3,1,0:T(8,128)(2,1)S(1)}, u32[]{:S(2)}, u32[]{:S(2)}) async-start(bf16[16,2,32,4,128]{4,2,3,1,0:T(8,128)(2,1)} %pad_maximum_fusion.4), calls=%async_computation | async-start | bytes 2097152 | tf_op jit(solution)/shard_map/all_to_all | solution.py:178
  26.2 22.6 %all-to-all-done = bf16[16,2,32,4,128]{4,2,3,1,0:T(8,128)(2,1)S(1)} async-done(((bf16[16,2,32,4,128]{4,2,3,1,0:T(8,128)(2,1)}), bf16[16,2,32,4,128]{4,2,3,1,0:T(8,128)(2,1)S(1)}, u32[]{:S(2)}, u32[]{:S(2)}) %all-to-all-start) | async-done | bytes 1048608 | tf_op jit(solution)/shard_map/all_to_all | solution.py:178
  51.2 6.9 %all-to-all-start.2 = ((bf16[16,2,3,2,32,128]{5,4,3,2,1,0:T(8,128)(2,1)}), bf16[16,2,3,2,32,128]{5,4,3,2,1,0:T(8,128)(2,1)S(1)}, u32[]{:S(2)}, u32[]{:S(2)}) async-start(bf16[16,2,3,2,32,128]{5,4,3,2,1,0:T(8,128)(2,1)} %bitcast.140), calls=%async_computation.2 | async-start | bytes 3145728 | tf_op jit(solution)/shard_map/all_to_all | solution.py:199
  60.7 29.4 %all-to-all-done.2 = bf16[16,2,3,2,32,128]{5,4,3,2,1,0:T(8,128)(2,1)S(1)} async-done(((bf16[16,2,3,2,32,128]{5,4,3,2,1,0:T(8,128)(2,1)}), bf16[16,2,3,2,32,128]{5,4,3,2,1,0:T(8,128)(2,1)S(1)}, u32[]{:S(2)}, u32[]{:S(2)}) %all-to-all-start.2) | async-done | bytes 1572896 | tf_op jit(solution)/shard_map/all_to_all | solution.py:199
  90.1 9.1 %all-to-all-start.1 = ((bf16[16,2,3,2,32,128]{5,4,3,2,1,0:T(8,128)(2,1)}), bf16[16,2,3,2,32,128]{5,4,3,2,1,0:T(8,128)(2,1)S(1)}, u32[]{:S(2)}, u32[]{:S(2)}) async-start(bf16[16,2,3,2,32,128]{5,4,3,2,1,0:T(8,128)(2,1)} %bitcast.12), calls=%async_computation.1 | async-start | bytes 3145728 | tf_op jit(solution)/shard_map/all_to_all | solution.py:199
  99.2 3.1 dynamic-slice_bitcast_fusion.2
  106.7 10.7 %collective-permute-done.6 = bf16[256,1024]{1,0:T(8,128)(2,1)} collective-permute-done((bf16[256,1024]{1,0:T(8,128)(2,1)}, bf16[256,1024]{1,0:T(8,128)(2,1)}, u32[]{:S(2)}, u32[]{:S(2)}) %collective-permute-start.6) | collective-permute-done | bytes 524320 | tf_op jit(solution)/shard_map/ppermute | solution.py:131
  119.7 8.4 %collective-permute-done.5 = bf16[256,1024]{1,0:T(8,128)(2,1)} collective-permute-done((bf16[256,1024]{1,0:T(8,128)(2,1)}, bf16[256,1024]{1,0:T(8,128)(2,1)}, u32[]{:S(2)}, u32[]{:S(2)}) %collective-permute-start.5) | collective-permute-done | bytes 524320 | tf_op jit(solution)/shard_map/ppermute | solution.py:131
  131.7 50.3 %shard_map.94 = (bf16[2,256,1024]{2,1,0:T(8,128)(2,1)}, bf16[2,256,1024]{2,1,0:T(8,128)(2,1)}, f32[2,3,2,512,128]{4,3,2,1,0:T(8,128)}, f32[512,256]{1,0:T(8,128)}, f32[512,256]{1,0:T(8,128)}) custom-call(s32[8]{0:T(128)} %reshape.120.live_ref, s32[1]{0:T(128)} %bitcast.2.tp_ref, bf16[2,256,1024]{2,1,0:T(8,128)(2,1)} %pad_maximum_fusion.6.q_ref, ...), custom_call_target="tpu_custom_call" | custom-call | flops 12884901888 | bytes 10485760 | tf_op jit(solution)/shard_map/pallas_call | solution.py:104
  185.8 5.8 %all-to-all-start.4 = ((bf16[2,3,2,16,32,128]{5,4,2,1,0,3:T(8,128)(2,1)}), bf16[2,3,2,16,32,128]{5,4,2,1,0,3:T(8,128)(2,1)S(1)}, u32[]{:S(2)}, u32[]{:S(2)}) async-start(bf16[2,3,2,16,32,128]{5,4,2,1,0,3:T(8,128)(2,1)} %copy.119), calls=%async_computation.4 | async-start | bytes 3145728 | tf_op jit(solution)/shard_map/all_to_all | solution.py:212
  194.3 12.4 %collective-permute-done.1 = bf16[256,1024]{1,0:T(8,128)(2,1)} collective-permute-done((bf16[256,1024]{1,0:T(8,128)(2,1)}, bf16[256,1024]{1,0:T(8,128)(2,1)}, u32[]{:S(2)}, u32[]{:S(2)}) %collective-permute-start.1) | collective-permute-done | bytes 524320 | tf_op jit(solution)/shard_map/ppermute | solution.py:131
  209.0 8.5 %collective-permute-done = bf16[256,1024]{1,0:T(8,128)(2,1)} collective-permute-done((bf16[256,1024]{1,0:T(8,128)(2,1)}, bf16[256,1024]{1,0:T(8,128)(2,1)}, u32[]{:S(2)}, u32[]{:S(2)}) %collective-permute-start) | collective-permute-done | bytes 524320 | tf_op jit(solution)/shard_map/ppermute | solution.py:131
  221.1 50.0 %shard_map.93 = (bf16[2,256,1024]{2,1,0:T(8,128)(2,1)}, bf16[2,256,1024]{2,1,0:T(8,128)(2,1)}, f32[2,3,2,512,128]{4,3,2,1,0:T(8,128)}, f32[512,256]{1,0:T(8,128)}, f32[512,256]{1,0:T(8,128)}) custom-call(s32[8]{0:T(128)} %reshape.116.live_ref, s32[1]{0:T(128)} %bitcast.2.tp_ref, bf16[2,256,1024]{2,1,0:T(8,128)(2,1)} %pad_maximum_fusion.2.q_ref, ...), custom_call_target="tpu_custom_call" | custom-call | flops 12884901888 | bytes 10485760 | tf_op jit(solution)/shard_map/pallas_call | solution.py:104
  275.0 5.7 %all-to-all-start.3 = ((bf16[2,3,2,16,32,128]{5,4,2,1,0,3:T(8,128)(2,1)}), bf16[2,3,2,16,32,128]{5,4,2,1,0,3:T(8,128)(2,1)S(1)}, u32[]{:S(2)}, u32[]{:S(2)}) async-start(bf16[2,3,2,16,32,128]{5,4,2,1,0,3:T(8,128)(2,1)} %copy.116), calls=%async_computation.3 | async-start | bytes 3145728 | tf_op jit(solution)/shard_map/all_to_all | solution.py:212
  286.4 3.7 reshape.126
  290.1 22.7 %all-to-all-done.3 = bf16[2,3,2,16,32,128]{5,4,2,1,0,3:T(8,128)(2,1)S(1)} async-done(((bf16[2,3,2,16,32,128]{5,4,2,1,0,3:T(8,128)(2,1)}), bf16[2,3,2,16,32,128]{5,4,2,1,0,3:T(8,128)(2,1)S(1)}, u32[]{:S(2)}, u32[]{:S(2)}) %all-to-all-start.3) | async-done | bytes 1572896 | tf_op jit(solution)/shard_map/all_to_all | solution.py:212
  318.4 9.3 %all-to-all-start.5 = ((bf16[4,16,2,32,128]{4,3,2,0,1:T(8,128)(2,1)}), bf16[4,16,2,32,128]{4,3,2,0,1:T(8,128)(2,1)}, u32[]{:S(2)}, u32[]{:S(2)}) async-start(bf16[4,16,2,32,128]{4,3,2,0,1:T(8,128)(2,1)} %copy.121), calls=%async_computation.5 | async-start | bytes 2097152 | tf_op jit(solution)/shard_map/all_to_all | solution.py:225
  336.0 7.3 %collective-permute-done.9 = bf16[256,1024]{1,0:T(8,128)(2,1)S(1)} collective-permute-done((bf16[256,1024]{1,0:T(8,128)(2,1)S(1)}, bf16[256,1024]{1,0:T(8,128)(2,1)S(1)}, u32[]{:S(2)}, u32[]{:S(2)}) %collective-permute-start.9) | collective-permute-done | bytes 524320 | tf_op jit(solution)/shard_map/ppermute | solution.py:131
  346.0 8.6 %collective-permute-done.7 = bf16[256,1024]{1,0:T(8,128)(2,1)} collective-permute-done((bf16[256,1024]{1,0:T(8,128)(2,1)}, bf16[256,1024]{1,0:T(8,128)(2,1)}, u32[]{:S(2)}, u32[]{:S(2)}) %collective-permute-start.7) | collective-permute-done | bytes 524320 | tf_op jit(solution)/shard_map/ppermute | solution.py:131
  358.8 6.6 %collective-permute-done.8 = bf16[256,1024]{1,0:T(8,128)(2,1)} collective-permute-done((bf16[256,1024]{1,0:T(8,128)(2,1)}, bf16[256,1024]{1,0:T(8,128)(2,1)}, u32[]{:S(2)}, u32[]{:S(2)}) %collective-permute-start.8) | collective-permute-done | bytes 524320 | tf_op jit(solution)/shard_map/ppermute | solution.py:131
  376.2 4.1 copy.128
  395.3 4.1 copy.127
  (147 shorter events, 100.3 us)
Async XLA Ops:
  1.7 10.2 %collective-permute-start.2 = (bf16[256,512]{1,0:T(8,128)(2,1)S(1)}, bf16[256,512]{1,0:T(8,128)(2,1)S(1)}, u32[]{:S(2)}, u32[]{:S(2)}) collective-permute-start(bf16[256,512]{1,0:T(8,128)(2,1)S(1)} %get-tuple-element.69), channel_id=1, source_target_pairs={{0,1},{1,0},{2,3},{3,2},{4,5},{5,4},{6,7},{7,6},{8,9},{9,8},{10,11... | collective-permute-start | bytes 786440 | tf_op jit(solution)/shard_map/ppermute | solution.py:131
  5.8 10.9 %collective-permute-start.3 = (bf16[256,512]{1,0:T(8,128)(2,1)S(1)}, bf16[256,512]{1,0:T(8,128)(2,1)S(1)}, u32[]{:S(2)}, u32[]{:S(2)}) collective-permute-start(bf16[256,512]{1,0:T(8,128)(2,1)S(1)} %get-tuple-element.71), channel_id=1, source_target_pairs={{0,1},{1,0},{2,3},{3,2},{4,5},{5,4},{6,7},{7,6},{8,9},{9,8},{10,11... | collective-permute-start | bytes 786440 | tf_op jit(solution)/shard_map/ppermute | solution.py:131
  19.6 6.3 %copy-start.15 = (s32[16,4,3]{0,1,2:T(4,128)S(1)}, s32[16,4,3]{0,1,2:T(4,128)}, u32[]{:S(2)}) copy-start(s32[16,4,3]{0,1,2:T(4,128)} %param.13) | copy-start | bytes 2308
  19.7 29.2 %all-to-all-start = ((bf16[16,2,32,4,128]{4,2,3,1,0:T(8,128)(2,1)}), bf16[16,2,32,4,128]{4,2,3,1,0:T(8,128)(2,1)S(1)}, u32[]{:S(2)}, u32[]{:S(2)}) async-start(bf16[16,2,32,4,128]{4,2,3,1,0:T(8,128)(2,1)} %pad_maximum_fusion.4), calls=%async_computation | async-start | bytes 2097152 | tf_op jit(solution)/shard_map/all_to_all | solution.py:178
  51.2 38.8 %all-to-all-start.2 = ((bf16[16,2,3,2,32,128]{5,4,3,2,1,0:T(8,128)(2,1)}), bf16[16,2,3,2,32,128]{5,4,3,2,1,0:T(8,128)(2,1)S(1)}, u32[]{:S(2)}, u32[]{:S(2)}) async-start(bf16[16,2,3,2,32,128]{5,4,3,2,1,0:T(8,128)(2,1)} %bitcast.140), calls=%async_computation.2 | async-start | bytes 3145728 | tf_op jit(solution)/shard_map/all_to_all | solution.py:199
  90.1 95.8 %all-to-all-start.1 = ((bf16[16,2,3,2,32,128]{5,4,3,2,1,0:T(8,128)(2,1)}), bf16[16,2,3,2,32,128]{5,4,3,2,1,0:T(8,128)(2,1)S(1)}, u32[]{:S(2)}, u32[]{:S(2)}) async-start(bf16[16,2,3,2,32,128]{5,4,3,2,1,0:T(8,128)(2,1)} %bitcast.12), calls=%async_computation.1 | async-start | bytes 3145728 | tf_op jit(solution)/shard_map/all_to_all | solution.py:199
  99.2 4.6 %copy-start.6 = (bf16[256,4096]{1,0:T(8,128)(2,1)S(1)}, bf16[256,4096]{1,0:T(8,128)(2,1)}, u32[]{:S(2)}) copy-start(bf16[256,4096]{1,0:T(8,128)(2,1)} %param.10) | copy-start | bytes 6291460
  102.3 3.6 copy-start.16
  102.3 15.1 %collective-permute-start.6 = (bf16[256,1024]{1,0:T(8,128)(2,1)}, bf16[256,1024]{1,0:T(8,128)(2,1)}, u32[]{:S(2)}, u32[]{:S(2)}) collective-permute-start(bf16[256,1024]{1,0:T(8,128)(2,1)} %get-tuple-element.50), channel_id=1, source_target_pairs={{0,1},{1,0},{2,3},{3,2},{4,5},{5,4},{6,7},{7,6},{8,9},{9,8},{10,11... | collective-permute-start | bytes 1572872 | tf_op jit(solution)/shard_map/ppermute | solution.py:131
  105.2 22.9 %collective-permute-start.5 = (bf16[256,1024]{1,0:T(8,128)(2,1)}, bf16[256,1024]{1,0:T(8,128)(2,1)}, u32[]{:S(2)}, u32[]{:S(2)}) collective-permute-start(bf16[256,1024]{1,0:T(8,128)(2,1)} %get-tuple-element.54), channel_id=1, source_target_pairs={{0,1},{1,0},{2,3},{3,2},{4,5},{5,4},{6,7},{7,6},{8,9},{9,8},{10,11... | collective-permute-start | bytes 1572872 | tf_op jit(solution)/shard_map/ppermute | solution.py:131
  106.7 21.4 %copy-start.9 = (bf16[1,256,1024]{2,1,0:T(8,128)(2,1)S(1)}, bf16[1,256,1024]{2,1,0:T(8,128)(2,1)}, u32[]{:S(2)}) copy-start(bf16[1,256,1024]{2,1,0:T(8,128)(2,1)} %get-tuple-element.55) | copy-start | bytes 1572868
  185.8 89.2 %all-to-all-start.4 = ((bf16[2,3,2,16,32,128]{5,4,2,1,0,3:T(8,128)(2,1)}), bf16[2,3,2,16,32,128]{5,4,2,1,0,3:T(8,128)(2,1)S(1)}, u32[]{:S(2)}, u32[]{:S(2)}) async-start(bf16[2,3,2,16,32,128]{5,4,2,1,0,3:T(8,128)(2,1)} %copy.119), calls=%async_computation.4 | async-start | bytes 3145728 | tf_op jit(solution)/shard_map/all_to_all | solution.py:212
  191.6 15.1 %collective-permute-start.1 = (bf16[256,1024]{1,0:T(8,128)(2,1)}, bf16[256,1024]{1,0:T(8,128)(2,1)}, u32[]{:S(2)}, u32[]{:S(2)}) collective-permute-start(bf16[256,1024]{1,0:T(8,128)(2,1)} %get-tuple-element.49), channel_id=1, source_target_pairs={{0,1},{1,0},{2,3},{3,2},{4,5},{5,4},{6,7},{7,6},{8,9},{9,8},{10,11... | collective-permute-start | bytes 1572872 | tf_op jit(solution)/shard_map/ppermute | solution.py:131
  193.2 24.3 %collective-permute-start = (bf16[256,1024]{1,0:T(8,128)(2,1)}, bf16[256,1024]{1,0:T(8,128)(2,1)}, u32[]{:S(2)}, u32[]{:S(2)}) collective-permute-start(bf16[256,1024]{1,0:T(8,128)(2,1)} %get-tuple-element.53), channel_id=1, source_target_pairs={{0,1},{1,0},{2,3},{3,2},{4,5},{5,4},{6,7},{7,6},{8,9},{9,8},{10,11... | collective-permute-start | bytes 1572872 | tf_op jit(solution)/shard_map/ppermute | solution.py:131
  194.3 23.2 %copy-start.8 = (bf16[1,256,1024]{2,1,0:T(8,128)(2,1)S(1)}, bf16[1,256,1024]{2,1,0:T(8,128)(2,1)}, u32[]{:S(2)}) copy-start(bf16[1,256,1024]{2,1,0:T(8,128)(2,1)} %get-tuple-element.52) | copy-start | bytes 1572868
  275.0 37.7 %all-to-all-start.3 = ((bf16[2,3,2,16,32,128]{5,4,2,1,0,3:T(8,128)(2,1)}), bf16[2,3,2,16,32,128]{5,4,2,1,0,3:T(8,128)(2,1)S(1)}, u32[]{:S(2)}, u32[]{:S(2)}) async-start(bf16[2,3,2,16,32,128]{5,4,2,1,0,3:T(8,128)(2,1)} %copy.116), calls=%async_computation.3 | async-start | bytes 3145728 | tf_op jit(solution)/shard_map/all_to_all | solution.py:212
  283.4 50.9 %collective-permute-start.4 = (bf16[256,1024]{1,0:T(8,128)(2,1)}, bf16[256,1024]{1,0:T(8,128)(2,1)}, u32[]{:S(2)}, u32[]{:S(2)}) collective-permute-start(bf16[256,1024]{1,0:T(8,128)(2,1)} %get-tuple-element.61), channel_id=1, source_target_pairs={{0,1},{1,0},{2,3},{3,2},{4,5},{5,4},{6,7},{7,6},{8,9},{9,8},{10,11... | collective-permute-start | bytes 1572872 | tf_op jit(solution)/shard_map/ppermute | solution.py:131
  318.4 9.3 %copy-start.11 = (bf16[2,256,1024]{2,1,0:T(8,128)(2,1)S(1)}, bf16[2,256,1024]{2,1,0:T(8,128)(2,1)}, u32[]{:S(2)}) copy-start(bf16[2,256,1024]{2,1,0:T(8,128)(2,1)} %get-tuple-element.19) | copy-start | bytes 3145732
  318.4 61.9 %all-to-all-start.5 = ((bf16[4,16,2,32,128]{4,3,2,0,1:T(8,128)(2,1)}), bf16[4,16,2,32,128]{4,3,2,0,1:T(8,128)(2,1)}, u32[]{:S(2)}, u32[]{:S(2)}) async-start(bf16[4,16,2,32,128]{4,3,2,0,1:T(8,128)(2,1)} %copy.121), calls=%async_computation.5 | async-start | bytes 2097152 | tf_op jit(solution)/shard_map/all_to_all | solution.py:225
  328.6 14.7 %collective-permute-start.9 = (bf16[256,1024]{1,0:T(8,128)(2,1)S(1)}, bf16[256,1024]{1,0:T(8,128)(2,1)S(1)}, u32[]{:S(2)}, u32[]{:S(2)}) collective-permute-start(bf16[256,1024]{1,0:T(8,128)(2,1)S(1)} %get-tuple-element.59), channel_id=1, source_target_pairs={{0,1},{1,0},{2,3},{3,2},{4,5},{5,4},{6,7},{7,6},{8,9},{9,8},{10,11... | collective-permute-start | bytes 1572872 | tf_op jit(solution)/shard_map/ppermute | solution.py:131
  331.1 23.5 %collective-permute-start.7 = (bf16[256,1024]{1,0:T(8,128)(2,1)}, bf16[256,1024]{1,0:T(8,128)(2,1)}, u32[]{:S(2)}, u32[]{:S(2)}) collective-permute-start(bf16[256,1024]{1,0:T(8,128)(2,1)} %get-tuple-element.63), channel_id=1, source_target_pairs={{0,1},{1,0},{2,3},{3,2},{4,5},{5,4},{6,7},{7,6},{8,9},{9,8},{10,11... | collective-permute-start | bytes 1572872 | tf_op jit(solution)/shard_map/ppermute | solution.py:131
  332.7 32.6 %collective-permute-start.8 = (bf16[256,1024]{1,0:T(8,128)(2,1)}, bf16[256,1024]{1,0:T(8,128)(2,1)}, u32[]{:S(2)}, u32[]{:S(2)}) collective-permute-start(bf16[256,1024]{1,0:T(8,128)(2,1)} %get-tuple-element.57), channel_id=1, source_target_pairs={{0,1},{1,0},{2,3},{3,2},{4,5},{5,4},{6,7},{7,6},{8,9},{9,8},{10,11... | collective-permute-start | bytes 1572872 | tf_op jit(solution)/shard_map/ppermute | solution.py:131
  390.3 9.4 %collective-permute-start.10 = (bf16[256,512]{1,0:T(8,128)(2,1)S(1)}, bf16[256,512]{1,0:T(8,128)(2,1)}, u32[]{:S(2)}, u32[]{:S(2)}) collective-permute-start(bf16[256,512]{1,0:T(8,128)(2,1)S(1)} %get-tuple-element.67), channel_id=1, source_target_pairs={{0,1},{1,0},{2,3},{3,2},{4,5},{5,4},{6,7},{7,6},{8,9},{9,8},{10,11... | collective-permute-start | bytes 786440 | tf_op jit(solution)/shard_map/ppermute | solution.py:131
  391.9 11.8 %collective-permute-start.11 = (bf16[256,512]{1,0:T(8,128)(2,1)S(1)}, bf16[256,512]{1,0:T(8,128)(2,1)S(1)}, u32[]{:S(2)}, u32[]{:S(2)}) collective-permute-start(bf16[256,512]{1,0:T(8,128)(2,1)S(1)} %get-tuple-element.65), channel_id=1, source_target_pairs={{0,1},{1,0},{2,3},{3,2},{4,5},{5,4},{6,7},{7,6},{8,9},{9,8},{10,11... | collective-permute-start | bytes 786440 | tf_op jit(solution)/shard_map/ppermute | solution.py:131
  (11 other events, 21.1 us)

commit v6 on v4

--- a/solution.py
+++ b/solution.py
@@ -15,7 +15,7 @@
 
 def attention_kernel(
     live_ref, tp_ref, q_ref, do_ref, kvs_ref, ko_ref, vo_ref,
-    o_ref, dq_ref, dsel_ref, dko_ref, dvo_ref, *, slot_count, row_tile, scale
+    o_ref, dq_ref, dsel_ref, dko_ref, dvo_ref, acc_ref, *, slot_count, row_tile, scale
 ):
     g = pl.program_id(0)
     h = pl.program_id(1)
@@ -23,16 +23,15 @@
 
     @pl.when((h == 0) & (t == 0))
     def _():
-        dsel_ref[...] = jnp.zeros(dsel_ref.shape, dsel_ref.dtype)
-        dko_ref[...] = jnp.zeros(dko_ref.shape, dko_ref.dtype)
-        dvo_ref[...] = jnp.zeros(dvo_ref.shape, dvo_ref.dtype)
+        acc_ref[...] = jnp.zeros(acc_ref.shape, acc_ref.dtype)
 
     q = q_ref[...]
     do = do_ref[...]
     keys = [kvs_ref[r, 0] for r in range(slot_count - 1)] + [ko_ref[...]]
     values = [kvs_ref[r, 1] for r in range(slot_count - 1)] + [vo_ref[...]]
     trans_b = (((1,), (1,)), ((), ()))
-    trans_a = (((0,), (0,)), ((), ()))
+    q_t = q.T
+    do_t = do.T
     scores = []
     for r in range(slot_count):
         s = lax.dot_general(q, keys[r], trans_b, preferred_element_type=jnp.float32) * scale
@@ -66,15 +65,17 @@
         grad_s = (probs[r] * (grad_p - delta)).astype(jnp.bfloat16)
         part = jnp.dot(grad_s, keys[r], preferred_element_type=jnp.float32)
         grad_q = part if grad_q is None else grad_q + part
-        key_part = lax.dot_general(grad_s, q, trans_a, preferred_element_type=jnp.float32) * scale
-        value_part = lax.dot_general(probs_low[r], do, trans_a, preferred_element_type=jnp.float32)
-        if r == slot_count - 1:
-            dko_ref[...] += key_part
-            dvo_ref[...] += value_part
-        else:
-            dsel_ref[r, 0] += key_part
-            dsel_ref[r, 1] += value_part
+        acc_ref[r, 0] += jnp.dot(q_t, grad_s, preferred_element_type=jnp.float32) * scale
+        acc_ref[r, 1] += jnp.dot(do_t, probs_low[r], preferred_element_type=jnp.float32)
     dq_ref[...] = (grad_q * scale).astype(jnp.bfloat16)
+
+    @pl.when((h == pl.num_programs(1) - 1) & (t == pl.num_programs(2) - 1))
+    def _():
+        for r in range(slot_count - 1):
+            dsel_ref[r, 0] = acc_ref[r, 0].T
+            dsel_ref[r, 1] = acc_ref[r, 1].T
+        dko_ref[...] = acc_ref[slot_count - 1, 0].T
+        dvo_ref[...] = acc_ref[slot_count - 1, 1].T
 
 
 def attention(live, tp_info, query_stack, upstream_stack, fetched, key_heads, value_heads, group_size, first):
@@ -108,6 +109,7 @@
             grid=grid,
             in_specs=[in_block, in_block, sel_block, own_in, own_in],
             out_specs=[out_block, out_block, sel_block, own_out, own_out],
+            scratch_shapes=[pltpu.VMEM((slot_count, 2, HD, BLK), jnp.float32)],
         ),
         out_shape=[
             jax.ShapeDtypeStruct((tp_size, row_tile, q_cols), jnp.bfloat16),

time: 384 us -> 375 us (0.977)
  Pallas kernels: 100 us -> 91.3 us
    pallas_call x2, Pallas kernels: 100 us -> 91.3 us  [attention(): pl.pallas_call(kernel, grid_spec=pltpu.PrefetchScalarGridSpec(num_scalar_...]
  transfers between devices with their start and end apart: 19 -> 19, of which waited for: 12 -> 12; matrix products, arithmetic and copies ran while one was open for 27% -> 28% of each run, Pallas kernels for 26% -> 24%
where the time goes in v6:
time: 375 us; the launch traced here: 373 us
  waiting for transfers between devices  99.6 us (27%)
  Pallas kernels  91.3 us (24%)
  local copies, waits for them, and re-layouts  89.7 us (24%)
  starting transfers between devices  65.1 us (17%)
  other arithmetic  25.5 us (7%)
    pallas_call x2, Pallas kernels, attention(): pl.pallas_call(kernel, grid_spec=pltpu.PrefetchScalarGridSpec(num_scalar_...  91.3 us
    ppermute x12, waiting for transfers between devices, shift(): lax.ppermute(x, axis, perm=[(s, (s + step) % size) for s in range(size)])  46.4 us
    all_to_all x1, waiting for transfers between devices, body(): spread = lax.all_to_all(kv, 'ctx', split_axis=0, concat_axis=0, tiled=True)  22.6 us
    slice x2, local copies, waits for them, and re-layouts, chunk_columns(): x.reshape(rows_in, tp_size, chunk_count, q_width)[:, :, chunk]  21.7 us
    all_to_all x2, waiting for transfers between devices, body(): lax.all_to_all(send_back, 'ctx', split_axis=3, concat_axis=1, tiled=True)  18.2 us
    ppermute x12, starting transfers between devices, shift(): lax.ppermute(x, axis, perm=[(s, (s + step) % size) for s in range(size)])  16.2 us
    all_to_all x2, starting transfers between devices, body(): got = lax.all_to_all(send, 'ctx', split_axis=0, concat_axis=4, tiled=True)  16.1 us
    all_to_all x2, starting transfers between devices, body(): back = lax.all_to_all(owner, 'ctx', split_axis=1, concat_axis=3, tiled=True)  15.1 us
  transfers between devices with their start and end apart: 19, of which 12 were waited for; matrix products, arithmetic and copies ran while one was open for 28% of the time, Pallas kernels for 24%

profile of v6, /device:TPU:0, one launch (start us, length us, event | category | flops | bytes accessed | tf_op | source)
XLA Modules:
  0.0 373.2 jit_solution(4944559927608668783)
XLA Ops:
  6.0 5.9 %collective-permute-done.2 = bf16[256,512]{1,0:T(8,128)(2,1)S(1)} collective-permute-done((bf16[256,512]{1,0:T(8,128)(2,1)S(1)}, bf16[256,512]{1,0:T(8,128)(2,1)S(1)}, u32[]{:S(2)}, u32[]{:S(2)}) %collective-permute-start.2) | collective-permute-done | bytes 262176 | tf_op jit(solution)/shard_map/ppermute | solution.py:133
  12.5 4.1 %collective-permute-done.3 = bf16[256,512]{1,0:T(8,128)(2,1)S(1)} collective-permute-done((bf16[256,512]{1,0:T(8,128)(2,1)S(1)}, bf16[256,512]{1,0:T(8,128)(2,1)S(1)}, u32[]{:S(2)}, u32[]{:S(2)}) %collective-permute-start.3) | collective-permute-done | bytes 262176 | tf_op jit(solution)/shard_map/ppermute | solution.py:133
  19.7 6.3 %all-to-all-start = ((bf16[16,2,32,4,128]{4,2,3,1,0:T(8,128)(2,1)}), bf16[16,2,32,4,128]{4,2,3,1,0:T(8,128)(2,1)S(1)}, u32[]{:S(2)}, u32[]{:S(2)}) async-start(bf16[16,2,32,4,128]{4,2,3,1,0:T(8,128)(2,1)} %pad_maximum_fusion.4), calls=%async_computation | async-start | bytes 2097152 | tf_op jit(solution)/shard_map/all_to_all | solution.py:178
  26.2 22.6 %all-to-all-done = bf16[16,2,32,4,128]{4,2,3,1,0:T(8,128)(2,1)S(1)} async-done(((bf16[16,2,32,4,128]{4,2,3,1,0:T(8,128)(2,1)}), bf16[16,2,32,4,128]{4,2,3,1,0:T(8,128)(2,1)S(1)}, u32[]{:S(2)}, u32[]{:S(2)}) %all-to-all-start) | async-done | bytes 1048608 | tf_op jit(solution)/shard_map/all_to_all | solution.py:178
  51.2 6.9 %all-to-all-start.2 = ((bf16[16,2,3,2,32,128]{5,4,3,2,1,0:T(8,128)(2,1)}), bf16[16,2,3,2,32,128]{5,4,3,2,1,0:T(8,128)(2,1)}, u32[]{:S(2)}, u32[]{:S(2)}) async-start(bf16[16,2,3,2,32,128]{5,4,3,2,1,0:T(8,128)(2,1)} %bitcast.27), calls=%async_computation.2 | async-start | bytes 3145728 | tf_op jit(solution)/shard_map/all_to_all | solution.py:205
  58.2 3.3 reshape.141
  61.5 11.0 %slice_reduce_fusion.3 = (bf16[256,2,1024]{2,1,0:T(2,128)(2,1)}, bf16[256,2,1024]{2,1,0:T(2,128)(2,1)S(1)}) fusion(bf16[256,2,2,1024]{3,2,1,0:T(2,128)(2,1)S(1)} %reshape.141), kind=kLoop, calls=%fused_computation.17 | loop fusion | bytes 4194304 | tf_op jit(solution)/shard_map/slice | solution.py:193
  81.2 9.0 %all-to-all-done.2 = bf16[16,2,3,2,32,128]{5,4,3,2,1,0:T(8,128)(2,1)} async-done(((bf16[16,2,3,2,32,128]{5,4,3,2,1,0:T(8,128)(2,1)}), bf16[16,2,3,2,32,128]{5,4,3,2,1,0:T(8,128)(2,1)}, u32[]{:S(2)}, u32[]{:S(2)}) %all-to-all-start.2) | async-done | bytes 1572896 | tf_op jit(solution)/shard_map/all_to_all | solution.py:205
  90.2 9.2 %all-to-all-start.1 = ((bf16[16,2,3,2,32,128]{5,4,3,2,1,0:T(8,128)(2,1)}), bf16[16,2,3,2,32,128]{5,4,3,2,1,0:T(8,128)(2,1)}, u32[]{:S(2)}, u32[]{:S(2)}) async-start(bf16[16,2,3,2,32,128]{5,4,3,2,1,0:T(8,128)(2,1)} %bitcast.185), calls=%async_computation.1 | async-start | bytes 3145728 | tf_op jit(solution)/shard_map/all_to_all | solution.py:205
  99.4 10.7 %slice_reduce_fusion.2 = (bf16[256,2,1024]{2,1,0:T(2,128)(2,1)S(1)}, bf16[256,2,1024]{2,1,0:T(2,128)(2,1)S(1)}) fusion(bf16[256,2,2,1024]{3,2,1,0:T(2,128)(2,1)S(1)} %reshape.142), kind=kLoop, calls=%fused_computation.16 | loop fusion | bytes 4194304 | tf_op jit(solution)/shard_map/slice | solution.py:193
  115.2 9.5 %collective-permute-done.6 = bf16[256,1024]{1,0:T(8,128)(2,1)S(1)} collective-permute-done((bf16[256,1024]{1,0:T(8,128)(2,1)S(1)}, bf16[256,1024]{1,0:T(8,128)(2,1)S(1)}, u32[]{:S(2)}, u32[]{:S(2)}) %collective-permute-start.6) | collective-permute-done | bytes 524320 | tf_op jit(solution)/shard_map/ppermute | solution.py:133
  128.6 45.8 %shard_map.94 = (bf16[2,256,1024]{2,1,0:T(8,128)(2,1)}, bf16[2,256,1024]{2,1,0:T(8,128)(2,1)}, f32[2,3,2,512,128]{4,3,2,1,0:T(8,128)}, f32[512,256]{1,0:T(8,128)}, f32[512,256]{1,0:T(8,128)}) custom-call(s32[8]{0:T(128)} %reshape.145.live_ref, s32[1]{0:T(128)} %bitcast.2.tp_ref, bf16[2,256,1024]{2,1,0:T(8,128)(2,1)} %pad_maximum_fusion.6.q_ref, ...), custom_call_target="tpu_custom_call" | custom-call | flops 12884901888 | bytes 10485760 | tf_op jit(solution)/shard_map/pallas_call | solution.py:105
  178.2 5.8 %all-to-all-start.5 = ((bf16[2,3,2,16,32,128]{5,4,2,1,0,3:T(8,128)(2,1)}), bf16[2,3,2,16,32,128]{5,4,2,1,0,3:T(8,128)(2,1)S(1)}, u32[]{:S(2)}, u32[]{:S(2)}) async-start(bf16[2,3,2,16,32,128]{5,4,2,1,0,3:T(8,128)(2,1)} %copy.151), calls=%async_computation.5 | async-start | bytes 3145728 | tf_op jit(solution)/shard_map/all_to_all | solution.py:218
  188.9 10.4 %collective-permute-done.1 = bf16[256,1024]{1,0:T(8,128)(2,1)} collective-permute-done((bf16[256,1024]{1,0:T(8,128)(2,1)S(1)}, bf16[256,1024]{1,0:T(8,128)(2,1)}, u32[]{:S(2)}, u32[]{:S(2)}) %collective-permute-start.1) | collective-permute-done | bytes 524320 | tf_op jit(solution)/shard_map/ppermute | solution.py:133
  201.5 8.6 %collective-permute-done = bf16[256,1024]{1,0:T(8,128)(2,1)} collective-permute-done((bf16[256,1024]{1,0:T(8,128)(2,1)}, bf16[256,1024]{1,0:T(8,128)(2,1)}, u32[]{:S(2)}, u32[]{:S(2)}) %collective-permute-start) | collective-permute-done | bytes 524320 | tf_op jit(solution)/shard_map/ppermute | solution.py:133
  215.1 45.5 %shard_map.93 = (bf16[2,256,1024]{2,1,0:T(8,128)(2,1)}, bf16[2,256,1024]{2,1,0:T(8,128)(2,1)}, f32[2,3,2,512,128]{4,3,2,1,0:T(8,128)}, f32[512,256]{1,0:T(8,128)}, f32[512,256]{1,0:T(8,128)}) custom-call(s32[8]{0:T(128)} %reshape.139.live_ref, s32[1]{0:T(128)} %bitcast.2.tp_ref, bf16[2,256,1024]{2,1,0:T(8,128)(2,1)} %pad_maximum_fusion.2.q_ref, ...), custom_call_target="tpu_custom_call" | custom-call | flops 12884901888 | bytes 10485760 | tf_op jit(solution)/shard_map/pallas_call | solution.py:105
  264.4 5.7 %all-to-all-start.3 = ((bf16[2,3,2,16,32,128]{5,4,2,1,0,3:T(8,128)(2,1)}), bf16[2,3,2,16,32,128]{5,4,2,1,0,3:T(8,128)(2,1)S(1)}, u32[]{:S(2)}, u32[]{:S(2)}) async-start(bf16[2,3,2,16,32,128]{5,4,2,1,0,3:T(8,128)(2,1)} %copy.145), calls=%async_computation.3 | async-start | bytes 3145728 | tf_op jit(solution)/shard_map/all_to_all | solution.py:218
  283.9 18.2 %all-to-all-done.3 = bf16[2,3,2,16,32,128]{5,4,2,1,0,3:T(8,128)(2,1)S(1)} async-done(((bf16[2,3,2,16,32,128]{5,4,2,1,0,3:T(8,128)(2,1)}), bf16[2,3,2,16,32,128]{5,4,2,1,0,3:T(8,128)(2,1)S(1)}, u32[]{:S(2)}, u32[]{:S(2)}) %all-to-all-start.3) | async-done | bytes 1572896 | tf_op jit(solution)/shard_map/all_to_all | solution.py:218
  302.1 9.2 %all-to-all-start.6 = ((bf16[2,16,2,32,128]{4,3,2,0,1:T(8,128)(2,1)}), bf16[2,16,2,32,128]{4,3,2,0,1:T(8,128)(2,1)}, u32[]{:S(2)}, u32[]{:S(2)}) async-start(bf16[2,16,2,32,128]{4,3,2,0,1:T(8,128)(2,1)} %copy.153), calls=%async_computation.6 | async-start | bytes 1048576 | tf_op jit(solution)/shard_map/all_to_all | solution.py:228
  322.2 4.6 %collective-permute-done.8 = bf16[256,1024]{1,0:T(8,128)(2,1)} collective-permute-done((bf16[256,1024]{1,0:T(8,128)(2,1)}, bf16[256,1024]{1,0:T(8,128)(2,1)}, u32[]{:S(2)}, u32[]{:S(2)}) %collective-permute-start.8) | collective-permute-done | bytes 524320 | tf_op jit(solution)/shard_map/ppermute | solution.py:133
  332.0 5.9 %all-to-all-start.4 = ((bf16[2,16,2,32,128]{4,3,2,0,1:T(8,128)(2,1)}), bf16[2,16,2,32,128]{4,3,2,0,1:T(8,128)(2,1)}, u32[]{:S(2)}, u32[]{:S(2)}) async-start(bf16[2,16,2,32,128]{4,3,2,0,1:T(8,128)(2,1)} %copy.147), calls=%async_computation.4 | async-start | bytes 1048576 | tf_op jit(solution)/shard_map/all_to_all | solution.py:228
  343.7 4.1 %copy.161 = bf16[256,4096]{1,0:T(8,128)(2,1)} copy(bf16[256,4096]{0,1:T(8,128)(2,1)} %bitcast.181) | data formatting | bytes 4194304
  349.1 3.4 all-to-all-done.4
  361.8 4.1 %copy.160 = bf16[256,4096]{1,0:T(8,128)(2,1)} copy(bf16[256,4096]{0,1:T(8,128)(2,1)} %bitcast.182) | data formatting | bytes 4194304
  (170 shorter events, 102.2 us)
Async XLA Ops:
  1.7 10.2 %collective-permute-start.2 = (bf16[256,512]{1,0:T(8,128)(2,1)S(1)}, bf16[256,512]{1,0:T(8,128)(2,1)S(1)}, u32[]{:S(2)}, u32[]{:S(2)}) collective-permute-start(bf16[256,512]{1,0:T(8,128)(2,1)S(1)} %get-tuple-element.75), channel_id=1, source_target_pairs={{0,1},{1,0},{2,3},{3,2},{4,5},{5,4},{6,7},{7,6},{8,9},{9,8},{10,11... | collective-permute-start | bytes 786440 | tf_op jit(solution)/shard_map/ppermute | solution.py:133
  5.8 10.9 %collective-permute-start.3 = (bf16[256,512]{1,0:T(8,128)(2,1)S(1)}, bf16[256,512]{1,0:T(8,128)(2,1)S(1)}, u32[]{:S(2)}, u32[]{:S(2)}) collective-permute-start(bf16[256,512]{1,0:T(8,128)(2,1)S(1)} %get-tuple-element.77), channel_id=1, source_target_pairs={{0,1},{1,0},{2,3},{3,2},{4,5},{5,4},{6,7},{7,6},{8,9},{9,8},{10,11... | collective-permute-start | bytes 786440 | tf_op jit(solution)/shard_map/ppermute | solution.py:133
  19.7 29.2 %all-to-all-start = ((bf16[16,2,32,4,128]{4,2,3,1,0:T(8,128)(2,1)}), bf16[16,2,32,4,128]{4,2,3,1,0:T(8,128)(2,1)S(1)}, u32[]{:S(2)}, u32[]{:S(2)}) async-start(bf16[16,2,32,4,128]{4,2,3,1,0:T(8,128)(2,1)} %pad_maximum_fusion.4), calls=%async_computation | async-start | bytes 2097152 | tf_op jit(solution)/shard_map/all_to_all | solution.py:178
  51.2 39.0 %all-to-all-start.2 = ((bf16[16,2,3,2,32,128]{5,4,3,2,1,0:T(8,128)(2,1)}), bf16[16,2,3,2,32,128]{5,4,3,2,1,0:T(8,128)(2,1)}, u32[]{:S(2)}, u32[]{:S(2)}) async-start(bf16[16,2,3,2,32,128]{5,4,3,2,1,0:T(8,128)(2,1)} %bitcast.27), calls=%async_computation.2 | async-start | bytes 3145728 | tf_op jit(solution)/shard_map/all_to_all | solution.py:205
  73.8 39.2 %collective-permute-start.5 = (bf16[256,1024]{1,0:T(8,128)(2,1)}, bf16[256,1024]{1,0:T(8,128)(2,1)}, u32[]{:S(2)}, u32[]{:S(2)}) collective-permute-start(bf16[256,1024]{1,0:T(8,128)(2,1)} %get-tuple-element.69), channel_id=1, source_target_pairs={{0,1},{1,0},{2,3},{3,2},{4,5},{5,4},{6,7},{7,6},{8,9},{9,8},{10,11... | collective-permute-start | bytes 1572872 | tf_op jit(solution)/shard_map/ppermute | solution.py:133
  90.2 88.0 %all-to-all-start.1 = ((bf16[16,2,3,2,32,128]{5,4,3,2,1,0:T(8,128)(2,1)}), bf16[16,2,3,2,32,128]{5,4,3,2,1,0:T(8,128)(2,1)}, u32[]{:S(2)}, u32[]{:S(2)}) async-start(bf16[16,2,3,2,32,128]{5,4,3,2,1,0:T(8,128)(2,1)} %bitcast.185), calls=%async_computation.1 | async-start | bytes 3145728 | tf_op jit(solution)/shard_map/all_to_all | solution.py:205
  110.4 14.2 %collective-permute-start.6 = (bf16[256,1024]{1,0:T(8,128)(2,1)S(1)}, bf16[256,1024]{1,0:T(8,128)(2,1)S(1)}, u32[]{:S(2)}, u32[]{:S(2)}) collective-permute-start(bf16[256,1024]{1,0:T(8,128)(2,1)S(1)} %get-tuple-element.67), channel_id=1, source_target_pairs={{0,1},{1,0},{2,3},{3,2},{4,5},{5,4},{6,7},{7,6},{8,9},{9,8},{10,11... | collective-permute-start | bytes 1572872 | tf_op jit(solution)/shard_map/ppermute | solution.py:133
  178.2 86.2 %all-to-all-start.5 = ((bf16[2,3,2,16,32,128]{5,4,2,1,0,3:T(8,128)(2,1)}), bf16[2,3,2,16,32,128]{5,4,2,1,0,3:T(8,128)(2,1)S(1)}, u32[]{:S(2)}, u32[]{:S(2)}) async-start(bf16[2,3,2,16,32,128]{5,4,2,1,0,3:T(8,128)(2,1)} %copy.151), calls=%async_computation.5 | async-start | bytes 3145728 | tf_op jit(solution)/shard_map/all_to_all | solution.py:218
  184.4 14.9 %collective-permute-start.1 = (bf16[256,1024]{1,0:T(8,128)(2,1)S(1)}, bf16[256,1024]{1,0:T(8,128)(2,1)}, u32[]{:S(2)}, u32[]{:S(2)}) collective-permute-start(bf16[256,1024]{1,0:T(8,128)(2,1)S(1)} %get-tuple-element.61), channel_id=1, source_target_pairs={{0,1},{1,0},{2,3},{3,2},{4,5},{5,4},{6,7},{7,6},{8,9},{9,8},{10,11... | collective-permute-start | bytes 1572872 | tf_op jit(solution)/shard_map/ppermute | solution.py:133
  187.1 22.9 %collective-permute-start = (bf16[256,1024]{1,0:T(8,128)(2,1)}, bf16[256,1024]{1,0:T(8,128)(2,1)}, u32[]{:S(2)}, u32[]{:S(2)}) collective-permute-start(bf16[256,1024]{1,0:T(8,128)(2,1)} %get-tuple-element.63), channel_id=1, source_target_pairs={{0,1},{1,0},{2,3},{3,2},{4,5},{5,4},{6,7},{7,6},{8,9},{9,8},{10,11... | collective-permute-start | bytes 1572872 | tf_op jit(solution)/shard_map/ppermute | solution.py:133
  264.4 37.7 %all-to-all-start.3 = ((bf16[2,3,2,16,32,128]{5,4,2,1,0,3:T(8,128)(2,1)}), bf16[2,3,2,16,32,128]{5,4,2,1,0,3:T(8,128)(2,1)S(1)}, u32[]{:S(2)}, u32[]{:S(2)}) async-start(bf16[2,3,2,16,32,128]{5,4,2,1,0,3:T(8,128)(2,1)} %copy.145), calls=%async_computation.3 | async-start | bytes 3145728 | tf_op jit(solution)/shard_map/all_to_all | solution.py:218
  272.9 41.0 %collective-permute-start.4 = (bf16[256,1024]{1,0:T(8,128)(2,1)}, bf16[256,1024]{1,0:T(8,128)(2,1)}, u32[]{:S(2)}, u32[]{:S(2)}) collective-permute-start(bf16[256,1024]{1,0:T(8,128)(2,1)} %get-tuple-element.59), channel_id=1, source_target_pairs={{0,1},{1,0},{2,3},{3,2},{4,5},{5,4},{6,7},{7,6},{8,9},{9,8},{10,11... | collective-permute-start | bytes 1572872 | tf_op jit(solution)/shard_map/ppermute | solution.py:133
  275.5 41.2 %collective-permute-start.9 = (bf16[256,1024]{1,0:T(8,128)(2,1)}, bf16[256,1024]{1,0:T(8,128)(2,1)}, u32[]{:S(2)}, u32[]{:S(2)}) collective-permute-start(bf16[256,1024]{1,0:T(8,128)(2,1)} %get-tuple-element.57), channel_id=1, source_target_pairs={{0,1},{1,0},{2,3},{3,2},{4,5},{5,4},{6,7},{7,6},{8,9},{9,8},{10,11... | collective-permute-start | bytes 1572872 | tf_op jit(solution)/shard_map/ppermute | solution.py:133
  277.0 42.5 %collective-permute-start.7 = (bf16[256,1024]{1,0:T(8,128)(2,1)}, bf16[256,1024]{1,0:T(8,128)(2,1)}, u32[]{:S(2)}, u32[]{:S(2)}) collective-permute-start(bf16[256,1024]{1,0:T(8,128)(2,1)} %get-tuple-element.65), channel_id=1, source_target_pairs={{0,1},{1,0},{2,3},{3,2},{4,5},{5,4},{6,7},{7,6},{8,9},{9,8},{10,11... | collective-permute-start | bytes 1572872 | tf_op jit(solution)/shard_map/ppermute | solution.py:133
  282.9 28.4 %copy-start.15 = (bf16[2,256,1024]{2,1,0:T(8,128)(2,1)S(1)}, bf16[2,256,1024]{2,1,0:T(8,128)(2,1)}, u32[]{:S(2)}) copy-start(bf16[2,256,1024]{2,1,0:T(8,128)(2,1)} %get-tuple-element.18) | copy-start | bytes 3145732
  283.9 30.0 %copy-start.11 = (bf16[1,256,1024]{2,1,0:T(8,128)(2,1)S(1)}, bf16[1,256,1024]{2,1,0:T(8,128)(2,1)}, u32[]{:S(2)}) copy-start(bf16[1,256,1024]{2,1,0:T(8,128)(2,1)} %get-tuple-element.58) | copy-start | bytes 1572868
  302.1 29.9 %all-to-all-start.6 = ((bf16[2,16,2,32,128]{4,3,2,0,1:T(8,128)(2,1)}), bf16[2,16,2,32,128]{4,3,2,0,1:T(8,128)(2,1)}, u32[]{:S(2)}, u32[]{:S(2)}) async-start(bf16[2,16,2,32,128]{4,3,2,0,1:T(8,128)(2,1)} %copy.153), calls=%async_computation.6 | async-start | bytes 1048576 | tf_op jit(solution)/shard_map/all_to_all | solution.py:228
  312.3 14.5 %collective-permute-start.8 = (bf16[256,1024]{1,0:T(8,128)(2,1)}, bf16[256,1024]{1,0:T(8,128)(2,1)}, u32[]{:S(2)}, u32[]{:S(2)}) collective-permute-start(bf16[256,1024]{1,0:T(8,128)(2,1)} %get-tuple-element.55), channel_id=1, source_target_pairs={{0,1},{1,0},{2,3},{3,2},{4,5},{5,4},{6,7},{7,6},{8,9},{9,8},{10,11... | collective-permute-start | bytes 1572872 | tf_op jit(solution)/shard_map/ppermute | solution.py:133
  331.0 6.9 %copy-start = (bf16[2,256,1024]{2,1,0:T(8,128)(2,1)S(1)}, bf16[2,256,1024]{2,1,0:T(8,128)(2,1)}, u32[]{:S(2)}) copy-start(bf16[2,256,1024]{2,1,0:T(8,128)(2,1)} %gather_fusion.4) | copy-start | bytes 3145732
  331.0 6.9 %copy-start.1 = (bf16[2,256,1024]{2,1,0:T(8,128)(2,1)S(1)}, bf16[2,256,1024]{2,1,0:T(8,128)(2,1)}, u32[]{:S(2)}) copy-start(bf16[2,256,1024]{2,1,0:T(8,128)(2,1)} %gather_fusion.7) | copy-start | bytes 3145732
  331.0 6.9 %copy-start.2 = (bf16[2,256,1024]{2,1,0:T(8,128)(2,1)S(1)}, bf16[2,256,1024]{2,1,0:T(8,128)(2,1)}, u32[]{:S(2)}) copy-start(bf16[2,256,1024]{2,1,0:T(8,128)(2,1)} %gather_fusion.5) | copy-start | bytes 3145732
  332.0 20.5 %all-to-all-start.4 = ((bf16[2,16,2,32,128]{4,3,2,0,1:T(8,128)(2,1)}), bf16[2,16,2,32,128]{4,3,2,0,1:T(8,128)(2,1)}, u32[]{:S(2)}, u32[]{:S(2)}) async-start(bf16[2,16,2,32,128]{4,3,2,0,1:T(8,128)(2,1)} %copy.147), calls=%async_computation.4 | async-start | bytes 1048576 | tf_op jit(solution)/shard_map/all_to_all | solution.py:228
  356.8 9.3 %collective-permute-start.10 = (bf16[256,512]{1,0:T(8,128)(2,1)S(1)}, bf16[256,512]{1,0:T(8,128)(2,1)}, u32[]{:S(2)}, u32[]{:S(2)}) collective-permute-start(bf16[256,512]{1,0:T(8,128)(2,1)S(1)} %get-tuple-element.73), channel_id=1, source_target_pairs={{0,1},{1,0},{2,3},{3,2},{4,5},{5,4},{6,7},{7,6},{8,9},{9,8},{10,11... | collective-permute-start | bytes 786440 | tf_op jit(solution)/shard_map/ppermute | solution.py:133
  358.4 12.3 %collective-permute-start.11 = (bf16[256,512]{1,0:T(8,128)(2,1)S(1)}, bf16[256,512]{1,0:T(8,128)(2,1)S(1)}, u32[]{:S(2)}, u32[]{:S(2)}) collective-permute-start(bf16[256,512]{1,0:T(8,128)(2,1)S(1)} %get-tuple-element.71), channel_id=1, source_target_pairs={{0,1},{1,0},{2,3},{3,2},{4,5},{5,4},{6,7},{7,6},{8,9},{9,8},{10,11... | collective-permute-start | bytes 786440 | tf_op jit(solution)/shard_map/ppermute | solution.py:133
  (17 other events, 43.3 us)

commit v7 on v6

--- a/solution.py
+++ b/solution.py
@@ -133,13 +133,32 @@
     return lax.ppermute(x, axis, perm=[(s, (s + step) % size) for s in range(size)])
 
 
-def tp_receive(x, me, size):
-    width = x.shape[1] // size
-    pieces = [lax.dynamic_slice_in_dim(x, me * width, width, 1)]
+def tp_receive(x, me, size, width, offset):
+    stride = x.shape[1] // size
+    pieces = [lax.dynamic_slice_in_dim(x, me * stride + offset, width, 1)]
     for step in range(1, size):
         dest = (me + step) % size
-        pieces.append(shift(lax.dynamic_slice_in_dim(x, dest * width, width, 1), "tp", step, size))
+        piece = lax.dynamic_slice_in_dim(x, dest * stride + offset, width, 1)
+        pieces.append(shift(piece, "tp", step, size))
     return jnp.stack(pieces)
+
+
+def tp_receive_many(items, me, size):
+    owns, sends = [], []
+    for x, width, offset in items:
+        stride = x.shape[1] // size
+        owns.append(lax.dynamic_slice_in_dim(x, me * stride + offset, width, 1))
+        sends.append(
+            [lax.dynamic_slice_in_dim(x, ((me + step) % size) * stride + offset, width, 1)
+             for step in range(1, size)]
+        )
+    received = [
+        shift(tuple(s[step - 1] for s in sends), "tp", step, size) for step in range(1, size)
+    ]
+    return [
+        jnp.stack([owns[i]] + [received[step - 1][i] for step in range(1, size)])
+        for i in range(len(items))
+    ]
 
 
 def tp_send(stack, me, size):
@@ -164,8 +183,17 @@
     k_cols = key_rows.shape[1] // tp_size
     tokens = rows_in * tp_size
     assert tokens == BLK
-    key_heads = source_order(tp_receive(key_rows, me, tp_size), me, tp_size).reshape(tokens, k_cols)
-    value_heads = source_order(tp_receive(value_rows, me, tp_size), me, tp_size).reshape(tokens, k_cols)
+    head_count = k_cols // HD
+    group_size = q_cols // k_cols
+    chunk_count = 2 if head_count % 2 == 0 else 1
+    chunk_heads = head_count // chunk_count
+    q_width = chunk_heads * group_size * HD
+    key_stack, value_stack, first_queries, first_upstream = tp_receive_many(
+        [(key_rows, k_cols, 0), (value_rows, k_cols, 0), (queries, q_width, 0), (cotangent, q_width, 0)],
+        me, tp_size,
+    )
+    key_heads = source_order(key_stack, me, tp_size).reshape(tokens, k_cols)
+    value_heads = source_order(value_stack, me, tp_size).reshape(tokens, k_cols)
     head_count = k_cols // HD
     group_size = q_cols // k_cols
     span_rows = BLK // holders
@@ -175,6 +203,7 @@
          value_heads.reshape(holders, span_rows, head_count, HD)],
         axis=1,
     )
+    kv, first_queries, first_upstream = lax.optimization_barrier((kv, first_queries, first_upstream))
     spread = lax.all_to_all(kv, "ctx", split_axis=0, concat_axis=0, tiled=True)
     my_selected = lax.dynamic_index_in_dim(selected, position, 0, keepdims=False)
     my_flags = lax.dynamic_index_in_dim(own_flag, position, 0, keepdims=False)
@@ -183,22 +212,16 @@
         axis=1,
     )
     tp_info = me.astype(jnp.int32).reshape(1)
-    chunk_count = 2 if head_count % 2 == 0 else 1
-    chunk_heads = head_count // chunk_count
     chunk_k_cols = chunk_heads * HD
-
-    q_width = chunk_heads * group_size * HD
-
-    def chunk_columns(x, chunk):
-        return x.reshape(rows_in, tp_size, chunk_count, q_width)[:, :, chunk].reshape(
-            rows_in, tp_size * q_width
-        )
 
     results = []
     for chunk in range(chunk_count):
         first = chunk * chunk_heads
-        query_stack = tp_receive(chunk_columns(queries, chunk), me, tp_size)
-        upstream_stack = tp_receive(chunk_columns(cotangent, chunk), me, tp_size)
+        if chunk == 0:
+            query_stack, upstream_stack = first_queries, first_upstream
+        else:
+            query_stack = tp_receive(queries, me, tp_size, q_width, chunk * q_width)
+            upstream_stack = tp_receive(cotangent, me, tp_size, q_width, chunk * q_width)
         chunk_selected = selected[:, first : first + chunk_heads]
         head_ids = jnp.arange(first, first + chunk_heads, dtype=jnp.int32)[None, :, None]
         send = spread[chunk_selected, :, :, head_ids, :]

time: 375 us -> 369 us (0.984)
  local copies, waits for them, and re-layouts: 89.7 us -> 59.6 us
  waiting for transfers between devices: 99.6 us -> 122 us
    slice x2 -> x0, local copies, waits for them, and re-layouts: 21.7 us -> none  [chunk_columns(): x.reshape(rows_in, tp_size, chunk_count, q_width)[:, :, chunk]]
    all_to_all x2, waiting for transfers between devices: 8.96 us -> 29.4 us  [body(): got = lax.all_to_all(send, 'ctx', split_axis=0, concat_axis=4, tiled=True)]
    reshape x2 -> x0, local copies, waits for them, and re-layouts: 6.6 us -> none  [chunk_columns(): x.reshape(rows_in, tp_size, chunk_count, q_width)[:, :, chunk]]
    another operation x4 -> x8, other arithmetic: 0.23 us -> 6.47 us  [the longest x4 6.25 us: tp_receive_many(): jnp.stack([owns[i]] + [received[step - 1][i] for step in range(1, size)])]
    another operation x6 -> x2, other arithmetic: 7.73 us -> 4.4 us  [tp_receive(): return jnp.stack(pieces)]
  transfers between devices with their start and end apart: 19 -> 19, of which waited for: 12 -> 13; matrix products, arithmetic and copies ran while one was open for 28% -> 20% of each run, Pallas kernels for 24% -> 25%
where the time goes in v7:
time: 369 us; the launch traced here: 367 us
  waiting for transfers between devices  122 us (33%)
  Pallas kernels  91.3 us (25%)
  starting transfers between devices  64.5 us (17%)
  local copies, waits for them, and re-layouts  59.6 us (16%)
  other arithmetic  28.4 us (8%)
    pallas_call x2, Pallas kernels, attention(): pl.pallas_call(kernel, grid_spec=pltpu.PrefetchScalarGridSpec(num_scalar_...  91.3 us
    ppermute x12, waiting for transfers between devices, shift(): lax.ppermute(x, axis, perm=[(s, (s + step) % size) for s in range(size)])  48.2 us
    all_to_all x2, waiting for transfers between devices, body(): got = lax.all_to_all(send, 'ctx', split_axis=0, concat_axis=4, tiled=True)  29.4 us
    all_to_all x1, waiting for transfers between devices, body(): spread = lax.all_to_all(kv, 'ctx', split_axis=0, concat_axis=0, tiled=True)  22.6 us
    all_to_all x2, waiting for transfers between devices, body(): lax.all_to_all(send_back, 'ctx', split_axis=3, concat_axis=1, tiled=True)  18.2 us
    all_to_all x2, starting transfers between devices, body(): got = lax.all_to_all(send, 'ctx', split_axis=0, concat_axis=4, tiled=True)  16.1 us
    ppermute x12, starting transfers between devices, shift(): lax.ppermute(x, axis, perm=[(s, (s + step) % size) for s in range(size)])  15.3 us
    all_to_all x2, starting transfers between devices, body(): back = lax.all_to_all(owner, 'ctx', split_axis=1, concat_axis=3, tiled=True)  15.1 us
  transfers between devices with their start and end apart: 19, of which 13 were waited for; matrix products, arithmetic and copies ran while one was open for 20% of the time, Pallas kernels for 25%

profile of v7, /device:TPU:0, one launch (start us, length us, event | category | flops | bytes accessed | tf_op | source)
XLA Modules:
  0.0 367.5 jit_solution(17518962827099233223)
XLA Ops:
  2.7 3.0 collective-permute-start.1
  14.7 4.0 %collective-permute-done = bf16[256,512]{1,0:T(8,128)(2,1)} collective-permute-done((bf16[256,512]{1,0:T(8,128)(2,1)}, bf16[256,512]{1,0:T(8,128)(2,1)}, u32[]{:S(2)}, u32[]{:S(2)}) %collective-permute-start) | collective-permute-done | bytes 262176 | tf_op jit(solution)/shard_map/ppermute | solution.py:133
  22.6 7.3 %collective-permute-done.2 = bf16[256,1024]{1,0:T(8,128)(2,1)} collective-permute-done((bf16[256,1024]{1,0:T(8,128)(2,1)}, bf16[256,1024]{1,0:T(8,128)(2,1)}, u32[]{:S(2)}, u32[]{:S(2)}) %collective-permute-start.2) | collective-permute-done | bytes 524320 | tf_op jit(solution)/shard_map/ppermute | solution.py:133
  32.0 8.3 %collective-permute-done.3 = bf16[256,1024]{1,0:T(8,128)(2,1)} collective-permute-done((bf16[256,1024]{1,0:T(8,128)(2,1)}, bf16[256,1024]{1,0:T(8,128)(2,1)}, u32[]{:S(2)}, u32[]{:S(2)}) %collective-permute-start.3) | collective-permute-done | bytes 524320 | tf_op jit(solution)/shard_map/ppermute | solution.py:133
  42.5 6.3 %all-to-all-start = ((bf16[16,2,32,4,128]{4,2,3,1,0:T(8,128)(2,1)}), bf16[16,2,32,4,128]{4,2,3,1,0:T(8,128)(2,1)S(1)}, u32[]{:S(2)}, u32[]{:S(2)}) async-start(bf16[16,2,32,4,128]{4,2,3,1,0:T(8,128)(2,1)} %pad_maximum_fusion.2), calls=%async_computation | async-start | bytes 2097152 | tf_op jit(solution)/shard_map/all_to_all | solution.py:207
  49.1 22.6 %all-to-all-done = bf16[16,2,32,4,128]{4,2,3,1,0:T(8,128)(2,1)S(1)} async-done(((bf16[16,2,32,4,128]{4,2,3,1,0:T(8,128)(2,1)}), bf16[16,2,32,4,128]{4,2,3,1,0:T(8,128)(2,1)S(1)}, u32[]{:S(2)}, u32[]{:S(2)}) %all-to-all-start) | async-done | bytes 1048608 | tf_op jit(solution)/shard_map/all_to_all | solution.py:207
  74.1 6.9 %all-to-all-start.2 = ((bf16[16,2,3,2,32,128]{5,4,3,2,1,0:T(8,128)(2,1)}), bf16[16,2,3,2,32,128]{5,4,3,2,1,0:T(8,128)(2,1)S(1)}, u32[]{:S(2)}, u32[]{:S(2)}) async-start(bf16[16,2,3,2,32,128]{5,4,3,2,1,0:T(8,128)(2,1)} %bitcast.179), calls=%async_computation.2 | async-start | bytes 3145728 | tf_op jit(solution)/shard_map/all_to_all | solution.py:228
  83.5 29.4 %all-to-all-done.2 = bf16[16,2,3,2,32,128]{5,4,3,2,1,0:T(8,128)(2,1)S(1)} async-done(((bf16[16,2,3,2,32,128]{5,4,3,2,1,0:T(8,128)(2,1)}), bf16[16,2,3,2,32,128]{5,4,3,2,1,0:T(8,128)(2,1)S(1)}, u32[]{:S(2)}, u32[]{:S(2)}) %all-to-all-start.2) | async-done | bytes 1572896 | tf_op jit(solution)/shard_map/all_to_all | solution.py:228
  112.9 9.2 %all-to-all-start.1 = ((bf16[16,2,3,2,32,128]{5,4,3,2,1,0:T(8,128)(2,1)}), bf16[16,2,3,2,32,128]{5,4,3,2,1,0:T(8,128)(2,1)S(1)}, u32[]{:S(2)}, u32[]{:S(2)}) async-start(bf16[16,2,3,2,32,128]{5,4,3,2,1,0:T(8,128)(2,1)} %bitcast.12), calls=%async_computation.1 | async-start | bytes 3145728 | tf_op jit(solution)/shard_map/all_to_all | solution.py:228
  125.2 12.1 %collective-permute-done.5 = bf16[256,1024]{1,0:T(8,128)(2,1)} collective-permute-done((bf16[256,1024]{1,0:T(8,128)(2,1)}, bf16[256,1024]{1,0:T(8,128)(2,1)}, u32[]{:S(2)}, u32[]{:S(2)}) %collective-permute-start.5) | collective-permute-done | bytes 524320 | tf_op jit(solution)/shard_map/ppermute | solution.py:133
  139.6 8.4 %collective-permute-done.6 = bf16[256,1024]{1,0:T(8,128)(2,1)} collective-permute-done((bf16[256,1024]{1,0:T(8,128)(2,1)}, bf16[256,1024]{1,0:T(8,128)(2,1)}, u32[]{:S(2)}, u32[]{:S(2)}) %collective-permute-start.6) | collective-permute-done | bytes 524320 | tf_op jit(solution)/shard_map/ppermute | solution.py:133
  151.6 45.8 %shard_map.94 = (bf16[2,256,1024]{2,1,0:T(8,128)(2,1)}, bf16[2,256,1024]{2,1,0:T(8,128)(2,1)}, f32[2,3,2,512,128]{4,3,2,1,0:T(8,128)}, f32[512,256]{1,0:T(8,128)}, f32[512,256]{1,0:T(8,128)}) custom-call(s32[8]{0:T(128)} %reshape.135.live_ref, s32[1]{0:T(128)} %bitcast.2.tp_ref, bf16[2,256,1024]{2,1,0:T(8,128)(2,1)} %pad_maximum_fusion.6.q_ref, ...), custom_call_target="tpu_custom_call" | custom-call | flops 12884901888 | bytes 10485760 | tf_op jit(solution)/shard_map/pallas_call | solution.py:105
  201.1 5.8 %all-to-all-start.5 = ((bf16[2,3,2,16,32,128]{5,4,2,1,0,3:T(8,128)(2,1)}), bf16[2,3,2,16,32,128]{5,4,2,1,0,3:T(8,128)(2,1)S(1)}, u32[]{:S(2)}, u32[]{:S(2)}) async-start(bf16[2,3,2,16,32,128]{5,4,2,1,0,3:T(8,128)(2,1)} %copy.127), calls=%async_computation.5 | async-start | bytes 3145728 | tf_op jit(solution)/shard_map/all_to_all | solution.py:241
  209.0 45.5 %shard_map.93 = (bf16[2,256,1024]{2,1,0:T(8,128)(2,1)}, bf16[2,256,1024]{2,1,0:T(8,128)(2,1)}, f32[2,3,2,512,128]{4,3,2,1,0:T(8,128)}, f32[512,256]{1,0:T(8,128)}, f32[512,256]{1,0:T(8,128)}) custom-call(s32[8]{0:T(128)} %reshape.131.live_ref, s32[1]{0:T(128)} %bitcast.2.tp_ref, bf16[2,256,1024]{2,1,0:T(8,128)(2,1)} %pad_maximum_fusion.3.q_ref, ...), custom_call_target="tpu_custom_call" | custom-call | flops 12884901888 | bytes 10485760 | tf_op jit(solution)/shard_map/pallas_call | solution.py:105
  258.4 6.0 %all-to-all-start.3 = ((bf16[2,3,2,16,32,128]{5,4,2,1,0,3:T(8,128)(2,1)}), bf16[2,3,2,16,32,128]{5,4,2,1,0,3:T(8,128)(2,1)S(1)}, u32[]{:S(2)}, u32[]{:S(2)}) async-start(bf16[2,3,2,16,32,128]{5,4,2,1,0,3:T(8,128)(2,1)} %copy.121), calls=%async_computation.3 | async-start | bytes 3145728 | tf_op jit(solution)/shard_map/all_to_all | solution.py:241
  278.2 18.2 %all-to-all-done.3 = bf16[2,3,2,16,32,128]{5,4,2,1,0,3:T(8,128)(2,1)S(1)} async-done(((bf16[2,3,2,16,32,128]{5,4,2,1,0,3:T(8,128)(2,1)}), bf16[2,3,2,16,32,128]{5,4,2,1,0,3:T(8,128)(2,1)S(1)}, u32[]{:S(2)}, u32[]{:S(2)}) %all-to-all-start.3) | async-done | bytes 1572896 | tf_op jit(solution)/shard_map/all_to_all | solution.py:241
  296.4 9.2 %all-to-all-start.6 = ((bf16[2,16,2,32,128]{4,3,2,0,1:T(8,128)(2,1)}), bf16[2,16,2,32,128]{4,3,2,0,1:T(8,128)(2,1)}, u32[]{:S(2)}, u32[]{:S(2)}) async-start(bf16[2,16,2,32,128]{4,3,2,0,1:T(8,128)(2,1)} %copy.129), calls=%async_computation.6 | async-start | bytes 1048576 | tf_op jit(solution)/shard_map/all_to_all | solution.py:251
  316.4 4.6 %collective-permute-done.8 = bf16[256,1024]{1,0:T(8,128)(2,1)} collective-permute-done((bf16[256,1024]{1,0:T(8,128)(2,1)}, bf16[256,1024]{1,0:T(8,128)(2,1)}, u32[]{:S(2)}, u32[]{:S(2)}) %collective-permute-start.8) | collective-permute-done | bytes 524320 | tf_op jit(solution)/shard_map/ppermute | solution.py:133
  326.2 5.9 %all-to-all-start.4 = ((bf16[2,16,2,32,128]{4,3,2,0,1:T(8,128)(2,1)}), bf16[2,16,2,32,128]{4,3,2,0,1:T(8,128)(2,1)}, u32[]{:S(2)}, u32[]{:S(2)}) async-start(bf16[2,16,2,32,128]{4,3,2,0,1:T(8,128)(2,1)} %copy.123), calls=%async_computation.4 | async-start | bytes 1048576 | tf_op jit(solution)/shard_map/all_to_all | solution.py:251
  332.2 3.0 select_bitcast_fusion.1
  338.0 4.1 %copy.137 = bf16[256,4096]{1,0:T(8,128)(2,1)} copy(bf16[256,4096]{0,1:T(8,128)(2,1)} %bitcast.173) | data formatting | bytes 4194304
  343.3 3.4 all-to-all-done.4
  356.0 4.1 %copy.136 = bf16[256,4096]{1,0:T(8,128)(2,1)} copy(bf16[256,4096]{0,1:T(8,128)(2,1)} %bitcast.174) | data formatting | bytes 4194304
  362.0 3.0 collective-permute-done.11
  (164 shorter events, 90.4 us)
Async XLA Ops:
  2.7 10.4 %collective-permute-start.1 = (bf16[256,512]{1,0:T(8,128)(2,1)}, bf16[256,512]{1,0:T(8,128)(2,1)}, u32[]{:S(2)}, u32[]{:S(2)}) collective-permute-start(bf16[256,512]{1,0:T(8,128)(2,1)} %get-tuple-element.79), channel_id=1, source_target_pairs={{0,1},{1,0},{2,3},{3,2},{4,5},{5,4},{6,7},{7,6},{8,9},{9,8},{10,11... | collective-permute-start | bytes 786440 | tf_op jit(solution)/shard_map/ppermute | solution.py:133
  7.4 11.3 %collective-permute-start = (bf16[256,512]{1,0:T(8,128)(2,1)}, bf16[256,512]{1,0:T(8,128)(2,1)}, u32[]{:S(2)}, u32[]{:S(2)}) collective-permute-start(bf16[256,512]{1,0:T(8,128)(2,1)} %get-tuple-element.77), channel_id=1, source_target_pairs={{0,1},{1,0},{2,3},{3,2},{4,5},{5,4},{6,7},{7,6},{8,9},{9,8},{10,11... | collective-permute-start | bytes 786440 | tf_op jit(solution)/shard_map/ppermute | solution.py:133
  8.6 21.3 %collective-permute-start.2 = (bf16[256,1024]{1,0:T(8,128)(2,1)}, bf16[256,1024]{1,0:T(8,128)(2,1)}, u32[]{:S(2)}, u32[]{:S(2)}) collective-permute-start(bf16[256,1024]{1,0:T(8,128)(2,1)} %get-tuple-element.57), channel_id=1, source_target_pairs={{0,1},{1,0},{2,3},{3,2},{4,5},{5,4},{6,7},{7,6},{8,9},{9,8},{10,11... | collective-permute-start | bytes 1572872 | tf_op jit(solution)/shard_map/ppermute | solution.py:133
  11.8 28.5 %collective-permute-start.3 = (bf16[256,1024]{1,0:T(8,128)(2,1)}, bf16[256,1024]{1,0:T(8,128)(2,1)}, u32[]{:S(2)}, u32[]{:S(2)}) collective-permute-start(bf16[256,1024]{1,0:T(8,128)(2,1)} %get-tuple-element.53), channel_id=1, source_target_pairs={{0,1},{1,0},{2,3},{3,2},{4,5},{5,4},{6,7},{7,6},{8,9},{9,8},{10,11... | collective-permute-start | bytes 1572872 | tf_op jit(solution)/shard_map/ppermute | solution.py:133
  42.5 29.2 %all-to-all-start = ((bf16[16,2,32,4,128]{4,2,3,1,0:T(8,128)(2,1)}), bf16[16,2,32,4,128]{4,2,3,1,0:T(8,128)(2,1)S(1)}, u32[]{:S(2)}, u32[]{:S(2)}) async-start(bf16[16,2,32,4,128]{4,2,3,1,0:T(8,128)(2,1)} %pad_maximum_fusion.2), calls=%async_computation | async-start | bytes 2097152 | tf_op jit(solution)/shard_map/all_to_all | solution.py:207
  74.1 38.8 %all-to-all-start.2 = ((bf16[16,2,3,2,32,128]{5,4,3,2,1,0:T(8,128)(2,1)}), bf16[16,2,3,2,32,128]{5,4,3,2,1,0:T(8,128)(2,1)S(1)}, u32[]{:S(2)}, u32[]{:S(2)}) async-start(bf16[16,2,3,2,32,128]{5,4,3,2,1,0:T(8,128)(2,1)} %bitcast.179), calls=%async_computation.2 | async-start | bytes 3145728 | tf_op jit(solution)/shard_map/all_to_all | solution.py:228
  112.9 11.5 %copy-start.23 = (s32[16,4]{0,1:T(4,128)S(1)}, s32[16,4]{0,1:T(4,128)}, u32[]{:S(2)}) copy-start(s32[16,4]{0,1:T(4,128)} %param.14) | copy-start | bytes 772
  112.9 88.2 %all-to-all-start.1 = ((bf16[16,2,3,2,32,128]{5,4,3,2,1,0:T(8,128)(2,1)}), bf16[16,2,3,2,32,128]{5,4,3,2,1,0:T(8,128)(2,1)S(1)}, u32[]{:S(2)}, u32[]{:S(2)}) async-start(bf16[16,2,3,2,32,128]{5,4,3,2,1,0:T(8,128)(2,1)} %bitcast.12), calls=%async_computation.1 | async-start | bytes 3145728 | tf_op jit(solution)/shard_map/all_to_all | solution.py:228
  122.2 15.1 %collective-permute-start.5 = (bf16[256,1024]{1,0:T(8,128)(2,1)}, bf16[256,1024]{1,0:T(8,128)(2,1)}, u32[]{:S(2)}, u32[]{:S(2)}) collective-permute-start(bf16[256,1024]{1,0:T(8,128)(2,1)} %get-tuple-element.58), channel_id=1, source_target_pairs={{0,1},{1,0},{2,3},{3,2},{4,5},{5,4},{6,7},{7,6},{8,9},{9,8},{10,11... | collective-permute-start | bytes 1572872 | tf_op jit(solution)/shard_map/ppermute | solution.py:133
  123.8 24.2 %collective-permute-start.6 = (bf16[256,1024]{1,0:T(8,128)(2,1)}, bf16[256,1024]{1,0:T(8,128)(2,1)}, u32[]{:S(2)}, u32[]{:S(2)}) collective-permute-start(bf16[256,1024]{1,0:T(8,128)(2,1)} %get-tuple-element.54), channel_id=1, source_target_pairs={{0,1},{1,0},{2,3},{3,2},{4,5},{5,4},{6,7},{7,6},{8,9},{9,8},{10,11... | collective-permute-start | bytes 1572872 | tf_op jit(solution)/shard_map/ppermute | solution.py:133
  125.2 22.7 %copy-start.13 = (bf16[1,256,1024]{2,1,0:T(8,128)(2,1)S(1)}, bf16[1,256,1024]{2,1,0:T(8,128)(2,1)}, u32[]{:S(2)}) copy-start(bf16[1,256,1024]{2,1,0:T(8,128)(2,1)} %get-tuple-element.55) | copy-start | bytes 1572868
  201.1 57.3 %all-to-all-start.5 = ((bf16[2,3,2,16,32,128]{5,4,2,1,0,3:T(8,128)(2,1)}), bf16[2,3,2,16,32,128]{5,4,2,1,0,3:T(8,128)(2,1)S(1)}, u32[]{:S(2)}, u32[]{:S(2)}) async-start(bf16[2,3,2,16,32,128]{5,4,2,1,0,3:T(8,128)(2,1)} %copy.127), calls=%async_computation.5 | async-start | bytes 3145728 | tf_op jit(solution)/shard_map/all_to_all | solution.py:241
  258.4 38.0 %all-to-all-start.3 = ((bf16[2,3,2,16,32,128]{5,4,2,1,0,3:T(8,128)(2,1)}), bf16[2,3,2,16,32,128]{5,4,2,1,0,3:T(8,128)(2,1)S(1)}, u32[]{:S(2)}, u32[]{:S(2)}) async-start(bf16[2,3,2,16,32,128]{5,4,2,1,0,3:T(8,128)(2,1)} %copy.121), calls=%async_computation.3 | async-start | bytes 3145728 | tf_op jit(solution)/shard_map/all_to_all | solution.py:241
  267.1 41.0 %collective-permute-start.4 = (bf16[256,1024]{1,0:T(8,128)(2,1)}, bf16[256,1024]{1,0:T(8,128)(2,1)}, u32[]{:S(2)}, u32[]{:S(2)}) collective-permute-start(bf16[256,1024]{1,0:T(8,128)(2,1)} %get-tuple-element.69), channel_id=1, source_target_pairs={{0,1},{1,0},{2,3},{3,2},{4,5},{5,4},{6,7},{7,6},{8,9},{9,8},{10,11... | collective-permute-start | bytes 1572872 | tf_op jit(solution)/shard_map/ppermute | solution.py:133
  269.7 41.2 %collective-permute-start.9 = (bf16[256,1024]{1,0:T(8,128)(2,1)}, bf16[256,1024]{1,0:T(8,128)(2,1)}, u32[]{:S(2)}, u32[]{:S(2)}) collective-permute-start(bf16[256,1024]{1,0:T(8,128)(2,1)} %get-tuple-element.67), channel_id=1, source_target_pairs={{0,1},{1,0},{2,3},{3,2},{4,5},{5,4},{6,7},{7,6},{8,9},{9,8},{10,11... | collective-permute-start | bytes 1572872 | tf_op jit(solution)/shard_map/ppermute | solution.py:133
  271.3 42.4 %collective-permute-start.7 = (bf16[256,1024]{1,0:T(8,128)(2,1)}, bf16[256,1024]{1,0:T(8,128)(2,1)}, u32[]{:S(2)}, u32[]{:S(2)}) collective-permute-start(bf16[256,1024]{1,0:T(8,128)(2,1)} %get-tuple-element.71), channel_id=1, source_target_pairs={{0,1},{1,0},{2,3},{3,2},{4,5},{5,4},{6,7},{7,6},{8,9},{9,8},{10,11... | collective-permute-start | bytes 1572872 | tf_op jit(solution)/shard_map/ppermute | solution.py:133
  277.2 28.4 %copy-start.15 = (bf16[2,256,1024]{2,1,0:T(8,128)(2,1)S(1)}, bf16[2,256,1024]{2,1,0:T(8,128)(2,1)}, u32[]{:S(2)}) copy-start(bf16[2,256,1024]{2,1,0:T(8,128)(2,1)} %get-tuple-element.24) | copy-start | bytes 3145732
  278.2 29.9 %copy-start.11 = (bf16[1,256,1024]{2,1,0:T(8,128)(2,1)S(1)}, bf16[1,256,1024]{2,1,0:T(8,128)(2,1)}, u32[]{:S(2)}) copy-start(bf16[1,256,1024]{2,1,0:T(8,128)(2,1)} %get-tuple-element.68) | copy-start | bytes 1572868
  296.4 29.8 %all-to-all-start.6 = ((bf16[2,16,2,32,128]{4,3,2,0,1:T(8,128)(2,1)}), bf16[2,16,2,32,128]{4,3,2,0,1:T(8,128)(2,1)}, u32[]{:S(2)}, u32[]{:S(2)}) async-start(bf16[2,16,2,32,128]{4,3,2,0,1:T(8,128)(2,1)} %copy.129), calls=%async_computation.6 | async-start | bytes 1048576 | tf_op jit(solution)/shard_map/all_to_all | solution.py:251
  306.6 14.5 %collective-permute-start.8 = (bf16[256,1024]{1,0:T(8,128)(2,1)}, bf16[256,1024]{1,0:T(8,128)(2,1)}, u32[]{:S(2)}, u32[]{:S(2)}) collective-permute-start(bf16[256,1024]{1,0:T(8,128)(2,1)} %get-tuple-element.65), channel_id=1, source_target_pairs={{0,1},{1,0},{2,3},{3,2},{4,5},{5,4},{6,7},{7,6},{8,9},{9,8},{10,11... | collective-permute-start | bytes 1572872 | tf_op jit(solution)/shard_map/ppermute | solution.py:133
  325.2 7.0 %copy-start = (bf16[2,256,1024]{2,1,0:T(8,128)(2,1)S(1)}, bf16[2,256,1024]{2,1,0:T(8,128)(2,1)}, u32[]{:S(2)}) copy-start(bf16[2,256,1024]{2,1,0:T(8,128)(2,1)} %gather_fusion.4) | copy-start | bytes 3145732
  326.2 20.5 %all-to-all-start.4 = ((bf16[2,16,2,32,128]{4,3,2,0,1:T(8,128)(2,1)}), bf16[2,16,2,32,128]{4,3,2,0,1:T(8,128)(2,1)}, u32[]{:S(2)}, u32[]{:S(2)}) async-start(bf16[2,16,2,32,128]{4,3,2,0,1:T(8,128)(2,1)} %copy.123), calls=%async_computation.4 | async-start | bytes 1048576 | tf_op jit(solution)/shard_map/all_to_all | solution.py:251
  351.0 9.3 %collective-permute-start.10 = (bf16[256,512]{1,0:T(8,128)(2,1)S(1)}, bf16[256,512]{1,0:T(8,128)(2,1)}, u32[]{:S(2)}, u32[]{:S(2)}) collective-permute-start(bf16[256,512]{1,0:T(8,128)(2,1)S(1)} %get-tuple-element.75), channel_id=1, source_target_pairs={{0,1},{1,0},{2,3},{3,2},{4,5},{5,4},{6,7},{7,6},{8,9},{9,8},{10,11... | collective-permute-start | bytes 786440 | tf_op jit(solution)/shard_map/ppermute | solution.py:133
  352.7 12.3 %collective-permute-start.11 = (bf16[256,512]{1,0:T(8,128)(2,1)S(1)}, bf16[256,512]{1,0:T(8,128)(2,1)S(1)}, u32[]{:S(2)}, u32[]{:S(2)}) collective-permute-start(bf16[256,512]{1,0:T(8,128)(2,1)S(1)} %get-tuple-element.73), channel_id=1, source_target_pairs={{0,1},{1,0},{2,3},{3,2},{4,5},{5,4},{6,7},{7,6},{8,9},{9,8},{10,11... | collective-permute-start | bytes 786440 | tf_op jit(solution)/shard_map/ppermute | solution.py:133
  (19 other events, 65.4 us)

commit v8 on v7

--- a/solution.py
+++ b/solution.py
@@ -214,17 +214,21 @@
     tp_info = me.astype(jnp.int32).reshape(1)
     chunk_k_cols = chunk_heads * HD
 
+    next_stacks = [
+        tp_receive(queries, me, tp_size, q_width, (chunk_count - 1) * q_width),
+        tp_receive(cotangent, me, tp_size, q_width, (chunk_count - 1) * q_width),
+    ]
     results = []
     for chunk in range(chunk_count):
         first = chunk * chunk_heads
-        if chunk == 0:
-            query_stack, upstream_stack = first_queries, first_upstream
-        else:
-            query_stack = tp_receive(queries, me, tp_size, q_width, chunk * q_width)
-            upstream_stack = tp_receive(cotangent, me, tp_size, q_width, chunk * q_width)
         chunk_selected = selected[:, first : first + chunk_heads]
         head_ids = jnp.arange(first, first + chunk_heads, dtype=jnp.int32)[None, :, None]
         send = spread[chunk_selected, :, :, head_ids, :]
+        if chunk == 0:
+            query_stack, upstream_stack = first_queries, first_upstream
+            send, *next_stacks = lax.optimization_barrier((send, *next_stacks))
+        else:
+            query_stack, upstream_stack = next_stacks
         got = lax.all_to_all(send, "ctx", split_axis=0, concat_axis=4, tiled=True)
         fetched = got[0]
         live = live_all[first : first + chunk_heads].reshape(-1)

time: 369 us -> 344 us (0.932)
  waiting for transfers between devices: 122 us -> 95.6 us
    all_to_all x2, waiting for transfers between devices: 29.4 us -> 1.73 us  [body(): got = lax.all_to_all(send, 'ctx', split_axis=0, concat_axis=4, tiled=True)]
    unnamed x55 -> x57, local copies, waits for them, and re-layouts: 10.6 us -> 10.6 us
  transfers between devices with their start and end apart: 19 -> 19, of which waited for: 13 -> 13; matrix products, arithmetic and copies ran while one was open for 20% -> 22% of each run, Pallas kernels for 25% -> 27%
where the time goes in v8:
time: 344 us; the launch traced here: 342 us
  waiting for transfers between devices  95.6 us (28%)
  Pallas kernels  91.2 us (27%)
  starting transfers between devices  64.8 us (19%)
  local copies, waits for them, and re-layouts  60.2 us (18%)
  other arithmetic  28.2 us (8%)
    pallas_call x2, Pallas kernels, attention(): pl.pallas_call(kernel, grid_spec=pltpu.PrefetchScalarGridSpec(num_scalar_...  91.2 us
    ppermute x12, waiting for transfers between devices, shift(): lax.ppermute(x, axis, perm=[(s, (s + step) % size) for s in range(size)])  49.6 us
    all_to_all x1, waiting for transfers between devices, body(): spread = lax.all_to_all(kv, 'ctx', split_axis=0, concat_axis=0, tiled=True)  22.6 us
    all_to_all x2, waiting for transfers between devices, body(): lax.all_to_all(send_back, 'ctx', split_axis=3, concat_axis=1, tiled=True)  18.3 us
    all_to_all x2, starting transfers between devices, body(): got = lax.all_to_all(send, 'ctx', split_axis=0, concat_axis=4, tiled=True)  16.1 us
    ppermute x12, starting transfers between devices, shift(): lax.ppermute(x, axis, perm=[(s, (s + step) % size) for s in range(size)])  15.3 us
    all_to_all x2, starting transfers between devices, body(): back = lax.all_to_all(owner, 'ctx', split_axis=1, concat_axis=3, tiled=True)  15.1 us
    all_to_all x2, starting transfers between devices, body(): lax.all_to_all(send_back, 'ctx', split_axis=3, concat_axis=1, tiled=True)  12 us
  transfers between devices with their start and end apart: 19, of which 13 were waited for; matrix products, arithmetic and copies ran while one was open for 22% of the time, Pallas kernels for 27%

profile of v8, /device:TPU:0, one launch (start us, length us, event | category | flops | bytes accessed | tf_op | source)
XLA Modules:
  0.0 342.0 jit_solution(3678588109845638151)
XLA Ops:
  2.6 3.0 collective-permute-start.1
  14.6 4.0 %collective-permute-done = bf16[256,512]{1,0:T(8,128)(2,1)} collective-permute-done((bf16[256,512]{1,0:T(8,128)(2,1)S(1)}, bf16[256,512]{1,0:T(8,128)(2,1)}, u32[]{:S(2)}, u32[]{:S(2)}) %collective-permute-start) | collective-permute-done | bytes 262176 | tf_op jit(solution)/shard_map/ppermute | solution.py:133
  22.5 7.3 %collective-permute-done.2 = bf16[256,1024]{1,0:T(8,128)(2,1)} collective-permute-done((bf16[256,1024]{1,0:T(8,128)(2,1)}, bf16[256,1024]{1,0:T(8,128)(2,1)}, u32[]{:S(2)}, u32[]{:S(2)}) %collective-permute-start.2) | collective-permute-done | bytes 524320 | tf_op jit(solution)/shard_map/ppermute | solution.py:133
  32.0 8.3 %collective-permute-done.3 = bf16[256,1024]{1,0:T(8,128)(2,1)} collective-permute-done((bf16[256,1024]{1,0:T(8,128)(2,1)}, bf16[256,1024]{1,0:T(8,128)(2,1)}, u32[]{:S(2)}, u32[]{:S(2)}) %collective-permute-start.3) | collective-permute-done | bytes 524320 | tf_op jit(solution)/shard_map/ppermute | solution.py:133
  42.4 6.3 %all-to-all-start = ((bf16[16,2,32,4,128]{4,2,3,1,0:T(8,128)(2,1)}), bf16[16,2,32,4,128]{4,2,3,1,0:T(8,128)(2,1)S(1)}, u32[]{:S(2)}, u32[]{:S(2)}) async-start(bf16[16,2,32,4,128]{4,2,3,1,0:T(8,128)(2,1)} %pad_maximum_fusion.2), calls=%async_computation | async-start | bytes 2097152 | tf_op jit(solution)/shard_map/all_to_all | solution.py:207
  48.9 22.6 %all-to-all-done = bf16[16,2,32,4,128]{4,2,3,1,0:T(8,128)(2,1)S(1)} async-done(((bf16[16,2,32,4,128]{4,2,3,1,0:T(8,128)(2,1)}), bf16[16,2,32,4,128]{4,2,3,1,0:T(8,128)(2,1)S(1)}, u32[]{:S(2)}, u32[]{:S(2)}) %all-to-all-start) | async-done | bytes 1048608 | tf_op jit(solution)/shard_map/all_to_all | solution.py:207
  73.9 7.0 %all-to-all-start.2 = ((bf16[16,2,3,2,32,128]{5,4,3,2,1,0:T(8,128)(2,1)}), bf16[16,2,3,2,32,128]{5,4,3,2,1,0:T(8,128)(2,1)S(1)}, u32[]{:S(2)}, u32[]{:S(2)}) async-start(bf16[16,2,3,2,32,128]{5,4,3,2,1,0:T(8,128)(2,1)} %bitcast.179), calls=%async_computation.2 | async-start | bytes 3145728 | tf_op jit(solution)/shard_map/all_to_all | solution.py:232
  83.3 12.8 %collective-permute-done.4 = bf16[256,1024]{1,0:T(8,128)(2,1)} collective-permute-done((bf16[256,1024]{1,0:T(8,128)(2,1)}, bf16[256,1024]{1,0:T(8,128)(2,1)}, u32[]{:S(2)}, u32[]{:S(2)}) %collective-permute-start.4) | collective-permute-done | bytes 524320 | tf_op jit(solution)/shard_map/ppermute | solution.py:133
  98.2 8.5 %collective-permute-done.5 = bf16[256,1024]{1,0:T(8,128)(2,1)} collective-permute-done((bf16[256,1024]{1,0:T(8,128)(2,1)}, bf16[256,1024]{1,0:T(8,128)(2,1)}, u32[]{:S(2)}, u32[]{:S(2)}) %collective-permute-start.5) | collective-permute-done | bytes 524320 | tf_op jit(solution)/shard_map/ppermute | solution.py:133
  112.9 9.2 %all-to-all-start.1 = ((bf16[16,2,3,2,32,128]{5,4,3,2,1,0:T(8,128)(2,1)}), bf16[16,2,3,2,32,128]{5,4,3,2,1,0:T(8,128)(2,1)}, u32[]{:S(2)}, u32[]{:S(2)}) async-start(bf16[16,2,3,2,32,128]{5,4,3,2,1,0:T(8,128)(2,1)} %bitcast.178), calls=%async_computation.1 | async-start | bytes 3145728 | tf_op jit(solution)/shard_map/all_to_all | solution.py:232
  124.5 45.7 %shard_map.94 = (bf16[2,256,1024]{2,1,0:T(8,128)(2,1)}, bf16[2,256,1024]{2,1,0:T(8,128)(2,1)}, f32[2,3,2,512,128]{4,3,2,1,0:T(8,128)}, f32[512,256]{1,0:T(8,128)}, f32[512,256]{1,0:T(8,128)}) custom-call(s32[8]{0:T(128)} %reshape.135.live_ref, s32[1]{0:T(128)} %bitcast.2.tp_ref, bf16[2,256,1024]{2,1,0:T(8,128)(2,1)} %pad_maximum_fusion.5.q_ref, ...), custom_call_target="tpu_custom_call" | custom-call | flops 12884901888 | bytes 10485760 | tf_op jit(solution)/shard_map/pallas_call | solution.py:105
  174.1 6.0 %all-to-all-start.5 = ((bf16[2,3,2,16,32,128]{5,4,2,1,0,3:T(8,128)(2,1)}), bf16[2,3,2,16,32,128]{5,4,2,1,0,3:T(8,128)(2,1)S(1)}, u32[]{:S(2)}, u32[]{:S(2)}) async-start(bf16[2,3,2,16,32,128]{5,4,2,1,0,3:T(8,128)(2,1)} %copy.127), calls=%async_computation.5 | async-start | bytes 3145728 | tf_op jit(solution)/shard_map/all_to_all | solution.py:245
  180.6 2.9 copy.115
  183.5 45.5 %shard_map.93 = (bf16[2,256,1024]{2,1,0:T(8,128)(2,1)}, bf16[2,256,1024]{2,1,0:T(8,128)(2,1)}, f32[2,3,2,512,128]{4,3,2,1,0:T(8,128)}, f32[512,256]{1,0:T(8,128)}, f32[512,256]{1,0:T(8,128)}) custom-call(s32[8]{0:T(128)} %reshape.131.live_ref, s32[1]{0:T(128)} %bitcast.2.tp_ref, bf16[2,256,1024]{2,1,0:T(8,128)(2,1)} %pad_maximum_fusion.3.q_ref, ...), custom_call_target="tpu_custom_call" | custom-call | flops 12884901888 | bytes 10485760 | tf_op jit(solution)/shard_map/pallas_call | solution.py:105
  232.9 6.0 %all-to-all-start.3 = ((bf16[2,3,2,16,32,128]{5,4,2,1,0,3:T(8,128)(2,1)}), bf16[2,3,2,16,32,128]{5,4,2,1,0,3:T(8,128)(2,1)S(1)}, u32[]{:S(2)}, u32[]{:S(2)}) async-start(bf16[2,3,2,16,32,128]{5,4,2,1,0,3:T(8,128)(2,1)} %copy.121), calls=%async_computation.3 | async-start | bytes 3145728 | tf_op jit(solution)/shard_map/all_to_all | solution.py:245
  252.6 18.3 %all-to-all-done.3 = bf16[2,3,2,16,32,128]{5,4,2,1,0,3:T(8,128)(2,1)S(1)} async-done(((bf16[2,3,2,16,32,128]{5,4,2,1,0,3:T(8,128)(2,1)}), bf16[2,3,2,16,32,128]{5,4,2,1,0,3:T(8,128)(2,1)S(1)}, u32[]{:S(2)}, u32[]{:S(2)}) %all-to-all-start.3) | async-done | bytes 1572896 | tf_op jit(solution)/shard_map/all_to_all | solution.py:245
  270.9 9.2 %all-to-all-start.6 = ((bf16[2,16,2,32,128]{4,3,2,0,1:T(8,128)(2,1)}), bf16[2,16,2,32,128]{4,3,2,0,1:T(8,128)(2,1)}, u32[]{:S(2)}, u32[]{:S(2)}) async-start(bf16[2,16,2,32,128]{4,3,2,0,1:T(8,128)(2,1)} %copy.129), calls=%async_computation.6 | async-start | bytes 1048576 | tf_op jit(solution)/shard_map/all_to_all | solution.py:255
  290.9 4.7 %collective-permute-done.8 = bf16[256,1024]{1,0:T(8,128)(2,1)} collective-permute-done((bf16[256,1024]{1,0:T(8,128)(2,1)}, bf16[256,1024]{1,0:T(8,128)(2,1)}, u32[]{:S(2)}, u32[]{:S(2)}) %collective-permute-start.8) | collective-permute-done | bytes 524320 | tf_op jit(solution)/shard_map/ppermute | solution.py:133
  300.8 5.9 %all-to-all-start.4 = ((bf16[2,16,2,32,128]{4,3,2,0,1:T(8,128)(2,1)}), bf16[2,16,2,32,128]{4,3,2,0,1:T(8,128)(2,1)}, u32[]{:S(2)}, u32[]{:S(2)}) async-start(bf16[2,16,2,32,128]{4,3,2,0,1:T(8,128)(2,1)} %copy.123), calls=%async_computation.4 | async-start | bytes 1048576 | tf_op jit(solution)/shard_map/all_to_all | solution.py:255
  306.7 3.0 select_bitcast_fusion.1
  312.5 4.1 %copy.137 = bf16[256,4096]{1,0:T(8,128)(2,1)} copy(bf16[256,4096]{0,1:T(8,128)(2,1)} %bitcast.173) | data formatting | bytes 4194304
  317.8 3.4 %all-to-all-done.4 = bf16[2,16,2,32,128]{4,3,2,0,1:T(8,128)(2,1)} async-done(((bf16[2,16,2,32,128]{4,3,2,0,1:T(8,128)(2,1)}), bf16[2,16,2,32,128]{4,3,2,0,1:T(8,128)(2,1)}, u32[]{:S(2)}, u32[]{:S(2)}) %all-to-all-start.4) | async-done | bytes 524320 | tf_op jit(solution)/shard_map/all_to_all | solution.py:255
  330.5 4.1 %copy.136 = bf16[256,4096]{1,0:T(8,128)(2,1)} copy(bf16[256,4096]{0,1:T(8,128)(2,1)} %bitcast.174) | data formatting | bytes 4194304
  336.5 3.0 collective-permute-done.11
  (166 shorter events, 90.1 us)
Async XLA Ops:
  2.6 10.4 %collective-permute-start.1 = (bf16[256,512]{1,0:T(8,128)(2,1)}, bf16[256,512]{1,0:T(8,128)(2,1)}, u32[]{:S(2)}, u32[]{:S(2)}) collective-permute-start(bf16[256,512]{1,0:T(8,128)(2,1)} %get-tuple-element.85), channel_id=1, source_target_pairs={{0,1},{1,0},{2,3},{3,2},{4,5},{5,4},{6,7},{7,6},{8,9},{9,8},{10,11... | collective-permute-start | bytes 786440 | tf_op jit(solution)/shard_map/ppermute | solution.py:133
  6.6 12.0 %collective-permute-start = (bf16[256,512]{1,0:T(8,128)(2,1)S(1)}, bf16[256,512]{1,0:T(8,128)(2,1)}, u32[]{:S(2)}, u32[]{:S(2)}) collective-permute-start(bf16[256,512]{1,0:T(8,128)(2,1)S(1)} %get-tuple-element.83), channel_id=1, source_target_pairs={{0,1},{1,0},{2,3},{3,2},{4,5},{5,4},{6,7},{7,6},{8,9},{9,8},{10,11... | collective-permute-start | bytes 786440 | tf_op jit(solution)/shard_map/ppermute | solution.py:133
  8.0 21.9 %collective-permute-start.2 = (bf16[256,1024]{1,0:T(8,128)(2,1)}, bf16[256,1024]{1,0:T(8,128)(2,1)}, u32[]{:S(2)}, u32[]{:S(2)}) collective-permute-start(bf16[256,1024]{1,0:T(8,128)(2,1)} %get-tuple-element.63), channel_id=1, source_target_pairs={{0,1},{1,0},{2,3},{3,2},{4,5},{5,4},{6,7},{7,6},{8,9},{9,8},{10,11... | collective-permute-start | bytes 1572872 | tf_op jit(solution)/shard_map/ppermute | solution.py:133
  11.3 28.9 %collective-permute-start.3 = (bf16[256,1024]{1,0:T(8,128)(2,1)}, bf16[256,1024]{1,0:T(8,128)(2,1)}, u32[]{:S(2)}, u32[]{:S(2)}) collective-permute-start(bf16[256,1024]{1,0:T(8,128)(2,1)} %get-tuple-element.59), channel_id=1, source_target_pairs={{0,1},{1,0},{2,3},{3,2},{4,5},{5,4},{6,7},{7,6},{8,9},{9,8},{10,11... | collective-permute-start | bytes 1572872 | tf_op jit(solution)/shard_map/ppermute | solution.py:133
  22.5 17.7 %copy-start.15 = (bf16[1,256,1024]{2,1,0:T(8,128)(2,1)S(1)}, bf16[1,256,1024]{2,1,0:T(8,128)(2,1)}, u32[]{:S(2)}) copy-start(bf16[1,256,1024]{2,1,0:T(8,128)(2,1)} %get-tuple-element.60) | copy-start | bytes 1572868
  42.4 29.2 %all-to-all-start = ((bf16[16,2,32,4,128]{4,2,3,1,0:T(8,128)(2,1)}), bf16[16,2,32,4,128]{4,2,3,1,0:T(8,128)(2,1)S(1)}, u32[]{:S(2)}, u32[]{:S(2)}) async-start(bf16[16,2,32,4,128]{4,2,3,1,0:T(8,128)(2,1)} %pad_maximum_fusion.2), calls=%async_computation | async-start | bytes 2097152 | tf_op jit(solution)/shard_map/all_to_all | solution.py:207
  73.9 22.1 %copy-start.13 = (bf16[1,256,1024]{2,1,0:T(8,128)(2,1)S(1)}, bf16[1,256,1024]{2,1,0:T(8,128)(2,1)}, u32[]{:S(2)}) copy-start(bf16[1,256,1024]{2,1,0:T(8,128)(2,1)} %get-tuple-element.62) | copy-start | bytes 1572868
  73.9 39.0 %all-to-all-start.2 = ((bf16[16,2,3,2,32,128]{5,4,3,2,1,0:T(8,128)(2,1)}), bf16[16,2,3,2,32,128]{5,4,3,2,1,0:T(8,128)(2,1)S(1)}, u32[]{:S(2)}, u32[]{:S(2)}) async-start(bf16[16,2,3,2,32,128]{5,4,3,2,1,0:T(8,128)(2,1)} %bitcast.179), calls=%async_computation.2 | async-start | bytes 3145728 | tf_op jit(solution)/shard_map/all_to_all | solution.py:232
  80.9 15.1 %collective-permute-start.4 = (bf16[256,1024]{1,0:T(8,128)(2,1)}, bf16[256,1024]{1,0:T(8,128)(2,1)}, u32[]{:S(2)}, u32[]{:S(2)}) collective-permute-start(bf16[256,1024]{1,0:T(8,128)(2,1)} %get-tuple-element.65), channel_id=1, source_target_pairs={{0,1},{1,0},{2,3},{3,2},{4,5},{5,4},{6,7},{7,6},{8,9},{9,8},{10,11... | collective-permute-start | bytes 1572872 | tf_op jit(solution)/shard_map/ppermute | solution.py:133
  82.5 24.2 %collective-permute-start.5 = (bf16[256,1024]{1,0:T(8,128)(2,1)}, bf16[256,1024]{1,0:T(8,128)(2,1)}, u32[]{:S(2)}, u32[]{:S(2)}) collective-permute-start(bf16[256,1024]{1,0:T(8,128)(2,1)} %get-tuple-element.61), channel_id=1, source_target_pairs={{0,1},{1,0},{2,3},{3,2},{4,5},{5,4},{6,7},{7,6},{8,9},{9,8},{10,11... | collective-permute-start | bytes 1572872 | tf_op jit(solution)/shard_map/ppermute | solution.py:133
  83.2 23.5 %copy-start.14 = (bf16[1,256,1024]{2,1,0:T(8,128)(2,1)S(1)}, bf16[1,256,1024]{2,1,0:T(8,128)(2,1)}, u32[]{:S(2)}) copy-start(bf16[1,256,1024]{2,1,0:T(8,128)(2,1)} %get-tuple-element.58) | copy-start | bytes 1572868
  112.9 61.2 %all-to-all-start.1 = ((bf16[16,2,3,2,32,128]{5,4,3,2,1,0:T(8,128)(2,1)}), bf16[16,2,3,2,32,128]{5,4,3,2,1,0:T(8,128)(2,1)}, u32[]{:S(2)}, u32[]{:S(2)}) async-start(bf16[16,2,3,2,32,128]{5,4,3,2,1,0:T(8,128)(2,1)} %bitcast.178), calls=%async_computation.1 | async-start | bytes 3145728 | tf_op jit(solution)/shard_map/all_to_all | solution.py:232
  174.1 58.8 %all-to-all-start.5 = ((bf16[2,3,2,16,32,128]{5,4,2,1,0,3:T(8,128)(2,1)}), bf16[2,3,2,16,32,128]{5,4,2,1,0,3:T(8,128)(2,1)S(1)}, u32[]{:S(2)}, u32[]{:S(2)}) async-start(bf16[2,3,2,16,32,128]{5,4,2,1,0,3:T(8,128)(2,1)} %copy.127), calls=%async_computation.5 | async-start | bytes 3145728 | tf_op jit(solution)/shard_map/all_to_all | solution.py:245
  232.9 38.0 %all-to-all-start.3 = ((bf16[2,3,2,16,32,128]{5,4,2,1,0,3:T(8,128)(2,1)}), bf16[2,3,2,16,32,128]{5,4,2,1,0,3:T(8,128)(2,1)S(1)}, u32[]{:S(2)}, u32[]{:S(2)}) async-start(bf16[2,3,2,16,32,128]{5,4,2,1,0,3:T(8,128)(2,1)} %copy.121), calls=%async_computation.3 | async-start | bytes 3145728 | tf_op jit(solution)/shard_map/all_to_all | solution.py:245
  241.6 41.0 %collective-permute-start.6 = (bf16[256,1024]{1,0:T(8,128)(2,1)}, bf16[256,1024]{1,0:T(8,128)(2,1)}, u32[]{:S(2)}, u32[]{:S(2)}) collective-permute-start(bf16[256,1024]{1,0:T(8,128)(2,1)} %get-tuple-element.75), channel_id=1, source_target_pairs={{0,1},{1,0},{2,3},{3,2},{4,5},{5,4},{6,7},{7,6},{8,9},{9,8},{10,11... | collective-permute-start | bytes 1572872 | tf_op jit(solution)/shard_map/ppermute | solution.py:133
  244.2 41.2 %collective-permute-start.9 = (bf16[256,1024]{1,0:T(8,128)(2,1)}, bf16[256,1024]{1,0:T(8,128)(2,1)}, u32[]{:S(2)}, u32[]{:S(2)}) collective-permute-start(bf16[256,1024]{1,0:T(8,128)(2,1)} %get-tuple-element.73), channel_id=1, source_target_pairs={{0,1},{1,0},{2,3},{3,2},{4,5},{5,4},{6,7},{7,6},{8,9},{9,8},{10,11... | collective-permute-start | bytes 1572872 | tf_op jit(solution)/shard_map/ppermute | solution.py:133
  245.7 42.5 %collective-permute-start.7 = (bf16[256,1024]{1,0:T(8,128)(2,1)}, bf16[256,1024]{1,0:T(8,128)(2,1)}, u32[]{:S(2)}, u32[]{:S(2)}) collective-permute-start(bf16[256,1024]{1,0:T(8,128)(2,1)} %get-tuple-element.77), channel_id=1, source_target_pairs={{0,1},{1,0},{2,3},{3,2},{4,5},{5,4},{6,7},{7,6},{8,9},{9,8},{10,11... | collective-permute-start | bytes 1572872 | tf_op jit(solution)/shard_map/ppermute | solution.py:133
  251.6 28.4 %copy-start.17 = (bf16[2,256,1024]{2,1,0:T(8,128)(2,1)S(1)}, bf16[2,256,1024]{2,1,0:T(8,128)(2,1)}, u32[]{:S(2)}) copy-start(bf16[2,256,1024]{2,1,0:T(8,128)(2,1)} %get-tuple-element.30) | copy-start | bytes 3145732
  252.6 30.0 %copy-start.11 = (bf16[1,256,1024]{2,1,0:T(8,128)(2,1)S(1)}, bf16[1,256,1024]{2,1,0:T(8,128)(2,1)}, u32[]{:S(2)}) copy-start(bf16[1,256,1024]{2,1,0:T(8,128)(2,1)} %get-tuple-element.74) | copy-start | bytes 1572868
  270.9 29.9 %all-to-all-start.6 = ((bf16[2,16,2,32,128]{4,3,2,0,1:T(8,128)(2,1)}), bf16[2,16,2,32,128]{4,3,2,0,1:T(8,128)(2,1)}, u32[]{:S(2)}, u32[]{:S(2)}) async-start(bf16[2,16,2,32,128]{4,3,2,0,1:T(8,128)(2,1)} %copy.129), calls=%async_computation.6 | async-start | bytes 1048576 | tf_op jit(solution)/shard_map/all_to_all | solution.py:255
  281.1 14.5 %collective-permute-start.8 = (bf16[256,1024]{1,0:T(8,128)(2,1)}, bf16[256,1024]{1,0:T(8,128)(2,1)}, u32[]{:S(2)}, u32[]{:S(2)}) collective-permute-start(bf16[256,1024]{1,0:T(8,128)(2,1)} %get-tuple-element.71), channel_id=1, source_target_pairs={{0,1},{1,0},{2,3},{3,2},{4,5},{5,4},{6,7},{7,6},{8,9},{9,8},{10,11... | collective-permute-start | bytes 1572872 | tf_op jit(solution)/shard_map/ppermute | solution.py:133
  300.8 20.5 %all-to-all-start.4 = ((bf16[2,16,2,32,128]{4,3,2,0,1:T(8,128)(2,1)}), bf16[2,16,2,32,128]{4,3,2,0,1:T(8,128)(2,1)}, u32[]{:S(2)}, u32[]{:S(2)}) async-start(bf16[2,16,2,32,128]{4,3,2,0,1:T(8,128)(2,1)} %copy.123), calls=%async_computation.4 | async-start | bytes 1048576 | tf_op jit(solution)/shard_map/all_to_all | solution.py:255
  325.6 9.3 %collective-permute-start.10 = (bf16[256,512]{1,0:T(8,128)(2,1)S(1)}, bf16[256,512]{1,0:T(8,128)(2,1)}, u32[]{:S(2)}, u32[]{:S(2)}) collective-permute-start(bf16[256,512]{1,0:T(8,128)(2,1)S(1)} %get-tuple-element.81), channel_id=1, source_target_pairs={{0,1},{1,0},{2,3},{3,2},{4,5},{5,4},{6,7},{7,6},{8,9},{9,8},{10,11... | collective-permute-start | bytes 786440 | tf_op jit(solution)/shard_map/ppermute | solution.py:133
  327.2 12.3 %collective-permute-start.11 = (bf16[256,512]{1,0:T(8,128)(2,1)S(1)}, bf16[256,512]{1,0:T(8,128)(2,1)S(1)}, u32[]{:S(2)}, u32[]{:S(2)}) collective-permute-start(bf16[256,512]{1,0:T(8,128)(2,1)S(1)} %get-tuple-element.79), channel_id=1, source_target_pairs={{0,1},{1,0},{2,3},{3,2},{4,5},{5,4},{6,7},{7,6},{8,9},{9,8},{10,11... | collective-permute-start | bytes 786440 | tf_op jit(solution)/shard_map/ppermute | solution.py:133
  (20 other events, 78.2 us)

commit v9 on v8

--- a/solution.py
+++ b/solution.py
@@ -203,7 +203,6 @@
          value_heads.reshape(holders, span_rows, head_count, HD)],
         axis=1,
     )
-    kv, first_queries, first_upstream = lax.optimization_barrier((kv, first_queries, first_upstream))
     spread = lax.all_to_all(kv, "ctx", split_axis=0, concat_axis=0, tiled=True)
     my_selected = lax.dynamic_index_in_dim(selected, position, 0, keepdims=False)
     my_flags = lax.dynamic_index_in_dim(own_flag, position, 0, keepdims=False)
@@ -229,6 +228,7 @@
             send, *next_stacks = lax.optimization_barrier((send, *next_stacks))
         else:
             query_stack, upstream_stack = next_stacks
+            send, _, _ = lax.optimization_barrier((send, first_queries, first_upstream))
         got = lax.all_to_all(send, "ctx", split_axis=0, concat_axis=4, tiled=True)
         fetched = got[0]
         live = live_all[first : first + chunk_heads].reshape(-1)

time: 344 us -> 325 us (0.945)
  waiting for transfers between devices: 95.6 us -> 83.3 us
  other arithmetic: 28.2 us -> 24.2 us
    all_to_all x1, waiting for transfers between devices: 22.6 us -> 0.01 us  [body(): spread = lax.all_to_all(kv, 'ctx', split_axis=0, concat_axis=0, tiled=True)]
    ppermute x12, waiting for transfers between devices: 49.6 us -> 59.9 us  [shift(): lax.ppermute(x, axis, perm=[(s, (s + step) % size) for s in range(size)])]
    another operation x4, other arithmetic: 6.24 us -> 2.25 us  [tp_receive_many(): jnp.stack([owns[i]] + [received[step - 1][i] for step in range(1, size)])]
  transfers between devices with their start and end apart: 19 -> 19, of which waited for: 13 -> 12; matrix products, arithmetic and copies ran while one was open for 22% -> 22% of each run, Pallas kernels for 27% -> 28%
where the time goes in v9:
time: 325 us; the launch traced here: 323 us
  Pallas kernels  91.2 us (28%)
  waiting for transfers between devices  83.3 us (26%)
  starting transfers between devices  63.3 us (19%)
  local copies, waits for them, and re-layouts  59.3 us (18%)
  other arithmetic  24.2 us (7%)
    pallas_call x2, Pallas kernels, attention(): pl.pallas_call(kernel, grid_spec=pltpu.PrefetchScalarGridSpec(num_scalar_...  91.2 us
    ppermute x12, waiting for transfers between devices, shift(): lax.ppermute(x, axis, perm=[(s, (s + step) % size) for s in range(size)])  59.9 us
    all_to_all x2, waiting for transfers between devices, body(): lax.all_to_all(send_back, 'ctx', split_axis=3, concat_axis=1, tiled=True)  18.3 us
    all_to_all x2, starting transfers between devices, body(): back = lax.all_to_all(owner, 'ctx', split_axis=1, concat_axis=3, tiled=True)  15.1 us
    all_to_all x2, starting transfers between devices, body(): got = lax.all_to_all(send, 'ctx', split_axis=0, concat_axis=4, tiled=True)  15 us
    ppermute x12, starting transfers between devices, shift(): lax.ppermute(x, axis, perm=[(s, (s + step) % size) for s in range(size)])  15 us
    all_to_all x2, starting transfers between devices, body(): lax.all_to_all(send_back, 'ctx', split_axis=3, concat_axis=1, tiled=True)  12 us
    unnamed x57, local copies, waits for them, and re-layouts  10.6 us
  transfers between devices with their start and end apart: 19, of which 12 were waited for; matrix products, arithmetic and copies ran while one was open for 22% of the time, Pallas kernels for 28%

profile of v9, /device:TPU:0, one launch (start us, length us, event | category | flops | bytes accessed | tf_op | source)
XLA Modules:
  0.0 323.4 jit_solution(7213173808272621683)
XLA Ops:
  1.7 3.0 collective-permute-start.2
  6.0 5.9 %collective-permute-done.2 = bf16[256,512]{1,0:T(8,128)(2,1)S(1)} collective-permute-done((bf16[256,512]{1,0:T(8,128)(2,1)S(1)}, bf16[256,512]{1,0:T(8,128)(2,1)S(1)}, u32[]{:S(2)}, u32[]{:S(2)}) %collective-permute-start.2) | collective-permute-done | bytes 262176 | tf_op jit(solution)/shard_map/ppermute | solution.py:133
  12.5 4.1 %collective-permute-done.3 = bf16[256,512]{1,0:T(8,128)(2,1)S(1)} collective-permute-done((bf16[256,512]{1,0:T(8,128)(2,1)S(1)}, bf16[256,512]{1,0:T(8,128)(2,1)S(1)}, u32[]{:S(2)}, u32[]{:S(2)}) %collective-permute-start.3) | collective-permute-done | bytes 262176 | tf_op jit(solution)/shard_map/ppermute | solution.py:133
  19.6 6.3 %all-to-all-start = ((bf16[16,2,32,4,128]{4,2,3,1,0:T(8,128)(2,1)}), bf16[16,2,32,4,128]{4,2,3,1,0:T(8,128)(2,1)S(1)}, u32[]{:S(2)}, u32[]{:S(2)}) async-start(bf16[16,2,32,4,128]{4,2,3,1,0:T(8,128)(2,1)} %pad_maximum_fusion.4), calls=%async_computation | async-start | bytes 2097152 | tf_op jit(solution)/shard_map/all_to_all | solution.py:206
  31.4 10.9 %collective-permute-done.1 = bf16[256,1024]{1,0:T(8,128)(2,1)S(1)} collective-permute-done((bf16[256,1024]{1,0:T(8,128)(2,1)}, bf16[256,1024]{1,0:T(8,128)(2,1)S(1)}, u32[]{:S(2)}, u32[]{:S(2)}) %collective-permute-start.1) | collective-permute-done | bytes 524320 | tf_op jit(solution)/shard_map/ppermute | solution.py:133
  43.4 9.6 %collective-permute-done = bf16[256,1024]{1,0:T(8,128)(2,1)S(1)} collective-permute-done((bf16[256,1024]{1,0:T(8,128)(2,1)}, bf16[256,1024]{1,0:T(8,128)(2,1)S(1)}, u32[]{:S(2)}, u32[]{:S(2)}) %collective-permute-start) | collective-permute-done | bytes 524320 | tf_op jit(solution)/shard_map/ppermute | solution.py:133
  56.4 5.9 %all-to-all-start.2 = ((bf16[16,2,3,2,32,128]{5,4,3,2,1,0:T(8,128)(2,1)}), bf16[16,2,3,2,32,128]{5,4,3,2,1,0:T(8,128)(2,1)S(1)}, u32[]{:S(2)}, u32[]{:S(2)}) async-start(bf16[16,2,3,2,32,128]{5,4,3,2,1,0:T(8,128)(2,1)} %bitcast.179), calls=%async_computation.2 | async-start | bytes 3145728 | tf_op jit(solution)/shard_map/all_to_all | solution.py:232
  64.6 12.8 %collective-permute-done.5 = bf16[256,1024]{1,0:T(8,128)(2,1)} collective-permute-done((bf16[256,1024]{1,0:T(8,128)(2,1)}, bf16[256,1024]{1,0:T(8,128)(2,1)}, u32[]{:S(2)}, u32[]{:S(2)}) %collective-permute-start.5) | collective-permute-done | bytes 524320 | tf_op jit(solution)/shard_map/ppermute | solution.py:133
  79.6 8.5 %collective-permute-done.4 = bf16[256,1024]{1,0:T(8,128)(2,1)} collective-permute-done((bf16[256,1024]{1,0:T(8,128)(2,1)}, bf16[256,1024]{1,0:T(8,128)(2,1)}, u32[]{:S(2)}, u32[]{:S(2)}) %collective-permute-start.4) | collective-permute-done | bytes 524320 | tf_op jit(solution)/shard_map/ppermute | solution.py:133
  94.3 9.2 %all-to-all-start.1 = ((bf16[16,2,3,2,32,128]{5,4,3,2,1,0:T(8,128)(2,1)}), bf16[16,2,3,2,32,128]{5,4,3,2,1,0:T(8,128)(2,1)}, u32[]{:S(2)}, u32[]{:S(2)}) async-start(bf16[16,2,3,2,32,128]{5,4,3,2,1,0:T(8,128)(2,1)} %bitcast.178), calls=%async_computation.1 | async-start | bytes 3145728 | tf_op jit(solution)/shard_map/all_to_all | solution.py:232
  105.9 45.7 %shard_map.94 = (bf16[2,256,1024]{2,1,0:T(8,128)(2,1)}, bf16[2,256,1024]{2,1,0:T(8,128)(2,1)}, f32[2,3,2,512,128]{4,3,2,1,0:T(8,128)}, f32[512,256]{1,0:T(8,128)}, f32[512,256]{1,0:T(8,128)}) custom-call(s32[8]{0:T(128)} %reshape.135.live_ref, s32[1]{0:T(128)} %bitcast.2.tp_ref, bf16[2,256,1024]{2,1,0:T(8,128)(2,1)} %pad_maximum_fusion.5.q_ref, ...), custom_call_target="tpu_custom_call" | custom-call | flops 12884901888 | bytes 10485760 | tf_op jit(solution)/shard_map/pallas_call | solution.py:105
  155.5 6.0 %all-to-all-start.5 = ((bf16[2,3,2,16,32,128]{5,4,2,1,0,3:T(8,128)(2,1)}), bf16[2,3,2,16,32,128]{5,4,2,1,0,3:T(8,128)(2,1)S(1)}, u32[]{:S(2)}, u32[]{:S(2)}) async-start(bf16[2,3,2,16,32,128]{5,4,2,1,0,3:T(8,128)(2,1)} %copy.127), calls=%async_computation.5 | async-start | bytes 3145728 | tf_op jit(solution)/shard_map/all_to_all | solution.py:245
  162.0 2.9 copy.115
  164.9 45.5 %shard_map.93 = (bf16[2,256,1024]{2,1,0:T(8,128)(2,1)}, bf16[2,256,1024]{2,1,0:T(8,128)(2,1)}, f32[2,3,2,512,128]{4,3,2,1,0:T(8,128)}, f32[512,256]{1,0:T(8,128)}, f32[512,256]{1,0:T(8,128)}) custom-call(s32[8]{0:T(128)} %reshape.131.live_ref, s32[1]{0:T(128)} %bitcast.2.tp_ref, bf16[2,256,1024]{2,1,0:T(8,128)(2,1)} %pad_maximum_fusion.2.q_ref, ...), custom_call_target="tpu_custom_call" | custom-call | flops 12884901888 | bytes 10485760 | tf_op jit(solution)/shard_map/pallas_call | solution.py:105
  214.3 6.0 %all-to-all-start.3 = ((bf16[2,3,2,16,32,128]{5,4,2,1,0,3:T(8,128)(2,1)}), bf16[2,3,2,16,32,128]{5,4,2,1,0,3:T(8,128)(2,1)S(1)}, u32[]{:S(2)}, u32[]{:S(2)}) async-start(bf16[2,3,2,16,32,128]{5,4,2,1,0,3:T(8,128)(2,1)} %copy.121), calls=%async_computation.3 | async-start | bytes 3145728 | tf_op jit(solution)/shard_map/all_to_all | solution.py:245
  234.0 18.3 %all-to-all-done.3 = bf16[2,3,2,16,32,128]{5,4,2,1,0,3:T(8,128)(2,1)S(1)} async-done(((bf16[2,3,2,16,32,128]{5,4,2,1,0,3:T(8,128)(2,1)}), bf16[2,3,2,16,32,128]{5,4,2,1,0,3:T(8,128)(2,1)S(1)}, u32[]{:S(2)}, u32[]{:S(2)}) %all-to-all-start.3) | async-done | bytes 1572896 | tf_op jit(solution)/shard_map/all_to_all | solution.py:245
  252.3 9.2 %all-to-all-start.6 = ((bf16[2,16,2,32,128]{4,3,2,0,1:T(8,128)(2,1)}), bf16[2,16,2,32,128]{4,3,2,0,1:T(8,128)(2,1)}, u32[]{:S(2)}, u32[]{:S(2)}) async-start(bf16[2,16,2,32,128]{4,3,2,0,1:T(8,128)(2,1)} %copy.129), calls=%async_computation.6 | async-start | bytes 1048576 | tf_op jit(solution)/shard_map/all_to_all | solution.py:255
  272.3 4.7 %collective-permute-done.8 = bf16[256,1024]{1,0:T(8,128)(2,1)} collective-permute-done((bf16[256,1024]{1,0:T(8,128)(2,1)}, bf16[256,1024]{1,0:T(8,128)(2,1)}, u32[]{:S(2)}, u32[]{:S(2)}) %collective-permute-start.8) | collective-permute-done | bytes 524320 | tf_op jit(solution)/shard_map/ppermute | solution.py:133
  282.1 5.9 %all-to-all-start.4 = ((bf16[2,16,2,32,128]{4,3,2,0,1:T(8,128)(2,1)}), bf16[2,16,2,32,128]{4,3,2,0,1:T(8,128)(2,1)}, u32[]{:S(2)}, u32[]{:S(2)}) async-start(bf16[2,16,2,32,128]{4,3,2,0,1:T(8,128)(2,1)} %copy.123), calls=%async_computation.4 | async-start | bytes 1048576 | tf_op jit(solution)/shard_map/all_to_all | solution.py:255
  288.1 3.0 select_bitcast_fusion.1
  293.9 4.1 %copy.137 = bf16[256,4096]{1,0:T(8,128)(2,1)} copy(bf16[256,4096]{0,1:T(8,128)(2,1)} %bitcast.173) | data formatting | bytes 4194304
  299.2 3.4 %all-to-all-done.4 = bf16[2,16,2,32,128]{4,3,2,0,1:T(8,128)(2,1)} async-done(((bf16[2,16,2,32,128]{4,3,2,0,1:T(8,128)(2,1)}), bf16[2,16,2,32,128]{4,3,2,0,1:T(8,128)(2,1)}, u32[]{:S(2)}, u32[]{:S(2)}) %all-to-all-start.4) | async-done | bytes 524320 | tf_op jit(solution)/shard_map/all_to_all | solution.py:255
  311.9 4.1 %copy.136 = bf16[256,4096]{1,0:T(8,128)(2,1)} copy(bf16[256,4096]{0,1:T(8,128)(2,1)} %bitcast.174) | data formatting | bytes 4194304
  317.9 3.0 collective-permute-done.11
  (166 shorter events, 84.2 us)
Async XLA Ops:
  1.7 10.2 %collective-permute-start.2 = (bf16[256,512]{1,0:T(8,128)(2,1)S(1)}, bf16[256,512]{1,0:T(8,128)(2,1)S(1)}, u32[]{:S(2)}, u32[]{:S(2)}) collective-permute-start(bf16[256,512]{1,0:T(8,128)(2,1)S(1)} %get-tuple-element.79), channel_id=1, source_target_pairs={{0,1},{1,0},{2,3},{3,2},{4,5},{5,4},{6,7},{7,6},{8,9},{9,8},{10,11... | collective-permute-start | bytes 786440 | tf_op jit(solution)/shard_map/ppermute | solution.py:133
  5.8 10.9 %collective-permute-start.3 = (bf16[256,512]{1,0:T(8,128)(2,1)S(1)}, bf16[256,512]{1,0:T(8,128)(2,1)S(1)}, u32[]{:S(2)}, u32[]{:S(2)}) collective-permute-start(bf16[256,512]{1,0:T(8,128)(2,1)S(1)} %get-tuple-element.81), channel_id=1, source_target_pairs={{0,1},{1,0},{2,3},{3,2},{4,5},{5,4},{6,7},{7,6},{8,9},{9,8},{10,11... | collective-permute-start | bytes 786440 | tf_op jit(solution)/shard_map/ppermute | solution.py:133
  19.6 34.4 %all-to-all-start = ((bf16[16,2,32,4,128]{4,2,3,1,0:T(8,128)(2,1)}), bf16[16,2,32,4,128]{4,2,3,1,0:T(8,128)(2,1)S(1)}, u32[]{:S(2)}, u32[]{:S(2)}) async-start(bf16[16,2,32,4,128]{4,2,3,1,0:T(8,128)(2,1)} %pad_maximum_fusion.4), calls=%async_computation | async-start | bytes 2097152 | tf_op jit(solution)/shard_map/all_to_all | solution.py:206
  27.3 15.0 %copy-start.15 = (bf16[1,256,1024]{2,1,0:T(8,128)(2,1)S(1)}, bf16[1,256,1024]{2,1,0:T(8,128)(2,1)}, u32[]{:S(2)}) copy-start(bf16[1,256,1024]{2,1,0:T(8,128)(2,1)} %get-tuple-element.54) | copy-start | bytes 1572868
  27.3 15.0 %collective-permute-start.1 = (bf16[256,1024]{1,0:T(8,128)(2,1)}, bf16[256,1024]{1,0:T(8,128)(2,1)S(1)}, u32[]{:S(2)}, u32[]{:S(2)}) collective-permute-start(bf16[256,1024]{1,0:T(8,128)(2,1)} %get-tuple-element.55), channel_id=1, source_target_pairs={{0,1},{1,0},{2,3},{3,2},{4,5},{5,4},{6,7},{7,6},{8,9},{9,8},{10,11... | collective-permute-start | bytes 1572872 | tf_op jit(solution)/shard_map/ppermute | solution.py:133
  30.1 22.9 %collective-permute-start = (bf16[256,1024]{1,0:T(8,128)(2,1)}, bf16[256,1024]{1,0:T(8,128)(2,1)S(1)}, u32[]{:S(2)}, u32[]{:S(2)}) collective-permute-start(bf16[256,1024]{1,0:T(8,128)(2,1)} %get-tuple-element.59), channel_id=1, source_target_pairs={{0,1},{1,0},{2,3},{3,2},{4,5},{5,4},{6,7},{7,6},{8,9},{9,8},{10,11... | collective-permute-start | bytes 1572872 | tf_op jit(solution)/shard_map/ppermute | solution.py:133
  56.4 21.0 %copy-start.13 = (bf16[1,256,1024]{2,1,0:T(8,128)(2,1)S(1)}, bf16[1,256,1024]{2,1,0:T(8,128)(2,1)}, u32[]{:S(2)}) copy-start(bf16[1,256,1024]{2,1,0:T(8,128)(2,1)} %get-tuple-element.57) | copy-start | bytes 1572868
  56.4 37.9 %all-to-all-start.2 = ((bf16[16,2,3,2,32,128]{5,4,3,2,1,0:T(8,128)(2,1)}), bf16[16,2,3,2,32,128]{5,4,3,2,1,0:T(8,128)(2,1)S(1)}, u32[]{:S(2)}, u32[]{:S(2)}) async-start(bf16[16,2,3,2,32,128]{5,4,3,2,1,0:T(8,128)(2,1)} %bitcast.179), calls=%async_computation.2 | async-start | bytes 3145728 | tf_op jit(solution)/shard_map/all_to_all | solution.py:232
  62.3 15.1 %collective-permute-start.5 = (bf16[256,1024]{1,0:T(8,128)(2,1)}, bf16[256,1024]{1,0:T(8,128)(2,1)}, u32[]{:S(2)}, u32[]{:S(2)}) collective-permute-start(bf16[256,1024]{1,0:T(8,128)(2,1)} %get-tuple-element.56), channel_id=1, source_target_pairs={{0,1},{1,0},{2,3},{3,2},{4,5},{5,4},{6,7},{7,6},{8,9},{9,8},{10,11... | collective-permute-start | bytes 1572872 | tf_op jit(solution)/shard_map/ppermute | solution.py:133
  63.9 24.2 %collective-permute-start.4 = (bf16[256,1024]{1,0:T(8,128)(2,1)}, bf16[256,1024]{1,0:T(8,128)(2,1)}, u32[]{:S(2)}, u32[]{:S(2)}) collective-permute-start(bf16[256,1024]{1,0:T(8,128)(2,1)} %get-tuple-element.60), channel_id=1, source_target_pairs={{0,1},{1,0},{2,3},{3,2},{4,5},{5,4},{6,7},{7,6},{8,9},{9,8},{10,11... | collective-permute-start | bytes 1572872 | tf_op jit(solution)/shard_map/ppermute | solution.py:133
  64.6 23.5 %copy-start.14 = (bf16[1,256,1024]{2,1,0:T(8,128)(2,1)S(1)}, bf16[1,256,1024]{2,1,0:T(8,128)(2,1)}, u32[]{:S(2)}) copy-start(bf16[1,256,1024]{2,1,0:T(8,128)(2,1)} %get-tuple-element.61) | copy-start | bytes 1572868
  94.3 61.2 %all-to-all-start.1 = ((bf16[16,2,3,2,32,128]{5,4,3,2,1,0:T(8,128)(2,1)}), bf16[16,2,3,2,32,128]{5,4,3,2,1,0:T(8,128)(2,1)}, u32[]{:S(2)}, u32[]{:S(2)}) async-start(bf16[16,2,3,2,32,128]{5,4,3,2,1,0:T(8,128)(2,1)} %bitcast.178), calls=%async_computation.1 | async-start | bytes 3145728 | tf_op jit(solution)/shard_map/all_to_all | solution.py:232
  155.5 58.8 %all-to-all-start.5 = ((bf16[2,3,2,16,32,128]{5,4,2,1,0,3:T(8,128)(2,1)}), bf16[2,3,2,16,32,128]{5,4,2,1,0,3:T(8,128)(2,1)S(1)}, u32[]{:S(2)}, u32[]{:S(2)}) async-start(bf16[2,3,2,16,32,128]{5,4,2,1,0,3:T(8,128)(2,1)} %copy.127), calls=%async_computation.5 | async-start | bytes 3145728 | tf_op jit(solution)/shard_map/all_to_all | solution.py:245
  214.3 38.0 %all-to-all-start.3 = ((bf16[2,3,2,16,32,128]{5,4,2,1,0,3:T(8,128)(2,1)}), bf16[2,3,2,16,32,128]{5,4,2,1,0,3:T(8,128)(2,1)S(1)}, u32[]{:S(2)}, u32[]{:S(2)}) async-start(bf16[2,3,2,16,32,128]{5,4,2,1,0,3:T(8,128)(2,1)} %copy.121), calls=%async_computation.3 | async-start | bytes 3145728 | tf_op jit(solution)/shard_map/all_to_all | solution.py:245
  223.0 41.0 %collective-permute-start.6 = (bf16[256,1024]{1,0:T(8,128)(2,1)}, bf16[256,1024]{1,0:T(8,128)(2,1)}, u32[]{:S(2)}, u32[]{:S(2)}) collective-permute-start(bf16[256,1024]{1,0:T(8,128)(2,1)} %get-tuple-element.71), channel_id=1, source_target_pairs={{0,1},{1,0},{2,3},{3,2},{4,5},{5,4},{6,7},{7,6},{8,9},{9,8},{10,11... | collective-permute-start | bytes 1572872 | tf_op jit(solution)/shard_map/ppermute | solution.py:133
  225.6 41.2 %collective-permute-start.9 = (bf16[256,1024]{1,0:T(8,128)(2,1)}, bf16[256,1024]{1,0:T(8,128)(2,1)}, u32[]{:S(2)}, u32[]{:S(2)}) collective-permute-start(bf16[256,1024]{1,0:T(8,128)(2,1)} %get-tuple-element.69), channel_id=1, source_target_pairs={{0,1},{1,0},{2,3},{3,2},{4,5},{5,4},{6,7},{7,6},{8,9},{9,8},{10,11... | collective-permute-start | bytes 1572872 | tf_op jit(solution)/shard_map/ppermute | solution.py:133
  227.1 42.5 %collective-permute-start.7 = (bf16[256,1024]{1,0:T(8,128)(2,1)}, bf16[256,1024]{1,0:T(8,128)(2,1)}, u32[]{:S(2)}, u32[]{:S(2)}) collective-permute-start(bf16[256,1024]{1,0:T(8,128)(2,1)} %get-tuple-element.73), channel_id=1, source_target_pairs={{0,1},{1,0},{2,3},{3,2},{4,5},{5,4},{6,7},{7,6},{8,9},{9,8},{10,11... | collective-permute-start | bytes 1572872 | tf_op jit(solution)/shard_map/ppermute | solution.py:133
  233.0 28.4 %copy-start.17 = (bf16[2,256,1024]{2,1,0:T(8,128)(2,1)S(1)}, bf16[2,256,1024]{2,1,0:T(8,128)(2,1)}, u32[]{:S(2)}) copy-start(bf16[2,256,1024]{2,1,0:T(8,128)(2,1)} %get-tuple-element.26) | copy-start | bytes 3145732
  234.0 30.0 %copy-start.11 = (bf16[1,256,1024]{2,1,0:T(8,128)(2,1)S(1)}, bf16[1,256,1024]{2,1,0:T(8,128)(2,1)}, u32[]{:S(2)}) copy-start(bf16[1,256,1024]{2,1,0:T(8,128)(2,1)} %get-tuple-element.70) | copy-start | bytes 1572868
  252.3 29.9 %all-to-all-start.6 = ((bf16[2,16,2,32,128]{4,3,2,0,1:T(8,128)(2,1)}), bf16[2,16,2,32,128]{4,3,2,0,1:T(8,128)(2,1)}, u32[]{:S(2)}, u32[]{:S(2)}) async-start(bf16[2,16,2,32,128]{4,3,2,0,1:T(8,128)(2,1)} %copy.129), calls=%async_computation.6 | async-start | bytes 1048576 | tf_op jit(solution)/shard_map/all_to_all | solution.py:255
  262.5 14.5 %collective-permute-start.8 = (bf16[256,1024]{1,0:T(8,128)(2,1)}, bf16[256,1024]{1,0:T(8,128)(2,1)}, u32[]{:S(2)}, u32[]{:S(2)}) collective-permute-start(bf16[256,1024]{1,0:T(8,128)(2,1)} %get-tuple-element.67), channel_id=1, source_target_pairs={{0,1},{1,0},{2,3},{3,2},{4,5},{5,4},{6,7},{7,6},{8,9},{9,8},{10,11... | collective-permute-start | bytes 1572872 | tf_op jit(solution)/shard_map/ppermute | solution.py:133
  282.1 20.5 %all-to-all-start.4 = ((bf16[2,16,2,32,128]{4,3,2,0,1:T(8,128)(2,1)}), bf16[2,16,2,32,128]{4,3,2,0,1:T(8,128)(2,1)}, u32[]{:S(2)}, u32[]{:S(2)}) async-start(bf16[2,16,2,32,128]{4,3,2,0,1:T(8,128)(2,1)} %copy.123), calls=%async_computation.4 | async-start | bytes 1048576 | tf_op jit(solution)/shard_map/all_to_all | solution.py:255
  307.0 9.3 %collective-permute-start.10 = (bf16[256,512]{1,0:T(8,128)(2,1)S(1)}, bf16[256,512]{1,0:T(8,128)(2,1)}, u32[]{:S(2)}, u32[]{:S(2)}) collective-permute-start(bf16[256,512]{1,0:T(8,128)(2,1)S(1)} %get-tuple-element.77), channel_id=1, source_target_pairs={{0,1},{1,0},{2,3},{3,2},{4,5},{5,4},{6,7},{7,6},{8,9},{9,8},{10,11... | collective-permute-start | bytes 786440 | tf_op jit(solution)/shard_map/ppermute | solution.py:133
  308.6 12.3 %collective-permute-start.11 = (bf16[256,512]{1,0:T(8,128)(2,1)S(1)}, bf16[256,512]{1,0:T(8,128)(2,1)S(1)}, u32[]{:S(2)}, u32[]{:S(2)}) collective-permute-start(bf16[256,512]{1,0:T(8,128)(2,1)S(1)} %get-tuple-element.75), channel_id=1, source_target_pairs={{0,1},{1,0},{2,3},{3,2},{4,5},{5,4},{6,7},{7,6},{8,9},{9,8},{10,11... | collective-permute-start | bytes 786440 | tf_op jit(solution)/shard_map/ppermute | solution.py:133
  (20 other events, 75.7 us)

commit v10 on v9

--- a/solution.py
+++ b/solution.py
@@ -217,7 +217,16 @@
         tp_receive(queries, me, tp_size, q_width, (chunk_count - 1) * q_width),
         tp_receive(cotangent, me, tp_size, q_width, (chunk_count - 1) * q_width),
     ]
+    def add_own(back, grad_key_own, grad_value_own):
+        back = back.astype(jnp.float32)
+        total_keys = back[:, 0].transpose(1, 0, 2).reshape(tokens, chunk_k_cols) + grad_key_own
+        total_values = (
+            back[:, 1].transpose(1, 0, 2).reshape(tokens, chunk_k_cols) + grad_value_own
+        )
+        return (total_keys, total_values)
+
     results = []
+    pending = []
     for chunk in range(chunk_count):
         first = chunk * chunk_heads
         chunk_selected = selected[:, first : first + chunk_heads]
@@ -242,23 +251,45 @@
         send_back = grad_sel.astype(jnp.bfloat16).reshape(
             chunk_heads, TOPK, 2, holders, span_rows, HD
         )
-        got_back = lax.all_to_all(send_back, "ctx", split_axis=3, concat_axis=1, tiled=True)
-        flat = got_back.reshape(chunk_heads, holders * TOPK, 2 * span_rows * HD).astype(
-            jnp.float32
-        )
+        if chunk == chunk_count - 1 and pending:
+            parts = [send_back.transpose(3, 0, 1, 2, 4, 5).reshape(holders, -1)] + [
+                p[0].transpose(1, 0, 2, 3, 4).reshape(holders, -1) for p in pending
+            ]
+            widths = [p.shape[1] for p in parts]
+            merged = lax.all_to_all(
+                jnp.concatenate(parts, axis=1), "ctx", split_axis=0, concat_axis=0, tiled=True
+            )
+            offsets = [sum(widths[:i]) for i in range(len(widths))]
+            flat = (
+                merged[:, : widths[0]]
+                .reshape(holders, chunk_heads, TOPK, 2, span_rows, HD)
+                .transpose(1, 0, 2, 3, 4, 5)
+                .reshape(chunk_heads, holders * TOPK, 2 * span_rows * HD)
+            )
+            for p, offset, width in zip(pending, offsets[1:], widths[1:]):
+                back = (
+                    merged[:, offset : offset + width]
+                    .reshape(holders, chunk_heads, 2, span_rows, HD)
+                    .transpose(1, 2, 0, 3, 4)
+                    .reshape(chunk_heads, 2, BLK, HD)
+                )
+                results.append(p[1:3] + add_own(back, *p[3:]))
+            pending = []
+        else:
+            got_back = lax.all_to_all(send_back, "ctx", split_axis=3, concat_axis=1, tiled=True)
+            flat = got_back.reshape(chunk_heads, holders * TOPK, 2 * span_rows * HD)
+        flat = flat.astype(jnp.float32)
         targets = chunk_selected.transpose(1, 0, 2).reshape(chunk_heads, holders * TOPK)
         table = (
             targets[:, None, :] == jnp.arange(holders, dtype=jnp.int32)[None, :, None]
         ).astype(jnp.float32)
         summed = jnp.einsum("gjn,gnx->gjx", table, flat, precision=lax.Precision.HIGHEST)
         owner = summed.reshape(chunk_heads, holders, 2, span_rows, HD).astype(jnp.bfloat16)
-        back = lax.all_to_all(owner, "ctx", split_axis=1, concat_axis=3, tiled=True)
-        back = back[:, 0].astype(jnp.float32)
-        total_keys = back[:, 0].transpose(1, 0, 2).reshape(tokens, chunk_k_cols) + grad_key_own
-        total_values = (
-            back[:, 1].transpose(1, 0, 2).reshape(tokens, chunk_k_cols) + grad_value_own
-        )
-        results.append((attended, grad_queries, total_keys, total_values))
+        pending.append((owner, attended, grad_queries, grad_key_own, grad_value_own))
+
+    for p in pending:
+        back = lax.all_to_all(p[0], "ctx", split_axis=1, concat_axis=3, tiled=True)[:, 0]
+        results.append(p[1:3] + add_own(back, *p[3:]))
 
     def rows_by_destination(total):
         stack = total.astype(jnp.bfloat16).reshape(tp_size, rows_in, k_cols)

time: 325 us -> 359 us (1.10)
  local copies, waits for them, and re-layouts: 59.3 us -> 81.2 us
  waiting for transfers between devices: 83.3 us -> 97.2 us
  starting transfers between devices: 63.3 us -> 53.6 us
  other arithmetic: 24.2 us -> 30.3 us
    ppermute x12, waiting for transfers between devices: 59.9 us -> 82.6 us  [shift(): lax.ppermute(x, axis, perm=[(s, (s + step) % size) for s in range(size)])]
    unnamed x57 -> x55, local copies, waits for them, and re-layouts: 10.6 us -> 29.8 us
    all_to_all x2 -> x1, waiting for transfers between devices: 18.3 us -> 0.01 us  [body(): lax.all_to_all(send_back, 'ctx', split_axis=3, concat_axis=1, tiled=True)]
    all_to_all x2, waiting for transfers between devices: 3.43 us -> 12.9 us  [the longest x1 12.9 us: body(): lax.all_to_all(p[0], 'ctx', split_axis=1, concat_axis=3, tiled=True)[:, 0]]
    all_to_all x2 -> x1, starting transfers between devices: 12 us -> 5.97 us  [body(): lax.all_to_all(send_back, 'ctx', split_axis=3, concat_axis=1, tiled=True)]
    gather x6, local copies, waits for them, and re-layouts: 7.55 us -> 11.5 us  [tp_send(): arranged = jnp.take(jnp.stack(pieces), order, axis=0)]
  transfers between devices with their start and end apart: 19 -> 18, of which waited for: 12 -> 14; matrix products, arithmetic and copies ran while one was open for 22% -> 20% of each run, Pallas kernels for 28% -> 26%
where the time goes in v10:
time: 359 us; the launch traced here: 357 us
  waiting for transfers between devices  97.2 us (27%)
  Pallas kernels  91.2 us (25%)
  local copies, waits for them, and re-layouts  81.2 us (23%)
  starting transfers between devices  53.6 us (15%)
  other arithmetic  30.3 us (8%)
    pallas_call x2, Pallas kernels, attention(): pl.pallas_call(kernel, grid_spec=pltpu.PrefetchScalarGridSpec(num_scalar_...  91.2 us
    ppermute x12, waiting for transfers between devices, shift(): lax.ppermute(x, axis, perm=[(s, (s + step) % size) for s in range(size)])  82.6 us
    unnamed x55, local copies, waits for them, and re-layouts  29.8 us
    all_to_all x2, starting transfers between devices, body(): got = lax.all_to_all(send, 'ctx', split_axis=0, concat_axis=4, tiled=True)  15 us
    ppermute x12, starting transfers between devices, shift(): lax.ppermute(x, axis, perm=[(s, (s + step) % size) for s in range(size)])  14.5 us
    all_to_all x1, waiting for transfers between devices, body(): lax.all_to_all(p[0], 'ctx', split_axis=1, concat_axis=3, tiled=True)[:, 0]  12.9 us
    gather x6, local copies, waits for them, and re-layouts, tp_send(): arranged = jnp.take(jnp.stack(pieces), order, axis=0)  11.5 us
    another operation x6, other arithmetic, tp_send(): arranged = jnp.take(jnp.stack(pieces), order, axis=0)  8.91 us
  transfers between devices with their start and end apart: 18, of which 14 were waited for; matrix products, arithmetic and copies ran while one was open for 20% of the time, Pallas kernels for 26%

profile of v10, /device:TPU:0, one launch (start us, length us, event | category | flops | bytes accessed | tf_op | source)
XLA Modules:
  0.0 356.9 jit_solution(6192328976534759528)
XLA Ops:
  6.0 5.9 %collective-permute-done.2 = bf16[256,512]{1,0:T(8,128)(2,1)S(1)} collective-permute-done((bf16[256,512]{1,0:T(8,128)(2,1)S(1)}, bf16[256,512]{1,0:T(8,128)(2,1)S(1)}, u32[]{:S(2)}, u32[]{:S(2)}) %collective-permute-start.2) | collective-permute-done | bytes 262176 | tf_op jit(solution)/shard_map/ppermute | solution.py:133
  12.5 4.1 %collective-permute-done.3 = bf16[256,512]{1,0:T(8,128)(2,1)S(1)} collective-permute-done((bf16[256,512]{1,0:T(8,128)(2,1)S(1)}, bf16[256,512]{1,0:T(8,128)(2,1)S(1)}, u32[]{:S(2)}, u32[]{:S(2)}) %collective-permute-start.3) | collective-permute-done | bytes 262176 | tf_op jit(solution)/shard_map/ppermute | solution.py:133
  19.6 6.3 %all-to-all-start = ((bf16[16,2,32,4,128]{4,2,3,1,0:T(8,128)(2,1)}), bf16[16,2,32,4,128]{4,2,3,1,0:T(8,128)(2,1)S(1)}, u32[]{:S(2)}, u32[]{:S(2)}) async-start(bf16[16,2,32,4,128]{4,2,3,1,0:T(8,128)(2,1)} %pad_maximum_fusion.4), calls=%async_computation | async-start | bytes 2097152 | tf_op jit(solution)/shard_map/all_to_all | solution.py:206
  31.3 11.0 %collective-permute-done.5 = bf16[256,1024]{1,0:T(8,128)(2,1)S(1)} collective-permute-done((bf16[256,1024]{1,0:T(8,128)(2,1)}, bf16[256,1024]{1,0:T(8,128)(2,1)S(1)}, u32[]{:S(2)}, u32[]{:S(2)}) %collective-permute-start.5) | collective-permute-done | bytes 524320 | tf_op jit(solution)/shard_map/ppermute | solution.py:133
  43.4 9.6 %collective-permute-done.4 = bf16[256,1024]{1,0:T(8,128)(2,1)S(1)} collective-permute-done((bf16[256,1024]{1,0:T(8,128)(2,1)}, bf16[256,1024]{1,0:T(8,128)(2,1)S(1)}, u32[]{:S(2)}, u32[]{:S(2)}) %collective-permute-start.4) | collective-permute-done | bytes 524320 | tf_op jit(solution)/shard_map/ppermute | solution.py:133
  56.5 5.9 %all-to-all-start.1 = ((bf16[16,2,3,2,32,128]{5,4,3,2,1,0:T(8,128)(2,1)}), bf16[16,2,3,2,32,128]{5,4,3,2,1,0:T(8,128)(2,1)S(1)}, u32[]{:S(2)}, u32[]{:S(2)}) async-start(bf16[16,2,3,2,32,128]{5,4,3,2,1,0:T(8,128)(2,1)} %bitcast.199), calls=%async_computation.1 | async-start | bytes 3145728 | tf_op jit(solution)/shard_map/all_to_all | solution.py:241
  64.7 12.8 %collective-permute-done.1 = bf16[256,1024]{1,0:T(8,128)(2,1)} collective-permute-done((bf16[256,1024]{1,0:T(8,128)(2,1)}, bf16[256,1024]{1,0:T(8,128)(2,1)}, u32[]{:S(2)}, u32[]{:S(2)}) %collective-permute-start.1) | collective-permute-done | bytes 524320 | tf_op jit(solution)/shard_map/ppermute | solution.py:133
  79.6 8.6 %collective-permute-done = bf16[256,1024]{1,0:T(8,128)(2,1)} collective-permute-done((bf16[256,1024]{1,0:T(8,128)(2,1)}, bf16[256,1024]{1,0:T(8,128)(2,1)}, u32[]{:S(2)}, u32[]{:S(2)}) %collective-permute-start) | collective-permute-done | bytes 524320 | tf_op jit(solution)/shard_map/ppermute | solution.py:133
  94.4 9.2 %all-to-all-start.2 = ((bf16[16,2,3,2,32,128]{5,4,3,2,1,0:T(8,128)(2,1)}), bf16[16,2,3,2,32,128]{5,4,3,2,1,0:T(8,128)(2,1)}, u32[]{:S(2)}, u32[]{:S(2)}) async-start(bf16[16,2,3,2,32,128]{5,4,3,2,1,0:T(8,128)(2,1)} %bitcast.197), calls=%async_computation.2 | async-start | bytes 3145728 | tf_op jit(solution)/shard_map/all_to_all | solution.py:241
  106.1 45.5 %shard_map.93 = (bf16[2,256,1024]{2,1,0:T(8,128)(2,1)}, bf16[2,256,1024]{2,1,0:T(8,128)(2,1)}, f32[2,3,2,512,128]{4,3,2,1,0:T(8,128)}, f32[512,256]{1,0:T(8,128)}, f32[512,256]{1,0:T(8,128)}) custom-call(s32[8]{0:T(128)} %reshape.142.live_ref, s32[1]{0:T(128)} %bitcast.2.tp_ref, bf16[2,256,1024]{2,1,0:T(8,128)(2,1)} %pad_maximum_fusion.2.q_ref, ...), custom_call_target="tpu_custom_call" | custom-call | flops 12884901888 | bytes 10485760 | tf_op jit(solution)/shard_map/pallas_call | solution.py:105
  155.4 6.0 %all-to-all-start.3 = ((bf16[2,3,2,16,32,128]{5,4,2,1,0,3:T(8,128)(2,1)}), bf16[2,3,2,16,32,128]{5,4,2,1,0,3:T(8,128)(2,1)S(1)}, u32[]{:S(2)}, u32[]{:S(2)}) async-start(bf16[2,3,2,16,32,128]{5,4,2,1,0,3:T(8,128)(2,1)} %copy.130), calls=%async_computation.3 | async-start | bytes 3145728 | tf_op jit(solution)/shard_map/all_to_all | solution.py:279
  165.0 45.7 %shard_map.94 = (bf16[2,256,1024]{2,1,0:T(8,128)(2,1)}, bf16[2,256,1024]{2,1,0:T(8,128)(2,1)}, f32[2,3,2,512,128]{4,3,2,1,0:T(8,128)}, f32[512,256]{1,0:T(8,128)}, f32[512,256]{1,0:T(8,128)}) custom-call(s32[8]{0:T(128)} %reshape.146.live_ref, s32[1]{0:T(128)} %bitcast.2.tp_ref, bf16[2,256,1024]{2,1,0:T(8,128)(2,1)} %pad_maximum_fusion.5.q_ref, ...), custom_call_target="tpu_custom_call" | custom-call | flops 12884901888 | bytes 10485760 | tf_op jit(solution)/shard_map/pallas_call | solution.py:105
  221.8 4.0 %reshape.298 = bf16[16,2,32768]{2,1,0:T(2,128)(2,1)} reshape(bf16[16,65536]{1,0:T(8,128)(2,1)} %reduce) | data formatting | bytes 4194304
  225.9 6.1 %all-to-all-start.4 = ((bf16[16,2,32768]{2,1,0:T(2,128)(2,1)}), bf16[16,2,32768]{2,1,0:T(2,128)(2,1)S(1)}, u32[]{:S(2)}, u32[]{:S(2)}) async-start(bf16[16,2,32768]{2,1,0:T(2,128)(2,1)} %reshape.298), calls=%async_computation.4 | async-start | bytes 4194304 | tf_op jit(solution)/shard_map/all_to_all | solution.py:259
  240.1 7.0 %collective-permute-done.6 = bf16[256,1024]{1,0:T(8,128)(2,1)S(1)} collective-permute-done((bf16[256,1024]{1,0:T(8,128)(2,1)S(1)}, bf16[256,1024]{1,0:T(8,128)(2,1)S(1)}, u32[]{:S(2)}, u32[]{:S(2)}) %collective-permute-start.6) | collective-permute-done | bytes 524320 | tf_op jit(solution)/shard_map/ppermute | solution.py:133
  250.0 8.4 %collective-permute-done.9 = bf16[256,1024]{1,0:T(8,128)(2,1)} collective-permute-done((bf16[256,1024]{1,0:T(8,128)(2,1)}, bf16[256,1024]{1,0:T(8,128)(2,1)}, u32[]{:S(2)}, u32[]{:S(2)}) %collective-permute-start.9) | collective-permute-done | bytes 524320 | tf_op jit(solution)/shard_map/ppermute | solution.py:133
  263.5 6.1 %collective-permute-done.7 = bf16[256,1024]{1,0:T(8,128)(2,1)} collective-permute-done((bf16[256,1024]{1,0:T(8,128)(2,1)}, bf16[256,1024]{1,0:T(8,128)(2,1)}, u32[]{:S(2)}, u32[]{:S(2)}) %collective-permute-start.7) | collective-permute-done | bytes 524320 | tf_op jit(solution)/shard_map/ppermute | solution.py:133
  274.8 5.7 %collective-permute-done.8 = bf16[256,1024]{1,0:T(8,128)(2,1)} collective-permute-done((bf16[256,1024]{1,0:T(8,128)(2,1)}, bf16[256,1024]{1,0:T(8,128)(2,1)}, u32[]{:S(2)}, u32[]{:S(2)}) %collective-permute-start.8) | collective-permute-done | bytes 524320 | tf_op jit(solution)/shard_map/ppermute | solution.py:133
  294.5 4.1 %copy.146 = bf16[256,4096]{1,0:T(8,128)(2,1)} copy(bf16[256,4096]{0,1:T(8,128)(2,1)} %bitcast.194) | data formatting | bytes 4194304
  298.6 6.8 %reshape.299 = bf16[16,1,65536]{2,1,0:T(2,128)(2,1)} reshape(bf16[16,2,32768]{2,1,0:T(2,128)(2,1)S(1)} %all-to-all-done.4) | data formatting | bytes 4194304
  305.4 4.5 %copy.169 = bf16[16,1,65536]{2,0,1:T(8,128)(2,1)S(1)} copy(bf16[16,1,65536]{2,1,0:T(2,128)(2,1)} %reshape.299) | data formatting | bytes 4194304
  318.1 5.7 %all-to-all-start.5 = ((bf16[2,16,2,32,128]{4,3,2,0,1:T(8,128)(2,1)}), bf16[2,16,2,32,128]{4,3,2,0,1:T(8,128)(2,1)S(1)}, u32[]{:S(2)}, u32[]{:S(2)}) async-start(bf16[2,16,2,32,128]{4,3,2,0,1:T(8,128)(2,1)} %copy.138), calls=%async_computation.5 | async-start | bytes 1048576 | tf_op jit(solution)/shard_map/all_to_all | solution.py:291
  325.4 12.9 %all-to-all-done.5 = bf16[2,16,2,32,128]{4,3,2,0,1:T(8,128)(2,1)S(1)} async-done(((bf16[2,16,2,32,128]{4,3,2,0,1:T(8,128)(2,1)}), bf16[2,16,2,32,128]{4,3,2,0,1:T(8,128)(2,1)S(1)}, u32[]{:S(2)}, u32[]{:S(2)}) %all-to-all-start.5) | async-done | bytes 524320 | tf_op jit(solution)/shard_map/all_to_all | solution.py:291
  345.4 4.1 %copy.145 = bf16[256,4096]{1,0:T(8,128)(2,1)} copy(bf16[256,4096]{0,1:T(8,128)(2,1)} %bitcast.195) | data formatting | bytes 4194304
  (166 shorter events, 109.7 us)
Async XLA Ops:
  1.7 10.2 %collective-permute-start.2 = (bf16[256,512]{1,0:T(8,128)(2,1)S(1)}, bf16[256,512]{1,0:T(8,128)(2,1)S(1)}, u32[]{:S(2)}, u32[]{:S(2)}) collective-permute-start(bf16[256,512]{1,0:T(8,128)(2,1)S(1)} %get-tuple-element.79), channel_id=1, source_target_pairs={{0,1},{1,0},{2,3},{3,2},{4,5},{5,4},{6,7},{7,6},{8,9},{9,8},{10,11... | collective-permute-start | bytes 786440 | tf_op jit(solution)/shard_map/ppermute | solution.py:133
  5.8 10.9 %collective-permute-start.3 = (bf16[256,512]{1,0:T(8,128)(2,1)S(1)}, bf16[256,512]{1,0:T(8,128)(2,1)S(1)}, u32[]{:S(2)}, u32[]{:S(2)}) collective-permute-start(bf16[256,512]{1,0:T(8,128)(2,1)S(1)} %get-tuple-element.81), channel_id=1, source_target_pairs={{0,1},{1,0},{2,3},{3,2},{4,5},{5,4},{6,7},{7,6},{8,9},{9,8},{10,11... | collective-permute-start | bytes 786440 | tf_op jit(solution)/shard_map/ppermute | solution.py:133
  19.6 34.6 %all-to-all-start = ((bf16[16,2,32,4,128]{4,2,3,1,0:T(8,128)(2,1)}), bf16[16,2,32,4,128]{4,2,3,1,0:T(8,128)(2,1)S(1)}, u32[]{:S(2)}, u32[]{:S(2)}) async-start(bf16[16,2,32,4,128]{4,2,3,1,0:T(8,128)(2,1)} %pad_maximum_fusion.4), calls=%async_computation | async-start | bytes 2097152 | tf_op jit(solution)/shard_map/all_to_all | solution.py:206
  27.3 15.0 %copy-start.9 = (bf16[1,256,1024]{2,1,0:T(8,128)(2,1)S(1)}, bf16[1,256,1024]{2,1,0:T(8,128)(2,1)}, u32[]{:S(2)}) copy-start(bf16[1,256,1024]{2,1,0:T(8,128)(2,1)} %get-tuple-element.57) | copy-start | bytes 1572868
  27.3 15.0 %collective-permute-start.5 = (bf16[256,1024]{1,0:T(8,128)(2,1)}, bf16[256,1024]{1,0:T(8,128)(2,1)S(1)}, u32[]{:S(2)}, u32[]{:S(2)}) collective-permute-start(bf16[256,1024]{1,0:T(8,128)(2,1)} %get-tuple-element.56), channel_id=1, source_target_pairs={{0,1},{1,0},{2,3},{3,2},{4,5},{5,4},{6,7},{7,6},{8,9},{9,8},{10,11... | collective-permute-start | bytes 1572872 | tf_op jit(solution)/shard_map/ppermute | solution.py:133
  30.1 22.9 %collective-permute-start.4 = (bf16[256,1024]{1,0:T(8,128)(2,1)}, bf16[256,1024]{1,0:T(8,128)(2,1)S(1)}, u32[]{:S(2)}, u32[]{:S(2)}) collective-permute-start(bf16[256,1024]{1,0:T(8,128)(2,1)} %get-tuple-element.60), channel_id=1, source_target_pairs={{0,1},{1,0},{2,3},{3,2},{4,5},{5,4},{6,7},{7,6},{8,9},{9,8},{10,11... | collective-permute-start | bytes 1572872 | tf_op jit(solution)/shard_map/ppermute | solution.py:133
  56.5 21.0 %copy-start.7 = (bf16[1,256,1024]{2,1,0:T(8,128)(2,1)S(1)}, bf16[1,256,1024]{2,1,0:T(8,128)(2,1)}, u32[]{:S(2)}) copy-start(bf16[1,256,1024]{2,1,0:T(8,128)(2,1)} %get-tuple-element.54) | copy-start | bytes 1572868
  56.5 37.9 %all-to-all-start.1 = ((bf16[16,2,3,2,32,128]{5,4,3,2,1,0:T(8,128)(2,1)}), bf16[16,2,3,2,32,128]{5,4,3,2,1,0:T(8,128)(2,1)S(1)}, u32[]{:S(2)}, u32[]{:S(2)}) async-start(bf16[16,2,3,2,32,128]{5,4,3,2,1,0:T(8,128)(2,1)} %bitcast.199), calls=%async_computation.1 | async-start | bytes 3145728 | tf_op jit(solution)/shard_map/all_to_all | solution.py:241
  62.4 15.1 %collective-permute-start.1 = (bf16[256,1024]{1,0:T(8,128)(2,1)}, bf16[256,1024]{1,0:T(8,128)(2,1)}, u32[]{:S(2)}, u32[]{:S(2)}) collective-permute-start(bf16[256,1024]{1,0:T(8,128)(2,1)} %get-tuple-element.55), channel_id=1, source_target_pairs={{0,1},{1,0},{2,3},{3,2},{4,5},{5,4},{6,7},{7,6},{8,9},{9,8},{10,11... | collective-permute-start | bytes 1572872 | tf_op jit(solution)/shard_map/ppermute | solution.py:133
  64.0 24.2 %collective-permute-start = (bf16[256,1024]{1,0:T(8,128)(2,1)}, bf16[256,1024]{1,0:T(8,128)(2,1)}, u32[]{:S(2)}, u32[]{:S(2)}) collective-permute-start(bf16[256,1024]{1,0:T(8,128)(2,1)} %get-tuple-element.59), channel_id=1, source_target_pairs={{0,1},{1,0},{2,3},{3,2},{4,5},{5,4},{6,7},{7,6},{8,9},{9,8},{10,11... | collective-permute-start | bytes 1572872 | tf_op jit(solution)/shard_map/ppermute | solution.py:133
  64.7 23.5 %copy-start.8 = (bf16[1,256,1024]{2,1,0:T(8,128)(2,1)S(1)}, bf16[1,256,1024]{2,1,0:T(8,128)(2,1)}, u32[]{:S(2)}) copy-start(bf16[1,256,1024]{2,1,0:T(8,128)(2,1)} %get-tuple-element.58) | copy-start | bytes 1572868
  92.7 11.1 %copy-start.19 = (s32[16,4]{0,1:T(4,128)S(1)}, s32[16,4]{0,1:T(4,128)}, u32[]{:S(2)}) copy-start(s32[16,4]{0,1:T(4,128)} %param.14) | copy-start | bytes 772
  94.4 61.0 %all-to-all-start.2 = ((bf16[16,2,3,2,32,128]{5,4,3,2,1,0:T(8,128)(2,1)}), bf16[16,2,3,2,32,128]{5,4,3,2,1,0:T(8,128)(2,1)}, u32[]{:S(2)}, u32[]{:S(2)}) async-start(bf16[16,2,3,2,32,128]{5,4,3,2,1,0:T(8,128)(2,1)} %bitcast.197), calls=%async_computation.2 | async-start | bytes 3145728 | tf_op jit(solution)/shard_map/all_to_all | solution.py:241
  155.4 60.1 %all-to-all-start.3 = ((bf16[2,3,2,16,32,128]{5,4,2,1,0,3:T(8,128)(2,1)}), bf16[2,3,2,16,32,128]{5,4,2,1,0,3:T(8,128)(2,1)S(1)}, u32[]{:S(2)}, u32[]{:S(2)}) async-start(bf16[2,3,2,16,32,128]{5,4,2,1,0,3:T(8,128)(2,1)} %copy.130), calls=%async_computation.3 | async-start | bytes 3145728 | tf_op jit(solution)/shard_map/all_to_all | solution.py:279
  225.9 6.3 %copy-start.11 = (bf16[2,256,1024]{2,1,0:T(8,128)(2,1)S(1)}, bf16[2,256,1024]{2,1,0:T(8,128)(2,1)}, u32[]{:S(2)}) copy-start(bf16[2,256,1024]{2,1,0:T(8,128)(2,1)} %get-tuple-element.21) | copy-start | bytes 3145732
  225.9 72.8 %all-to-all-start.4 = ((bf16[16,2,32768]{2,1,0:T(2,128)(2,1)}), bf16[16,2,32768]{2,1,0:T(2,128)(2,1)S(1)}, u32[]{:S(2)}, u32[]{:S(2)}) async-start(bf16[16,2,32768]{2,1,0:T(2,128)(2,1)} %reshape.298), calls=%async_computation.4 | async-start | bytes 4194304 | tf_op jit(solution)/shard_map/all_to_all | solution.py:259
  232.3 14.8 %collective-permute-start.6 = (bf16[256,1024]{1,0:T(8,128)(2,1)S(1)}, bf16[256,1024]{1,0:T(8,128)(2,1)S(1)}, u32[]{:S(2)}, u32[]{:S(2)}) collective-permute-start(bf16[256,1024]{1,0:T(8,128)(2,1)S(1)} %get-tuple-element.71), channel_id=1, source_target_pairs={{0,1},{1,0},{2,3},{3,2},{4,5},{5,4},{6,7},{7,6},{8,9},{9,8},{10,11... | collective-permute-start | bytes 1572872 | tf_op jit(solution)/shard_map/ppermute | solution.py:133
  234.9 23.5 %collective-permute-start.9 = (bf16[256,1024]{1,0:T(8,128)(2,1)}, bf16[256,1024]{1,0:T(8,128)(2,1)}, u32[]{:S(2)}, u32[]{:S(2)}) collective-permute-start(bf16[256,1024]{1,0:T(8,128)(2,1)} %get-tuple-element.69), channel_id=1, source_target_pairs={{0,1},{1,0},{2,3},{3,2},{4,5},{5,4},{6,7},{7,6},{8,9},{9,8},{10,11... | collective-permute-start | bytes 1572872 | tf_op jit(solution)/shard_map/ppermute | solution.py:133
  237.0 32.7 %collective-permute-start.7 = (bf16[256,1024]{1,0:T(8,128)(2,1)}, bf16[256,1024]{1,0:T(8,128)(2,1)}, u32[]{:S(2)}, u32[]{:S(2)}) collective-permute-start(bf16[256,1024]{1,0:T(8,128)(2,1)} %get-tuple-element.73), channel_id=1, source_target_pairs={{0,1},{1,0},{2,3},{3,2},{4,5},{5,4},{6,7},{7,6},{8,9},{9,8},{10,11... | collective-permute-start | bytes 1572872 | tf_op jit(solution)/shard_map/ppermute | solution.py:133
  239.0 41.4 %collective-permute-start.8 = (bf16[256,1024]{1,0:T(8,128)(2,1)}, bf16[256,1024]{1,0:T(8,128)(2,1)}, u32[]{:S(2)}, u32[]{:S(2)}) collective-permute-start(bf16[256,1024]{1,0:T(8,128)(2,1)} %get-tuple-element.67), channel_id=1, source_target_pairs={{0,1},{1,0},{2,3},{3,2},{4,5},{5,4},{6,7},{7,6},{8,9},{9,8},{10,11... | collective-permute-start | bytes 1572872 | tf_op jit(solution)/shard_map/ppermute | solution.py:133
  318.1 20.2 %all-to-all-start.5 = ((bf16[2,16,2,32,128]{4,3,2,0,1:T(8,128)(2,1)}), bf16[2,16,2,32,128]{4,3,2,0,1:T(8,128)(2,1)S(1)}, u32[]{:S(2)}, u32[]{:S(2)}) async-start(bf16[2,16,2,32,128]{4,3,2,0,1:T(8,128)(2,1)} %copy.138), calls=%async_computation.5 | async-start | bytes 1048576 | tf_op jit(solution)/shard_map/all_to_all | solution.py:291
  325.4 13.1 %copy-start.17 = (f32[512,256]{1,0:T(8,128)S(1)}, f32[512,256]{1,0:T(8,128)}, u32[]{:S(2)}) copy-start(f32[512,256]{1,0:T(8,128)} %get-tuple-element.31) | copy-start | bytes 1572868
  340.5 9.3 %collective-permute-start.10 = (bf16[256,512]{1,0:T(8,128)(2,1)S(1)}, bf16[256,512]{1,0:T(8,128)(2,1)}, u32[]{:S(2)}, u32[]{:S(2)}) collective-permute-start(bf16[256,512]{1,0:T(8,128)(2,1)S(1)} %get-tuple-element.77), channel_id=1, source_target_pairs={{0,1},{1,0},{2,3},{3,2},{4,5},{5,4},{6,7},{7,6},{8,9},{9,8},{10,11... | collective-permute-start | bytes 786440 | tf_op jit(solution)/shard_map/ppermute | solution.py:133
  342.1 12.3 %collective-permute-start.11 = (bf16[256,512]{1,0:T(8,128)(2,1)S(1)}, bf16[256,512]{1,0:T(8,128)(2,1)S(1)}, u32[]{:S(2)}, u32[]{:S(2)}) collective-permute-start(bf16[256,512]{1,0:T(8,128)(2,1)S(1)} %get-tuple-element.75), channel_id=1, source_target_pairs={{0,1},{1,0},{2,3},{3,2},{4,5},{5,4},{6,7},{7,6},{8,9},{9,8},{10,11... | collective-permute-start | bytes 786440 | tf_op jit(solution)/shard_map/ppermute | solution.py:133
  (14 other events, 33.8 us)

commit v11 on v9

--- a/solution.py
+++ b/solution.py
@@ -162,10 +162,16 @@
 
 
 def tp_send(stack, me, size):
-    pieces = [stack[0]] + [shift(stack[step], "tp", step, size) for step in range(1, size)]
-    order = (me - jnp.arange(size, dtype=jnp.int32)) % size
-    arranged = jnp.take(jnp.stack(pieces), order, axis=0)
-    return arranged.transpose(1, 0, 2).reshape(stack.shape[1], size * stack.shape[2])
+    return [stack[0]] + [shift(stack[step], "tp", step, size) for step in range(1, size)]
+
+
+def tp_columns(chunk_pieces, me, size):
+    parts = []
+    for source in range(size):
+        step = (me - source) % size
+        for pieces in chunk_pieces:
+            parts.append(lax.dynamic_index_in_dim(jnp.stack(pieces), step, 0, keepdims=False))
+    return jnp.concatenate(parts, axis=1)
 
 
 def source_order(stack, me, size):
@@ -263,14 +269,10 @@
     def rows_by_destination(total):
         stack = total.astype(jnp.bfloat16).reshape(tp_size, rows_in, k_cols)
         order = (me + jnp.arange(tp_size, dtype=jnp.int32)) % tp_size
-        return tp_send(jnp.take(stack, order, axis=0), me, tp_size)
-
-    def interleave(parts, width):
-        stacked = jnp.stack([p.reshape(rows_in, tp_size, width) for p in parts], axis=2)
-        return stacked.reshape(rows_in, tp_size * len(parts) * width)
-
-    attended = interleave([r[0] for r in results], q_width)
-    grad_queries = interleave([r[1] for r in results], q_width)
+        return tp_columns([tp_send(jnp.take(stack, order, axis=0), me, tp_size)], me, tp_size)
+
+    attended = tp_columns([r[0] for r in results], me, tp_size)
+    grad_queries = tp_columns([r[1] for r in results], me, tp_size)
     total_keys = jnp.concatenate([r[2] for r in results], axis=1)
     total_values = jnp.concatenate([r[3] for r in results], axis=1)
     return (attended, grad_queries, rows_by_destination(total_keys), rows_by_destination(total_values))

time: 325 us -> 319 us (0.982)
  local copies, waits for them, and re-layouts: 59.3 us -> 35.6 us
  waiting for transfers between devices: 83.3 us -> 98 us
  other arithmetic: 24.2 us -> 27.8 us
    squeeze x0 -> x6, other arithmetic: none -> 9.05 us  [tp_columns(): lax.dynamic_index_in_dim(jnp.stack(pieces), step, 0, keepdims=False)]
    another operation x13 -> x4, other arithmetic: 9.2 us -> 0.23 us  [the longest x6 5.61 us: tp_send(): arranged = jnp.take(jnp.stack(pieces), order, axis=0)]
    unnamed x57 -> x59, local copies, waits for them, and re-layouts: 10.6 us -> 2.23 us
    all_to_all x2, waiting for transfers between devices: 3.43 us -> 11.7 us  [body(): back = lax.all_to_all(owner, 'ctx', split_axis=1, concat_axis=3, tiled=True)]
    gather x8 -> x2, local copies, waits for them, and re-layouts: 8.72 us -> 1.16 us  [rows_by_destination(): jnp.take(stack, order, axis=0)]
    ppermute x12, waiting for transfers between devices: 59.9 us -> 66.5 us  [shift(): lax.ppermute(x, axis, perm=[(s, (s + step) % size) for s in range(size)])]
    slice x6 -> x0, local copies, waits for them, and re-layouts: 5.53 us -> none  [tp_send(): stack[0]]
    another operation x2 -> x0, local copies, waits for them, and re-layouts: 5.14 us -> none  [interleave(): jnp.stack([p.reshape(rows_in, tp_size, width) for p in parts], axis=2)]
  transfers between devices with their start and end apart: 19 -> 19, of which waited for: 12 -> 12; matrix products, arithmetic and copies ran while one was open for 22% -> 17% of each run, Pallas kernels for 28% -> 29%
where the time goes in v11:
time: 319 us; the launch traced here: 318 us
  waiting for transfers between devices  98 us (31%)
  Pallas kernels  91.2 us (29%)
  starting transfers between devices  63.2 us (20%)
  local copies, waits for them, and re-layouts  35.6 us (11%)
  other arithmetic  27.8 us (9%)
    pallas_call x2, Pallas kernels, attention(): pl.pallas_call(kernel, grid_spec=pltpu.PrefetchScalarGridSpec(num_scalar_...  91.2 us
    ppermute x12, waiting for transfers between devices, shift(): lax.ppermute(x, axis, perm=[(s, (s + step) % size) for s in range(size)])  66.5 us
    all_to_all x2, waiting for transfers between devices, body(): lax.all_to_all(send_back, 'ctx', split_axis=3, concat_axis=1, tiled=True)  18.1 us
    all_to_all x2, starting transfers between devices, body(): got = lax.all_to_all(send, 'ctx', split_axis=0, concat_axis=4, tiled=True)  15 us
    ppermute x12, starting transfers between devices, shift(): lax.ppermute(x, axis, perm=[(s, (s + step) % size) for s in range(size)])  15 us
    all_to_all x2, starting transfers between devices, body(): back = lax.all_to_all(owner, 'ctx', split_axis=1, concat_axis=3, tiled=True)  14.9 us
    all_to_all x2, starting transfers between devices, body(): lax.all_to_all(send_back, 'ctx', split_axis=3, concat_axis=1, tiled=True)  12 us
    all_to_all x2, waiting for transfers between devices, body(): back = lax.all_to_all(owner, 'ctx', split_axis=1, concat_axis=3, tiled=True)  11.7 us
  transfers between devices with their start and end apart: 19, of which 12 were waited for; matrix products, arithmetic and copies ran while one was open for 17% of the time, Pallas kernels for 29%

profile of v11, /device:TPU:0, one launch (start us, length us, event | category | flops | bytes accessed | tf_op | source)
XLA Modules:
  0.0 317.8 jit_solution(15085937212071265785)
XLA Ops:
  1.7 3.0 collective-permute-start.3
  6.0 5.9 %collective-permute-done.3 = bf16[256,512]{1,0:T(8,128)(2,1)S(1)} collective-permute-done((bf16[256,512]{1,0:T(8,128)(2,1)S(1)}, bf16[256,512]{1,0:T(8,128)(2,1)S(1)}, u32[]{:S(2)}, u32[]{:S(2)}) %collective-permute-start.3) | collective-permute-done | bytes 262176 | tf_op jit(solution)/shard_map/ppermute | solution.py:133
  12.5 4.1 %collective-permute-done.2 = bf16[256,512]{1,0:T(8,128)(2,1)S(1)} collective-permute-done((bf16[256,512]{1,0:T(8,128)(2,1)S(1)}, bf16[256,512]{1,0:T(8,128)(2,1)S(1)}, u32[]{:S(2)}, u32[]{:S(2)}) %collective-permute-start.2) | collective-permute-done | bytes 262176 | tf_op jit(solution)/shard_map/ppermute | solution.py:133
  19.5 6.3 %all-to-all-start = ((bf16[16,2,32,4,128]{4,2,3,1,0:T(8,128)(2,1)}), bf16[16,2,32,4,128]{4,2,3,1,0:T(8,128)(2,1)S(1)}, u32[]{:S(2)}, u32[]{:S(2)}) async-start(bf16[16,2,32,4,128]{4,2,3,1,0:T(8,128)(2,1)} %pad_maximum_fusion.4), calls=%async_computation | async-start | bytes 2097152 | tf_op jit(solution)/shard_map/all_to_all | solution.py:212
  31.2 10.9 %collective-permute-done.4 = bf16[256,1024]{1,0:T(8,128)(2,1)S(1)} collective-permute-done((bf16[256,1024]{1,0:T(8,128)(2,1)}, bf16[256,1024]{1,0:T(8,128)(2,1)S(1)}, u32[]{:S(2)}, u32[]{:S(2)}) %collective-permute-start.4) | collective-permute-done | bytes 524320 | tf_op jit(solution)/shard_map/ppermute | solution.py:133
  43.3 9.6 %collective-permute-done.5 = bf16[256,1024]{1,0:T(8,128)(2,1)S(1)} collective-permute-done((bf16[256,1024]{1,0:T(8,128)(2,1)}, bf16[256,1024]{1,0:T(8,128)(2,1)S(1)}, u32[]{:S(2)}, u32[]{:S(2)}) %collective-permute-start.5) | collective-permute-done | bytes 524320 | tf_op jit(solution)/shard_map/ppermute | solution.py:133
  56.3 5.9 %all-to-all-start.1 = ((bf16[16,2,3,2,32,128]{5,4,3,2,1,0:T(8,128)(2,1)}), bf16[16,2,3,2,32,128]{5,4,3,2,1,0:T(8,128)(2,1)S(1)}, u32[]{:S(2)}, u32[]{:S(2)}) async-start(bf16[16,2,3,2,32,128]{5,4,3,2,1,0:T(8,128)(2,1)} %bitcast.175), calls=%async_computation.1 | async-start | bytes 3145728 | tf_op jit(solution)/shard_map/all_to_all | solution.py:238
  64.5 12.8 %collective-permute-done = bf16[256,1024]{1,0:T(8,128)(2,1)} collective-permute-done((bf16[256,1024]{1,0:T(8,128)(2,1)}, bf16[256,1024]{1,0:T(8,128)(2,1)}, u32[]{:S(2)}, u32[]{:S(2)}) %collective-permute-start) | collective-permute-done | bytes 524320 | tf_op jit(solution)/shard_map/ppermute | solution.py:133
  79.4 8.6 %collective-permute-done.1 = bf16[256,1024]{1,0:T(8,128)(2,1)} collective-permute-done((bf16[256,1024]{1,0:T(8,128)(2,1)}, bf16[256,1024]{1,0:T(8,128)(2,1)}, u32[]{:S(2)}, u32[]{:S(2)}) %collective-permute-start.1) | collective-permute-done | bytes 524320 | tf_op jit(solution)/shard_map/ppermute | solution.py:133
  94.2 9.2 %all-to-all-start.2 = ((bf16[16,2,3,2,32,128]{5,4,3,2,1,0:T(8,128)(2,1)}), bf16[16,2,3,2,32,128]{5,4,3,2,1,0:T(8,128)(2,1)}, u32[]{:S(2)}, u32[]{:S(2)}) async-start(bf16[16,2,3,2,32,128]{5,4,3,2,1,0:T(8,128)(2,1)} %bitcast.174), calls=%async_computation.2 | async-start | bytes 3145728 | tf_op jit(solution)/shard_map/all_to_all | solution.py:238
  105.8 45.5 %shard_map.93 = (bf16[2,256,1024]{2,1,0:T(8,128)(2,1)}, bf16[2,256,1024]{2,1,0:T(8,128)(2,1)}, f32[2,3,2,512,128]{4,3,2,1,0:T(8,128)}, f32[512,256]{1,0:T(8,128)}, f32[512,256]{1,0:T(8,128)}) custom-call(s32[8]{0:T(128)} %reshape.114.live_ref, s32[1]{0:T(128)} %bitcast.2.tp_ref, bf16[2,256,1024]{2,1,0:T(8,128)(2,1)} %pad_maximum_fusion.2.q_ref, ...), custom_call_target="tpu_custom_call" | custom-call | flops 12884901888 | bytes 10485760 | tf_op jit(solution)/shard_map/pallas_call | solution.py:105
  155.1 6.0 %all-to-all-start.3 = ((bf16[2,3,2,16,32,128]{5,4,2,1,0,3:T(8,128)(2,1)}), bf16[2,3,2,16,32,128]{5,4,2,1,0,3:T(8,128)(2,1)S(1)}, u32[]{:S(2)}, u32[]{:S(2)}) async-start(bf16[2,3,2,16,32,128]{5,4,2,1,0,3:T(8,128)(2,1)} %copy.93), calls=%async_computation.3 | async-start | bytes 3145728 | tf_op jit(solution)/shard_map/all_to_all | solution.py:251
  161.7 2.9 copy.91
  164.6 45.7 %shard_map.94 = (bf16[2,256,1024]{2,1,0:T(8,128)(2,1)}, bf16[2,256,1024]{2,1,0:T(8,128)(2,1)}, f32[2,3,2,512,128]{4,3,2,1,0:T(8,128)}, f32[512,256]{1,0:T(8,128)}, f32[512,256]{1,0:T(8,128)}) custom-call(s32[8]{0:T(128)} %reshape.118.live_ref, s32[1]{0:T(128)} %bitcast.2.tp_ref, bf16[2,256,1024]{2,1,0:T(8,128)(2,1)} %pad_maximum_fusion.5.q_ref, ...), custom_call_target="tpu_custom_call" | custom-call | flops 12884901888 | bytes 10485760 | tf_op jit(solution)/shard_map/pallas_call | solution.py:105
  214.1 6.0 %all-to-all-start.5 = ((bf16[2,3,2,16,32,128]{5,4,2,1,0,3:T(8,128)(2,1)}), bf16[2,3,2,16,32,128]{5,4,2,1,0,3:T(8,128)(2,1)S(1)}, u32[]{:S(2)}, u32[]{:S(2)}) async-start(bf16[2,3,2,16,32,128]{5,4,2,1,0,3:T(8,128)(2,1)} %copy.99), calls=%async_computation.5 | async-start | bytes 3145728 | tf_op jit(solution)/shard_map/all_to_all | solution.py:251
  230.1 2.5 reshape.120
  234.0 18.1 %all-to-all-done.5 = bf16[2,3,2,16,32,128]{5,4,2,1,0,3:T(8,128)(2,1)S(1)} async-done(((bf16[2,3,2,16,32,128]{5,4,2,1,0,3:T(8,128)(2,1)}), bf16[2,3,2,16,32,128]{5,4,2,1,0,3:T(8,128)(2,1)S(1)}, u32[]{:S(2)}, u32[]{:S(2)}) %all-to-all-start.5) | async-done | bytes 1572896 | tf_op jit(solution)/shard_map/all_to_all | solution.py:251
  252.1 9.2 %all-to-all-start.4 = ((bf16[2,16,2,32,128]{4,3,2,0,1:T(8,128)(2,1)}), bf16[2,16,2,32,128]{4,3,2,0,1:T(8,128)(2,1)}, u32[]{:S(2)}, u32[]{:S(2)}) async-start(bf16[2,16,2,32,128]{4,3,2,0,1:T(8,128)(2,1)} %copy.95), calls=%async_computation.4 | async-start | bytes 1048576 | tf_op jit(solution)/shard_map/all_to_all | solution.py:261
  263.0 2.5 fusion.7
  270.3 5.3 %collective-permute-done.7 = bf16[256,1024]{1,0:T(8,128)(2,1)S(1)} collective-permute-done((bf16[256,1024]{1,0:T(8,128)(2,1)S(1)}, bf16[256,1024]{1,0:T(8,128)(2,1)S(1)}, u32[]{:S(2)}, u32[]{:S(2)}) %collective-permute-start.7) | collective-permute-done | bytes 524320 | tf_op jit(solution)/shard_map/ppermute | solution.py:133
  279.4 5.8 %all-to-all-start.6 = ((bf16[2,16,2,32,128]{4,3,2,0,1:T(8,128)(2,1)}), bf16[2,16,2,32,128]{4,3,2,0,1:T(8,128)(2,1)S(1)}, u32[]{:S(2)}, u32[]{:S(2)}) async-start(bf16[2,16,2,32,128]{4,3,2,0,1:T(8,128)(2,1)} %copy.101), calls=%async_computation.6 | async-start | bytes 1048576 | tf_op jit(solution)/shard_map/all_to_all | solution.py:261
  287.9 11.7 %all-to-all-done.6 = bf16[2,16,2,32,128]{4,3,2,0,1:T(8,128)(2,1)S(1)} async-done(((bf16[2,16,2,32,128]{4,3,2,0,1:T(8,128)(2,1)}), bf16[2,16,2,32,128]{4,3,2,0,1:T(8,128)(2,1)S(1)}, u32[]{:S(2)}, u32[]{:S(2)}) %all-to-all-start.6) | async-done | bytes 524320 | tf_op jit(solution)/shard_map/all_to_all | solution.py:261
  306.5 5.5 %collective-permute-done.11 = bf16[256,512]{1,0:T(8,128)(2,1)S(1)} collective-permute-done((bf16[256,512]{1,0:T(8,128)(2,1)S(1)}, bf16[256,512]{1,0:T(8,128)(2,1)S(1)}, u32[]{:S(2)}, u32[]{:S(2)}) %collective-permute-start.11) | collective-permute-done | bytes 262176 | tf_op jit(solution)/shard_map/ppermute | solution.py:133
  313.1 3.6 %collective-permute-done.10 = bf16[256,512]{1,0:T(8,128)(2,1)S(1)} collective-permute-done((bf16[256,512]{1,0:T(8,128)(2,1)S(1)}, bf16[256,512]{1,0:T(8,128)(2,1)S(1)}, u32[]{:S(2)}, u32[]{:S(2)}) %collective-permute-start.10) | collective-permute-done | bytes 262176 | tf_op jit(solution)/shard_map/ppermute | solution.py:133
  (158 shorter events, 69.9 us)
Async XLA Ops:
  1.7 10.2 %collective-permute-start.3 = (bf16[256,512]{1,0:T(8,128)(2,1)S(1)}, bf16[256,512]{1,0:T(8,128)(2,1)S(1)}, u32[]{:S(2)}, u32[]{:S(2)}) collective-permute-start(bf16[256,512]{1,0:T(8,128)(2,1)S(1)} %get-tuple-element.72), channel_id=1, source_target_pairs={{0,1},{1,0},{2,3},{3,2},{4,5},{5,4},{6,7},{7,6},{8,9},{9,8},{10,11... | collective-permute-start | bytes 786440 | tf_op jit(solution)/shard_map/ppermute | solution.py:133
  5.8 10.9 %collective-permute-start.2 = (bf16[256,512]{1,0:T(8,128)(2,1)S(1)}, bf16[256,512]{1,0:T(8,128)(2,1)S(1)}, u32[]{:S(2)}, u32[]{:S(2)}) collective-permute-start(bf16[256,512]{1,0:T(8,128)(2,1)S(1)} %get-tuple-element.70), channel_id=1, source_target_pairs={{0,1},{1,0},{2,3},{3,2},{4,5},{5,4},{6,7},{7,6},{8,9},{9,8},{10,11... | collective-permute-start | bytes 786440 | tf_op jit(solution)/shard_map/ppermute | solution.py:133
  19.5 34.4 %all-to-all-start = ((bf16[16,2,32,4,128]{4,2,3,1,0:T(8,128)(2,1)}), bf16[16,2,32,4,128]{4,2,3,1,0:T(8,128)(2,1)S(1)}, u32[]{:S(2)}, u32[]{:S(2)}) async-start(bf16[16,2,32,4,128]{4,2,3,1,0:T(8,128)(2,1)} %pad_maximum_fusion.4), calls=%async_computation | async-start | bytes 2097152 | tf_op jit(solution)/shard_map/all_to_all | solution.py:212
  27.2 15.0 %copy-start.17 = (bf16[1,256,1024]{2,1,0:T(8,128)(2,1)S(1)}, bf16[1,256,1024]{2,1,0:T(8,128)(2,1)}, u32[]{:S(2)}) copy-start(bf16[1,256,1024]{2,1,0:T(8,128)(2,1)} %get-tuple-element.40) | copy-start | bytes 1572868
  27.2 15.0 %collective-permute-start.4 = (bf16[256,1024]{1,0:T(8,128)(2,1)}, bf16[256,1024]{1,0:T(8,128)(2,1)S(1)}, u32[]{:S(2)}, u32[]{:S(2)}) collective-permute-start(bf16[256,1024]{1,0:T(8,128)(2,1)} %get-tuple-element.39), channel_id=1, source_target_pairs={{0,1},{1,0},{2,3},{3,2},{4,5},{5,4},{6,7},{7,6},{8,9},{9,8},{10,11... | collective-permute-start | bytes 1572872 | tf_op jit(solution)/shard_map/ppermute | solution.py:133
  30.0 22.9 %collective-permute-start.5 = (bf16[256,1024]{1,0:T(8,128)(2,1)}, bf16[256,1024]{1,0:T(8,128)(2,1)S(1)}, u32[]{:S(2)}, u32[]{:S(2)}) collective-permute-start(bf16[256,1024]{1,0:T(8,128)(2,1)} %get-tuple-element.35), channel_id=1, source_target_pairs={{0,1},{1,0},{2,3},{3,2},{4,5},{5,4},{6,7},{7,6},{8,9},{9,8},{10,11... | collective-permute-start | bytes 1572872 | tf_op jit(solution)/shard_map/ppermute | solution.py:133
  56.3 21.0 %copy-start.11 = (bf16[1,256,1024]{2,1,0:T(8,128)(2,1)S(1)}, bf16[1,256,1024]{2,1,0:T(8,128)(2,1)}, u32[]{:S(2)}) copy-start(bf16[1,256,1024]{2,1,0:T(8,128)(2,1)} %get-tuple-element.37) | copy-start | bytes 1572868
  56.3 37.9 %all-to-all-start.1 = ((bf16[16,2,3,2,32,128]{5,4,3,2,1,0:T(8,128)(2,1)}), bf16[16,2,3,2,32,128]{5,4,3,2,1,0:T(8,128)(2,1)S(1)}, u32[]{:S(2)}, u32[]{:S(2)}) async-start(bf16[16,2,3,2,32,128]{5,4,3,2,1,0:T(8,128)(2,1)} %bitcast.175), calls=%async_computation.1 | async-start | bytes 3145728 | tf_op jit(solution)/shard_map/all_to_all | solution.py:238
  62.2 15.1 %collective-permute-start = (bf16[256,1024]{1,0:T(8,128)(2,1)}, bf16[256,1024]{1,0:T(8,128)(2,1)}, u32[]{:S(2)}, u32[]{:S(2)}) collective-permute-start(bf16[256,1024]{1,0:T(8,128)(2,1)} %get-tuple-element.38), channel_id=1, source_target_pairs={{0,1},{1,0},{2,3},{3,2},{4,5},{5,4},{6,7},{7,6},{8,9},{9,8},{10,11... | collective-permute-start | bytes 1572872 | tf_op jit(solution)/shard_map/ppermute | solution.py:133
  63.8 24.2 %collective-permute-start.1 = (bf16[256,1024]{1,0:T(8,128)(2,1)}, bf16[256,1024]{1,0:T(8,128)(2,1)}, u32[]{:S(2)}, u32[]{:S(2)}) collective-permute-start(bf16[256,1024]{1,0:T(8,128)(2,1)} %get-tuple-element.34), channel_id=1, source_target_pairs={{0,1},{1,0},{2,3},{3,2},{4,5},{5,4},{6,7},{7,6},{8,9},{9,8},{10,11... | collective-permute-start | bytes 1572872 | tf_op jit(solution)/shard_map/ppermute | solution.py:133
  64.5 23.5 %copy-start.12 = (bf16[1,256,1024]{2,1,0:T(8,128)(2,1)S(1)}, bf16[1,256,1024]{2,1,0:T(8,128)(2,1)}, u32[]{:S(2)}) copy-start(bf16[1,256,1024]{2,1,0:T(8,128)(2,1)} %get-tuple-element.33) | copy-start | bytes 1572868
  94.2 61.0 %all-to-all-start.2 = ((bf16[16,2,3,2,32,128]{5,4,3,2,1,0:T(8,128)(2,1)}), bf16[16,2,3,2,32,128]{5,4,3,2,1,0:T(8,128)(2,1)}, u32[]{:S(2)}, u32[]{:S(2)}) async-start(bf16[16,2,3,2,32,128]{5,4,3,2,1,0:T(8,128)(2,1)} %bitcast.174), calls=%async_computation.2 | async-start | bytes 3145728 | tf_op jit(solution)/shard_map/all_to_all | solution.py:238
  155.1 59.0 %all-to-all-start.3 = ((bf16[2,3,2,16,32,128]{5,4,2,1,0,3:T(8,128)(2,1)}), bf16[2,3,2,16,32,128]{5,4,2,1,0,3:T(8,128)(2,1)S(1)}, u32[]{:S(2)}, u32[]{:S(2)}) async-start(bf16[2,3,2,16,32,128]{5,4,2,1,0,3:T(8,128)(2,1)} %copy.93), calls=%async_computation.3 | async-start | bytes 3145728 | tf_op jit(solution)/shard_map/all_to_all | solution.py:251
  214.1 38.0 %all-to-all-start.5 = ((bf16[2,3,2,16,32,128]{5,4,2,1,0,3:T(8,128)(2,1)}), bf16[2,3,2,16,32,128]{5,4,2,1,0,3:T(8,128)(2,1)S(1)}, u32[]{:S(2)}, u32[]{:S(2)}) async-start(bf16[2,3,2,16,32,128]{5,4,2,1,0,3:T(8,128)(2,1)} %copy.99), calls=%async_computation.5 | async-start | bytes 3145728 | tf_op jit(solution)/shard_map/all_to_all | solution.py:251
  222.9 40.0 %collective-permute-start.8 = (bf16[256,1024]{1,0:T(8,128)(2,1)}, bf16[256,1024]{1,0:T(8,128)(2,1)}, u32[]{:S(2)}, u32[]{:S(2)}) collective-permute-start(bf16[256,1024]{1,0:T(8,128)(2,1)} %get-tuple-element.49), channel_id=1, source_target_pairs={{0,1},{1,0},{2,3},{3,2},{4,5},{5,4},{6,7},{7,6},{8,9},{9,8},{10,11... | collective-permute-start | bytes 1572872 | tf_op jit(solution)/shard_map/ppermute | solution.py:133
  225.5 39.9 %collective-permute-start.9 = (bf16[256,1024]{1,0:T(8,128)(2,1)}, bf16[256,1024]{1,0:T(8,128)(2,1)}, u32[]{:S(2)}, u32[]{:S(2)}) collective-permute-start(bf16[256,1024]{1,0:T(8,128)(2,1)} %get-tuple-element.51), channel_id=1, source_target_pairs={{0,1},{1,0},{2,3},{3,2},{4,5},{5,4},{6,7},{7,6},{8,9},{9,8},{10,11... | collective-permute-start | bytes 1572872 | tf_op jit(solution)/shard_map/ppermute | solution.py:133
  227.1 40.8 %collective-permute-start.6 = (bf16[256,1024]{1,0:T(8,128)(2,1)}, bf16[256,1024]{1,0:T(8,128)(2,1)}, u32[]{:S(2)}, u32[]{:S(2)}) collective-permute-start(bf16[256,1024]{1,0:T(8,128)(2,1)} %get-tuple-element.57), channel_id=1, source_target_pairs={{0,1},{1,0},{2,3},{3,2},{4,5},{5,4},{6,7},{7,6},{8,9},{9,8},{10,11... | collective-permute-start | bytes 1572872 | tf_op jit(solution)/shard_map/ppermute | solution.py:133
  233.0 28.3 %copy-start.19 = (bf16[2,256,1024]{2,1,0:T(8,128)(2,1)S(1)}, bf16[2,256,1024]{2,1,0:T(8,128)(2,1)}, u32[]{:S(2)}) copy-start(bf16[2,256,1024]{2,1,0:T(8,128)(2,1)} %get-tuple-element.24) | copy-start | bytes 3145732
  233.1 29.8 %copy-start.6 = (bf16[1,256,1024]{2,1,0:T(8,128)(2,1)S(1)}, bf16[1,256,1024]{2,1,0:T(8,128)(2,1)}, u32[]{:S(2)}) copy-start(bf16[1,256,1024]{2,1,0:T(8,128)(2,1)} %get-tuple-element.50) | copy-start | bytes 1572868
  252.1 27.3 %all-to-all-start.4 = ((bf16[2,16,2,32,128]{4,3,2,0,1:T(8,128)(2,1)}), bf16[2,16,2,32,128]{4,3,2,0,1:T(8,128)(2,1)}, u32[]{:S(2)}, u32[]{:S(2)}) async-start(bf16[2,16,2,32,128]{4,3,2,0,1:T(8,128)(2,1)} %copy.95), calls=%async_computation.4 | async-start | bytes 1048576 | tf_op jit(solution)/shard_map/all_to_all | solution.py:261
  261.4 14.2 %collective-permute-start.7 = (bf16[256,1024]{1,0:T(8,128)(2,1)S(1)}, bf16[256,1024]{1,0:T(8,128)(2,1)S(1)}, u32[]{:S(2)}, u32[]{:S(2)}) collective-permute-start(bf16[256,1024]{1,0:T(8,128)(2,1)S(1)} %get-tuple-element.59), channel_id=1, source_target_pairs={{0,1},{1,0},{2,3},{3,2},{4,5},{5,4},{6,7},{7,6},{8,9},{9,8},{10,11... | collective-permute-start | bytes 1572872 | tf_op jit(solution)/shard_map/ppermute | solution.py:133
  279.4 20.2 %all-to-all-start.6 = ((bf16[2,16,2,32,128]{4,3,2,0,1:T(8,128)(2,1)}), bf16[2,16,2,32,128]{4,3,2,0,1:T(8,128)(2,1)S(1)}, u32[]{:S(2)}, u32[]{:S(2)}) async-start(bf16[2,16,2,32,128]{4,3,2,0,1:T(8,128)(2,1)} %copy.101), calls=%async_computation.6 | async-start | bytes 1048576 | tf_op jit(solution)/shard_map/all_to_all | solution.py:261
  302.8 9.2 %collective-permute-start.11 = (bf16[256,512]{1,0:T(8,128)(2,1)S(1)}, bf16[256,512]{1,0:T(8,128)(2,1)S(1)}, u32[]{:S(2)}, u32[]{:S(2)}) collective-permute-start(bf16[256,512]{1,0:T(8,128)(2,1)S(1)} %get-tuple-element.63), channel_id=1, source_target_pairs={{0,1},{1,0},{2,3},{3,2},{4,5},{5,4},{6,7},{7,6},{8,9},{9,8},{10,11... | collective-permute-start | bytes 786440 | tf_op jit(solution)/shard_map/ppermute | solution.py:133
  304.4 12.3 %collective-permute-start.10 = (bf16[256,512]{1,0:T(8,128)(2,1)S(1)}, bf16[256,512]{1,0:T(8,128)(2,1)S(1)}, u32[]{:S(2)}, u32[]{:S(2)}) collective-permute-start(bf16[256,512]{1,0:T(8,128)(2,1)S(1)} %get-tuple-element.67), channel_id=1, source_target_pairs={{0,1},{1,0},{2,3},{3,2},{4,5},{5,4},{6,7},{7,6},{8,9},{9,8},{10,11... | collective-permute-start | bytes 786440 | tf_op jit(solution)/shard_map/ppermute | solution.py:133
  (22 other events, 96.8 us)

commit v12 on v11

--- a/solution.py
+++ b/solution.py
@@ -15,7 +15,7 @@
 
 def attention_kernel(
     live_ref, tp_ref, q_ref, do_ref, kvs_ref, ko_ref, vo_ref,
-    o_ref, dq_ref, dsel_ref, dko_ref, dvo_ref, acc_ref, *, slot_count, row_tile, scale
+    o_ref, dq_ref, dsel_ref, dko_ref, dvo_ref, acc_ref, *, slot_count, row_tile, scale, tiles, own_rows
 ):
     g = pl.program_id(0)
     h = pl.program_id(1)
@@ -25,49 +25,55 @@
     def _():
         acc_ref[...] = jnp.zeros(acc_ref.shape, acc_ref.dtype)
 
-    q = q_ref[...]
-    do = do_ref[...]
-    keys = [kvs_ref[r, 0] for r in range(slot_count - 1)] + [ko_ref[...]]
-    values = [kvs_ref[r, 1] for r in range(slot_count - 1)] + [vo_ref[...]]
-    trans_b = (((1,), (1,)), ((), ()))
-    q_t = q.T
-    do_t = do.T
-    scores = []
-    for r in range(slot_count):
-        s = lax.dot_general(q, keys[r], trans_b, preferred_element_type=jnp.float32) * scale
-        live = live_ref[g * slot_count + r] > 0
-        if r == slot_count - 1:
-            row = t * row_tile + lax.broadcasted_iota(jnp.int32, s.shape, 0)
-            col = lax.broadcasted_iota(jnp.int32, s.shape, 1)
-            s = jnp.where(live & (row >= col), s, -jnp.inf)
-        else:
-            s = jnp.where(live, s, -jnp.inf)
-        scores.append(s)
-    row_max = scores[0].max(axis=1, keepdims=True)
-    for s in scores[1:]:
-        row_max = jnp.maximum(row_max, s.max(axis=1, keepdims=True))
-    weights = [jnp.exp(s - row_max) for s in scores]
-    total = weights[0].sum(axis=1, keepdims=True)
-    for w in weights[1:]:
-        total = total + w.sum(axis=1, keepdims=True)
-    inverse = 1.0 / total
-    probs = [w * inverse for w in weights]
-    probs_low = [p.astype(jnp.bfloat16) for p in probs]
-    out = jnp.dot(probs_low[0], values[0], preferred_element_type=jnp.float32)
-    for r in range(1, slot_count):
-        out = out + jnp.dot(probs_low[r], values[r], preferred_element_type=jnp.float32)
-    out_low = out.astype(jnp.bfloat16)
-    o_ref[...] = out_low
-    delta = jnp.sum(do.astype(jnp.float32) * out_low.astype(jnp.float32), axis=1, keepdims=True)
-    grad_q = None
-    for r in range(slot_count):
-        grad_p = lax.dot_general(do, values[r], trans_b, preferred_element_type=jnp.float32)
-        grad_s = (probs[r] * (grad_p - delta)).astype(jnp.bfloat16)
-        part = jnp.dot(grad_s, keys[r], preferred_element_type=jnp.float32)
-        grad_q = part if grad_q is None else grad_q + part
-        acc_ref[r, 0] += jnp.dot(q_t, grad_s, preferred_element_type=jnp.float32) * scale
-        acc_ref[r, 1] += jnp.dot(do_t, probs_low[r], preferred_element_type=jnp.float32)
-    dq_ref[...] = (grad_q * scale).astype(jnp.bfloat16)
+    def run(own_width):
+        q = q_ref[...]
+        do = do_ref[...]
+        keys = [kvs_ref[r, 0] for r in range(slot_count - 1)] + [ko_ref[:own_width]]
+        values = [kvs_ref[r, 1] for r in range(slot_count - 1)] + [vo_ref[:own_width]]
+        trans_b = (((1,), (1,)), ((), ()))
+        q_t = q.T
+        do_t = do.T
+        scores = []
+        for r in range(slot_count):
+            s = lax.dot_general(q, keys[r], trans_b, preferred_element_type=jnp.float32) * scale
+            live = live_ref[g * slot_count + r] > 0
+            if r == slot_count - 1:
+                row = t * row_tile + lax.broadcasted_iota(jnp.int32, s.shape, 0)
+                col = lax.broadcasted_iota(jnp.int32, s.shape, 1)
+                s = jnp.where(live & (row >= col), s, -jnp.inf)
+            else:
+                s = jnp.where(live, s, -jnp.inf)
+            scores.append(s)
+        row_max = scores[0].max(axis=1, keepdims=True)
+        for s in scores[1:]:
+            row_max = jnp.maximum(row_max, s.max(axis=1, keepdims=True))
+        weights = [jnp.exp(s - row_max) for s in scores]
+        total = weights[0].sum(axis=1, keepdims=True)
+        for w in weights[1:]:
+            total = total + w.sum(axis=1, keepdims=True)
+        inverse = 1.0 / total
+        probs = [w * inverse for w in weights]
+        probs_low = [p.astype(jnp.bfloat16) for p in probs]
+        out = jnp.dot(probs_low[0], values[0], preferred_element_type=jnp.float32)
+        for r in range(1, slot_count):
+            out = out + jnp.dot(probs_low[r], values[r], preferred_element_type=jnp.float32)
+        out_low = out.astype(jnp.bfloat16)
+        o_ref[...] = out_low
+        delta = jnp.sum(do.astype(jnp.float32) * out_low.astype(jnp.float32), axis=1, keepdims=True)
+        grad_q = None
+        for r in range(slot_count):
+            grad_p = lax.dot_general(do, values[r], trans_b, preferred_element_type=jnp.float32)
+            grad_s = (probs[r] * (grad_p - delta)).astype(jnp.bfloat16)
+            part = jnp.dot(grad_s, keys[r], preferred_element_type=jnp.float32)
+            grad_q = part if grad_q is None else grad_q + part
+            width = keys[r].shape[0]
+            acc_ref[r, 0, :, :width] += jnp.dot(q_t, grad_s, preferred_element_type=jnp.float32) * scale
+            acc_ref[r, 1, :, :width] += jnp.dot(do_t, probs_low[r], preferred_element_type=jnp.float32)
+        dq_ref[...] = (grad_q * scale).astype(jnp.bfloat16)
+
+    for tile in range(tiles):
+        width = -(-(tile + 1) * row_tile // HD) * HD
+        pl.when(t == tile)(functools.partial(run, min(width, own_rows)))
 
     @pl.when((h == pl.num_programs(1) - 1) & (t == pl.num_programs(2) - 1))
     def _():
@@ -86,7 +92,8 @@
     slot_count = TOPK + 1
     grid = (head_count, group_size, tp_size)
     kernel = functools.partial(
-        attention_kernel, slot_count=slot_count, row_tile=row_tile, scale=1.0 / math.sqrt(HD)
+        attention_kernel, slot_count=slot_count, row_tile=row_tile, scale=1.0 / math.sqrt(HD),
+        tiles=tp_size, own_rows=BLK,
     )
 
     def piece_in(g, h, t, live, tp):

time: 319 us -> 318 us (level)
  transfers between devices with their start and end apart: 19 -> 19, of which waited for: 12 -> 12; matrix products, arithmetic and copies ran while one was open for 17% -> 17% of each run, Pallas kernels for 29% -> 28%
where the time goes in v12:
time: 318 us; the launch traced here: 317 us
  waiting for transfers between devices  98.1 us (31%)
  Pallas kernels  90.1 us (28%)
  starting transfers between devices  63.1 us (20%)
  local copies, waits for them, and re-layouts  35.6 us (11%)
  other arithmetic  27.8 us (9%)
    pallas_call x2, Pallas kernels, attention(): pl.pallas_call(kernel, grid_spec=pltpu.PrefetchScalarGridSpec(num_scalar_...  90.1 us
    ppermute x12, waiting for transfers between devices, shift(): lax.ppermute(x, axis, perm=[(s, (s + step) % size) for s in range(size)])  66.5 us
    all_to_all x2, waiting for transfers between devices, body(): lax.all_to_all(send_back, 'ctx', split_axis=3, concat_axis=1, tiled=True)  18.1 us
    all_to_all x2, starting transfers between devices, body(): got = lax.all_to_all(send, 'ctx', split_axis=0, concat_axis=4, tiled=True)  15 us
    ppermute x12, starting transfers between devices, shift(): lax.ppermute(x, axis, perm=[(s, (s + step) % size) for s in range(size)])  15 us
    all_to_all x2, starting transfers between devices, body(): back = lax.all_to_all(owner, 'ctx', split_axis=1, concat_axis=3, tiled=True)  14.9 us
    all_to_all x2, starting transfers between devices, body(): lax.all_to_all(send_back, 'ctx', split_axis=3, concat_axis=1, tiled=True)  12 us
    all_to_all x2, waiting for transfers between devices, body(): back = lax.all_to_all(owner, 'ctx', split_axis=1, concat_axis=3, tiled=True)  11.7 us
  transfers between devices with their start and end apart: 19, of which 12 were waited for; matrix products, arithmetic and copies ran while one was open for 17% of the time, Pallas kernels for 28%

profile of v12, /device:TPU:0, one launch (start us, length us, event | category | flops | bytes accessed | tf_op | source)
XLA Modules:
  0.0 316.7 jit_solution(10064180597110665468)
XLA Ops:
  1.7 3.0 collective-permute-start.3
  6.0 5.9 %collective-permute-done.3 = bf16[256,512]{1,0:T(8,128)(2,1)S(1)} collective-permute-done((bf16[256,512]{1,0:T(8,128)(2,1)S(1)}, bf16[256,512]{1,0:T(8,128)(2,1)S(1)}, u32[]{:S(2)}, u32[]{:S(2)}) %collective-permute-start.3) | collective-permute-done | bytes 262176 | tf_op jit(solution)/shard_map/ppermute | solution.py:140
  12.5 4.1 %collective-permute-done.2 = bf16[256,512]{1,0:T(8,128)(2,1)S(1)} collective-permute-done((bf16[256,512]{1,0:T(8,128)(2,1)S(1)}, bf16[256,512]{1,0:T(8,128)(2,1)S(1)}, u32[]{:S(2)}, u32[]{:S(2)}) %collective-permute-start.2) | collective-permute-done | bytes 262176 | tf_op jit(solution)/shard_map/ppermute | solution.py:140
  19.5 6.3 %all-to-all-start = ((bf16[16,2,32,4,128]{4,2,3,1,0:T(8,128)(2,1)}), bf16[16,2,32,4,128]{4,2,3,1,0:T(8,128)(2,1)S(1)}, u32[]{:S(2)}, u32[]{:S(2)}) async-start(bf16[16,2,32,4,128]{4,2,3,1,0:T(8,128)(2,1)} %pad_maximum_fusion.4), calls=%async_computation | async-start | bytes 2097152 | tf_op jit(solution)/shard_map/all_to_all | solution.py:219
  31.2 10.9 %collective-permute-done.4 = bf16[256,1024]{1,0:T(8,128)(2,1)S(1)} collective-permute-done((bf16[256,1024]{1,0:T(8,128)(2,1)}, bf16[256,1024]{1,0:T(8,128)(2,1)S(1)}, u32[]{:S(2)}, u32[]{:S(2)}) %collective-permute-start.4) | collective-permute-done | bytes 524320 | tf_op jit(solution)/shard_map/ppermute | solution.py:140
  43.3 9.6 %collective-permute-done.5 = bf16[256,1024]{1,0:T(8,128)(2,1)S(1)} collective-permute-done((bf16[256,1024]{1,0:T(8,128)(2,1)}, bf16[256,1024]{1,0:T(8,128)(2,1)S(1)}, u32[]{:S(2)}, u32[]{:S(2)}) %collective-permute-start.5) | collective-permute-done | bytes 524320 | tf_op jit(solution)/shard_map/ppermute | solution.py:140
  56.3 5.9 %all-to-all-start.1 = ((bf16[16,2,3,2,32,128]{5,4,3,2,1,0:T(8,128)(2,1)}), bf16[16,2,3,2,32,128]{5,4,3,2,1,0:T(8,128)(2,1)S(1)}, u32[]{:S(2)}, u32[]{:S(2)}) async-start(bf16[16,2,3,2,32,128]{5,4,3,2,1,0:T(8,128)(2,1)} %bitcast.175), calls=%async_computation.1 | async-start | bytes 3145728 | tf_op jit(solution)/shard_map/all_to_all | solution.py:245
  64.5 12.8 %collective-permute-done = bf16[256,1024]{1,0:T(8,128)(2,1)} collective-permute-done((bf16[256,1024]{1,0:T(8,128)(2,1)}, bf16[256,1024]{1,0:T(8,128)(2,1)}, u32[]{:S(2)}, u32[]{:S(2)}) %collective-permute-start) | collective-permute-done | bytes 524320 | tf_op jit(solution)/shard_map/ppermute | solution.py:140
  79.4 8.6 %collective-permute-done.1 = bf16[256,1024]{1,0:T(8,128)(2,1)} collective-permute-done((bf16[256,1024]{1,0:T(8,128)(2,1)}, bf16[256,1024]{1,0:T(8,128)(2,1)}, u32[]{:S(2)}, u32[]{:S(2)}) %collective-permute-start.1) | collective-permute-done | bytes 524320 | tf_op jit(solution)/shard_map/ppermute | solution.py:140
  94.2 9.2 %all-to-all-start.2 = ((bf16[16,2,3,2,32,128]{5,4,3,2,1,0:T(8,128)(2,1)}), bf16[16,2,3,2,32,128]{5,4,3,2,1,0:T(8,128)(2,1)}, u32[]{:S(2)}, u32[]{:S(2)}) async-start(bf16[16,2,3,2,32,128]{5,4,3,2,1,0:T(8,128)(2,1)} %bitcast.174), calls=%async_computation.2 | async-start | bytes 3145728 | tf_op jit(solution)/shard_map/all_to_all | solution.py:245
  105.8 45.0 %shard_map.93 = (bf16[2,256,1024]{2,1,0:T(8,128)(2,1)}, bf16[2,256,1024]{2,1,0:T(8,128)(2,1)}, f32[2,3,2,512,128]{4,3,2,1,0:T(8,128)}, f32[512,256]{1,0:T(8,128)}, f32[512,256]{1,0:T(8,128)}) custom-call(s32[8]{0:T(128)} %reshape.114.live_ref, s32[1]{0:T(128)} %bitcast.2.tp_ref, bf16[2,256,1024]{2,1,0:T(8,128)(2,1)} %pad_maximum_fusion.2.q_ref, ...), custom_call_target="tpu_custom_call" | custom-call | flops 12884901888 | bytes 10485760 | tf_op jit(solution)/shard_map/pallas_call | solution.py:112
  154.6 6.0 %all-to-all-start.3 = ((bf16[2,3,2,16,32,128]{5,4,2,1,0,3:T(8,128)(2,1)}), bf16[2,3,2,16,32,128]{5,4,2,1,0,3:T(8,128)(2,1)S(1)}, u32[]{:S(2)}, u32[]{:S(2)}) async-start(bf16[2,3,2,16,32,128]{5,4,2,1,0,3:T(8,128)(2,1)} %copy.93), calls=%async_computation.3 | async-start | bytes 3145728 | tf_op jit(solution)/shard_map/all_to_all | solution.py:258
  161.2 2.9 copy.91
  164.1 45.1 %shard_map.94 = (bf16[2,256,1024]{2,1,0:T(8,128)(2,1)}, bf16[2,256,1024]{2,1,0:T(8,128)(2,1)}, f32[2,3,2,512,128]{4,3,2,1,0:T(8,128)}, f32[512,256]{1,0:T(8,128)}, f32[512,256]{1,0:T(8,128)}) custom-call(s32[8]{0:T(128)} %reshape.118.live_ref, s32[1]{0:T(128)} %bitcast.2.tp_ref, bf16[2,256,1024]{2,1,0:T(8,128)(2,1)} %pad_maximum_fusion.5.q_ref, ...), custom_call_target="tpu_custom_call" | custom-call | flops 12884901888 | bytes 10485760 | tf_op jit(solution)/shard_map/pallas_call | solution.py:112
  213.0 6.0 %all-to-all-start.5 = ((bf16[2,3,2,16,32,128]{5,4,2,1,0,3:T(8,128)(2,1)}), bf16[2,3,2,16,32,128]{5,4,2,1,0,3:T(8,128)(2,1)S(1)}, u32[]{:S(2)}, u32[]{:S(2)}) async-start(bf16[2,3,2,16,32,128]{5,4,2,1,0,3:T(8,128)(2,1)} %copy.99), calls=%async_computation.5 | async-start | bytes 3145728 | tf_op jit(solution)/shard_map/all_to_all | solution.py:258
  229.0 2.5 reshape.120
  232.8 18.1 %all-to-all-done.5 = bf16[2,3,2,16,32,128]{5,4,2,1,0,3:T(8,128)(2,1)S(1)} async-done(((bf16[2,3,2,16,32,128]{5,4,2,1,0,3:T(8,128)(2,1)}), bf16[2,3,2,16,32,128]{5,4,2,1,0,3:T(8,128)(2,1)S(1)}, u32[]{:S(2)}, u32[]{:S(2)}) %all-to-all-start.5) | async-done | bytes 1572896 | tf_op jit(solution)/shard_map/all_to_all | solution.py:258
  251.0 9.2 %all-to-all-start.4 = ((bf16[2,16,2,32,128]{4,3,2,0,1:T(8,128)(2,1)}), bf16[2,16,2,32,128]{4,3,2,0,1:T(8,128)(2,1)}, u32[]{:S(2)}, u32[]{:S(2)}) async-start(bf16[2,16,2,32,128]{4,3,2,0,1:T(8,128)(2,1)} %copy.95), calls=%async_computation.4 | async-start | bytes 1048576 | tf_op jit(solution)/shard_map/all_to_all | solution.py:268
  261.8 2.5 fusion.7
  269.2 5.3 %collective-permute-done.7 = bf16[256,1024]{1,0:T(8,128)(2,1)S(1)} collective-permute-done((bf16[256,1024]{1,0:T(8,128)(2,1)S(1)}, bf16[256,1024]{1,0:T(8,128)(2,1)S(1)}, u32[]{:S(2)}, u32[]{:S(2)}) %collective-permute-start.7) | collective-permute-done | bytes 524320 | tf_op jit(solution)/shard_map/ppermute | solution.py:140
  278.3 5.7 %all-to-all-start.6 = ((bf16[2,16,2,32,128]{4,3,2,0,1:T(8,128)(2,1)}), bf16[2,16,2,32,128]{4,3,2,0,1:T(8,128)(2,1)S(1)}, u32[]{:S(2)}, u32[]{:S(2)}) async-start(bf16[2,16,2,32,128]{4,3,2,0,1:T(8,128)(2,1)} %copy.101), calls=%async_computation.6 | async-start | bytes 1048576 | tf_op jit(solution)/shard_map/all_to_all | solution.py:268
  286.8 11.7 %all-to-all-done.6 = bf16[2,16,2,32,128]{4,3,2,0,1:T(8,128)(2,1)S(1)} async-done(((bf16[2,16,2,32,128]{4,3,2,0,1:T(8,128)(2,1)}), bf16[2,16,2,32,128]{4,3,2,0,1:T(8,128)(2,1)S(1)}, u32[]{:S(2)}, u32[]{:S(2)}) %all-to-all-start.6) | async-done | bytes 524320 | tf_op jit(solution)/shard_map/all_to_all | solution.py:268
  305.4 5.5 %collective-permute-done.11 = bf16[256,512]{1,0:T(8,128)(2,1)S(1)} collective-permute-done((bf16[256,512]{1,0:T(8,128)(2,1)S(1)}, bf16[256,512]{1,0:T(8,128)(2,1)S(1)}, u32[]{:S(2)}, u32[]{:S(2)}) %collective-permute-start.11) | collective-permute-done | bytes 262176 | tf_op jit(solution)/shard_map/ppermute | solution.py:140
  312.0 3.6 %collective-permute-done.10 = bf16[256,512]{1,0:T(8,128)(2,1)S(1)} collective-permute-done((bf16[256,512]{1,0:T(8,128)(2,1)S(1)}, bf16[256,512]{1,0:T(8,128)(2,1)S(1)}, u32[]{:S(2)}, u32[]{:S(2)}) %collective-permute-start.10) | collective-permute-done | bytes 262176 | tf_op jit(solution)/shard_map/ppermute | solution.py:140
  (158 shorter events, 69.8 us)
Async XLA Ops:
  1.7 10.2 %collective-permute-start.3 = (bf16[256,512]{1,0:T(8,128)(2,1)S(1)}, bf16[256,512]{1,0:T(8,128)(2,1)S(1)}, u32[]{:S(2)}, u32[]{:S(2)}) collective-permute-start(bf16[256,512]{1,0:T(8,128)(2,1)S(1)} %get-tuple-element.72), channel_id=1, source_target_pairs={{0,1},{1,0},{2,3},{3,2},{4,5},{5,4},{6,7},{7,6},{8,9},{9,8},{10,11... | collective-permute-start | bytes 786440 | tf_op jit(solution)/shard_map/ppermute | solution.py:140
  5.8 10.9 %collective-permute-start.2 = (bf16[256,512]{1,0:T(8,128)(2,1)S(1)}, bf16[256,512]{1,0:T(8,128)(2,1)S(1)}, u32[]{:S(2)}, u32[]{:S(2)}) collective-permute-start(bf16[256,512]{1,0:T(8,128)(2,1)S(1)} %get-tuple-element.70), channel_id=1, source_target_pairs={{0,1},{1,0},{2,3},{3,2},{4,5},{5,4},{6,7},{7,6},{8,9},{9,8},{10,11... | collective-permute-start | bytes 786440 | tf_op jit(solution)/shard_map/ppermute | solution.py:140
  19.5 34.4 %all-to-all-start = ((bf16[16,2,32,4,128]{4,2,3,1,0:T(8,128)(2,1)}), bf16[16,2,32,4,128]{4,2,3,1,0:T(8,128)(2,1)S(1)}, u32[]{:S(2)}, u32[]{:S(2)}) async-start(bf16[16,2,32,4,128]{4,2,3,1,0:T(8,128)(2,1)} %pad_maximum_fusion.4), calls=%async_computation | async-start | bytes 2097152 | tf_op jit(solution)/shard_map/all_to_all | solution.py:219
  27.2 15.0 %copy-start.17 = (bf16[1,256,1024]{2,1,0:T(8,128)(2,1)S(1)}, bf16[1,256,1024]{2,1,0:T(8,128)(2,1)}, u32[]{:S(2)}) copy-start(bf16[1,256,1024]{2,1,0:T(8,128)(2,1)} %get-tuple-element.40) | copy-start | bytes 1572868
  27.2 15.0 %collective-permute-start.4 = (bf16[256,1024]{1,0:T(8,128)(2,1)}, bf16[256,1024]{1,0:T(8,128)(2,1)S(1)}, u32[]{:S(2)}, u32[]{:S(2)}) collective-permute-start(bf16[256,1024]{1,0:T(8,128)(2,1)} %get-tuple-element.39), channel_id=1, source_target_pairs={{0,1},{1,0},{2,3},{3,2},{4,5},{5,4},{6,7},{7,6},{8,9},{9,8},{10,11... | collective-permute-start | bytes 1572872 | tf_op jit(solution)/shard_map/ppermute | solution.py:140
  30.0 22.9 %collective-permute-start.5 = (bf16[256,1024]{1,0:T(8,128)(2,1)}, bf16[256,1024]{1,0:T(8,128)(2,1)S(1)}, u32[]{:S(2)}, u32[]{:S(2)}) collective-permute-start(bf16[256,1024]{1,0:T(8,128)(2,1)} %get-tuple-element.35), channel_id=1, source_target_pairs={{0,1},{1,0},{2,3},{3,2},{4,5},{5,4},{6,7},{7,6},{8,9},{9,8},{10,11... | collective-permute-start | bytes 1572872 | tf_op jit(solution)/shard_map/ppermute | solution.py:140
  56.3 21.0 %copy-start.11 = (bf16[1,256,1024]{2,1,0:T(8,128)(2,1)S(1)}, bf16[1,256,1024]{2,1,0:T(8,128)(2,1)}, u32[]{:S(2)}) copy-start(bf16[1,256,1024]{2,1,0:T(8,128)(2,1)} %get-tuple-element.37) | copy-start | bytes 1572868
  56.3 37.9 %all-to-all-start.1 = ((bf16[16,2,3,2,32,128]{5,4,3,2,1,0:T(8,128)(2,1)}), bf16[16,2,3,2,32,128]{5,4,3,2,1,0:T(8,128)(2,1)S(1)}, u32[]{:S(2)}, u32[]{:S(2)}) async-start(bf16[16,2,3,2,32,128]{5,4,3,2,1,0:T(8,128)(2,1)} %bitcast.175), calls=%async_computation.1 | async-start | bytes 3145728 | tf_op jit(solution)/shard_map/all_to_all | solution.py:245
  62.2 15.1 %collective-permute-start = (bf16[256,1024]{1,0:T(8,128)(2,1)}, bf16[256,1024]{1,0:T(8,128)(2,1)}, u32[]{:S(2)}, u32[]{:S(2)}) collective-permute-start(bf16[256,1024]{1,0:T(8,128)(2,1)} %get-tuple-element.38), channel_id=1, source_target_pairs={{0,1},{1,0},{2,3},{3,2},{4,5},{5,4},{6,7},{7,6},{8,9},{9,8},{10,11... | collective-permute-start | bytes 1572872 | tf_op jit(solution)/shard_map/ppermute | solution.py:140
  63.8 24.2 %collective-permute-start.1 = (bf16[256,1024]{1,0:T(8,128)(2,1)}, bf16[256,1024]{1,0:T(8,128)(2,1)}, u32[]{:S(2)}, u32[]{:S(2)}) collective-permute-start(bf16[256,1024]{1,0:T(8,128)(2,1)} %get-tuple-element.34), channel_id=1, source_target_pairs={{0,1},{1,0},{2,3},{3,2},{4,5},{5,4},{6,7},{7,6},{8,9},{9,8},{10,11... | collective-permute-start | bytes 1572872 | tf_op jit(solution)/shard_map/ppermute | solution.py:140
  64.5 23.5 %copy-start.12 = (bf16[1,256,1024]{2,1,0:T(8,128)(2,1)S(1)}, bf16[1,256,1024]{2,1,0:T(8,128)(2,1)}, u32[]{:S(2)}) copy-start(bf16[1,256,1024]{2,1,0:T(8,128)(2,1)} %get-tuple-element.33) | copy-start | bytes 1572868
  94.2 60.5 %all-to-all-start.2 = ((bf16[16,2,3,2,32,128]{5,4,3,2,1,0:T(8,128)(2,1)}), bf16[16,2,3,2,32,128]{5,4,3,2,1,0:T(8,128)(2,1)}, u32[]{:S(2)}, u32[]{:S(2)}) async-start(bf16[16,2,3,2,32,128]{5,4,3,2,1,0:T(8,128)(2,1)} %bitcast.174), calls=%async_computation.2 | async-start | bytes 3145728 | tf_op jit(solution)/shard_map/all_to_all | solution.py:245
  154.6 58.4 %all-to-all-start.3 = ((bf16[2,3,2,16,32,128]{5,4,2,1,0,3:T(8,128)(2,1)}), bf16[2,3,2,16,32,128]{5,4,2,1,0,3:T(8,128)(2,1)S(1)}, u32[]{:S(2)}, u32[]{:S(2)}) async-start(bf16[2,3,2,16,32,128]{5,4,2,1,0,3:T(8,128)(2,1)} %copy.93), calls=%async_computation.3 | async-start | bytes 3145728 | tf_op jit(solution)/shard_map/all_to_all | solution.py:258
  213.0 38.0 %all-to-all-start.5 = ((bf16[2,3,2,16,32,128]{5,4,2,1,0,3:T(8,128)(2,1)}), bf16[2,3,2,16,32,128]{5,4,2,1,0,3:T(8,128)(2,1)S(1)}, u32[]{:S(2)}, u32[]{:S(2)}) async-start(bf16[2,3,2,16,32,128]{5,4,2,1,0,3:T(8,128)(2,1)} %copy.99), calls=%async_computation.5 | async-start | bytes 3145728 | tf_op jit(solution)/shard_map/all_to_all | solution.py:258
  221.8 40.0 %collective-permute-start.8 = (bf16[256,1024]{1,0:T(8,128)(2,1)}, bf16[256,1024]{1,0:T(8,128)(2,1)}, u32[]{:S(2)}, u32[]{:S(2)}) collective-permute-start(bf16[256,1024]{1,0:T(8,128)(2,1)} %get-tuple-element.49), channel_id=1, source_target_pairs={{0,1},{1,0},{2,3},{3,2},{4,5},{5,4},{6,7},{7,6},{8,9},{9,8},{10,11... | collective-permute-start | bytes 1572872 | tf_op jit(solution)/shard_map/ppermute | solution.py:140
  224.4 39.9 %collective-permute-start.9 = (bf16[256,1024]{1,0:T(8,128)(2,1)}, bf16[256,1024]{1,0:T(8,128)(2,1)}, u32[]{:S(2)}, u32[]{:S(2)}) collective-permute-start(bf16[256,1024]{1,0:T(8,128)(2,1)} %get-tuple-element.51), channel_id=1, source_target_pairs={{0,1},{1,0},{2,3},{3,2},{4,5},{5,4},{6,7},{7,6},{8,9},{9,8},{10,11... | collective-permute-start | bytes 1572872 | tf_op jit(solution)/shard_map/ppermute | solution.py:140
  226.0 40.8 %collective-permute-start.6 = (bf16[256,1024]{1,0:T(8,128)(2,1)}, bf16[256,1024]{1,0:T(8,128)(2,1)}, u32[]{:S(2)}, u32[]{:S(2)}) collective-permute-start(bf16[256,1024]{1,0:T(8,128)(2,1)} %get-tuple-element.57), channel_id=1, source_target_pairs={{0,1},{1,0},{2,3},{3,2},{4,5},{5,4},{6,7},{7,6},{8,9},{9,8},{10,11... | collective-permute-start | bytes 1572872 | tf_op jit(solution)/shard_map/ppermute | solution.py:140
  231.8 28.3 %copy-start.19 = (bf16[2,256,1024]{2,1,0:T(8,128)(2,1)S(1)}, bf16[2,256,1024]{2,1,0:T(8,128)(2,1)}, u32[]{:S(2)}) copy-start(bf16[2,256,1024]{2,1,0:T(8,128)(2,1)} %get-tuple-element.24) | copy-start | bytes 3145732
  232.0 29.8 %copy-start.6 = (bf16[1,256,1024]{2,1,0:T(8,128)(2,1)S(1)}, bf16[1,256,1024]{2,1,0:T(8,128)(2,1)}, u32[]{:S(2)}) copy-start(bf16[1,256,1024]{2,1,0:T(8,128)(2,1)} %get-tuple-element.50) | copy-start | bytes 1572868
  251.0 27.3 %all-to-all-start.4 = ((bf16[2,16,2,32,128]{4,3,2,0,1:T(8,128)(2,1)}), bf16[2,16,2,32,128]{4,3,2,0,1:T(8,128)(2,1)}, u32[]{:S(2)}, u32[]{:S(2)}) async-start(bf16[2,16,2,32,128]{4,3,2,0,1:T(8,128)(2,1)} %copy.95), calls=%async_computation.4 | async-start | bytes 1048576 | tf_op jit(solution)/shard_map/all_to_all | solution.py:268
  260.2 14.2 %collective-permute-start.7 = (bf16[256,1024]{1,0:T(8,128)(2,1)S(1)}, bf16[256,1024]{1,0:T(8,128)(2,1)S(1)}, u32[]{:S(2)}, u32[]{:S(2)}) collective-permute-start(bf16[256,1024]{1,0:T(8,128)(2,1)S(1)} %get-tuple-element.59), channel_id=1, source_target_pairs={{0,1},{1,0},{2,3},{3,2},{4,5},{5,4},{6,7},{7,6},{8,9},{9,8},{10,11... | collective-permute-start | bytes 1572872 | tf_op jit(solution)/shard_map/ppermute | solution.py:140
  278.3 20.2 %all-to-all-start.6 = ((bf16[2,16,2,32,128]{4,3,2,0,1:T(8,128)(2,1)}), bf16[2,16,2,32,128]{4,3,2,0,1:T(8,128)(2,1)S(1)}, u32[]{:S(2)}, u32[]{:S(2)}) async-start(bf16[2,16,2,32,128]{4,3,2,0,1:T(8,128)(2,1)} %copy.101), calls=%async_computation.6 | async-start | bytes 1048576 | tf_op jit(solution)/shard_map/all_to_all | solution.py:268
  301.7 9.2 %collective-permute-start.11 = (bf16[256,512]{1,0:T(8,128)(2,1)S(1)}, bf16[256,512]{1,0:T(8,128)(2,1)S(1)}, u32[]{:S(2)}, u32[]{:S(2)}) collective-permute-start(bf16[256,512]{1,0:T(8,128)(2,1)S(1)} %get-tuple-element.63), channel_id=1, source_target_pairs={{0,1},{1,0},{2,3},{3,2},{4,5},{5,4},{6,7},{7,6},{8,9},{9,8},{10,11... | collective-permute-start | bytes 786440 | tf_op jit(solution)/shard_map/ppermute | solution.py:140
  303.3 12.3 %collective-permute-start.10 = (bf16[256,512]{1,0:T(8,128)(2,1)S(1)}, bf16[256,512]{1,0:T(8,128)(2,1)S(1)}, u32[]{:S(2)}, u32[]{:S(2)}) collective-permute-start(bf16[256,512]{1,0:T(8,128)(2,1)S(1)} %get-tuple-element.67), channel_id=1, source_target_pairs={{0,1},{1,0},{2,3},{3,2},{4,5},{5,4},{6,7},{7,6},{8,9},{9,8},{10,11... | collective-permute-start | bytes 786440 | tf_op jit(solution)/shard_map/ppermute | solution.py:140
  (22 other events, 96.8 us)

commit v13 on v12

--- a/solution.py
+++ b/solution.py
@@ -35,7 +35,7 @@
         do_t = do.T
         scores = []
         for r in range(slot_count):
-            s = lax.dot_general(q, keys[r], trans_b, preferred_element_type=jnp.float32) * scale
+            s = lax.dot_general(q, keys[r], trans_b, preferred_element_type=jnp.float32)
             live = live_ref[g * slot_count + r] > 0
             if r == slot_count - 1:
                 row = t * row_tile + lax.broadcasted_iota(jnp.int32, s.shape, 0)
@@ -47,7 +47,7 @@
         row_max = scores[0].max(axis=1, keepdims=True)
         for s in scores[1:]:
             row_max = jnp.maximum(row_max, s.max(axis=1, keepdims=True))
-        weights = [jnp.exp(s - row_max) for s in scores]
+        weights = [jnp.exp((s - row_max) * scale) for s in scores]
         total = weights[0].sum(axis=1, keepdims=True)
         for w in weights[1:]:
             total = total + w.sum(axis=1, keepdims=True)

time: 318 us -> 320 us (level)
  transfers between devices with their start and end apart: 19 -> 19, of which waited for: 12 -> 12; matrix products, arithmetic and copies ran while one was open for 17% -> 17% of each run, Pallas kernels for 28% -> 29%
where the time goes in v13:
time: 320 us; the launch traced here: 318 us
  waiting for transfers between devices  98 us (31%)
  Pallas kernels  91.7 us (29%)
  starting transfers between devices  63.2 us (20%)
  local copies, waits for them, and re-layouts  35.6 us (11%)
  other arithmetic  27.8 us (9%)
    pallas_call x2, Pallas kernels, attention(): pl.pallas_call(kernel, grid_spec=pltpu.PrefetchScalarGridSpec(num_scalar_...  91.7 us
    ppermute x12, waiting for transfers between devices, shift(): lax.ppermute(x, axis, perm=[(s, (s + step) % size) for s in range(size)])  66.5 us
    all_to_all x2, waiting for transfers between devices, body(): lax.all_to_all(send_back, 'ctx', split_axis=3, concat_axis=1, tiled=True)  18.1 us
    all_to_all x2, starting transfers between devices, body(): got = lax.all_to_all(send, 'ctx', split_axis=0, concat_axis=4, tiled=True)  15 us
    ppermute x12, starting transfers between devices, shift(): lax.ppermute(x, axis, perm=[(s, (s + step) % size) for s in range(size)])  15 us
    all_to_all x2, starting transfers between devices, body(): back = lax.all_to_all(owner, 'ctx', split_axis=1, concat_axis=3, tiled=True)  14.9 us
    all_to_all x2, starting transfers between devices, body(): lax.all_to_all(send_back, 'ctx', split_axis=3, concat_axis=1, tiled=True)  12 us
    all_to_all x2, waiting for transfers between devices, body(): back = lax.all_to_all(owner, 'ctx', split_axis=1, concat_axis=3, tiled=True)  11.7 us
  transfers between devices with their start and end apart: 19, of which 12 were waited for; matrix products, arithmetic and copies ran while one was open for 17% of the time, Pallas kernels for 29%

profile of v13, /device:TPU:0, one launch (start us, length us, event | category | flops | bytes accessed | tf_op | source)
XLA Modules:
  0.0 318.3 jit_solution(1902773167145786588)
XLA Ops:
  1.7 3.0 collective-permute-start.3
  6.0 5.9 %collective-permute-done.3 = bf16[256,512]{1,0:T(8,128)(2,1)S(1)} collective-permute-done((bf16[256,512]{1,0:T(8,128)(2,1)S(1)}, bf16[256,512]{1,0:T(8,128)(2,1)S(1)}, u32[]{:S(2)}, u32[]{:S(2)}) %collective-permute-start.3) | collective-permute-done | bytes 262176 | tf_op jit(solution)/shard_map/ppermute | solution.py:140
  12.5 4.1 %collective-permute-done.2 = bf16[256,512]{1,0:T(8,128)(2,1)S(1)} collective-permute-done((bf16[256,512]{1,0:T(8,128)(2,1)S(1)}, bf16[256,512]{1,0:T(8,128)(2,1)S(1)}, u32[]{:S(2)}, u32[]{:S(2)}) %collective-permute-start.2) | collective-permute-done | bytes 262176 | tf_op jit(solution)/shard_map/ppermute | solution.py:140
  19.5 6.3 %all-to-all-start = ((bf16[16,2,32,4,128]{4,2,3,1,0:T(8,128)(2,1)}), bf16[16,2,32,4,128]{4,2,3,1,0:T(8,128)(2,1)S(1)}, u32[]{:S(2)}, u32[]{:S(2)}) async-start(bf16[16,2,32,4,128]{4,2,3,1,0:T(8,128)(2,1)} %pad_maximum_fusion.4), calls=%async_computation | async-start | bytes 2097152 | tf_op jit(solution)/shard_map/all_to_all | solution.py:219
  31.2 10.9 %collective-permute-done.4 = bf16[256,1024]{1,0:T(8,128)(2,1)S(1)} collective-permute-done((bf16[256,1024]{1,0:T(8,128)(2,1)}, bf16[256,1024]{1,0:T(8,128)(2,1)S(1)}, u32[]{:S(2)}, u32[]{:S(2)}) %collective-permute-start.4) | collective-permute-done | bytes 524320 | tf_op jit(solution)/shard_map/ppermute | solution.py:140
  43.3 9.6 %collective-permute-done.5 = bf16[256,1024]{1,0:T(8,128)(2,1)S(1)} collective-permute-done((bf16[256,1024]{1,0:T(8,128)(2,1)}, bf16[256,1024]{1,0:T(8,128)(2,1)S(1)}, u32[]{:S(2)}, u32[]{:S(2)}) %collective-permute-start.5) | collective-permute-done | bytes 524320 | tf_op jit(solution)/shard_map/ppermute | solution.py:140
  56.3 5.9 %all-to-all-start.1 = ((bf16[16,2,3,2,32,128]{5,4,3,2,1,0:T(8,128)(2,1)}), bf16[16,2,3,2,32,128]{5,4,3,2,1,0:T(8,128)(2,1)S(1)}, u32[]{:S(2)}, u32[]{:S(2)}) async-start(bf16[16,2,3,2,32,128]{5,4,3,2,1,0:T(8,128)(2,1)} %bitcast.175), calls=%async_computation.1 | async-start | bytes 3145728 | tf_op jit(solution)/shard_map/all_to_all | solution.py:245
  64.5 12.8 %collective-permute-done = bf16[256,1024]{1,0:T(8,128)(2,1)} collective-permute-done((bf16[256,1024]{1,0:T(8,128)(2,1)}, bf16[256,1024]{1,0:T(8,128)(2,1)}, u32[]{:S(2)}, u32[]{:S(2)}) %collective-permute-start) | collective-permute-done | bytes 524320 | tf_op jit(solution)/shard_map/ppermute | solution.py:140
  79.4 8.6 %collective-permute-done.1 = bf16[256,1024]{1,0:T(8,128)(2,1)} collective-permute-done((bf16[256,1024]{1,0:T(8,128)(2,1)}, bf16[256,1024]{1,0:T(8,128)(2,1)}, u32[]{:S(2)}, u32[]{:S(2)}) %collective-permute-start.1) | collective-permute-done | bytes 524320 | tf_op jit(solution)/shard_map/ppermute | solution.py:140
  94.2 9.2 %all-to-all-start.2 = ((bf16[16,2,3,2,32,128]{5,4,3,2,1,0:T(8,128)(2,1)}), bf16[16,2,3,2,32,128]{5,4,3,2,1,0:T(8,128)(2,1)}, u32[]{:S(2)}, u32[]{:S(2)}) async-start(bf16[16,2,3,2,32,128]{5,4,3,2,1,0:T(8,128)(2,1)} %bitcast.174), calls=%async_computation.2 | async-start | bytes 3145728 | tf_op jit(solution)/shard_map/all_to_all | solution.py:245
  105.8 45.8 %shard_map.93 = (bf16[2,256,1024]{2,1,0:T(8,128)(2,1)}, bf16[2,256,1024]{2,1,0:T(8,128)(2,1)}, f32[2,3,2,512,128]{4,3,2,1,0:T(8,128)}, f32[512,256]{1,0:T(8,128)}, f32[512,256]{1,0:T(8,128)}) custom-call(s32[8]{0:T(128)} %reshape.114.live_ref, s32[1]{0:T(128)} %bitcast.2.tp_ref, bf16[2,256,1024]{2,1,0:T(8,128)(2,1)} %pad_maximum_fusion.2.q_ref, ...), custom_call_target="tpu_custom_call" | custom-call | flops 12884901888 | bytes 10485760 | tf_op jit(solution)/shard_map/pallas_call | solution.py:112
  155.4 6.0 %all-to-all-start.3 = ((bf16[2,3,2,16,32,128]{5,4,2,1,0,3:T(8,128)(2,1)}), bf16[2,3,2,16,32,128]{5,4,2,1,0,3:T(8,128)(2,1)S(1)}, u32[]{:S(2)}, u32[]{:S(2)}) async-start(bf16[2,3,2,16,32,128]{5,4,2,1,0,3:T(8,128)(2,1)} %copy.93), calls=%async_computation.3 | async-start | bytes 3145728 | tf_op jit(solution)/shard_map/all_to_all | solution.py:258
  162.0 2.9 copy.91
  164.9 45.9 %shard_map.94 = (bf16[2,256,1024]{2,1,0:T(8,128)(2,1)}, bf16[2,256,1024]{2,1,0:T(8,128)(2,1)}, f32[2,3,2,512,128]{4,3,2,1,0:T(8,128)}, f32[512,256]{1,0:T(8,128)}, f32[512,256]{1,0:T(8,128)}) custom-call(s32[8]{0:T(128)} %reshape.118.live_ref, s32[1]{0:T(128)} %bitcast.2.tp_ref, bf16[2,256,1024]{2,1,0:T(8,128)(2,1)} %pad_maximum_fusion.5.q_ref, ...), custom_call_target="tpu_custom_call" | custom-call | flops 12884901888 | bytes 10485760 | tf_op jit(solution)/shard_map/pallas_call | solution.py:112
  214.6 6.0 %all-to-all-start.5 = ((bf16[2,3,2,16,32,128]{5,4,2,1,0,3:T(8,128)(2,1)}), bf16[2,3,2,16,32,128]{5,4,2,1,0,3:T(8,128)(2,1)S(1)}, u32[]{:S(2)}, u32[]{:S(2)}) async-start(bf16[2,3,2,16,32,128]{5,4,2,1,0,3:T(8,128)(2,1)} %copy.99), calls=%async_computation.5 | async-start | bytes 3145728 | tf_op jit(solution)/shard_map/all_to_all | solution.py:258
  230.6 2.5 reshape.120
  234.4 18.1 %all-to-all-done.5 = bf16[2,3,2,16,32,128]{5,4,2,1,0,3:T(8,128)(2,1)S(1)} async-done(((bf16[2,3,2,16,32,128]{5,4,2,1,0,3:T(8,128)(2,1)}), bf16[2,3,2,16,32,128]{5,4,2,1,0,3:T(8,128)(2,1)S(1)}, u32[]{:S(2)}, u32[]{:S(2)}) %all-to-all-start.5) | async-done | bytes 1572896 | tf_op jit(solution)/shard_map/all_to_all | solution.py:258
  252.6 9.2 %all-to-all-start.4 = ((bf16[2,16,2,32,128]{4,3,2,0,1:T(8,128)(2,1)}), bf16[2,16,2,32,128]{4,3,2,0,1:T(8,128)(2,1)}, u32[]{:S(2)}, u32[]{:S(2)}) async-start(bf16[2,16,2,32,128]{4,3,2,0,1:T(8,128)(2,1)} %copy.95), calls=%async_computation.4 | async-start | bytes 1048576 | tf_op jit(solution)/shard_map/all_to_all | solution.py:268
  263.4 2.5 fusion.7
  270.8 5.3 %collective-permute-done.7 = bf16[256,1024]{1,0:T(8,128)(2,1)S(1)} collective-permute-done((bf16[256,1024]{1,0:T(8,128)(2,1)S(1)}, bf16[256,1024]{1,0:T(8,128)(2,1)S(1)}, u32[]{:S(2)}, u32[]{:S(2)}) %collective-permute-start.7) | collective-permute-done | bytes 524320 | tf_op jit(solution)/shard_map/ppermute | solution.py:140
  279.9 5.7 %all-to-all-start.6 = ((bf16[2,16,2,32,128]{4,3,2,0,1:T(8,128)(2,1)}), bf16[2,16,2,32,128]{4,3,2,0,1:T(8,128)(2,1)S(1)}, u32[]{:S(2)}, u32[]{:S(2)}) async-start(bf16[2,16,2,32,128]{4,3,2,0,1:T(8,128)(2,1)} %copy.101), calls=%async_computation.6 | async-start | bytes 1048576 | tf_op jit(solution)/shard_map/all_to_all | solution.py:268
  288.4 11.7 %all-to-all-done.6 = bf16[2,16,2,32,128]{4,3,2,0,1:T(8,128)(2,1)S(1)} async-done(((bf16[2,16,2,32,128]{4,3,2,0,1:T(8,128)(2,1)}), bf16[2,16,2,32,128]{4,3,2,0,1:T(8,128)(2,1)S(1)}, u32[]{:S(2)}, u32[]{:S(2)}) %all-to-all-start.6) | async-done | bytes 524320 | tf_op jit(solution)/shard_map/all_to_all | solution.py:268
  307.0 5.5 %collective-permute-done.11 = bf16[256,512]{1,0:T(8,128)(2,1)S(1)} collective-permute-done((bf16[256,512]{1,0:T(8,128)(2,1)S(1)}, bf16[256,512]{1,0:T(8,128)(2,1)S(1)}, u32[]{:S(2)}, u32[]{:S(2)}) %collective-permute-start.11) | collective-permute-done | bytes 262176 | tf_op jit(solution)/shard_map/ppermute | solution.py:140
  313.6 3.6 %collective-permute-done.10 = bf16[256,512]{1,0:T(8,128)(2,1)S(1)} collective-permute-done((bf16[256,512]{1,0:T(8,128)(2,1)S(1)}, bf16[256,512]{1,0:T(8,128)(2,1)S(1)}, u32[]{:S(2)}, u32[]{:S(2)}) %collective-permute-start.10) | collective-permute-done | bytes 262176 | tf_op jit(solution)/shard_map/ppermute | solution.py:140
  (158 shorter events, 69.9 us)
Async XLA Ops:
  1.7 10.2 %collective-permute-start.3 = (bf16[256,512]{1,0:T(8,128)(2,1)S(1)}, bf16[256,512]{1,0:T(8,128)(2,1)S(1)}, u32[]{:S(2)}, u32[]{:S(2)}) collective-permute-start(bf16[256,512]{1,0:T(8,128)(2,1)S(1)} %get-tuple-element.72), channel_id=1, source_target_pairs={{0,1},{1,0},{2,3},{3,2},{4,5},{5,4},{6,7},{7,6},{8,9},{9,8},{10,11... | collective-permute-start | bytes 786440 | tf_op jit(solution)/shard_map/ppermute | solution.py:140
  5.8 10.9 %collective-permute-start.2 = (bf16[256,512]{1,0:T(8,128)(2,1)S(1)}, bf16[256,512]{1,0:T(8,128)(2,1)S(1)}, u32[]{:S(2)}, u32[]{:S(2)}) collective-permute-start(bf16[256,512]{1,0:T(8,128)(2,1)S(1)} %get-tuple-element.70), channel_id=1, source_target_pairs={{0,1},{1,0},{2,3},{3,2},{4,5},{5,4},{6,7},{7,6},{8,9},{9,8},{10,11... | collective-permute-start | bytes 786440 | tf_op jit(solution)/shard_map/ppermute | solution.py:140
  19.5 34.4 %all-to-all-start = ((bf16[16,2,32,4,128]{4,2,3,1,0:T(8,128)(2,1)}), bf16[16,2,32,4,128]{4,2,3,1,0:T(8,128)(2,1)S(1)}, u32[]{:S(2)}, u32[]{:S(2)}) async-start(bf16[16,2,32,4,128]{4,2,3,1,0:T(8,128)(2,1)} %pad_maximum_fusion.4), calls=%async_computation | async-start | bytes 2097152 | tf_op jit(solution)/shard_map/all_to_all | solution.py:219
  27.2 15.0 %copy-start.17 = (bf16[1,256,1024]{2,1,0:T(8,128)(2,1)S(1)}, bf16[1,256,1024]{2,1,0:T(8,128)(2,1)}, u32[]{:S(2)}) copy-start(bf16[1,256,1024]{2,1,0:T(8,128)(2,1)} %get-tuple-element.40) | copy-start | bytes 1572868
  27.2 15.0 %collective-permute-start.4 = (bf16[256,1024]{1,0:T(8,128)(2,1)}, bf16[256,1024]{1,0:T(8,128)(2,1)S(1)}, u32[]{:S(2)}, u32[]{:S(2)}) collective-permute-start(bf16[256,1024]{1,0:T(8,128)(2,1)} %get-tuple-element.39), channel_id=1, source_target_pairs={{0,1},{1,0},{2,3},{3,2},{4,5},{5,4},{6,7},{7,6},{8,9},{9,8},{10,11... | collective-permute-start | bytes 1572872 | tf_op jit(solution)/shard_map/ppermute | solution.py:140
  30.0 22.9 %collective-permute-start.5 = (bf16[256,1024]{1,0:T(8,128)(2,1)}, bf16[256,1024]{1,0:T(8,128)(2,1)S(1)}, u32[]{:S(2)}, u32[]{:S(2)}) collective-permute-start(bf16[256,1024]{1,0:T(8,128)(2,1)} %get-tuple-element.35), channel_id=1, source_target_pairs={{0,1},{1,0},{2,3},{3,2},{4,5},{5,4},{6,7},{7,6},{8,9},{9,8},{10,11... | collective-permute-start | bytes 1572872 | tf_op jit(solution)/shard_map/ppermute | solution.py:140
  56.3 21.0 %copy-start.11 = (bf16[1,256,1024]{2,1,0:T(8,128)(2,1)S(1)}, bf16[1,256,1024]{2,1,0:T(8,128)(2,1)}, u32[]{:S(2)}) copy-start(bf16[1,256,1024]{2,1,0:T(8,128)(2,1)} %get-tuple-element.37) | copy-start | bytes 1572868
  56.3 37.9 %all-to-all-start.1 = ((bf16[16,2,3,2,32,128]{5,4,3,2,1,0:T(8,128)(2,1)}), bf16[16,2,3,2,32,128]{5,4,3,2,1,0:T(8,128)(2,1)S(1)}, u32[]{:S(2)}, u32[]{:S(2)}) async-start(bf16[16,2,3,2,32,128]{5,4,3,2,1,0:T(8,128)(2,1)} %bitcast.175), calls=%async_computation.1 | async-start | bytes 3145728 | tf_op jit(solution)/shard_map/all_to_all | solution.py:245
  62.2 15.1 %collective-permute-start = (bf16[256,1024]{1,0:T(8,128)(2,1)}, bf16[256,1024]{1,0:T(8,128)(2,1)}, u32[]{:S(2)}, u32[]{:S(2)}) collective-permute-start(bf16[256,1024]{1,0:T(8,128)(2,1)} %get-tuple-element.38), channel_id=1, source_target_pairs={{0,1},{1,0},{2,3},{3,2},{4,5},{5,4},{6,7},{7,6},{8,9},{9,8},{10,11... | collective-permute-start | bytes 1572872 | tf_op jit(solution)/shard_map/ppermute | solution.py:140
  63.8 24.2 %collective-permute-start.1 = (bf16[256,1024]{1,0:T(8,128)(2,1)}, bf16[256,1024]{1,0:T(8,128)(2,1)}, u32[]{:S(2)}, u32[]{:S(2)}) collective-permute-start(bf16[256,1024]{1,0:T(8,128)(2,1)} %get-tuple-element.34), channel_id=1, source_target_pairs={{0,1},{1,0},{2,3},{3,2},{4,5},{5,4},{6,7},{7,6},{8,9},{9,8},{10,11... | collective-permute-start | bytes 1572872 | tf_op jit(solution)/shard_map/ppermute | solution.py:140
  64.5 23.5 %copy-start.12 = (bf16[1,256,1024]{2,1,0:T(8,128)(2,1)S(1)}, bf16[1,256,1024]{2,1,0:T(8,128)(2,1)}, u32[]{:S(2)}) copy-start(bf16[1,256,1024]{2,1,0:T(8,128)(2,1)} %get-tuple-element.33) | copy-start | bytes 1572868
  94.2 61.2 %all-to-all-start.2 = ((bf16[16,2,3,2,32,128]{5,4,3,2,1,0:T(8,128)(2,1)}), bf16[16,2,3,2,32,128]{5,4,3,2,1,0:T(8,128)(2,1)}, u32[]{:S(2)}, u32[]{:S(2)}) async-start(bf16[16,2,3,2,32,128]{5,4,3,2,1,0:T(8,128)(2,1)} %bitcast.174), calls=%async_computation.2 | async-start | bytes 3145728 | tf_op jit(solution)/shard_map/all_to_all | solution.py:245
  155.4 59.2 %all-to-all-start.3 = ((bf16[2,3,2,16,32,128]{5,4,2,1,0,3:T(8,128)(2,1)}), bf16[2,3,2,16,32,128]{5,4,2,1,0,3:T(8,128)(2,1)S(1)}, u32[]{:S(2)}, u32[]{:S(2)}) async-start(bf16[2,3,2,16,32,128]{5,4,2,1,0,3:T(8,128)(2,1)} %copy.93), calls=%async_computation.3 | async-start | bytes 3145728 | tf_op jit(solution)/shard_map/all_to_all | solution.py:258
  214.6 38.0 %all-to-all-start.5 = ((bf16[2,3,2,16,32,128]{5,4,2,1,0,3:T(8,128)(2,1)}), bf16[2,3,2,16,32,128]{5,4,2,1,0,3:T(8,128)(2,1)S(1)}, u32[]{:S(2)}, u32[]{:S(2)}) async-start(bf16[2,3,2,16,32,128]{5,4,2,1,0,3:T(8,128)(2,1)} %copy.99), calls=%async_computation.5 | async-start | bytes 3145728 | tf_op jit(solution)/shard_map/all_to_all | solution.py:258
  223.4 40.0 %collective-permute-start.8 = (bf16[256,1024]{1,0:T(8,128)(2,1)}, bf16[256,1024]{1,0:T(8,128)(2,1)}, u32[]{:S(2)}, u32[]{:S(2)}) collective-permute-start(bf16[256,1024]{1,0:T(8,128)(2,1)} %get-tuple-element.49), channel_id=1, source_target_pairs={{0,1},{1,0},{2,3},{3,2},{4,5},{5,4},{6,7},{7,6},{8,9},{9,8},{10,11... | collective-permute-start | bytes 1572872 | tf_op jit(solution)/shard_map/ppermute | solution.py:140
  226.0 39.9 %collective-permute-start.9 = (bf16[256,1024]{1,0:T(8,128)(2,1)}, bf16[256,1024]{1,0:T(8,128)(2,1)}, u32[]{:S(2)}, u32[]{:S(2)}) collective-permute-start(bf16[256,1024]{1,0:T(8,128)(2,1)} %get-tuple-element.51), channel_id=1, source_target_pairs={{0,1},{1,0},{2,3},{3,2},{4,5},{5,4},{6,7},{7,6},{8,9},{9,8},{10,11... | collective-permute-start | bytes 1572872 | tf_op jit(solution)/shard_map/ppermute | solution.py:140
  227.6 40.8 %collective-permute-start.6 = (bf16[256,1024]{1,0:T(8,128)(2,1)}, bf16[256,1024]{1,0:T(8,128)(2,1)}, u32[]{:S(2)}, u32[]{:S(2)}) collective-permute-start(bf16[256,1024]{1,0:T(8,128)(2,1)} %get-tuple-element.57), channel_id=1, source_target_pairs={{0,1},{1,0},{2,3},{3,2},{4,5},{5,4},{6,7},{7,6},{8,9},{9,8},{10,11... | collective-permute-start | bytes 1572872 | tf_op jit(solution)/shard_map/ppermute | solution.py:140
  233.5 28.3 %copy-start.19 = (bf16[2,256,1024]{2,1,0:T(8,128)(2,1)S(1)}, bf16[2,256,1024]{2,1,0:T(8,128)(2,1)}, u32[]{:S(2)}) copy-start(bf16[2,256,1024]{2,1,0:T(8,128)(2,1)} %get-tuple-element.24) | copy-start | bytes 3145732
  233.6 29.8 %copy-start.6 = (bf16[1,256,1024]{2,1,0:T(8,128)(2,1)S(1)}, bf16[1,256,1024]{2,1,0:T(8,128)(2,1)}, u32[]{:S(2)}) copy-start(bf16[1,256,1024]{2,1,0:T(8,128)(2,1)} %get-tuple-element.50) | copy-start | bytes 1572868
  252.6 27.3 %all-to-all-start.4 = ((bf16[2,16,2,32,128]{4,3,2,0,1:T(8,128)(2,1)}), bf16[2,16,2,32,128]{4,3,2,0,1:T(8,128)(2,1)}, u32[]{:S(2)}, u32[]{:S(2)}) async-start(bf16[2,16,2,32,128]{4,3,2,0,1:T(8,128)(2,1)} %copy.95), calls=%async_computation.4 | async-start | bytes 1048576 | tf_op jit(solution)/shard_map/all_to_all | solution.py:268
  261.8 14.2 %collective-permute-start.7 = (bf16[256,1024]{1,0:T(8,128)(2,1)S(1)}, bf16[256,1024]{1,0:T(8,128)(2,1)S(1)}, u32[]{:S(2)}, u32[]{:S(2)}) collective-permute-start(bf16[256,1024]{1,0:T(8,128)(2,1)S(1)} %get-tuple-element.59), channel_id=1, source_target_pairs={{0,1},{1,0},{2,3},{3,2},{4,5},{5,4},{6,7},{7,6},{8,9},{9,8},{10,11... | collective-permute-start | bytes 1572872 | tf_op jit(solution)/shard_map/ppermute | solution.py:140
  279.9 20.2 %all-to-all-start.6 = ((bf16[2,16,2,32,128]{4,3,2,0,1:T(8,128)(2,1)}), bf16[2,16,2,32,128]{4,3,2,0,1:T(8,128)(2,1)S(1)}, u32[]{:S(2)}, u32[]{:S(2)}) async-start(bf16[2,16,2,32,128]{4,3,2,0,1:T(8,128)(2,1)} %copy.101), calls=%async_computation.6 | async-start | bytes 1048576 | tf_op jit(solution)/shard_map/all_to_all | solution.py:268
  303.3 9.2 %collective-permute-start.11 = (bf16[256,512]{1,0:T(8,128)(2,1)S(1)}, bf16[256,512]{1,0:T(8,128)(2,1)S(1)}, u32[]{:S(2)}, u32[]{:S(2)}) collective-permute-start(bf16[256,512]{1,0:T(8,128)(2,1)S(1)} %get-tuple-element.63), channel_id=1, source_target_pairs={{0,1},{1,0},{2,3},{3,2},{4,5},{5,4},{6,7},{7,6},{8,9},{9,8},{10,11... | collective-permute-start | bytes 786440 | tf_op jit(solution)/shard_map/ppermute | solution.py:140
  304.9 12.3 %collective-permute-start.10 = (bf16[256,512]{1,0:T(8,128)(2,1)S(1)}, bf16[256,512]{1,0:T(8,128)(2,1)S(1)}, u32[]{:S(2)}, u32[]{:S(2)}) collective-permute-start(bf16[256,512]{1,0:T(8,128)(2,1)S(1)} %get-tuple-element.67), channel_id=1, source_target_pairs={{0,1},{1,0},{2,3},{3,2},{4,5},{5,4},{6,7},{7,6},{8,9},{9,8},{10,11... | collective-permute-start | bytes 786440 | tf_op jit(solution)/shard_map/ppermute | solution.py:140
  (22 other events, 96.8 us)

commit v14 on v12

--- a/solution.py
+++ b/solution.py
@@ -52,8 +52,7 @@
         for w in weights[1:]:
             total = total + w.sum(axis=1, keepdims=True)
         inverse = 1.0 / total
-        probs = [w * inverse for w in weights]
-        probs_low = [p.astype(jnp.bfloat16) for p in probs]
+        probs_low = [(w * inverse).astype(jnp.bfloat16) for w in weights]
         out = jnp.dot(probs_low[0], values[0], preferred_element_type=jnp.float32)
         for r in range(1, slot_count):
             out = out + jnp.dot(probs_low[r], values[r], preferred_element_type=jnp.float32)
@@ -63,7 +62,7 @@
         grad_q = None
         for r in range(slot_count):
             grad_p = lax.dot_general(do, values[r], trans_b, preferred_element_type=jnp.float32)
-            grad_s = (probs[r] * (grad_p - delta)).astype(jnp.bfloat16)
+            grad_s = (probs_low[r].astype(jnp.float32) * (grad_p - delta)).astype(jnp.bfloat16)
             part = jnp.dot(grad_s, keys[r], preferred_element_type=jnp.float32)
             grad_q = part if grad_q is None else grad_q + part
             width = keys[r].shape[0]

time: 318 us -> 317 us (level)
  no operation moved by 1% of the time
where the time goes in v14:
time: 317 us; the launch traced here: 316 us
  waiting for transfers between devices  98 us (31%)
  Pallas kernels  89.6 us (28%)
  starting transfers between devices  63.2 us (20%)
  local copies, waits for them, and re-layouts  35.6 us (11%)
  other arithmetic  27.8 us (9%)
    pallas_call x2, Pallas kernels, attention(): pl.pallas_call(kernel, grid_spec=pltpu.PrefetchScalarGridSpec(num_scalar_...  89.6 us
    ppermute x12, waiting for transfers between devices, shift(): lax.ppermute(x, axis, perm=[(s, (s + step) % size) for s in range(size)])  66.5 us
    all_to_all x2, waiting for transfers between devices, body(): lax.all_to_all(send_back, 'ctx', split_axis=3, concat_axis=1, tiled=True)  18.1 us
    all_to_all x2, starting transfers between devices, body(): got = lax.all_to_all(send, 'ctx', split_axis=0, concat_axis=4, tiled=True)  15 us
    ppermute x12, starting transfers between devices, shift(): lax.ppermute(x, axis, perm=[(s, (s + step) % size) for s in range(size)])  15 us
    all_to_all x2, starting transfers between devices, body(): back = lax.all_to_all(owner, 'ctx', split_axis=1, concat_axis=3, tiled=True)  14.9 us
    all_to_all x2, starting transfers between devices, body(): lax.all_to_all(send_back, 'ctx', split_axis=3, concat_axis=1, tiled=True)  12 us
    all_to_all x2, waiting for transfers between devices, body(): back = lax.all_to_all(owner, 'ctx', split_axis=1, concat_axis=3, tiled=True)  11.7 us
  transfers between devices with their start and end apart: 19, of which 12 were waited for; matrix products, arithmetic and copies ran while one was open for 17% of the time, Pallas kernels for 28%

profile of v14, /device:TPU:0, one launch (start us, length us, event | category | flops | bytes accessed | tf_op | source)
XLA Modules:
  0.0 316.1 jit_solution(2298999460699665239)
XLA Ops:
  1.7 3.0 collective-permute-start.3
  6.0 5.9 %collective-permute-done.3 = bf16[256,512]{1,0:T(8,128)(2,1)S(1)} collective-permute-done((bf16[256,512]{1,0:T(8,128)(2,1)S(1)}, bf16[256,512]{1,0:T(8,128)(2,1)S(1)}, u32[]{:S(2)}, u32[]{:S(2)}) %collective-permute-start.3) | collective-permute-done | bytes 262176 | tf_op jit(solution)/shard_map/ppermute | solution.py:139
  12.5 4.1 %collective-permute-done.2 = bf16[256,512]{1,0:T(8,128)(2,1)S(1)} collective-permute-done((bf16[256,512]{1,0:T(8,128)(2,1)S(1)}, bf16[256,512]{1,0:T(8,128)(2,1)S(1)}, u32[]{:S(2)}, u32[]{:S(2)}) %collective-permute-start.2) | collective-permute-done | bytes 262176 | tf_op jit(solution)/shard_map/ppermute | solution.py:139
  19.5 6.3 %all-to-all-start = ((bf16[16,2,32,4,128]{4,2,3,1,0:T(8,128)(2,1)}), bf16[16,2,32,4,128]{4,2,3,1,0:T(8,128)(2,1)S(1)}, u32[]{:S(2)}, u32[]{:S(2)}) async-start(bf16[16,2,32,4,128]{4,2,3,1,0:T(8,128)(2,1)} %pad_maximum_fusion.4), calls=%async_computation | async-start | bytes 2097152 | tf_op jit(solution)/shard_map/all_to_all | solution.py:218
  31.2 10.9 %collective-permute-done.4 = bf16[256,1024]{1,0:T(8,128)(2,1)S(1)} collective-permute-done((bf16[256,1024]{1,0:T(8,128)(2,1)}, bf16[256,1024]{1,0:T(8,128)(2,1)S(1)}, u32[]{:S(2)}, u32[]{:S(2)}) %collective-permute-start.4) | collective-permute-done | bytes 524320 | tf_op jit(solution)/shard_map/ppermute | solution.py:139
  43.3 9.6 %collective-permute-done.5 = bf16[256,1024]{1,0:T(8,128)(2,1)S(1)} collective-permute-done((bf16[256,1024]{1,0:T(8,128)(2,1)}, bf16[256,1024]{1,0:T(8,128)(2,1)S(1)}, u32[]{:S(2)}, u32[]{:S(2)}) %collective-permute-start.5) | collective-permute-done | bytes 524320 | tf_op jit(solution)/shard_map/ppermute | solution.py:139
  56.3 5.9 %all-to-all-start.1 = ((bf16[16,2,3,2,32,128]{5,4,3,2,1,0:T(8,128)(2,1)}), bf16[16,2,3,2,32,128]{5,4,3,2,1,0:T(8,128)(2,1)S(1)}, u32[]{:S(2)}, u32[]{:S(2)}) async-start(bf16[16,2,3,2,32,128]{5,4,3,2,1,0:T(8,128)(2,1)} %bitcast.175), calls=%async_computation.1 | async-start | bytes 3145728 | tf_op jit(solution)/shard_map/all_to_all | solution.py:244
  64.5 12.8 %collective-permute-done = bf16[256,1024]{1,0:T(8,128)(2,1)} collective-permute-done((bf16[256,1024]{1,0:T(8,128)(2,1)}, bf16[256,1024]{1,0:T(8,128)(2,1)}, u32[]{:S(2)}, u32[]{:S(2)}) %collective-permute-start) | collective-permute-done | bytes 524320 | tf_op jit(solution)/shard_map/ppermute | solution.py:139
  79.4 8.6 %collective-permute-done.1 = bf16[256,1024]{1,0:T(8,128)(2,1)} collective-permute-done((bf16[256,1024]{1,0:T(8,128)(2,1)}, bf16[256,1024]{1,0:T(8,128)(2,1)}, u32[]{:S(2)}, u32[]{:S(2)}) %collective-permute-start.1) | collective-permute-done | bytes 524320 | tf_op jit(solution)/shard_map/ppermute | solution.py:139
  94.2 9.2 %all-to-all-start.2 = ((bf16[16,2,3,2,32,128]{5,4,3,2,1,0:T(8,128)(2,1)}), bf16[16,2,3,2,32,128]{5,4,3,2,1,0:T(8,128)(2,1)}, u32[]{:S(2)}, u32[]{:S(2)}) async-start(bf16[16,2,3,2,32,128]{5,4,3,2,1,0:T(8,128)(2,1)} %bitcast.174), calls=%async_computation.2 | async-start | bytes 3145728 | tf_op jit(solution)/shard_map/all_to_all | solution.py:244
  105.8 44.7 %shard_map.93 = (bf16[2,256,1024]{2,1,0:T(8,128)(2,1)}, bf16[2,256,1024]{2,1,0:T(8,128)(2,1)}, f32[2,3,2,512,128]{4,3,2,1,0:T(8,128)}, f32[512,256]{1,0:T(8,128)}, f32[512,256]{1,0:T(8,128)}) custom-call(s32[8]{0:T(128)} %reshape.114.live_ref, s32[1]{0:T(128)} %bitcast.2.tp_ref, bf16[2,256,1024]{2,1,0:T(8,128)(2,1)} %pad_maximum_fusion.2.q_ref, ...), custom_call_target="tpu_custom_call" | custom-call | flops 12884901888 | bytes 10485760 | tf_op jit(solution)/shard_map/pallas_call | solution.py:111
  154.3 6.0 %all-to-all-start.3 = ((bf16[2,3,2,16,32,128]{5,4,2,1,0,3:T(8,128)(2,1)}), bf16[2,3,2,16,32,128]{5,4,2,1,0,3:T(8,128)(2,1)S(1)}, u32[]{:S(2)}, u32[]{:S(2)}) async-start(bf16[2,3,2,16,32,128]{5,4,2,1,0,3:T(8,128)(2,1)} %copy.93), calls=%async_computation.3 | async-start | bytes 3145728 | tf_op jit(solution)/shard_map/all_to_all | solution.py:257
  160.9 2.9 copy.91
  163.8 44.9 %shard_map.94 = (bf16[2,256,1024]{2,1,0:T(8,128)(2,1)}, bf16[2,256,1024]{2,1,0:T(8,128)(2,1)}, f32[2,3,2,512,128]{4,3,2,1,0:T(8,128)}, f32[512,256]{1,0:T(8,128)}, f32[512,256]{1,0:T(8,128)}) custom-call(s32[8]{0:T(128)} %reshape.118.live_ref, s32[1]{0:T(128)} %bitcast.2.tp_ref, bf16[2,256,1024]{2,1,0:T(8,128)(2,1)} %pad_maximum_fusion.5.q_ref, ...), custom_call_target="tpu_custom_call" | custom-call | flops 12884901888 | bytes 10485760 | tf_op jit(solution)/shard_map/pallas_call | solution.py:111
  212.5 6.0 %all-to-all-start.5 = ((bf16[2,3,2,16,32,128]{5,4,2,1,0,3:T(8,128)(2,1)}), bf16[2,3,2,16,32,128]{5,4,2,1,0,3:T(8,128)(2,1)S(1)}, u32[]{:S(2)}, u32[]{:S(2)}) async-start(bf16[2,3,2,16,32,128]{5,4,2,1,0,3:T(8,128)(2,1)} %copy.99), calls=%async_computation.5 | async-start | bytes 3145728 | tf_op jit(solution)/shard_map/all_to_all | solution.py:257
  228.4 2.5 reshape.120
  232.3 18.1 %all-to-all-done.5 = bf16[2,3,2,16,32,128]{5,4,2,1,0,3:T(8,128)(2,1)S(1)} async-done(((bf16[2,3,2,16,32,128]{5,4,2,1,0,3:T(8,128)(2,1)}), bf16[2,3,2,16,32,128]{5,4,2,1,0,3:T(8,128)(2,1)S(1)}, u32[]{:S(2)}, u32[]{:S(2)}) %all-to-all-start.5) | async-done | bytes 1572896 | tf_op jit(solution)/shard_map/all_to_all | solution.py:257
  250.5 9.2 %all-to-all-start.4 = ((bf16[2,16,2,32,128]{4,3,2,0,1:T(8,128)(2,1)}), bf16[2,16,2,32,128]{4,3,2,0,1:T(8,128)(2,1)}, u32[]{:S(2)}, u32[]{:S(2)}) async-start(bf16[2,16,2,32,128]{4,3,2,0,1:T(8,128)(2,1)} %copy.95), calls=%async_computation.4 | async-start | bytes 1048576 | tf_op jit(solution)/shard_map/all_to_all | solution.py:267
  261.3 2.5 fusion.7
  268.7 5.3 %collective-permute-done.7 = bf16[256,1024]{1,0:T(8,128)(2,1)S(1)} collective-permute-done((bf16[256,1024]{1,0:T(8,128)(2,1)S(1)}, bf16[256,1024]{1,0:T(8,128)(2,1)S(1)}, u32[]{:S(2)}, u32[]{:S(2)}) %collective-permute-start.7) | collective-permute-done | bytes 524320 | tf_op jit(solution)/shard_map/ppermute | solution.py:139
  277.8 5.7 %all-to-all-start.6 = ((bf16[2,16,2,32,128]{4,3,2,0,1:T(8,128)(2,1)}), bf16[2,16,2,32,128]{4,3,2,0,1:T(8,128)(2,1)S(1)}, u32[]{:S(2)}, u32[]{:S(2)}) async-start(bf16[2,16,2,32,128]{4,3,2,0,1:T(8,128)(2,1)} %copy.101), calls=%async_computation.6 | async-start | bytes 1048576 | tf_op jit(solution)/shard_map/all_to_all | solution.py:267
  286.3 11.7 %all-to-all-done.6 = bf16[2,16,2,32,128]{4,3,2,0,1:T(8,128)(2,1)S(1)} async-done(((bf16[2,16,2,32,128]{4,3,2,0,1:T(8,128)(2,1)}), bf16[2,16,2,32,128]{4,3,2,0,1:T(8,128)(2,1)S(1)}, u32[]{:S(2)}, u32[]{:S(2)}) %all-to-all-start.6) | async-done | bytes 524320 | tf_op jit(solution)/shard_map/all_to_all | solution.py:267
  304.9 5.5 %collective-permute-done.11 = bf16[256,512]{1,0:T(8,128)(2,1)S(1)} collective-permute-done((bf16[256,512]{1,0:T(8,128)(2,1)S(1)}, bf16[256,512]{1,0:T(8,128)(2,1)S(1)}, u32[]{:S(2)}, u32[]{:S(2)}) %collective-permute-start.11) | collective-permute-done | bytes 262176 | tf_op jit(solution)/shard_map/ppermute | solution.py:139
  311.5 3.6 %collective-permute-done.10 = bf16[256,512]{1,0:T(8,128)(2,1)S(1)} collective-permute-done((bf16[256,512]{1,0:T(8,128)(2,1)S(1)}, bf16[256,512]{1,0:T(8,128)(2,1)S(1)}, u32[]{:S(2)}, u32[]{:S(2)}) %collective-permute-start.10) | collective-permute-done | bytes 262176 | tf_op jit(solution)/shard_map/ppermute | solution.py:139
  (158 shorter events, 69.9 us)
Async XLA Ops:
  1.7 10.2 %collective-permute-start.3 = (bf16[256,512]{1,0:T(8,128)(2,1)S(1)}, bf16[256,512]{1,0:T(8,128)(2,1)S(1)}, u32[]{:S(2)}, u32[]{:S(2)}) collective-permute-start(bf16[256,512]{1,0:T(8,128)(2,1)S(1)} %get-tuple-element.72), channel_id=1, source_target_pairs={{0,1},{1,0},{2,3},{3,2},{4,5},{5,4},{6,7},{7,6},{8,9},{9,8},{10,11... | collective-permute-start | bytes 786440 | tf_op jit(solution)/shard_map/ppermute | solution.py:139
  5.8 10.9 %collective-permute-start.2 = (bf16[256,512]{1,0:T(8,128)(2,1)S(1)}, bf16[256,512]{1,0:T(8,128)(2,1)S(1)}, u32[]{:S(2)}, u32[]{:S(2)}) collective-permute-start(bf16[256,512]{1,0:T(8,128)(2,1)S(1)} %get-tuple-element.70), channel_id=1, source_target_pairs={{0,1},{1,0},{2,3},{3,2},{4,5},{5,4},{6,7},{7,6},{8,9},{9,8},{10,11... | collective-permute-start | bytes 786440 | tf_op jit(solution)/shard_map/ppermute | solution.py:139
  19.5 34.4 %all-to-all-start = ((bf16[16,2,32,4,128]{4,2,3,1,0:T(8,128)(2,1)}), bf16[16,2,32,4,128]{4,2,3,1,0:T(8,128)(2,1)S(1)}, u32[]{:S(2)}, u32[]{:S(2)}) async-start(bf16[16,2,32,4,128]{4,2,3,1,0:T(8,128)(2,1)} %pad_maximum_fusion.4), calls=%async_computation | async-start | bytes 2097152 | tf_op jit(solution)/shard_map/all_to_all | solution.py:218
  27.2 15.0 %copy-start.17 = (bf16[1,256,1024]{2,1,0:T(8,128)(2,1)S(1)}, bf16[1,256,1024]{2,1,0:T(8,128)(2,1)}, u32[]{:S(2)}) copy-start(bf16[1,256,1024]{2,1,0:T(8,128)(2,1)} %get-tuple-element.40) | copy-start | bytes 1572868
  27.2 15.0 %collective-permute-start.4 = (bf16[256,1024]{1,0:T(8,128)(2,1)}, bf16[256,1024]{1,0:T(8,128)(2,1)S(1)}, u32[]{:S(2)}, u32[]{:S(2)}) collective-permute-start(bf16[256,1024]{1,0:T(8,128)(2,1)} %get-tuple-element.39), channel_id=1, source_target_pairs={{0,1},{1,0},{2,3},{3,2},{4,5},{5,4},{6,7},{7,6},{8,9},{9,8},{10,11... | collective-permute-start | bytes 1572872 | tf_op jit(solution)/shard_map/ppermute | solution.py:139
  30.0 22.9 %collective-permute-start.5 = (bf16[256,1024]{1,0:T(8,128)(2,1)}, bf16[256,1024]{1,0:T(8,128)(2,1)S(1)}, u32[]{:S(2)}, u32[]{:S(2)}) collective-permute-start(bf16[256,1024]{1,0:T(8,128)(2,1)} %get-tuple-element.35), channel_id=1, source_target_pairs={{0,1},{1,0},{2,3},{3,2},{4,5},{5,4},{6,7},{7,6},{8,9},{9,8},{10,11... | collective-permute-start | bytes 1572872 | tf_op jit(solution)/shard_map/ppermute | solution.py:139
  56.3 21.0 %copy-start.11 = (bf16[1,256,1024]{2,1,0:T(8,128)(2,1)S(1)}, bf16[1,256,1024]{2,1,0:T(8,128)(2,1)}, u32[]{:S(2)}) copy-start(bf16[1,256,1024]{2,1,0:T(8,128)(2,1)} %get-tuple-element.37) | copy-start | bytes 1572868
  56.3 37.9 %all-to-all-start.1 = ((bf16[16,2,3,2,32,128]{5,4,3,2,1,0:T(8,128)(2,1)}), bf16[16,2,3,2,32,128]{5,4,3,2,1,0:T(8,128)(2,1)S(1)}, u32[]{:S(2)}, u32[]{:S(2)}) async-start(bf16[16,2,3,2,32,128]{5,4,3,2,1,0:T(8,128)(2,1)} %bitcast.175), calls=%async_computation.1 | async-start | bytes 3145728 | tf_op jit(solution)/shard_map/all_to_all | solution.py:244
  62.2 15.1 %collective-permute-start = (bf16[256,1024]{1,0:T(8,128)(2,1)}, bf16[256,1024]{1,0:T(8,128)(2,1)}, u32[]{:S(2)}, u32[]{:S(2)}) collective-permute-start(bf16[256,1024]{1,0:T(8,128)(2,1)} %get-tuple-element.38), channel_id=1, source_target_pairs={{0,1},{1,0},{2,3},{3,2},{4,5},{5,4},{6,7},{7,6},{8,9},{9,8},{10,11... | collective-permute-start | bytes 1572872 | tf_op jit(solution)/shard_map/ppermute | solution.py:139
  63.8 24.2 %collective-permute-start.1 = (bf16[256,1024]{1,0:T(8,128)(2,1)}, bf16[256,1024]{1,0:T(8,128)(2,1)}, u32[]{:S(2)}, u32[]{:S(2)}) collective-permute-start(bf16[256,1024]{1,0:T(8,128)(2,1)} %get-tuple-element.34), channel_id=1, source_target_pairs={{0,1},{1,0},{2,3},{3,2},{4,5},{5,4},{6,7},{7,6},{8,9},{9,8},{10,11... | collective-permute-start | bytes 1572872 | tf_op jit(solution)/shard_map/ppermute | solution.py:139
  64.5 23.5 %copy-start.12 = (bf16[1,256,1024]{2,1,0:T(8,128)(2,1)S(1)}, bf16[1,256,1024]{2,1,0:T(8,128)(2,1)}, u32[]{:S(2)}) copy-start(bf16[1,256,1024]{2,1,0:T(8,128)(2,1)} %get-tuple-element.33) | copy-start | bytes 1572868
  94.2 60.2 %all-to-all-start.2 = ((bf16[16,2,3,2,32,128]{5,4,3,2,1,0:T(8,128)(2,1)}), bf16[16,2,3,2,32,128]{5,4,3,2,1,0:T(8,128)(2,1)}, u32[]{:S(2)}, u32[]{:S(2)}) async-start(bf16[16,2,3,2,32,128]{5,4,3,2,1,0:T(8,128)(2,1)} %bitcast.174), calls=%async_computation.2 | async-start | bytes 3145728 | tf_op jit(solution)/shard_map/all_to_all | solution.py:244
  154.3 58.1 %all-to-all-start.3 = ((bf16[2,3,2,16,32,128]{5,4,2,1,0,3:T(8,128)(2,1)}), bf16[2,3,2,16,32,128]{5,4,2,1,0,3:T(8,128)(2,1)S(1)}, u32[]{:S(2)}, u32[]{:S(2)}) async-start(bf16[2,3,2,16,32,128]{5,4,2,1,0,3:T(8,128)(2,1)} %copy.93), calls=%async_computation.3 | async-start | bytes 3145728 | tf_op jit(solution)/shard_map/all_to_all | solution.py:257
  212.5 38.0 %all-to-all-start.5 = ((bf16[2,3,2,16,32,128]{5,4,2,1,0,3:T(8,128)(2,1)}), bf16[2,3,2,16,32,128]{5,4,2,1,0,3:T(8,128)(2,1)S(1)}, u32[]{:S(2)}, u32[]{:S(2)}) async-start(bf16[2,3,2,16,32,128]{5,4,2,1,0,3:T(8,128)(2,1)} %copy.99), calls=%async_computation.5 | async-start | bytes 3145728 | tf_op jit(solution)/shard_map/all_to_all | solution.py:257
  221.3 40.0 %collective-permute-start.8 = (bf16[256,1024]{1,0:T(8,128)(2,1)}, bf16[256,1024]{1,0:T(8,128)(2,1)}, u32[]{:S(2)}, u32[]{:S(2)}) collective-permute-start(bf16[256,1024]{1,0:T(8,128)(2,1)} %get-tuple-element.49), channel_id=1, source_target_pairs={{0,1},{1,0},{2,3},{3,2},{4,5},{5,4},{6,7},{7,6},{8,9},{9,8},{10,11... | collective-permute-start | bytes 1572872 | tf_op jit(solution)/shard_map/ppermute | solution.py:139
  223.9 39.9 %collective-permute-start.9 = (bf16[256,1024]{1,0:T(8,128)(2,1)}, bf16[256,1024]{1,0:T(8,128)(2,1)}, u32[]{:S(2)}, u32[]{:S(2)}) collective-permute-start(bf16[256,1024]{1,0:T(8,128)(2,1)} %get-tuple-element.51), channel_id=1, source_target_pairs={{0,1},{1,0},{2,3},{3,2},{4,5},{5,4},{6,7},{7,6},{8,9},{9,8},{10,11... | collective-permute-start | bytes 1572872 | tf_op jit(solution)/shard_map/ppermute | solution.py:139
  225.4 40.8 %collective-permute-start.6 = (bf16[256,1024]{1,0:T(8,128)(2,1)}, bf16[256,1024]{1,0:T(8,128)(2,1)}, u32[]{:S(2)}, u32[]{:S(2)}) collective-permute-start(bf16[256,1024]{1,0:T(8,128)(2,1)} %get-tuple-element.57), channel_id=1, source_target_pairs={{0,1},{1,0},{2,3},{3,2},{4,5},{5,4},{6,7},{7,6},{8,9},{9,8},{10,11... | collective-permute-start | bytes 1572872 | tf_op jit(solution)/shard_map/ppermute | solution.py:139
  231.3 28.3 %copy-start.19 = (bf16[2,256,1024]{2,1,0:T(8,128)(2,1)S(1)}, bf16[2,256,1024]{2,1,0:T(8,128)(2,1)}, u32[]{:S(2)}) copy-start(bf16[2,256,1024]{2,1,0:T(8,128)(2,1)} %get-tuple-element.24) | copy-start | bytes 3145732
  231.5 29.8 %copy-start.6 = (bf16[1,256,1024]{2,1,0:T(8,128)(2,1)S(1)}, bf16[1,256,1024]{2,1,0:T(8,128)(2,1)}, u32[]{:S(2)}) copy-start(bf16[1,256,1024]{2,1,0:T(8,128)(2,1)} %get-tuple-element.50) | copy-start | bytes 1572868
  250.5 27.3 %all-to-all-start.4 = ((bf16[2,16,2,32,128]{4,3,2,0,1:T(8,128)(2,1)}), bf16[2,16,2,32,128]{4,3,2,0,1:T(8,128)(2,1)}, u32[]{:S(2)}, u32[]{:S(2)}) async-start(bf16[2,16,2,32,128]{4,3,2,0,1:T(8,128)(2,1)} %copy.95), calls=%async_computation.4 | async-start | bytes 1048576 | tf_op jit(solution)/shard_map/all_to_all | solution.py:267
  259.7 14.2 %collective-permute-start.7 = (bf16[256,1024]{1,0:T(8,128)(2,1)S(1)}, bf16[256,1024]{1,0:T(8,128)(2,1)S(1)}, u32[]{:S(2)}, u32[]{:S(2)}) collective-permute-start(bf16[256,1024]{1,0:T(8,128)(2,1)S(1)} %get-tuple-element.59), channel_id=1, source_target_pairs={{0,1},{1,0},{2,3},{3,2},{4,5},{5,4},{6,7},{7,6},{8,9},{9,8},{10,11... | collective-permute-start | bytes 1572872 | tf_op jit(solution)/shard_map/ppermute | solution.py:139
  277.8 20.2 %all-to-all-start.6 = ((bf16[2,16,2,32,128]{4,3,2,0,1:T(8,128)(2,1)}), bf16[2,16,2,32,128]{4,3,2,0,1:T(8,128)(2,1)S(1)}, u32[]{:S(2)}, u32[]{:S(2)}) async-start(bf16[2,16,2,32,128]{4,3,2,0,1:T(8,128)(2,1)} %copy.101), calls=%async_computation.6 | async-start | bytes 1048576 | tf_op jit(solution)/shard_map/all_to_all | solution.py:267
  301.2 9.2 %collective-permute-start.11 = (bf16[256,512]{1,0:T(8,128)(2,1)S(1)}, bf16[256,512]{1,0:T(8,128)(2,1)S(1)}, u32[]{:S(2)}, u32[]{:S(2)}) collective-permute-start(bf16[256,512]{1,0:T(8,128)(2,1)S(1)} %get-tuple-element.63), channel_id=1, source_target_pairs={{0,1},{1,0},{2,3},{3,2},{4,5},{5,4},{6,7},{7,6},{8,9},{9,8},{10,11... | collective-permute-start | bytes 786440 | tf_op jit(solution)/shard_map/ppermute | solution.py:139
  302.8 12.3 %collective-permute-start.10 = (bf16[256,512]{1,0:T(8,128)(2,1)S(1)}, bf16[256,512]{1,0:T(8,128)(2,1)S(1)}, u32[]{:S(2)}, u32[]{:S(2)}) collective-permute-start(bf16[256,512]{1,0:T(8,128)(2,1)S(1)} %get-tuple-element.67), channel_id=1, source_target_pairs={{0,1},{1,0},{2,3},{3,2},{4,5},{5,4},{6,7},{7,6},{8,9},{9,8},{10,11... | collective-permute-start | bytes 786440 | tf_op jit(solution)/shard_map/ppermute | solution.py:139
  (22 other events, 96.8 us)

commit v15 on v12

--- a/solution.py
+++ b/solution.py
@@ -15,7 +15,7 @@
 
 def attention_kernel(
     live_ref, tp_ref, q_ref, do_ref, kvs_ref, ko_ref, vo_ref,
-    o_ref, dq_ref, dsel_ref, dko_ref, dvo_ref, acc_ref, *, slot_count, row_tile, scale, tiles, own_rows
+    o_ref, dq_ref, dsel_ref, dko_ref, dvo_ref, acc_ref, kt_ref, vt_ref, *, slot_count, row_tile, scale, tiles, own_rows
 ):
     g = pl.program_id(0)
     h = pl.program_id(1)
@@ -24,18 +24,24 @@
     @pl.when((h == 0) & (t == 0))
     def _():
         acc_ref[...] = jnp.zeros(acc_ref.shape, acc_ref.dtype)
+        for r in range(slot_count - 1):
+            kt_ref[r] = kvs_ref[r, 0].T
+            vt_ref[r] = kvs_ref[r, 1].T
+        kt_ref[slot_count - 1] = ko_ref[...].T
+        vt_ref[slot_count - 1] = vo_ref[...].T
 
     def run(own_width):
         q = q_ref[...]
         do = do_ref[...]
         keys = [kvs_ref[r, 0] for r in range(slot_count - 1)] + [ko_ref[:own_width]]
         values = [kvs_ref[r, 1] for r in range(slot_count - 1)] + [vo_ref[:own_width]]
-        trans_b = (((1,), (1,)), ((), ()))
+        keys_t = [kt_ref[r] for r in range(slot_count - 1)] + [kt_ref[slot_count - 1, :, :own_width]]
+        values_t = [vt_ref[r] for r in range(slot_count - 1)] + [vt_ref[slot_count - 1, :, :own_width]]
         q_t = q.T
         do_t = do.T
         scores = []
         for r in range(slot_count):
-            s = lax.dot_general(q, keys[r], trans_b, preferred_element_type=jnp.float32) * scale
+            s = jnp.dot(q, keys_t[r], preferred_element_type=jnp.float32) * scale
             live = live_ref[g * slot_count + r] > 0
             if r == slot_count - 1:
                 row = t * row_tile + lax.broadcasted_iota(jnp.int32, s.shape, 0)
@@ -62,7 +68,7 @@
         delta = jnp.sum(do.astype(jnp.float32) * out_low.astype(jnp.float32), axis=1, keepdims=True)
         grad_q = None
         for r in range(slot_count):
-            grad_p = lax.dot_general(do, values[r], trans_b, preferred_element_type=jnp.float32)
+            grad_p = jnp.dot(do, values_t[r], preferred_element_type=jnp.float32)
             grad_s = (probs[r] * (grad_p - delta)).astype(jnp.bfloat16)
             part = jnp.dot(grad_s, keys[r], preferred_element_type=jnp.float32)
             grad_q = part if grad_q is None else grad_q + part
@@ -116,7 +122,11 @@
             grid=grid,
             in_specs=[in_block, in_block, sel_block, own_in, own_in],
             out_specs=[out_block, out_block, sel_block, own_out, own_out],
-            scratch_shapes=[pltpu.VMEM((slot_count, 2, HD, BLK), jnp.float32)],
+            scratch_shapes=[
+                pltpu.VMEM((slot_count, 2, HD, BLK), jnp.float32),
+                pltpu.VMEM((slot_count, HD, BLK), jnp.bfloat16),
+                pltpu.VMEM((slot_count, HD, BLK), jnp.bfloat16),
+            ],
         ),
         out_shape=[
             jax.ShapeDtypeStruct((tp_size, row_tile, q_cols), jnp.bfloat16),

time: 318 us -> 318 us (level)
  no operation moved by 1% of the time
where the time goes in v15:
time: 318 us; the launch traced here: 316 us
  waiting for transfers between devices  98 us (31%)
  Pallas kernels  89.9 us (28%)
  starting transfers between devices  63.2 us (20%)
  local copies, waits for them, and re-layouts  35.6 us (11%)
  other arithmetic  27.8 us (9%)
    pallas_call x2, Pallas kernels, attention(): pl.pallas_call(kernel, grid_spec=pltpu.PrefetchScalarGridSpec(num_scalar_...  89.9 us
    ppermute x12, waiting for transfers between devices, shift(): lax.ppermute(x, axis, perm=[(s, (s + step) % size) for s in range(size)])  66.5 us
    all_to_all x2, waiting for transfers between devices, body(): lax.all_to_all(send_back, 'ctx', split_axis=3, concat_axis=1, tiled=True)  18.1 us
    all_to_all x2, starting transfers between devices, body(): got = lax.all_to_all(send, 'ctx', split_axis=0, concat_axis=4, tiled=True)  15 us
    ppermute x12, starting transfers between devices, shift(): lax.ppermute(x, axis, perm=[(s, (s + step) % size) for s in range(size)])  15 us
    all_to_all x2, starting transfers between devices, body(): back = lax.all_to_all(owner, 'ctx', split_axis=1, concat_axis=3, tiled=True)  14.9 us
    all_to_all x2, starting transfers between devices, body(): lax.all_to_all(send_back, 'ctx', split_axis=3, concat_axis=1, tiled=True)  12 us
    all_to_all x2, waiting for transfers between devices, body(): back = lax.all_to_all(owner, 'ctx', split_axis=1, concat_axis=3, tiled=True)  11.7 us
  transfers between devices with their start and end apart: 19, of which 12 were waited for; matrix products, arithmetic and copies ran while one was open for 17% of the time, Pallas kernels for 28%

profile of v15, /device:TPU:0, one launch (start us, length us, event | category | flops | bytes accessed | tf_op | source)
XLA Modules:
  0.0 316.5 jit_solution(1736528843183911593)
XLA Ops:
  1.7 3.0 collective-permute-start.3
  6.0 5.9 %collective-permute-done.3 = bf16[256,512]{1,0:T(8,128)(2,1)S(1)} collective-permute-done((bf16[256,512]{1,0:T(8,128)(2,1)S(1)}, bf16[256,512]{1,0:T(8,128)(2,1)S(1)}, u32[]{:S(2)}, u32[]{:S(2)}) %collective-permute-start.3) | collective-permute-done | bytes 262176 | tf_op jit(solution)/shard_map/ppermute | solution.py:150
  12.5 4.1 %collective-permute-done.2 = bf16[256,512]{1,0:T(8,128)(2,1)S(1)} collective-permute-done((bf16[256,512]{1,0:T(8,128)(2,1)S(1)}, bf16[256,512]{1,0:T(8,128)(2,1)S(1)}, u32[]{:S(2)}, u32[]{:S(2)}) %collective-permute-start.2) | collective-permute-done | bytes 262176 | tf_op jit(solution)/shard_map/ppermute | solution.py:150
  19.5 6.3 %all-to-all-start = ((bf16[16,2,32,4,128]{4,2,3,1,0:T(8,128)(2,1)}), bf16[16,2,32,4,128]{4,2,3,1,0:T(8,128)(2,1)S(1)}, u32[]{:S(2)}, u32[]{:S(2)}) async-start(bf16[16,2,32,4,128]{4,2,3,1,0:T(8,128)(2,1)} %pad_maximum_fusion.4), calls=%async_computation | async-start | bytes 2097152 | tf_op jit(solution)/shard_map/all_to_all | solution.py:229
  31.2 10.9 %collective-permute-done.4 = bf16[256,1024]{1,0:T(8,128)(2,1)S(1)} collective-permute-done((bf16[256,1024]{1,0:T(8,128)(2,1)}, bf16[256,1024]{1,0:T(8,128)(2,1)S(1)}, u32[]{:S(2)}, u32[]{:S(2)}) %collective-permute-start.4) | collective-permute-done | bytes 524320 | tf_op jit(solution)/shard_map/ppermute | solution.py:150
  43.3 9.6 %collective-permute-done.5 = bf16[256,1024]{1,0:T(8,128)(2,1)S(1)} collective-permute-done((bf16[256,1024]{1,0:T(8,128)(2,1)}, bf16[256,1024]{1,0:T(8,128)(2,1)S(1)}, u32[]{:S(2)}, u32[]{:S(2)}) %collective-permute-start.5) | collective-permute-done | bytes 524320 | tf_op jit(solution)/shard_map/ppermute | solution.py:150
  56.3 5.9 %all-to-all-start.1 = ((bf16[16,2,3,2,32,128]{5,4,3,2,1,0:T(8,128)(2,1)}), bf16[16,2,3,2,32,128]{5,4,3,2,1,0:T(8,128)(2,1)S(1)}, u32[]{:S(2)}, u32[]{:S(2)}) async-start(bf16[16,2,3,2,32,128]{5,4,3,2,1,0:T(8,128)(2,1)} %bitcast.175), calls=%async_computation.1 | async-start | bytes 3145728 | tf_op jit(solution)/shard_map/all_to_all | solution.py:255
  64.5 12.8 %collective-permute-done = bf16[256,1024]{1,0:T(8,128)(2,1)} collective-permute-done((bf16[256,1024]{1,0:T(8,128)(2,1)}, bf16[256,1024]{1,0:T(8,128)(2,1)}, u32[]{:S(2)}, u32[]{:S(2)}) %collective-permute-start) | collective-permute-done | bytes 524320 | tf_op jit(solution)/shard_map/ppermute | solution.py:150
  79.4 8.6 %collective-permute-done.1 = bf16[256,1024]{1,0:T(8,128)(2,1)} collective-permute-done((bf16[256,1024]{1,0:T(8,128)(2,1)}, bf16[256,1024]{1,0:T(8,128)(2,1)}, u32[]{:S(2)}, u32[]{:S(2)}) %collective-permute-start.1) | collective-permute-done | bytes 524320 | tf_op jit(solution)/shard_map/ppermute | solution.py:150
  94.2 9.2 %all-to-all-start.2 = ((bf16[16,2,3,2,32,128]{5,4,3,2,1,0:T(8,128)(2,1)}), bf16[16,2,3,2,32,128]{5,4,3,2,1,0:T(8,128)(2,1)}, u32[]{:S(2)}, u32[]{:S(2)}) async-start(bf16[16,2,3,2,32,128]{5,4,3,2,1,0:T(8,128)(2,1)} %bitcast.174), calls=%async_computation.2 | async-start | bytes 3145728 | tf_op jit(solution)/shard_map/all_to_all | solution.py:255
  105.8 44.9 %shard_map.93 = (bf16[2,256,1024]{2,1,0:T(8,128)(2,1)}, bf16[2,256,1024]{2,1,0:T(8,128)(2,1)}, f32[2,3,2,512,128]{4,3,2,1,0:T(8,128)}, f32[512,256]{1,0:T(8,128)}, f32[512,256]{1,0:T(8,128)}) custom-call(s32[8]{0:T(128)} %reshape.114.live_ref, s32[1]{0:T(128)} %bitcast.2.tp_ref, bf16[2,256,1024]{2,1,0:T(8,128)(2,1)} %pad_maximum_fusion.2.q_ref, ...), custom_call_target="tpu_custom_call" | custom-call | flops 12884901888 | bytes 10485760 | tf_op jit(solution)/shard_map/pallas_call | solution.py:118
  154.5 6.0 %all-to-all-start.3 = ((bf16[2,3,2,16,32,128]{5,4,2,1,0,3:T(8,128)(2,1)}), bf16[2,3,2,16,32,128]{5,4,2,1,0,3:T(8,128)(2,1)S(1)}, u32[]{:S(2)}, u32[]{:S(2)}) async-start(bf16[2,3,2,16,32,128]{5,4,2,1,0,3:T(8,128)(2,1)} %copy.93), calls=%async_computation.3 | async-start | bytes 3145728 | tf_op jit(solution)/shard_map/all_to_all | solution.py:268
  161.1 2.9 copy.91
  164.0 45.0 %shard_map.94 = (bf16[2,256,1024]{2,1,0:T(8,128)(2,1)}, bf16[2,256,1024]{2,1,0:T(8,128)(2,1)}, f32[2,3,2,512,128]{4,3,2,1,0:T(8,128)}, f32[512,256]{1,0:T(8,128)}, f32[512,256]{1,0:T(8,128)}) custom-call(s32[8]{0:T(128)} %reshape.118.live_ref, s32[1]{0:T(128)} %bitcast.2.tp_ref, bf16[2,256,1024]{2,1,0:T(8,128)(2,1)} %pad_maximum_fusion.5.q_ref, ...), custom_call_target="tpu_custom_call" | custom-call | flops 12884901888 | bytes 10485760 | tf_op jit(solution)/shard_map/pallas_call | solution.py:118
  212.8 6.0 %all-to-all-start.5 = ((bf16[2,3,2,16,32,128]{5,4,2,1,0,3:T(8,128)(2,1)}), bf16[2,3,2,16,32,128]{5,4,2,1,0,3:T(8,128)(2,1)S(1)}, u32[]{:S(2)}, u32[]{:S(2)}) async-start(bf16[2,3,2,16,32,128]{5,4,2,1,0,3:T(8,128)(2,1)} %copy.99), calls=%async_computation.5 | async-start | bytes 3145728 | tf_op jit(solution)/shard_map/all_to_all | solution.py:268
  228.8 2.5 reshape.120
  232.7 18.1 %all-to-all-done.5 = bf16[2,3,2,16,32,128]{5,4,2,1,0,3:T(8,128)(2,1)S(1)} async-done(((bf16[2,3,2,16,32,128]{5,4,2,1,0,3:T(8,128)(2,1)}), bf16[2,3,2,16,32,128]{5,4,2,1,0,3:T(8,128)(2,1)S(1)}, u32[]{:S(2)}, u32[]{:S(2)}) %all-to-all-start.5) | async-done | bytes 1572896 | tf_op jit(solution)/shard_map/all_to_all | solution.py:268
  250.8 9.2 %all-to-all-start.4 = ((bf16[2,16,2,32,128]{4,3,2,0,1:T(8,128)(2,1)}), bf16[2,16,2,32,128]{4,3,2,0,1:T(8,128)(2,1)}, u32[]{:S(2)}, u32[]{:S(2)}) async-start(bf16[2,16,2,32,128]{4,3,2,0,1:T(8,128)(2,1)} %copy.95), calls=%async_computation.4 | async-start | bytes 1048576 | tf_op jit(solution)/shard_map/all_to_all | solution.py:278
  261.7 2.5 fusion.7
  269.0 5.3 %collective-permute-done.7 = bf16[256,1024]{1,0:T(8,128)(2,1)S(1)} collective-permute-done((bf16[256,1024]{1,0:T(8,128)(2,1)S(1)}, bf16[256,1024]{1,0:T(8,128)(2,1)S(1)}, u32[]{:S(2)}, u32[]{:S(2)}) %collective-permute-start.7) | collective-permute-done | bytes 524320 | tf_op jit(solution)/shard_map/ppermute | solution.py:150
  278.1 5.8 %all-to-all-start.6 = ((bf16[2,16,2,32,128]{4,3,2,0,1:T(8,128)(2,1)}), bf16[2,16,2,32,128]{4,3,2,0,1:T(8,128)(2,1)S(1)}, u32[]{:S(2)}, u32[]{:S(2)}) async-start(bf16[2,16,2,32,128]{4,3,2,0,1:T(8,128)(2,1)} %copy.101), calls=%async_computation.6 | async-start | bytes 1048576 | tf_op jit(solution)/shard_map/all_to_all | solution.py:278
  286.6 11.7 %all-to-all-done.6 = bf16[2,16,2,32,128]{4,3,2,0,1:T(8,128)(2,1)S(1)} async-done(((bf16[2,16,2,32,128]{4,3,2,0,1:T(8,128)(2,1)}), bf16[2,16,2,32,128]{4,3,2,0,1:T(8,128)(2,1)S(1)}, u32[]{:S(2)}, u32[]{:S(2)}) %all-to-all-start.6) | async-done | bytes 524320 | tf_op jit(solution)/shard_map/all_to_all | solution.py:278
  305.2 5.5 %collective-permute-done.11 = bf16[256,512]{1,0:T(8,128)(2,1)S(1)} collective-permute-done((bf16[256,512]{1,0:T(8,128)(2,1)S(1)}, bf16[256,512]{1,0:T(8,128)(2,1)S(1)}, u32[]{:S(2)}, u32[]{:S(2)}) %collective-permute-start.11) | collective-permute-done | bytes 262176 | tf_op jit(solution)/shard_map/ppermute | solution.py:150
  311.8 3.6 %collective-permute-done.10 = bf16[256,512]{1,0:T(8,128)(2,1)S(1)} collective-permute-done((bf16[256,512]{1,0:T(8,128)(2,1)S(1)}, bf16[256,512]{1,0:T(8,128)(2,1)S(1)}, u32[]{:S(2)}, u32[]{:S(2)}) %collective-permute-start.10) | collective-permute-done | bytes 262176 | tf_op jit(solution)/shard_map/ppermute | solution.py:150
  (158 shorter events, 69.9 us)
Async XLA Ops:
  1.7 10.2 %collective-permute-start.3 = (bf16[256,512]{1,0:T(8,128)(2,1)S(1)}, bf16[256,512]{1,0:T(8,128)(2,1)S(1)}, u32[]{:S(2)}, u32[]{:S(2)}) collective-permute-start(bf16[256,512]{1,0:T(8,128)(2,1)S(1)} %get-tuple-element.72), channel_id=1, source_target_pairs={{0,1},{1,0},{2,3},{3,2},{4,5},{5,4},{6,7},{7,6},{8,9},{9,8},{10,11... | collective-permute-start | bytes 786440 | tf_op jit(solution)/shard_map/ppermute | solution.py:150
  5.8 10.9 %collective-permute-start.2 = (bf16[256,512]{1,0:T(8,128)(2,1)S(1)}, bf16[256,512]{1,0:T(8,128)(2,1)S(1)}, u32[]{:S(2)}, u32[]{:S(2)}) collective-permute-start(bf16[256,512]{1,0:T(8,128)(2,1)S(1)} %get-tuple-element.70), channel_id=1, source_target_pairs={{0,1},{1,0},{2,3},{3,2},{4,5},{5,4},{6,7},{7,6},{8,9},{9,8},{10,11... | collective-permute-start | bytes 786440 | tf_op jit(solution)/shard_map/ppermute | solution.py:150
  19.5 34.4 %all-to-all-start = ((bf16[16,2,32,4,128]{4,2,3,1,0:T(8,128)(2,1)}), bf16[16,2,32,4,128]{4,2,3,1,0:T(8,128)(2,1)S(1)}, u32[]{:S(2)}, u32[]{:S(2)}) async-start(bf16[16,2,32,4,128]{4,2,3,1,0:T(8,128)(2,1)} %pad_maximum_fusion.4), calls=%async_computation | async-start | bytes 2097152 | tf_op jit(solution)/shard_map/all_to_all | solution.py:229
  27.2 15.0 %copy-start.17 = (bf16[1,256,1024]{2,1,0:T(8,128)(2,1)S(1)}, bf16[1,256,1024]{2,1,0:T(8,128)(2,1)}, u32[]{:S(2)}) copy-start(bf16[1,256,1024]{2,1,0:T(8,128)(2,1)} %get-tuple-element.40) | copy-start | bytes 1572868
  27.2 15.0 %collective-permute-start.4 = (bf16[256,1024]{1,0:T(8,128)(2,1)}, bf16[256,1024]{1,0:T(8,128)(2,1)S(1)}, u32[]{:S(2)}, u32[]{:S(2)}) collective-permute-start(bf16[256,1024]{1,0:T(8,128)(2,1)} %get-tuple-element.39), channel_id=1, source_target_pairs={{0,1},{1,0},{2,3},{3,2},{4,5},{5,4},{6,7},{7,6},{8,9},{9,8},{10,11... | collective-permute-start | bytes 1572872 | tf_op jit(solution)/shard_map/ppermute | solution.py:150
  30.0 22.9 %collective-permute-start.5 = (bf16[256,1024]{1,0:T(8,128)(2,1)}, bf16[256,1024]{1,0:T(8,128)(2,1)S(1)}, u32[]{:S(2)}, u32[]{:S(2)}) collective-permute-start(bf16[256,1024]{1,0:T(8,128)(2,1)} %get-tuple-element.35), channel_id=1, source_target_pairs={{0,1},{1,0},{2,3},{3,2},{4,5},{5,4},{6,7},{7,6},{8,9},{9,8},{10,11... | collective-permute-start | bytes 1572872 | tf_op jit(solution)/shard_map/ppermute | solution.py:150
  56.3 21.0 %copy-start.11 = (bf16[1,256,1024]{2,1,0:T(8,128)(2,1)S(1)}, bf16[1,256,1024]{2,1,0:T(8,128)(2,1)}, u32[]{:S(2)}) copy-start(bf16[1,256,1024]{2,1,0:T(8,128)(2,1)} %get-tuple-element.37) | copy-start | bytes 1572868
  56.3 37.9 %all-to-all-start.1 = ((bf16[16,2,3,2,32,128]{5,4,3,2,1,0:T(8,128)(2,1)}), bf16[16,2,3,2,32,128]{5,4,3,2,1,0:T(8,128)(2,1)S(1)}, u32[]{:S(2)}, u32[]{:S(2)}) async-start(bf16[16,2,3,2,32,128]{5,4,3,2,1,0:T(8,128)(2,1)} %bitcast.175), calls=%async_computation.1 | async-start | bytes 3145728 | tf_op jit(solution)/shard_map/all_to_all | solution.py:255
  62.2 15.1 %collective-permute-start = (bf16[256,1024]{1,0:T(8,128)(2,1)}, bf16[256,1024]{1,0:T(8,128)(2,1)}, u32[]{:S(2)}, u32[]{:S(2)}) collective-permute-start(bf16[256,1024]{1,0:T(8,128)(2,1)} %get-tuple-element.38), channel_id=1, source_target_pairs={{0,1},{1,0},{2,3},{3,2},{4,5},{5,4},{6,7},{7,6},{8,9},{9,8},{10,11... | collective-permute-start | bytes 1572872 | tf_op jit(solution)/shard_map/ppermute | solution.py:150
  63.8 24.2 %collective-permute-start.1 = (bf16[256,1024]{1,0:T(8,128)(2,1)}, bf16[256,1024]{1,0:T(8,128)(2,1)}, u32[]{:S(2)}, u32[]{:S(2)}) collective-permute-start(bf16[256,1024]{1,0:T(8,128)(2,1)} %get-tuple-element.34), channel_id=1, source_target_pairs={{0,1},{1,0},{2,3},{3,2},{4,5},{5,4},{6,7},{7,6},{8,9},{9,8},{10,11... | collective-permute-start | bytes 1572872 | tf_op jit(solution)/shard_map/ppermute | solution.py:150
  64.5 23.5 %copy-start.12 = (bf16[1,256,1024]{2,1,0:T(8,128)(2,1)S(1)}, bf16[1,256,1024]{2,1,0:T(8,128)(2,1)}, u32[]{:S(2)}) copy-start(bf16[1,256,1024]{2,1,0:T(8,128)(2,1)} %get-tuple-element.33) | copy-start | bytes 1572868
  94.2 60.3 %all-to-all-start.2 = ((bf16[16,2,3,2,32,128]{5,4,3,2,1,0:T(8,128)(2,1)}), bf16[16,2,3,2,32,128]{5,4,3,2,1,0:T(8,128)(2,1)}, u32[]{:S(2)}, u32[]{:S(2)}) async-start(bf16[16,2,3,2,32,128]{5,4,3,2,1,0:T(8,128)(2,1)} %bitcast.174), calls=%async_computation.2 | async-start | bytes 3145728 | tf_op jit(solution)/shard_map/all_to_all | solution.py:255
  154.5 58.3 %all-to-all-start.3 = ((bf16[2,3,2,16,32,128]{5,4,2,1,0,3:T(8,128)(2,1)}), bf16[2,3,2,16,32,128]{5,4,2,1,0,3:T(8,128)(2,1)S(1)}, u32[]{:S(2)}, u32[]{:S(2)}) async-start(bf16[2,3,2,16,32,128]{5,4,2,1,0,3:T(8,128)(2,1)} %copy.93), calls=%async_computation.3 | async-start | bytes 3145728 | tf_op jit(solution)/shard_map/all_to_all | solution.py:268
  212.8 38.0 %all-to-all-start.5 = ((bf16[2,3,2,16,32,128]{5,4,2,1,0,3:T(8,128)(2,1)}), bf16[2,3,2,16,32,128]{5,4,2,1,0,3:T(8,128)(2,1)S(1)}, u32[]{:S(2)}, u32[]{:S(2)}) async-start(bf16[2,3,2,16,32,128]{5,4,2,1,0,3:T(8,128)(2,1)} %copy.99), calls=%async_computation.5 | async-start | bytes 3145728 | tf_op jit(solution)/shard_map/all_to_all | solution.py:268
  221.6 40.0 %collective-permute-start.8 = (bf16[256,1024]{1,0:T(8,128)(2,1)}, bf16[256,1024]{1,0:T(8,128)(2,1)}, u32[]{:S(2)}, u32[]{:S(2)}) collective-permute-start(bf16[256,1024]{1,0:T(8,128)(2,1)} %get-tuple-element.49), channel_id=1, source_target_pairs={{0,1},{1,0},{2,3},{3,2},{4,5},{5,4},{6,7},{7,6},{8,9},{9,8},{10,11... | collective-permute-start | bytes 1572872 | tf_op jit(solution)/shard_map/ppermute | solution.py:150
  224.2 39.9 %collective-permute-start.9 = (bf16[256,1024]{1,0:T(8,128)(2,1)}, bf16[256,1024]{1,0:T(8,128)(2,1)}, u32[]{:S(2)}, u32[]{:S(2)}) collective-permute-start(bf16[256,1024]{1,0:T(8,128)(2,1)} %get-tuple-element.51), channel_id=1, source_target_pairs={{0,1},{1,0},{2,3},{3,2},{4,5},{5,4},{6,7},{7,6},{8,9},{9,8},{10,11... | collective-permute-start | bytes 1572872 | tf_op jit(solution)/shard_map/ppermute | solution.py:150
  225.8 40.8 %collective-permute-start.6 = (bf16[256,1024]{1,0:T(8,128)(2,1)}, bf16[256,1024]{1,0:T(8,128)(2,1)}, u32[]{:S(2)}, u32[]{:S(2)}) collective-permute-start(bf16[256,1024]{1,0:T(8,128)(2,1)} %get-tuple-element.57), channel_id=1, source_target_pairs={{0,1},{1,0},{2,3},{3,2},{4,5},{5,4},{6,7},{7,6},{8,9},{9,8},{10,11... | collective-permute-start | bytes 1572872 | tf_op jit(solution)/shard_map/ppermute | solution.py:150
  231.7 28.3 %copy-start.19 = (bf16[2,256,1024]{2,1,0:T(8,128)(2,1)S(1)}, bf16[2,256,1024]{2,1,0:T(8,128)(2,1)}, u32[]{:S(2)}) copy-start(bf16[2,256,1024]{2,1,0:T(8,128)(2,1)} %get-tuple-element.24) | copy-start | bytes 3145732
  231.8 29.8 %copy-start.6 = (bf16[1,256,1024]{2,1,0:T(8,128)(2,1)S(1)}, bf16[1,256,1024]{2,1,0:T(8,128)(2,1)}, u32[]{:S(2)}) copy-start(bf16[1,256,1024]{2,1,0:T(8,128)(2,1)} %get-tuple-element.50) | copy-start | bytes 1572868
  250.8 27.3 %all-to-all-start.4 = ((bf16[2,16,2,32,128]{4,3,2,0,1:T(8,128)(2,1)}), bf16[2,16,2,32,128]{4,3,2,0,1:T(8,128)(2,1)}, u32[]{:S(2)}, u32[]{:S(2)}) async-start(bf16[2,16,2,32,128]{4,3,2,0,1:T(8,128)(2,1)} %copy.95), calls=%async_computation.4 | async-start | bytes 1048576 | tf_op jit(solution)/shard_map/all_to_all | solution.py:278
  260.0 14.2 %collective-permute-start.7 = (bf16[256,1024]{1,0:T(8,128)(2,1)S(1)}, bf16[256,1024]{1,0:T(8,128)(2,1)S(1)}, u32[]{:S(2)}, u32[]{:S(2)}) collective-permute-start(bf16[256,1024]{1,0:T(8,128)(2,1)S(1)} %get-tuple-element.59), channel_id=1, source_target_pairs={{0,1},{1,0},{2,3},{3,2},{4,5},{5,4},{6,7},{7,6},{8,9},{9,8},{10,11... | collective-permute-start | bytes 1572872 | tf_op jit(solution)/shard_map/ppermute | solution.py:150
  278.1 20.2 %all-to-all-start.6 = ((bf16[2,16,2,32,128]{4,3,2,0,1:T(8,128)(2,1)}), bf16[2,16,2,32,128]{4,3,2,0,1:T(8,128)(2,1)S(1)}, u32[]{:S(2)}, u32[]{:S(2)}) async-start(bf16[2,16,2,32,128]{4,3,2,0,1:T(8,128)(2,1)} %copy.101), calls=%async_computation.6 | async-start | bytes 1048576 | tf_op jit(solution)/shard_map/all_to_all | solution.py:278
  301.5 9.2 %collective-permute-start.11 = (bf16[256,512]{1,0:T(8,128)(2,1)S(1)}, bf16[256,512]{1,0:T(8,128)(2,1)S(1)}, u32[]{:S(2)}, u32[]{:S(2)}) collective-permute-start(bf16[256,512]{1,0:T(8,128)(2,1)S(1)} %get-tuple-element.63), channel_id=1, source_target_pairs={{0,1},{1,0},{2,3},{3,2},{4,5},{5,4},{6,7},{7,6},{8,9},{9,8},{10,11... | collective-permute-start | bytes 786440 | tf_op jit(solution)/shard_map/ppermute | solution.py:150
  303.1 12.3 %collective-permute-start.10 = (bf16[256,512]{1,0:T(8,128)(2,1)S(1)}, bf16[256,512]{1,0:T(8,128)(2,1)S(1)}, u32[]{:S(2)}, u32[]{:S(2)}) collective-permute-start(bf16[256,512]{1,0:T(8,128)(2,1)S(1)} %get-tuple-element.67), channel_id=1, source_target_pairs={{0,1},{1,0},{2,3},{3,2},{4,5},{5,4},{6,7},{7,6},{8,9},{9,8},{10,11... | collective-permute-start | bytes 786440 | tf_op jit(solution)/shard_map/ppermute | solution.py:150
  (22 other events, 96.8 us)

commit v16 on v15

--- a/solution.py
+++ b/solution.py
@@ -73,7 +73,7 @@
             part = jnp.dot(grad_s, keys[r], preferred_element_type=jnp.float32)
             grad_q = part if grad_q is None else grad_q + part
             width = keys[r].shape[0]
-            acc_ref[r, 0, :, :width] += jnp.dot(q_t, grad_s, preferred_element_type=jnp.float32) * scale
+            acc_ref[r, 0, :, :width] += jnp.dot(q_t, grad_s, preferred_element_type=jnp.float32)
             acc_ref[r, 1, :, :width] += jnp.dot(do_t, probs_low[r], preferred_element_type=jnp.float32)
         dq_ref[...] = (grad_q * scale).astype(jnp.bfloat16)
 
@@ -84,9 +84,9 @@
     @pl.when((h == pl.num_programs(1) - 1) & (t == pl.num_programs(2) - 1))
     def _():
         for r in range(slot_count - 1):
-            dsel_ref[r, 0] = acc_ref[r, 0].T
+            dsel_ref[r, 0] = acc_ref[r, 0].T * scale
             dsel_ref[r, 1] = acc_ref[r, 1].T
-        dko_ref[...] = acc_ref[slot_count - 1, 0].T
+        dko_ref[...] = acc_ref[slot_count - 1, 0].T * scale
         dvo_ref[...] = acc_ref[slot_count - 1, 1].T
 
 

time: 318 us -> 318 us (level)
  no operation moved by 1% of the time
where the time goes in v16:
time: 318 us; the launch traced here: 316 us
  waiting for transfers between devices  98 us (31%)
  Pallas kernels  89.9 us (28%)
  starting transfers between devices  63.2 us (20%)
  local copies, waits for them, and re-layouts  35.6 us (11%)
  other arithmetic  27.8 us (9%)
    pallas_call x2, Pallas kernels, attention(): pl.pallas_call(kernel, grid_spec=pltpu.PrefetchScalarGridSpec(num_scalar_...  89.9 us
    ppermute x12, waiting for transfers between devices, shift(): lax.ppermute(x, axis, perm=[(s, (s + step) % size) for s in range(size)])  66.5 us
    all_to_all x2, waiting for transfers between devices, body(): lax.all_to_all(send_back, 'ctx', split_axis=3, concat_axis=1, tiled=True)  18.1 us
    all_to_all x2, starting transfers between devices, body(): got = lax.all_to_all(send, 'ctx', split_axis=0, concat_axis=4, tiled=True)  15 us
    ppermute x12, starting transfers between devices, shift(): lax.ppermute(x, axis, perm=[(s, (s + step) % size) for s in range(size)])  15 us
    all_to_all x2, starting transfers between devices, body(): back = lax.all_to_all(owner, 'ctx', split_axis=1, concat_axis=3, tiled=True)  14.9 us
    all_to_all x2, starting transfers between devices, body(): lax.all_to_all(send_back, 'ctx', split_axis=3, concat_axis=1, tiled=True)  12 us
    all_to_all x2, waiting for transfers between devices, body(): back = lax.all_to_all(owner, 'ctx', split_axis=1, concat_axis=3, tiled=True)  11.7 us
  transfers between devices with their start and end apart: 19, of which 12 were waited for; matrix products, arithmetic and copies ran while one was open for 17% of the time, Pallas kernels for 28%

profile of v16, /device:TPU:0, one launch (start us, length us, event | category | flops | bytes accessed | tf_op | source)
XLA Modules:
  0.0 316.5 jit_solution(15712343467638126904)
XLA Ops:
  1.7 3.0 collective-permute-start.3
  6.0 5.9 %collective-permute-done.3 = bf16[256,512]{1,0:T(8,128)(2,1)S(1)} collective-permute-done((bf16[256,512]{1,0:T(8,128)(2,1)S(1)}, bf16[256,512]{1,0:T(8,128)(2,1)S(1)}, u32[]{:S(2)}, u32[]{:S(2)}) %collective-permute-start.3) | collective-permute-done | bytes 262176 | tf_op jit(solution)/shard_map/ppermute | solution.py:150
  12.5 4.1 %collective-permute-done.2 = bf16[256,512]{1,0:T(8,128)(2,1)S(1)} collective-permute-done((bf16[256,512]{1,0:T(8,128)(2,1)S(1)}, bf16[256,512]{1,0:T(8,128)(2,1)S(1)}, u32[]{:S(2)}, u32[]{:S(2)}) %collective-permute-start.2) | collective-permute-done | bytes 262176 | tf_op jit(solution)/shard_map/ppermute | solution.py:150
  19.5 6.3 %all-to-all-start = ((bf16[16,2,32,4,128]{4,2,3,1,0:T(8,128)(2,1)}), bf16[16,2,32,4,128]{4,2,3,1,0:T(8,128)(2,1)S(1)}, u32[]{:S(2)}, u32[]{:S(2)}) async-start(bf16[16,2,32,4,128]{4,2,3,1,0:T(8,128)(2,1)} %pad_maximum_fusion.4), calls=%async_computation | async-start | bytes 2097152 | tf_op jit(solution)/shard_map/all_to_all | solution.py:229
  31.2 10.9 %collective-permute-done.4 = bf16[256,1024]{1,0:T(8,128)(2,1)S(1)} collective-permute-done((bf16[256,1024]{1,0:T(8,128)(2,1)}, bf16[256,1024]{1,0:T(8,128)(2,1)S(1)}, u32[]{:S(2)}, u32[]{:S(2)}) %collective-permute-start.4) | collective-permute-done | bytes 524320 | tf_op jit(solution)/shard_map/ppermute | solution.py:150
  43.3 9.6 %collective-permute-done.5 = bf16[256,1024]{1,0:T(8,128)(2,1)S(1)} collective-permute-done((bf16[256,1024]{1,0:T(8,128)(2,1)}, bf16[256,1024]{1,0:T(8,128)(2,1)S(1)}, u32[]{:S(2)}, u32[]{:S(2)}) %collective-permute-start.5) | collective-permute-done | bytes 524320 | tf_op jit(solution)/shard_map/ppermute | solution.py:150
  56.3 5.9 %all-to-all-start.1 = ((bf16[16,2,3,2,32,128]{5,4,3,2,1,0:T(8,128)(2,1)}), bf16[16,2,3,2,32,128]{5,4,3,2,1,0:T(8,128)(2,1)S(1)}, u32[]{:S(2)}, u32[]{:S(2)}) async-start(bf16[16,2,3,2,32,128]{5,4,3,2,1,0:T(8,128)(2,1)} %bitcast.175), calls=%async_computation.1 | async-start | bytes 3145728 | tf_op jit(solution)/shard_map/all_to_all | solution.py:255
  64.5 12.8 %collective-permute-done = bf16[256,1024]{1,0:T(8,128)(2,1)} collective-permute-done((bf16[256,1024]{1,0:T(8,128)(2,1)}, bf16[256,1024]{1,0:T(8,128)(2,1)}, u32[]{:S(2)}, u32[]{:S(2)}) %collective-permute-start) | collective-permute-done | bytes 524320 | tf_op jit(solution)/shard_map/ppermute | solution.py:150
  79.4 8.6 %collective-permute-done.1 = bf16[256,1024]{1,0:T(8,128)(2,1)} collective-permute-done((bf16[256,1024]{1,0:T(8,128)(2,1)}, bf16[256,1024]{1,0:T(8,128)(2,1)}, u32[]{:S(2)}, u32[]{:S(2)}) %collective-permute-start.1) | collective-permute-done | bytes 524320 | tf_op jit(solution)/shard_map/ppermute | solution.py:150
  94.2 9.2 %all-to-all-start.2 = ((bf16[16,2,3,2,32,128]{5,4,3,2,1,0:T(8,128)(2,1)}), bf16[16,2,3,2,32,128]{5,4,3,2,1,0:T(8,128)(2,1)}, u32[]{:S(2)}, u32[]{:S(2)}) async-start(bf16[16,2,3,2,32,128]{5,4,3,2,1,0:T(8,128)(2,1)} %bitcast.174), calls=%async_computation.2 | async-start | bytes 3145728 | tf_op jit(solution)/shard_map/all_to_all | solution.py:255
  105.8 44.9 %shard_map.93 = (bf16[2,256,1024]{2,1,0:T(8,128)(2,1)}, bf16[2,256,1024]{2,1,0:T(8,128)(2,1)}, f32[2,3,2,512,128]{4,3,2,1,0:T(8,128)}, f32[512,256]{1,0:T(8,128)}, f32[512,256]{1,0:T(8,128)}) custom-call(s32[8]{0:T(128)} %reshape.114.live_ref, s32[1]{0:T(128)} %bitcast.2.tp_ref, bf16[2,256,1024]{2,1,0:T(8,128)(2,1)} %pad_maximum_fusion.2.q_ref, ...), custom_call_target="tpu_custom_call" | custom-call | flops 12884901888 | bytes 10485760 | tf_op jit(solution)/shard_map/pallas_call | solution.py:118
  154.5 6.0 %all-to-all-start.3 = ((bf16[2,3,2,16,32,128]{5,4,2,1,0,3:T(8,128)(2,1)}), bf16[2,3,2,16,32,128]{5,4,2,1,0,3:T(8,128)(2,1)S(1)}, u32[]{:S(2)}, u32[]{:S(2)}) async-start(bf16[2,3,2,16,32,128]{5,4,2,1,0,3:T(8,128)(2,1)} %copy.93), calls=%async_computation.3 | async-start | bytes 3145728 | tf_op jit(solution)/shard_map/all_to_all | solution.py:268
  161.1 2.9 copy.91
  164.0 45.0 %shard_map.94 = (bf16[2,256,1024]{2,1,0:T(8,128)(2,1)}, bf16[2,256,1024]{2,1,0:T(8,128)(2,1)}, f32[2,3,2,512,128]{4,3,2,1,0:T(8,128)}, f32[512,256]{1,0:T(8,128)}, f32[512,256]{1,0:T(8,128)}) custom-call(s32[8]{0:T(128)} %reshape.118.live_ref, s32[1]{0:T(128)} %bitcast.2.tp_ref, bf16[2,256,1024]{2,1,0:T(8,128)(2,1)} %pad_maximum_fusion.5.q_ref, ...), custom_call_target="tpu_custom_call" | custom-call | flops 12884901888 | bytes 10485760 | tf_op jit(solution)/shard_map/pallas_call | solution.py:118
  212.8 6.0 %all-to-all-start.5 = ((bf16[2,3,2,16,32,128]{5,4,2,1,0,3:T(8,128)(2,1)}), bf16[2,3,2,16,32,128]{5,4,2,1,0,3:T(8,128)(2,1)S(1)}, u32[]{:S(2)}, u32[]{:S(2)}) async-start(bf16[2,3,2,16,32,128]{5,4,2,1,0,3:T(8,128)(2,1)} %copy.99), calls=%async_computation.5 | async-start | bytes 3145728 | tf_op jit(solution)/shard_map/all_to_all | solution.py:268
  228.8 2.5 reshape.120
  232.7 18.1 %all-to-all-done.5 = bf16[2,3,2,16,32,128]{5,4,2,1,0,3:T(8,128)(2,1)S(1)} async-done(((bf16[2,3,2,16,32,128]{5,4,2,1,0,3:T(8,128)(2,1)}), bf16[2,3,2,16,32,128]{5,4,2,1,0,3:T(8,128)(2,1)S(1)}, u32[]{:S(2)}, u32[]{:S(2)}) %all-to-all-start.5) | async-done | bytes 1572896 | tf_op jit(solution)/shard_map/all_to_all | solution.py:268
  250.8 9.2 %all-to-all-start.4 = ((bf16[2,16,2,32,128]{4,3,2,0,1:T(8,128)(2,1)}), bf16[2,16,2,32,128]{4,3,2,0,1:T(8,128)(2,1)}, u32[]{:S(2)}, u32[]{:S(2)}) async-start(bf16[2,16,2,32,128]{4,3,2,0,1:T(8,128)(2,1)} %copy.95), calls=%async_computation.4 | async-start | bytes 1048576 | tf_op jit(solution)/shard_map/all_to_all | solution.py:278
  261.7 2.5 fusion.7
  269.0 5.3 %collective-permute-done.7 = bf16[256,1024]{1,0:T(8,128)(2,1)S(1)} collective-permute-done((bf16[256,1024]{1,0:T(8,128)(2,1)S(1)}, bf16[256,1024]{1,0:T(8,128)(2,1)S(1)}, u32[]{:S(2)}, u32[]{:S(2)}) %collective-permute-start.7) | collective-permute-done | bytes 524320 | tf_op jit(solution)/shard_map/ppermute | solution.py:150
  278.1 5.8 %all-to-all-start.6 = ((bf16[2,16,2,32,128]{4,3,2,0,1:T(8,128)(2,1)}), bf16[2,16,2,32,128]{4,3,2,0,1:T(8,128)(2,1)S(1)}, u32[]{:S(2)}, u32[]{:S(2)}) async-start(bf16[2,16,2,32,128]{4,3,2,0,1:T(8,128)(2,1)} %copy.101), calls=%async_computation.6 | async-start | bytes 1048576 | tf_op jit(solution)/shard_map/all_to_all | solution.py:278
  286.6 11.7 %all-to-all-done.6 = bf16[2,16,2,32,128]{4,3,2,0,1:T(8,128)(2,1)S(1)} async-done(((bf16[2,16,2,32,128]{4,3,2,0,1:T(8,128)(2,1)}), bf16[2,16,2,32,128]{4,3,2,0,1:T(8,128)(2,1)S(1)}, u32[]{:S(2)}, u32[]{:S(2)}) %all-to-all-start.6) | async-done | bytes 524320 | tf_op jit(solution)/shard_map/all_to_all | solution.py:278
  305.2 5.5 %collective-permute-done.11 = bf16[256,512]{1,0:T(8,128)(2,1)S(1)} collective-permute-done((bf16[256,512]{1,0:T(8,128)(2,1)S(1)}, bf16[256,512]{1,0:T(8,128)(2,1)S(1)}, u32[]{:S(2)}, u32[]{:S(2)}) %collective-permute-start.11) | collective-permute-done | bytes 262176 | tf_op jit(solution)/shard_map/ppermute | solution.py:150
  311.8 3.6 %collective-permute-done.10 = bf16[256,512]{1,0:T(8,128)(2,1)S(1)} collective-permute-done((bf16[256,512]{1,0:T(8,128)(2,1)S(1)}, bf16[256,512]{1,0:T(8,128)(2,1)S(1)}, u32[]{:S(2)}, u32[]{:S(2)}) %collective-permute-start.10) | collective-permute-done | bytes 262176 | tf_op jit(solution)/shard_map/ppermute | solution.py:150
  (158 shorter events, 69.9 us)
Async XLA Ops:
  1.7 10.2 %collective-permute-start.3 = (bf16[256,512]{1,0:T(8,128)(2,1)S(1)}, bf16[256,512]{1,0:T(8,128)(2,1)S(1)}, u32[]{:S(2)}, u32[]{:S(2)}) collective-permute-start(bf16[256,512]{1,0:T(8,128)(2,1)S(1)} %get-tuple-element.72), channel_id=1, source_target_pairs={{0,1},{1,0},{2,3},{3,2},{4,5},{5,4},{6,7},{7,6},{8,9},{9,8},{10,11... | collective-permute-start | bytes 786440 | tf_op jit(solution)/shard_map/ppermute | solution.py:150
  5.8 10.9 %collective-permute-start.2 = (bf16[256,512]{1,0:T(8,128)(2,1)S(1)}, bf16[256,512]{1,0:T(8,128)(2,1)S(1)}, u32[]{:S(2)}, u32[]{:S(2)}) collective-permute-start(bf16[256,512]{1,0:T(8,128)(2,1)S(1)} %get-tuple-element.70), channel_id=1, source_target_pairs={{0,1},{1,0},{2,3},{3,2},{4,5},{5,4},{6,7},{7,6},{8,9},{9,8},{10,11... | collective-permute-start | bytes 786440 | tf_op jit(solution)/shard_map/ppermute | solution.py:150
  19.5 34.4 %all-to-all-start = ((bf16[16,2,32,4,128]{4,2,3,1,0:T(8,128)(2,1)}), bf16[16,2,32,4,128]{4,2,3,1,0:T(8,128)(2,1)S(1)}, u32[]{:S(2)}, u32[]{:S(2)}) async-start(bf16[16,2,32,4,128]{4,2,3,1,0:T(8,128)(2,1)} %pad_maximum_fusion.4), calls=%async_computation | async-start | bytes 2097152 | tf_op jit(solution)/shard_map/all_to_all | solution.py:229
  27.2 15.0 %copy-start.17 = (bf16[1,256,1024]{2,1,0:T(8,128)(2,1)S(1)}, bf16[1,256,1024]{2,1,0:T(8,128)(2,1)}, u32[]{:S(2)}) copy-start(bf16[1,256,1024]{2,1,0:T(8,128)(2,1)} %get-tuple-element.40) | copy-start | bytes 1572868
  27.2 15.0 %collective-permute-start.4 = (bf16[256,1024]{1,0:T(8,128)(2,1)}, bf16[256,1024]{1,0:T(8,128)(2,1)S(1)}, u32[]{:S(2)}, u32[]{:S(2)}) collective-permute-start(bf16[256,1024]{1,0:T(8,128)(2,1)} %get-tuple-element.39), channel_id=1, source_target_pairs={{0,1},{1,0},{2,3},{3,2},{4,5},{5,4},{6,7},{7,6},{8,9},{9,8},{10,11... | collective-permute-start | bytes 1572872 | tf_op jit(solution)/shard_map/ppermute | solution.py:150
  30.0 22.9 %collective-permute-start.5 = (bf16[256,1024]{1,0:T(8,128)(2,1)}, bf16[256,1024]{1,0:T(8,128)(2,1)S(1)}, u32[]{:S(2)}, u32[]{:S(2)}) collective-permute-start(bf16[256,1024]{1,0:T(8,128)(2,1)} %get-tuple-element.35), channel_id=1, source_target_pairs={{0,1},{1,0},{2,3},{3,2},{4,5},{5,4},{6,7},{7,6},{8,9},{9,8},{10,11... | collective-permute-start | bytes 1572872 | tf_op jit(solution)/shard_map/ppermute | solution.py:150
  56.3 21.0 %copy-start.11 = (bf16[1,256,1024]{2,1,0:T(8,128)(2,1)S(1)}, bf16[1,256,1024]{2,1,0:T(8,128)(2,1)}, u32[]{:S(2)}) copy-start(bf16[1,256,1024]{2,1,0:T(8,128)(2,1)} %get-tuple-element.37) | copy-start | bytes 1572868
  56.3 37.9 %all-to-all-start.1 = ((bf16[16,2,3,2,32,128]{5,4,3,2,1,0:T(8,128)(2,1)}), bf16[16,2,3,2,32,128]{5,4,3,2,1,0:T(8,128)(2,1)S(1)}, u32[]{:S(2)}, u32[]{:S(2)}) async-start(bf16[16,2,3,2,32,128]{5,4,3,2,1,0:T(8,128)(2,1)} %bitcast.175), calls=%async_computation.1 | async-start | bytes 3145728 | tf_op jit(solution)/shard_map/all_to_all | solution.py:255
  62.2 15.1 %collective-permute-start = (bf16[256,1024]{1,0:T(8,128)(2,1)}, bf16[256,1024]{1,0:T(8,128)(2,1)}, u32[]{:S(2)}, u32[]{:S(2)}) collective-permute-start(bf16[256,1024]{1,0:T(8,128)(2,1)} %get-tuple-element.38), channel_id=1, source_target_pairs={{0,1},{1,0},{2,3},{3,2},{4,5},{5,4},{6,7},{7,6},{8,9},{9,8},{10,11... | collective-permute-start | bytes 1572872 | tf_op jit(solution)/shard_map/ppermute | solution.py:150
  63.8 24.2 %collective-permute-start.1 = (bf16[256,1024]{1,0:T(8,128)(2,1)}, bf16[256,1024]{1,0:T(8,128)(2,1)}, u32[]{:S(2)}, u32[]{:S(2)}) collective-permute-start(bf16[256,1024]{1,0:T(8,128)(2,1)} %get-tuple-element.34), channel_id=1, source_target_pairs={{0,1},{1,0},{2,3},{3,2},{4,5},{5,4},{6,7},{7,6},{8,9},{9,8},{10,11... | collective-permute-start | bytes 1572872 | tf_op jit(solution)/shard_map/ppermute | solution.py:150
  64.5 23.5 %copy-start.12 = (bf16[1,256,1024]{2,1,0:T(8,128)(2,1)S(1)}, bf16[1,256,1024]{2,1,0:T(8,128)(2,1)}, u32[]{:S(2)}) copy-start(bf16[1,256,1024]{2,1,0:T(8,128)(2,1)} %get-tuple-element.33) | copy-start | bytes 1572868
  94.2 60.3 %all-to-all-start.2 = ((bf16[16,2,3,2,32,128]{5,4,3,2,1,0:T(8,128)(2,1)}), bf16[16,2,3,2,32,128]{5,4,3,2,1,0:T(8,128)(2,1)}, u32[]{:S(2)}, u32[]{:S(2)}) async-start(bf16[16,2,3,2,32,128]{5,4,3,2,1,0:T(8,128)(2,1)} %bitcast.174), calls=%async_computation.2 | async-start | bytes 3145728 | tf_op jit(solution)/shard_map/all_to_all | solution.py:255
  154.5 58.3 %all-to-all-start.3 = ((bf16[2,3,2,16,32,128]{5,4,2,1,0,3:T(8,128)(2,1)}), bf16[2,3,2,16,32,128]{5,4,2,1,0,3:T(8,128)(2,1)S(1)}, u32[]{:S(2)}, u32[]{:S(2)}) async-start(bf16[2,3,2,16,32,128]{5,4,2,1,0,3:T(8,128)(2,1)} %copy.93), calls=%async_computation.3 | async-start | bytes 3145728 | tf_op jit(solution)/shard_map/all_to_all | solution.py:268
  212.8 38.0 %all-to-all-start.5 = ((bf16[2,3,2,16,32,128]{5,4,2,1,0,3:T(8,128)(2,1)}), bf16[2,3,2,16,32,128]{5,4,2,1,0,3:T(8,128)(2,1)S(1)}, u32[]{:S(2)}, u32[]{:S(2)}) async-start(bf16[2,3,2,16,32,128]{5,4,2,1,0,3:T(8,128)(2,1)} %copy.99), calls=%async_computation.5 | async-start | bytes 3145728 | tf_op jit(solution)/shard_map/all_to_all | solution.py:268
  221.6 40.0 %collective-permute-start.8 = (bf16[256,1024]{1,0:T(8,128)(2,1)}, bf16[256,1024]{1,0:T(8,128)(2,1)}, u32[]{:S(2)}, u32[]{:S(2)}) collective-permute-start(bf16[256,1024]{1,0:T(8,128)(2,1)} %get-tuple-element.49), channel_id=1, source_target_pairs={{0,1},{1,0},{2,3},{3,2},{4,5},{5,4},{6,7},{7,6},{8,9},{9,8},{10,11... | collective-permute-start | bytes 1572872 | tf_op jit(solution)/shard_map/ppermute | solution.py:150
  224.2 39.9 %collective-permute-start.9 = (bf16[256,1024]{1,0:T(8,128)(2,1)}, bf16[256,1024]{1,0:T(8,128)(2,1)}, u32[]{:S(2)}, u32[]{:S(2)}) collective-permute-start(bf16[256,1024]{1,0:T(8,128)(2,1)} %get-tuple-element.51), channel_id=1, source_target_pairs={{0,1},{1,0},{2,3},{3,2},{4,5},{5,4},{6,7},{7,6},{8,9},{9,8},{10,11... | collective-permute-start | bytes 1572872 | tf_op jit(solution)/shard_map/ppermute | solution.py:150
  225.8 40.8 %collective-permute-start.6 = (bf16[256,1024]{1,0:T(8,128)(2,1)}, bf16[256,1024]{1,0:T(8,128)(2,1)}, u32[]{:S(2)}, u32[]{:S(2)}) collective-permute-start(bf16[256,1024]{1,0:T(8,128)(2,1)} %get-tuple-element.57), channel_id=1, source_target_pairs={{0,1},{1,0},{2,3},{3,2},{4,5},{5,4},{6,7},{7,6},{8,9},{9,8},{10,11... | collective-permute-start | bytes 1572872 | tf_op jit(solution)/shard_map/ppermute | solution.py:150
  231.7 28.3 %copy-start.19 = (bf16[2,256,1024]{2,1,0:T(8,128)(2,1)S(1)}, bf16[2,256,1024]{2,1,0:T(8,128)(2,1)}, u32[]{:S(2)}) copy-start(bf16[2,256,1024]{2,1,0:T(8,128)(2,1)} %get-tuple-element.24) | copy-start | bytes 3145732
  231.8 29.8 %copy-start.6 = (bf16[1,256,1024]{2,1,0:T(8,128)(2,1)S(1)}, bf16[1,256,1024]{2,1,0:T(8,128)(2,1)}, u32[]{:S(2)}) copy-start(bf16[1,256,1024]{2,1,0:T(8,128)(2,1)} %get-tuple-element.50) | copy-start | bytes 1572868
  250.8 27.3 %all-to-all-start.4 = ((bf16[2,16,2,32,128]{4,3,2,0,1:T(8,128)(2,1)}), bf16[2,16,2,32,128]{4,3,2,0,1:T(8,128)(2,1)}, u32[]{:S(2)}, u32[]{:S(2)}) async-start(bf16[2,16,2,32,128]{4,3,2,0,1:T(8,128)(2,1)} %copy.95), calls=%async_computation.4 | async-start | bytes 1048576 | tf_op jit(solution)/shard_map/all_to_all | solution.py:278
  260.0 14.2 %collective-permute-start.7 = (bf16[256,1024]{1,0:T(8,128)(2,1)S(1)}, bf16[256,1024]{1,0:T(8,128)(2,1)S(1)}, u32[]{:S(2)}, u32[]{:S(2)}) collective-permute-start(bf16[256,1024]{1,0:T(8,128)(2,1)S(1)} %get-tuple-element.59), channel_id=1, source_target_pairs={{0,1},{1,0},{2,3},{3,2},{4,5},{5,4},{6,7},{7,6},{8,9},{9,8},{10,11... | collective-permute-start | bytes 1572872 | tf_op jit(solution)/shard_map/ppermute | solution.py:150
  278.1 20.2 %all-to-all-start.6 = ((bf16[2,16,2,32,128]{4,3,2,0,1:T(8,128)(2,1)}), bf16[2,16,2,32,128]{4,3,2,0,1:T(8,128)(2,1)S(1)}, u32[]{:S(2)}, u32[]{:S(2)}) async-start(bf16[2,16,2,32,128]{4,3,2,0,1:T(8,128)(2,1)} %copy.101), calls=%async_computation.6 | async-start | bytes 1048576 | tf_op jit(solution)/shard_map/all_to_all | solution.py:278
  301.5 9.2 %collective-permute-start.11 = (bf16[256,512]{1,0:T(8,128)(2,1)S(1)}, bf16[256,512]{1,0:T(8,128)(2,1)S(1)}, u32[]{:S(2)}, u32[]{:S(2)}) collective-permute-start(bf16[256,512]{1,0:T(8,128)(2,1)S(1)} %get-tuple-element.63), channel_id=1, source_target_pairs={{0,1},{1,0},{2,3},{3,2},{4,5},{5,4},{6,7},{7,6},{8,9},{9,8},{10,11... | collective-permute-start | bytes 786440 | tf_op jit(solution)/shard_map/ppermute | solution.py:150
  303.1 12.3 %collective-permute-start.10 = (bf16[256,512]{1,0:T(8,128)(2,1)S(1)}, bf16[256,512]{1,0:T(8,128)(2,1)S(1)}, u32[]{:S(2)}, u32[]{:S(2)}) collective-permute-start(bf16[256,512]{1,0:T(8,128)(2,1)S(1)} %get-tuple-element.67), channel_id=1, source_target_pairs={{0,1},{1,0},{2,3},{3,2},{4,5},{5,4},{6,7},{7,6},{8,9},{9,8},{10,11... | collective-permute-start | bytes 786440 | tf_op jit(solution)/shard_map/ppermute | solution.py:150
  (22 other events, 96.8 us)

commit v17 on v15

--- a/solution.py
+++ b/solution.py
@@ -58,8 +58,7 @@
         for w in weights[1:]:
             total = total + w.sum(axis=1, keepdims=True)
         inverse = 1.0 / total
-        probs = [w * inverse for w in weights]
-        probs_low = [p.astype(jnp.bfloat16) for p in probs]
+        probs_low = [(w * inverse).astype(jnp.bfloat16) for w in weights]
         out = jnp.dot(probs_low[0], values[0], preferred_element_type=jnp.float32)
         for r in range(1, slot_count):
             out = out + jnp.dot(probs_low[r], values[r], preferred_element_type=jnp.float32)
@@ -69,7 +68,7 @@
         grad_q = None
         for r in range(slot_count):
             grad_p = jnp.dot(do, values_t[r], preferred_element_type=jnp.float32)
-            grad_s = (probs[r] * (grad_p - delta)).astype(jnp.bfloat16)
+            grad_s = (probs_low[r].astype(jnp.float32) * (grad_p - delta)).astype(jnp.bfloat16)
             part = jnp.dot(grad_s, keys[r], preferred_element_type=jnp.float32)
             grad_q = part if grad_q is None else grad_q + part
             width = keys[r].shape[0]

time: 318 us -> 318 us (level)
  no operation moved by 1% of the time
where the time goes in v17:
time: 318 us; the launch traced here: 317 us
  waiting for transfers between devices  98 us (31%)
  Pallas kernels  90 us (28%)
  starting transfers between devices  63.2 us (20%)
  local copies, waits for them, and re-layouts  35.6 us (11%)
  other arithmetic  27.8 us (9%)
    pallas_call x2, Pallas kernels, attention(): pl.pallas_call(kernel, grid_spec=pltpu.PrefetchScalarGridSpec(num_scalar_...  90 us
    ppermute x12, waiting for transfers between devices, shift(): lax.ppermute(x, axis, perm=[(s, (s + step) % size) for s in range(size)])  66.5 us
    all_to_all x2, waiting for transfers between devices, body(): lax.all_to_all(send_back, 'ctx', split_axis=3, concat_axis=1, tiled=True)  18.1 us
    all_to_all x2, starting transfers between devices, body(): got = lax.all_to_all(send, 'ctx', split_axis=0, concat_axis=4, tiled=True)  15 us
    ppermute x12, starting transfers between devices, shift(): lax.ppermute(x, axis, perm=[(s, (s + step) % size) for s in range(size)])  15 us
    all_to_all x2, starting transfers between devices, body(): back = lax.all_to_all(owner, 'ctx', split_axis=1, concat_axis=3, tiled=True)  14.9 us
    all_to_all x2, starting transfers between devices, body(): lax.all_to_all(send_back, 'ctx', split_axis=3, concat_axis=1, tiled=True)  12 us
    all_to_all x2, waiting for transfers between devices, body(): back = lax.all_to_all(owner, 'ctx', split_axis=1, concat_axis=3, tiled=True)  11.7 us
  transfers between devices with their start and end apart: 19, of which 12 were waited for; matrix products, arithmetic and copies ran while one was open for 17% of the time, Pallas kernels for 28%

profile of v17, /device:TPU:0, one launch (start us, length us, event | category | flops | bytes accessed | tf_op | source)
XLA Modules:
  0.0 316.6 jit_solution(4028222623422058045)
XLA Ops:
  1.7 3.0 collective-permute-start.3
  6.0 5.9 %collective-permute-done.3 = bf16[256,512]{1,0:T(8,128)(2,1)S(1)} collective-permute-done((bf16[256,512]{1,0:T(8,128)(2,1)S(1)}, bf16[256,512]{1,0:T(8,128)(2,1)S(1)}, u32[]{:S(2)}, u32[]{:S(2)}) %collective-permute-start.3) | collective-permute-done | bytes 262176 | tf_op jit(solution)/shard_map/ppermute | solution.py:149
  12.5 4.1 %collective-permute-done.2 = bf16[256,512]{1,0:T(8,128)(2,1)S(1)} collective-permute-done((bf16[256,512]{1,0:T(8,128)(2,1)S(1)}, bf16[256,512]{1,0:T(8,128)(2,1)S(1)}, u32[]{:S(2)}, u32[]{:S(2)}) %collective-permute-start.2) | collective-permute-done | bytes 262176 | tf_op jit(solution)/shard_map/ppermute | solution.py:149
  19.5 6.3 %all-to-all-start = ((bf16[16,2,32,4,128]{4,2,3,1,0:T(8,128)(2,1)}), bf16[16,2,32,4,128]{4,2,3,1,0:T(8,128)(2,1)S(1)}, u32[]{:S(2)}, u32[]{:S(2)}) async-start(bf16[16,2,32,4,128]{4,2,3,1,0:T(8,128)(2,1)} %pad_maximum_fusion.4), calls=%async_computation | async-start | bytes 2097152 | tf_op jit(solution)/shard_map/all_to_all | solution.py:228
  31.2 10.9 %collective-permute-done.4 = bf16[256,1024]{1,0:T(8,128)(2,1)S(1)} collective-permute-done((bf16[256,1024]{1,0:T(8,128)(2,1)}, bf16[256,1024]{1,0:T(8,128)(2,1)S(1)}, u32[]{:S(2)}, u32[]{:S(2)}) %collective-permute-start.4) | collective-permute-done | bytes 524320 | tf_op jit(solution)/shard_map/ppermute | solution.py:149
  43.3 9.6 %collective-permute-done.5 = bf16[256,1024]{1,0:T(8,128)(2,1)S(1)} collective-permute-done((bf16[256,1024]{1,0:T(8,128)(2,1)}, bf16[256,1024]{1,0:T(8,128)(2,1)S(1)}, u32[]{:S(2)}, u32[]{:S(2)}) %collective-permute-start.5) | collective-permute-done | bytes 524320 | tf_op jit(solution)/shard_map/ppermute | solution.py:149
  56.3 5.9 %all-to-all-start.1 = ((bf16[16,2,3,2,32,128]{5,4,3,2,1,0:T(8,128)(2,1)}), bf16[16,2,3,2,32,128]{5,4,3,2,1,0:T(8,128)(2,1)S(1)}, u32[]{:S(2)}, u32[]{:S(2)}) async-start(bf16[16,2,3,2,32,128]{5,4,3,2,1,0:T(8,128)(2,1)} %bitcast.175), calls=%async_computation.1 | async-start | bytes 3145728 | tf_op jit(solution)/shard_map/all_to_all | solution.py:254
  64.5 12.8 %collective-permute-done = bf16[256,1024]{1,0:T(8,128)(2,1)} collective-permute-done((bf16[256,1024]{1,0:T(8,128)(2,1)}, bf16[256,1024]{1,0:T(8,128)(2,1)}, u32[]{:S(2)}, u32[]{:S(2)}) %collective-permute-start) | collective-permute-done | bytes 524320 | tf_op jit(solution)/shard_map/ppermute | solution.py:149
  79.4 8.6 %collective-permute-done.1 = bf16[256,1024]{1,0:T(8,128)(2,1)} collective-permute-done((bf16[256,1024]{1,0:T(8,128)(2,1)}, bf16[256,1024]{1,0:T(8,128)(2,1)}, u32[]{:S(2)}, u32[]{:S(2)}) %collective-permute-start.1) | collective-permute-done | bytes 524320 | tf_op jit(solution)/shard_map/ppermute | solution.py:149
  94.2 9.2 %all-to-all-start.2 = ((bf16[16,2,3,2,32,128]{5,4,3,2,1,0:T(8,128)(2,1)}), bf16[16,2,3,2,32,128]{5,4,3,2,1,0:T(8,128)(2,1)}, u32[]{:S(2)}, u32[]{:S(2)}) async-start(bf16[16,2,3,2,32,128]{5,4,3,2,1,0:T(8,128)(2,1)} %bitcast.174), calls=%async_computation.2 | async-start | bytes 3145728 | tf_op jit(solution)/shard_map/all_to_all | solution.py:254
  105.8 44.9 %shard_map.93 = (bf16[2,256,1024]{2,1,0:T(8,128)(2,1)}, bf16[2,256,1024]{2,1,0:T(8,128)(2,1)}, f32[2,3,2,512,128]{4,3,2,1,0:T(8,128)}, f32[512,256]{1,0:T(8,128)}, f32[512,256]{1,0:T(8,128)}) custom-call(s32[8]{0:T(128)} %reshape.114.live_ref, s32[1]{0:T(128)} %bitcast.2.tp_ref, bf16[2,256,1024]{2,1,0:T(8,128)(2,1)} %pad_maximum_fusion.2.q_ref, ...), custom_call_target="tpu_custom_call" | custom-call | flops 12884901888 | bytes 10485760 | tf_op jit(solution)/shard_map/pallas_call | solution.py:117
  154.5 6.0 %all-to-all-start.3 = ((bf16[2,3,2,16,32,128]{5,4,2,1,0,3:T(8,128)(2,1)}), bf16[2,3,2,16,32,128]{5,4,2,1,0,3:T(8,128)(2,1)S(1)}, u32[]{:S(2)}, u32[]{:S(2)}) async-start(bf16[2,3,2,16,32,128]{5,4,2,1,0,3:T(8,128)(2,1)} %copy.93), calls=%async_computation.3 | async-start | bytes 3145728 | tf_op jit(solution)/shard_map/all_to_all | solution.py:267
  161.1 2.9 copy.91
  164.0 45.1 %shard_map.94 = (bf16[2,256,1024]{2,1,0:T(8,128)(2,1)}, bf16[2,256,1024]{2,1,0:T(8,128)(2,1)}, f32[2,3,2,512,128]{4,3,2,1,0:T(8,128)}, f32[512,256]{1,0:T(8,128)}, f32[512,256]{1,0:T(8,128)}) custom-call(s32[8]{0:T(128)} %reshape.118.live_ref, s32[1]{0:T(128)} %bitcast.2.tp_ref, bf16[2,256,1024]{2,1,0:T(8,128)(2,1)} %pad_maximum_fusion.5.q_ref, ...), custom_call_target="tpu_custom_call" | custom-call | flops 12884901888 | bytes 10485760 | tf_op jit(solution)/shard_map/pallas_call | solution.py:117
  212.9 6.0 %all-to-all-start.5 = ((bf16[2,3,2,16,32,128]{5,4,2,1,0,3:T(8,128)(2,1)}), bf16[2,3,2,16,32,128]{5,4,2,1,0,3:T(8,128)(2,1)S(1)}, u32[]{:S(2)}, u32[]{:S(2)}) async-start(bf16[2,3,2,16,32,128]{5,4,2,1,0,3:T(8,128)(2,1)} %copy.99), calls=%async_computation.5 | async-start | bytes 3145728 | tf_op jit(solution)/shard_map/all_to_all | solution.py:267
  228.9 2.5 reshape.120
  232.8 18.1 %all-to-all-done.5 = bf16[2,3,2,16,32,128]{5,4,2,1,0,3:T(8,128)(2,1)S(1)} async-done(((bf16[2,3,2,16,32,128]{5,4,2,1,0,3:T(8,128)(2,1)}), bf16[2,3,2,16,32,128]{5,4,2,1,0,3:T(8,128)(2,1)S(1)}, u32[]{:S(2)}, u32[]{:S(2)}) %all-to-all-start.5) | async-done | bytes 1572896 | tf_op jit(solution)/shard_map/all_to_all | solution.py:267
  250.9 9.2 %all-to-all-start.4 = ((bf16[2,16,2,32,128]{4,3,2,0,1:T(8,128)(2,1)}), bf16[2,16,2,32,128]{4,3,2,0,1:T(8,128)(2,1)}, u32[]{:S(2)}, u32[]{:S(2)}) async-start(bf16[2,16,2,32,128]{4,3,2,0,1:T(8,128)(2,1)} %copy.95), calls=%async_computation.4 | async-start | bytes 1048576 | tf_op jit(solution)/shard_map/all_to_all | solution.py:277
  261.8 2.5 fusion.7
  269.1 5.3 %collective-permute-done.7 = bf16[256,1024]{1,0:T(8,128)(2,1)S(1)} collective-permute-done((bf16[256,1024]{1,0:T(8,128)(2,1)S(1)}, bf16[256,1024]{1,0:T(8,128)(2,1)S(1)}, u32[]{:S(2)}, u32[]{:S(2)}) %collective-permute-start.7) | collective-permute-done | bytes 524320 | tf_op jit(solution)/shard_map/ppermute | solution.py:149
  278.2 5.7 %all-to-all-start.6 = ((bf16[2,16,2,32,128]{4,3,2,0,1:T(8,128)(2,1)}), bf16[2,16,2,32,128]{4,3,2,0,1:T(8,128)(2,1)S(1)}, u32[]{:S(2)}, u32[]{:S(2)}) async-start(bf16[2,16,2,32,128]{4,3,2,0,1:T(8,128)(2,1)} %copy.101), calls=%async_computation.6 | async-start | bytes 1048576 | tf_op jit(solution)/shard_map/all_to_all | solution.py:277
  286.7 11.7 %all-to-all-done.6 = bf16[2,16,2,32,128]{4,3,2,0,1:T(8,128)(2,1)S(1)} async-done(((bf16[2,16,2,32,128]{4,3,2,0,1:T(8,128)(2,1)}), bf16[2,16,2,32,128]{4,3,2,0,1:T(8,128)(2,1)S(1)}, u32[]{:S(2)}, u32[]{:S(2)}) %all-to-all-start.6) | async-done | bytes 524320 | tf_op jit(solution)/shard_map/all_to_all | solution.py:277
  305.3 5.5 %collective-permute-done.11 = bf16[256,512]{1,0:T(8,128)(2,1)S(1)} collective-permute-done((bf16[256,512]{1,0:T(8,128)(2,1)S(1)}, bf16[256,512]{1,0:T(8,128)(2,1)S(1)}, u32[]{:S(2)}, u32[]{:S(2)}) %collective-permute-start.11) | collective-permute-done | bytes 262176 | tf_op jit(solution)/shard_map/ppermute | solution.py:149
  311.9 3.6 %collective-permute-done.10 = bf16[256,512]{1,0:T(8,128)(2,1)S(1)} collective-permute-done((bf16[256,512]{1,0:T(8,128)(2,1)S(1)}, bf16[256,512]{1,0:T(8,128)(2,1)S(1)}, u32[]{:S(2)}, u32[]{:S(2)}) %collective-permute-start.10) | collective-permute-done | bytes 262176 | tf_op jit(solution)/shard_map/ppermute | solution.py:149
  (158 shorter events, 69.8 us)
Async XLA Ops:
  1.7 10.2 %collective-permute-start.3 = (bf16[256,512]{1,0:T(8,128)(2,1)S(1)}, bf16[256,512]{1,0:T(8,128)(2,1)S(1)}, u32[]{:S(2)}, u32[]{:S(2)}) collective-permute-start(bf16[256,512]{1,0:T(8,128)(2,1)S(1)} %get-tuple-element.72), channel_id=1, source_target_pairs={{0,1},{1,0},{2,3},{3,2},{4,5},{5,4},{6,7},{7,6},{8,9},{9,8},{10,11... | collective-permute-start | bytes 786440 | tf_op jit(solution)/shard_map/ppermute | solution.py:149
  5.8 10.9 %collective-permute-start.2 = (bf16[256,512]{1,0:T(8,128)(2,1)S(1)}, bf16[256,512]{1,0:T(8,128)(2,1)S(1)}, u32[]{:S(2)}, u32[]{:S(2)}) collective-permute-start(bf16[256,512]{1,0:T(8,128)(2,1)S(1)} %get-tuple-element.70), channel_id=1, source_target_pairs={{0,1},{1,0},{2,3},{3,2},{4,5},{5,4},{6,7},{7,6},{8,9},{9,8},{10,11... | collective-permute-start | bytes 786440 | tf_op jit(solution)/shard_map/ppermute | solution.py:149
  19.5 34.4 %all-to-all-start = ((bf16[16,2,32,4,128]{4,2,3,1,0:T(8,128)(2,1)}), bf16[16,2,32,4,128]{4,2,3,1,0:T(8,128)(2,1)S(1)}, u32[]{:S(2)}, u32[]{:S(2)}) async-start(bf16[16,2,32,4,128]{4,2,3,1,0:T(8,128)(2,1)} %pad_maximum_fusion.4), calls=%async_computation | async-start | bytes 2097152 | tf_op jit(solution)/shard_map/all_to_all | solution.py:228
  27.2 15.0 %copy-start.17 = (bf16[1,256,1024]{2,1,0:T(8,128)(2,1)S(1)}, bf16[1,256,1024]{2,1,0:T(8,128)(2,1)}, u32[]{:S(2)}) copy-start(bf16[1,256,1024]{2,1,0:T(8,128)(2,1)} %get-tuple-element.40) | copy-start | bytes 1572868
  27.2 15.0 %collective-permute-start.4 = (bf16[256,1024]{1,0:T(8,128)(2,1)}, bf16[256,1024]{1,0:T(8,128)(2,1)S(1)}, u32[]{:S(2)}, u32[]{:S(2)}) collective-permute-start(bf16[256,1024]{1,0:T(8,128)(2,1)} %get-tuple-element.39), channel_id=1, source_target_pairs={{0,1},{1,0},{2,3},{3,2},{4,5},{5,4},{6,7},{7,6},{8,9},{9,8},{10,11... | collective-permute-start | bytes 1572872 | tf_op jit(solution)/shard_map/ppermute | solution.py:149
  30.0 22.9 %collective-permute-start.5 = (bf16[256,1024]{1,0:T(8,128)(2,1)}, bf16[256,1024]{1,0:T(8,128)(2,1)S(1)}, u32[]{:S(2)}, u32[]{:S(2)}) collective-permute-start(bf16[256,1024]{1,0:T(8,128)(2,1)} %get-tuple-element.35), channel_id=1, source_target_pairs={{0,1},{1,0},{2,3},{3,2},{4,5},{5,4},{6,7},{7,6},{8,9},{9,8},{10,11... | collective-permute-start | bytes 1572872 | tf_op jit(solution)/shard_map/ppermute | solution.py:149
  56.3 21.0 %copy-start.11 = (bf16[1,256,1024]{2,1,0:T(8,128)(2,1)S(1)}, bf16[1,256,1024]{2,1,0:T(8,128)(2,1)}, u32[]{:S(2)}) copy-start(bf16[1,256,1024]{2,1,0:T(8,128)(2,1)} %get-tuple-element.37) | copy-start | bytes 1572868
  56.3 37.9 %all-to-all-start.1 = ((bf16[16,2,3,2,32,128]{5,4,3,2,1,0:T(8,128)(2,1)}), bf16[16,2,3,2,32,128]{5,4,3,2,1,0:T(8,128)(2,1)S(1)}, u32[]{:S(2)}, u32[]{:S(2)}) async-start(bf16[16,2,3,2,32,128]{5,4,3,2,1,0:T(8,128)(2,1)} %bitcast.175), calls=%async_computation.1 | async-start | bytes 3145728 | tf_op jit(solution)/shard_map/all_to_all | solution.py:254
  62.2 15.1 %collective-permute-start = (bf16[256,1024]{1,0:T(8,128)(2,1)}, bf16[256,1024]{1,0:T(8,128)(2,1)}, u32[]{:S(2)}, u32[]{:S(2)}) collective-permute-start(bf16[256,1024]{1,0:T(8,128)(2,1)} %get-tuple-element.38), channel_id=1, source_target_pairs={{0,1},{1,0},{2,3},{3,2},{4,5},{5,4},{6,7},{7,6},{8,9},{9,8},{10,11... | collective-permute-start | bytes 1572872 | tf_op jit(solution)/shard_map/ppermute | solution.py:149
  63.8 24.2 %collective-permute-start.1 = (bf16[256,1024]{1,0:T(8,128)(2,1)}, bf16[256,1024]{1,0:T(8,128)(2,1)}, u32[]{:S(2)}, u32[]{:S(2)}) collective-permute-start(bf16[256,1024]{1,0:T(8,128)(2,1)} %get-tuple-element.34), channel_id=1, source_target_pairs={{0,1},{1,0},{2,3},{3,2},{4,5},{5,4},{6,7},{7,6},{8,9},{9,8},{10,11... | collective-permute-start | bytes 1572872 | tf_op jit(solution)/shard_map/ppermute | solution.py:149
  64.5 23.5 %copy-start.12 = (bf16[1,256,1024]{2,1,0:T(8,128)(2,1)S(1)}, bf16[1,256,1024]{2,1,0:T(8,128)(2,1)}, u32[]{:S(2)}) copy-start(bf16[1,256,1024]{2,1,0:T(8,128)(2,1)} %get-tuple-element.33) | copy-start | bytes 1572868
  94.2 60.4 %all-to-all-start.2 = ((bf16[16,2,3,2,32,128]{5,4,3,2,1,0:T(8,128)(2,1)}), bf16[16,2,3,2,32,128]{5,4,3,2,1,0:T(8,128)(2,1)}, u32[]{:S(2)}, u32[]{:S(2)}) async-start(bf16[16,2,3,2,32,128]{5,4,3,2,1,0:T(8,128)(2,1)} %bitcast.174), calls=%async_computation.2 | async-start | bytes 3145728 | tf_op jit(solution)/shard_map/all_to_all | solution.py:254
  154.5 58.4 %all-to-all-start.3 = ((bf16[2,3,2,16,32,128]{5,4,2,1,0,3:T(8,128)(2,1)}), bf16[2,3,2,16,32,128]{5,4,2,1,0,3:T(8,128)(2,1)S(1)}, u32[]{:S(2)}, u32[]{:S(2)}) async-start(bf16[2,3,2,16,32,128]{5,4,2,1,0,3:T(8,128)(2,1)} %copy.93), calls=%async_computation.3 | async-start | bytes 3145728 | tf_op jit(solution)/shard_map/all_to_all | solution.py:267
  212.9 38.0 %all-to-all-start.5 = ((bf16[2,3,2,16,32,128]{5,4,2,1,0,3:T(8,128)(2,1)}), bf16[2,3,2,16,32,128]{5,4,2,1,0,3:T(8,128)(2,1)S(1)}, u32[]{:S(2)}, u32[]{:S(2)}) async-start(bf16[2,3,2,16,32,128]{5,4,2,1,0,3:T(8,128)(2,1)} %copy.99), calls=%async_computation.5 | async-start | bytes 3145728 | tf_op jit(solution)/shard_map/all_to_all | solution.py:267
  221.7 40.0 %collective-permute-start.8 = (bf16[256,1024]{1,0:T(8,128)(2,1)}, bf16[256,1024]{1,0:T(8,128)(2,1)}, u32[]{:S(2)}, u32[]{:S(2)}) collective-permute-start(bf16[256,1024]{1,0:T(8,128)(2,1)} %get-tuple-element.49), channel_id=1, source_target_pairs={{0,1},{1,0},{2,3},{3,2},{4,5},{5,4},{6,7},{7,6},{8,9},{9,8},{10,11... | collective-permute-start | bytes 1572872 | tf_op jit(solution)/shard_map/ppermute | solution.py:149
  224.3 39.9 %collective-permute-start.9 = (bf16[256,1024]{1,0:T(8,128)(2,1)}, bf16[256,1024]{1,0:T(8,128)(2,1)}, u32[]{:S(2)}, u32[]{:S(2)}) collective-permute-start(bf16[256,1024]{1,0:T(8,128)(2,1)} %get-tuple-element.51), channel_id=1, source_target_pairs={{0,1},{1,0},{2,3},{3,2},{4,5},{5,4},{6,7},{7,6},{8,9},{9,8},{10,11... | collective-permute-start | bytes 1572872 | tf_op jit(solution)/shard_map/ppermute | solution.py:149
  225.9 40.8 %collective-permute-start.6 = (bf16[256,1024]{1,0:T(8,128)(2,1)}, bf16[256,1024]{1,0:T(8,128)(2,1)}, u32[]{:S(2)}, u32[]{:S(2)}) collective-permute-start(bf16[256,1024]{1,0:T(8,128)(2,1)} %get-tuple-element.57), channel_id=1, source_target_pairs={{0,1},{1,0},{2,3},{3,2},{4,5},{5,4},{6,7},{7,6},{8,9},{9,8},{10,11... | collective-permute-start | bytes 1572872 | tf_op jit(solution)/shard_map/ppermute | solution.py:149
  231.8 28.3 %copy-start.19 = (bf16[2,256,1024]{2,1,0:T(8,128)(2,1)S(1)}, bf16[2,256,1024]{2,1,0:T(8,128)(2,1)}, u32[]{:S(2)}) copy-start(bf16[2,256,1024]{2,1,0:T(8,128)(2,1)} %get-tuple-element.24) | copy-start | bytes 3145732
  231.9 29.8 %copy-start.6 = (bf16[1,256,1024]{2,1,0:T(8,128)(2,1)S(1)}, bf16[1,256,1024]{2,1,0:T(8,128)(2,1)}, u32[]{:S(2)}) copy-start(bf16[1,256,1024]{2,1,0:T(8,128)(2,1)} %get-tuple-element.50) | copy-start | bytes 1572868
  250.9 27.3 %all-to-all-start.4 = ((bf16[2,16,2,32,128]{4,3,2,0,1:T(8,128)(2,1)}), bf16[2,16,2,32,128]{4,3,2,0,1:T(8,128)(2,1)}, u32[]{:S(2)}, u32[]{:S(2)}) async-start(bf16[2,16,2,32,128]{4,3,2,0,1:T(8,128)(2,1)} %copy.95), calls=%async_computation.4 | async-start | bytes 1048576 | tf_op jit(solution)/shard_map/all_to_all | solution.py:277
  260.2 14.2 %collective-permute-start.7 = (bf16[256,1024]{1,0:T(8,128)(2,1)S(1)}, bf16[256,1024]{1,0:T(8,128)(2,1)S(1)}, u32[]{:S(2)}, u32[]{:S(2)}) collective-permute-start(bf16[256,1024]{1,0:T(8,128)(2,1)S(1)} %get-tuple-element.59), channel_id=1, source_target_pairs={{0,1},{1,0},{2,3},{3,2},{4,5},{5,4},{6,7},{7,6},{8,9},{9,8},{10,11... | collective-permute-start | bytes 1572872 | tf_op jit(solution)/shard_map/ppermute | solution.py:149
  278.2 20.2 %all-to-all-start.6 = ((bf16[2,16,2,32,128]{4,3,2,0,1:T(8,128)(2,1)}), bf16[2,16,2,32,128]{4,3,2,0,1:T(8,128)(2,1)S(1)}, u32[]{:S(2)}, u32[]{:S(2)}) async-start(bf16[2,16,2,32,128]{4,3,2,0,1:T(8,128)(2,1)} %copy.101), calls=%async_computation.6 | async-start | bytes 1048576 | tf_op jit(solution)/shard_map/all_to_all | solution.py:277
  301.6 9.2 %collective-permute-start.11 = (bf16[256,512]{1,0:T(8,128)(2,1)S(1)}, bf16[256,512]{1,0:T(8,128)(2,1)S(1)}, u32[]{:S(2)}, u32[]{:S(2)}) collective-permute-start(bf16[256,512]{1,0:T(8,128)(2,1)S(1)} %get-tuple-element.63), channel_id=1, source_target_pairs={{0,1},{1,0},{2,3},{3,2},{4,5},{5,4},{6,7},{7,6},{8,9},{9,8},{10,11... | collective-permute-start | bytes 786440 | tf_op jit(solution)/shard_map/ppermute | solution.py:149
  303.2 12.3 %collective-permute-start.10 = (bf16[256,512]{1,0:T(8,128)(2,1)S(1)}, bf16[256,512]{1,0:T(8,128)(2,1)S(1)}, u32[]{:S(2)}, u32[]{:S(2)}) collective-permute-start(bf16[256,512]{1,0:T(8,128)(2,1)S(1)} %get-tuple-element.67), channel_id=1, source_target_pairs={{0,1},{1,0},{2,3},{3,2},{4,5},{5,4},{6,7},{7,6},{8,9},{9,8},{10,11... | collective-permute-start | bytes 786440 | tf_op jit(solution)/shard_map/ppermute | solution.py:149
  (22 other events, 96.8 us)
